TPU v7x, 32 devices: a whole 2x2x4 slice. The times are simulated.
32 devices in a mesh: cells: 8 (over z, y), slab: 4 (over x, core).
Axes of the slice: x: 2, y: 2, z: 4, core: 2. Of those that a mesh axis runs over, the one named last changes fastest.
Arguments:
- grad: float32 [2, 2, 64, 8192], P(None, None, 'slab', 'cells'), may hold values from -6 to 6
- acc_block: float32 [2, 4, 64, 8192], P(None, None, 'slab', 'cells')
- mobility: float32 [2, 2, 64, 8192], P(None, None, 'slab', 'cells'), may hold values from 0.2 to 1.5
- store: float32 [2, 2, 64, 8192], P(None, None, 'slab', 'cells'), may hold values from 0.1 to 0.5
- trans_h: float32 [64, 8192], P('slab', 'cells'), may hold values from 0.3 to 3
- trans_v: float32 [64, 8192], P('slab', 'cells'), may hold values from 0.3 to 3
- fault_near: int32 [4, 16384], P('slab', 'cells'), may hold values from 0 to 16383
- fault_far: int32 [4, 16384], P('slab', 'cells'), may hold values from 0 to 16383
- fault_trans: float32 [4, 16384], P('slab', 'cells'), may hold values from 0.3 to 3
- fault_count: int32 [4, 8], P('slab', 'cells'), may hold values from 256 to 2048, as said below
- compl_cell: int32 [4, 1024], P('slab', 'cells'), may hold values from 0 to 16383
- compl_well: int32 [4, 1024], P('slab', 'cells'), may hold values from 0 to 15, as said below
- compl_wi: float32 [4, 1024], P('slab', 'cells'), may hold values from 0.5 to 5
Outputs:
- adjoint: float32 [2, 2, 64, 8192], P(None, None, 'slab', 'cells')
- res_history: float32 [2, 2], replicated
Inputs may be any that keep to these rules, and one draw needn't show every extreme that they name: `fault_count`: slots past a pair's count are padding; in every draw some pair of column blocks c, c+1 with c < 7 holds exactly 2048 live slots; the count of the last column block is unused. `compl_well`: every well of a group has at least one completion on the group's device of slab 0.
All inputs are finite; a program needn't handle non-finite values.
Results may differ from a plain program's by a relative error of at most 0.0001.
Values sent between devices are 32-bit elements; how exact they have to be, the bound alone decides.
No kernel may reach another device: no remote copies, remote signals or barrier semaphores. Data moves between devices by JAX's collectives and lax.ppermute only.
A program may use at most 128 MiB of HBM per device.

v0:
```python
import jax
import jax.numpy as jnp
from jax import lax
from jax.sharding import PartitionSpec as P

WELLS = 16
NSTEPS = 2


def shifted(value, axis, by):
    length = lax.axis_size(axis)
    pairs = [(i, i + by) for i in range(length) if 0 <= i + by < length]
    return lax.ppermute(value, axis, pairs)


def global_sum(values):
    stacked = lax.psum(jnp.stack(values), "slab")
    count = lax.axis_size("cells")
    if count & (count - 1):
        stacked = lax.psum(stacked, "cells")
    else:
        step = 1
        while step < count:
            stacked = stacked + lax.ppermute(
                stacked, "cells", [(i, i ^ step) for i in range(count)]
            )
            step *= 2
    return [stacked[i] for i in range(len(values))]


def split3(value):
    high = value.astype(jnp.bfloat16)
    rest = value - high.astype(value.dtype)
    middle = rest.astype(jnp.bfloat16)
    low = (rest - middle.astype(value.dtype)).astype(jnp.bfloat16)
    return high, middle, low


def onehot_dot(value, onehot, dims):
    total = None
    for piece in split3(value):
        part = lax.dot_general(
            piece, onehot, (dims, ((), ())), preferred_element_type=jnp.float32
        )
        total = part if total is None else total + part
    return total


def per_device(
    grad,
    acc_block,
    mobility,
    store,
    trans_h,
    trans_v,
    fault_near,
    fault_far,
    fault_trans,
    fault_count,
    compl_cell,
    compl_well,
    compl_wi,
):
    highest = lax.Precision.HIGHEST
    layer_count, column_count = trans_h.shape
    cells_size = lax.axis_size("cells")
    slab_size = lax.axis_size("slab")
    cells_place = lax.axis_index("cells")
    slab_place = lax.axis_index("slab")
    column_ids = lax.broadcasted_iota(jnp.int32, (layer_count, column_count), 1)
    layer_ids = lax.broadcasted_iota(jnp.int32, (layer_count, column_count), 0)
    zero_value = jnp.zeros((), trans_h.dtype)
    trans_east = jnp.where(
        (cells_place == cells_size - 1) & (column_ids == column_count - 1), zero_value, trans_h
    )
    trans_down = jnp.where(
        (slab_place == slab_size - 1) & (layer_ids == layer_count - 1), zero_value, trans_v
    )
    slot_count = fault_near.size
    slot_live = (jnp.arange(slot_count, dtype=jnp.int32) < fault_count.reshape(())) & (
        cells_place < cells_size - 1
    )
    weight_here = jnp.where(slot_live, fault_trans.reshape(-1), zero_value)
    from_left_setup = shifted(jnp.concatenate([trans_east[:, -1], weight_here]), "cells", 1)
    east_edge = from_left_setup[:layer_count]
    weight_left = from_left_setup[layer_count:]
    down_edge = shifted(trans_down[-1, :], "slab", 1)
    trans_west = jnp.concatenate([east_edge[:, None], trans_east[:, :-1]], axis=1)
    trans_up = jnp.concatenate([down_edge[None, :], trans_down[:-1, :]], axis=0)
    face_total = trans_east + trans_west + trans_down + trans_up

    column_iota = jnp.arange(column_count, dtype=jnp.int32)
    layer_iota = jnp.arange(layer_count, dtype=jnp.int32)

    def locate(cells):
        cells = cells.reshape(-1)
        onehot = (cells % column_count)[:, None] == column_iota[None, :]
        rows = (layer_iota[:, None] == (cells // column_count)[None, :]).astype(jnp.float32)
        return onehot.astype(jnp.bfloat16), rows

    def gather(field, where):
        onehot, rows = where
        parts = field.shape[0]
        flat = field.reshape(parts * layer_count, column_count)
        picked = onehot_dot(flat, onehot, ((1,), (1,)))
        picked = picked.reshape(parts, layer_count, -1) * rows[None]
        return jnp.sum(picked, axis=1)

    def scatter(values, where):
        onehot, rows = where
        parts = values.shape[0]
        spread = (values[:, None, :] * rows[None]).reshape(parts * layer_count, -1)
        placed = onehot_dot(spread, onehot, ((1,), (0,)))
        return placed.reshape(parts, layer_count, column_count)

    near_at = locate(fault_near)
    far_at = locate(fault_far)
    well_at = locate(compl_cell)
    well_index = compl_wi.reshape(-1)
    well_onehot = (
        compl_well.reshape(-1)[:, None] == jnp.arange(WELLS, dtype=jnp.int32)[None, :]
    ).astype(trans_h.dtype)

    def inverse_of(newton):
        block = acc_block[newton]
        mobile = mobility[newton]
        diag_first = block[0] + mobile[0] * face_total
        diag_second = block[3] + mobile[1] * face_total
        determinant = diag_first * diag_second - block[1] * block[2]
        return (
            diag_second / determinant,
            -block[1] / determinant,
            -block[2] / determinant,
            diag_first / determinant,
        )

    def precondition(inverse, residual):
        inverse_aa, inverse_ab, inverse_ba, inverse_bb = inverse
        return jnp.stack(
            [
                inverse_aa * residual[0] + inverse_ab * residual[1],
                inverse_ba * residual[0] + inverse_bb * residual[1],
            ]
        )

    def operator(fields, mobile, block):
        count = fields.shape[0]
        scaled = (mobile * fields).reshape(count * 2, layer_count, column_count)
        picks_near = gather(scaled, near_at)
        picks_far = gather(scaled, far_at)
        from_left = shifted(jnp.concatenate([scaled[:, :, -1], picks_near], axis=1), "cells", 1)
        from_right = shifted(jnp.concatenate([scaled[:, :, 0], picks_far], axis=1), "cells", -1)
        from_above = shifted(scaled[:, -1, :], "slab", 1)
        from_below = shifted(scaled[:, 0, :], "slab", -1)
        west = jnp.concatenate([from_left[:, :layer_count, None], scaled[:, :, :-1]], axis=2)
        east = jnp.concatenate([scaled[:, :, 1:], from_right[:, :layer_count, None]], axis=2)
        above = jnp.concatenate([from_above[:, None, :], scaled[:, :-1, :]], axis=1)
        below = jnp.concatenate([scaled[:, 1:, :], from_below[:, None, :]], axis=1)
        laplace = (
            trans_east * (scaled - east)
            + trans_west * (scaled - west)
            + trans_down * (scaled - below)
            + trans_up * (scaled - above)
        )
        flux_right = weight_here * (picks_near - from_right[:, layer_count:])
        flux_left = weight_left * (from_left[:, layer_count:] - picks_far)
        fault_term = scatter(flux_right, near_at) - scatter(flux_left, far_at)
        laplace = (laplace + fault_term).reshape(count, 2, layer_count, column_count)
        pressure = fields[:, 0]
        values = gather(pressure, well_at)
        local = jnp.concatenate(
            [
                jnp.dot(well_index, well_onehot, precision=highest)[None],
                jnp.dot(well_index * values, well_onehot, precision=highest),
            ]
        )
        summed = lax.psum(local, "slab")
        back = jnp.dot(summed[1:] / summed[0], well_onehot.T, precision=highest)
        well_term = scatter(well_index * (values - back), well_at)
        first = (
            block[:, 0] * fields[:, 0]
            + block[:, 1] * fields[:, 1]
            + laplace[:, 0]
            + well_term
        )
        second = block[:, 2] * fields[:, 0] + block[:, 3] * fields[:, 1] + laplace[:, 1]
        return jnp.stack([first, second], axis=1)

    inverse_last = inverse_of(1)
    inverse_first = inverse_of(0)
    grad_last = grad[1]
    grad_first = grad[0]
    z_last = precondition(inverse_last, grad_last)
    carried = store[0] * z_last
    fields = jnp.stack(
        [z_last, precondition(inverse_first, grad_first), precondition(inverse_first, carried)]
    )
    mobile = jnp.stack([mobility[1], mobility[0], mobility[0]])
    block = jnp.stack([acc_block[1], acc_block[0], acc_block[0]])
    images = operator(fields, mobile, block)
    image_last, direct, coupled = images[0], images[1], images[2]
    (
        along_last,
        energy_last,
        norm_last,
        grad_direct,
        grad_coupled,
        carried_direct,
        carried_coupled,
        direct_direct,
        direct_coupled,
        coupled_coupled,
    ) = global_sum(
        [
            jnp.sum(grad_last * image_last),
            jnp.sum(image_last * image_last),
            jnp.sum(grad_last * grad_last),
            jnp.sum(grad_first * direct),
            jnp.sum(grad_first * coupled),
            jnp.sum(carried * direct),
            jnp.sum(carried * coupled),
            jnp.sum(direct * direct),
            jnp.sum(direct * coupled),
            jnp.sum(coupled * coupled),
        ]
    )
    alpha_last = along_last / energy_last
    along_first = grad_direct + alpha_last * (grad_coupled + carried_direct) + (
        alpha_last * alpha_last
    ) * carried_coupled
    energy_first = direct_direct + (2.0 * alpha_last) * direct_coupled + (
        alpha_last * alpha_last
    ) * coupled_coupled
    alpha_first = along_first / energy_first
    solution_last = alpha_last * z_last
    residual_last = grad_last - alpha_last * image_last
    residual_first = grad_first + store[0] * solution_last
    solution_first = alpha_first * precondition(inverse_first, residual_first)
    image_first = direct + alpha_last * coupled
    closing_first = residual_first - alpha_first * image_first
    norm_first, end_first, end_last = global_sum(
        [
            jnp.sum(residual_first * residual_first),
            jnp.sum(closing_first * closing_first),
            jnp.sum(residual_last * residual_last),
        ]
    )
    norms = jnp.sqrt(jnp.stack([norm_first, end_first, norm_last, end_last])).reshape(2, 2)
    return (jnp.stack([solution_first, solution_last]), norms)


def solution(mesh):
    placed = (
        P(None, None, "slab", "cells"),
        P(None, None, "slab", "cells"),
        P(None, None, "slab", "cells"),
        P(None, None, "slab", "cells"),
        P("slab", "cells"),
        P("slab", "cells"),
        P("slab", "cells"),
        P("slab", "cells"),
        P("slab", "cells"),
        P("slab", "cells"),
        P("slab", "cells"),
        P("slab", "cells"),
        P("slab", "cells"),
    )
    return jax.shard_map(
        per_device,
        mesh=mesh,
        in_specs=placed,
        out_specs=(P(None, None, "slab", "cells"), P()),
        check_vma=False,
    )
```

profile of v0, /device:TPU:0, one launch (start us, length us, event | category | flops | bytes accessed | tf_op | source)
XLA Modules:
  0.0 140.2 jit_solution(15573614585365710244)
XLA Ops:
  3.2 4.9 %collective-permute-start = (f32[2064]{0:T(1024)S(1)}, f32[2064]{0:T(1024)S(1)}, u32[]{:S(2)}, u32[]{:S(2)}) collective-permute-start(f32[2064]{0:T(1024)S(1)} %pad_maximum_fusion.9), channel_id=1, source_target_pairs={{0,4},{4,8},{8,12},{12,16},{16,20},{20,24},{24,28},{1,5},{5,9},{9,... | collective-permute-start | bytes 24776 | tf_op jit(solution)/shard_map/ppermute | solution.py:13
  9.0 1.5 %collective-permute-start.1 = (f32[1024]{0:T(1024)S(1)}, f32[1024]{0:T(1024)S(1)}, u32[]{:S(2)}, u32[]{:S(2)}) collective-permute-start(f32[1024]{0:T(1024)S(1)} %bitcast.389), channel_id=1, source_target_pairs={{0,1},{1,2},{2,3},{4,5},{5,6},{6,7},{8,9},{9,10},{10,11},{12,13},{... | collective-permute-start | bytes 12296 | tf_op jit(solution)/shard_map/ppermute | solution.py:13
  19.2 7.7 %psum.21 = f32[4,16]{1,0:T(4,128)S(1)} all-reduce(f32[4,16]{1,0:T(4,128)S(1)} %pad_maximum_fusion.10), channel_id=1, replica_groups=mesh['cells'=8,'slab'=4] {'slab'}, use_global_device_ids=true, to_apply=%region_3.4 | all-reduce | flops 64 | bytes 512 | tf_op jit(solution)/shard_map/psum | solution.py:177
  27.3 2.1 %fusion.9 = f32[96,2048]{1,0:T(8,128)S(1)} fusion(bf16[96,1024]{1,0:T(8,128)(2,1)S(1)} %get-tuple-element.50, s32[2048]{0:T(1024)S(1)} %add_select_fusion.1), kind=kOutput, calls=%fused_computation.11 | convolution fusion | flops 404750336 | bytes 991232 | tf_op jit(solution)/shard_map/dot_general | solution.py:42
  29.4 2.1 %fusion.10 = f32[96,2048]{1,0:T(8,128)S(1)} fusion(bf16[96,1024]{1,0:T(8,128)(2,1)S(1)} %get-tuple-element.49, s32[2048]{0:T(1024)S(1)} %add_select_fusion.1), kind=kOutput, calls=%fused_computation.12 | convolution fusion | flops 404750336 | bytes 991232 | tf_op jit(solution)/shard_map/dot_general | solution.py:42
  31.5 2.1 %fusion.3 = f32[96,2048]{1,0:T(8,128)S(1)} fusion(bf16[96,1024]{1,0:T(8,128)(2,1)S(1)} %get-tuple-element.50, s32[2048]{0:T(1024)S(1)} %add_select_fusion), kind=kOutput, calls=%fused_computation.4 | convolution fusion | flops 404750336 | bytes 991232 | tf_op jit(solution)/shard_map/dot_general | solution.py:42
  33.6 2.1 %fusion.4 = f32[96,2048]{1,0:T(8,128)S(1)} fusion(bf16[96,1024]{1,0:T(8,128)(2,1)S(1)} %get-tuple-element.49, s32[2048]{0:T(1024)S(1)} %add_select_fusion), kind=kOutput, calls=%fused_computation.5 | convolution fusion | flops 404750336 | bytes 991232 | tf_op jit(solution)/shard_map/dot_general | solution.py:42
  37.3 2.9 %fusion.27 = f32[96,2048]{1,0:T(8,128)S(1)} fusion(f32[96,2048]{1,0:T(8,128)S(1)} %fusion.3, f32[96,2048]{1,0:T(8,128)S(1)} %fusion.4, bf16[96,1024]{1,0:T(8,128)(2,1)S(1)} %bitcast_convert_fusion.2, s32[2048]{0:T(1024)S(1)} %add_select_fusion), kind=kOutput, calls=%fused_computation.29 | convolution fusion | flops 405143552 | bytes 2564096 | tf_op jit(solution)/shard_map/dot_general | solution.py:42
  41.1 4.2 %collective-permute-start.3 = (f32[6,2064]{1,0:T(8,128)}, f32[6,2064]{1,0:T(8,128)}, u32[]{:S(2)}, u32[]{:S(2)}) collective-permute-start(f32[6,2064]{1,0:T(8,128)} %pad_maximum_fusion.6), channel_id=1, source_target_pairs={{0,4},{4,8},{8,12},{12,16},{16,20},{20,24},{24,28},{1,5},{5,9},{9,... | collective-permute-start | bytes 148616 | tf_op jit(solution)/shard_map/ppermute | solution.py:13
  45.2 2.9 %fusion.25 = f32[96,2048]{1,0:T(8,128)S(1)} fusion(f32[96,2048]{1,0:T(8,128)S(1)} %fusion.9, f32[96,2048]{1,0:T(8,128)S(1)} %fusion.10, bf16[96,1024]{1,0:T(8,128)(2,1)S(1)} %bitcast_convert_fusion.2, s32[2048]{0:T(1024)S(1)} %copy-done.46), kind=kOutput, calls=%fused_computation.27 | convolution fusion | flops 405143552 | bytes 2564096 | tf_op jit(solution)/shard_map/dot_general | solution.py:42
  52.2 3.6 %collective-permute-start.5 = (f32[6,1024]{1,0:T(8,128)}, f32[6,1024]{1,0:T(8,128)}, u32[]{:S(2)}, u32[]{:S(2)}) collective-permute-start(f32[6,1024]{1,0:T(8,128)} %bitcast.353), channel_id=1, source_target_pairs={{0,1},{1,2},{2,3},{4,5},{5,6},{6,7},{8,9},{9,10},{10,11},{12,13},{... | collective-permute-start | bytes 73736 | tf_op jit(solution)/shard_map/ppermute | solution.py:13
  66.4 2.5 %fusion.7 = f32[96,1024]{1,0:T(8,128)} fusion(bf16[96,2048]{1,0:T(8,128)(2,1)S(1)} %get-tuple-element.34, s32[2048]{0:T(1024)S(1)} %copy-done.47), kind=kOutput, calls=%fused_computation.9 | convolution fusion | flops 404750336 | bytes 794624 | tf_op jit(solution)/shard_map/dot_general | solution.py:42
  68.9 2.5 %fusion.1 = f32[96,1024]{1,0:T(8,128)} fusion(bf16[96,2048]{1,0:T(8,128)(2,1)S(1)} %get-tuple-element.32, s32[2048]{0:T(1024)S(1)} %copy-done.44), kind=kOutput, calls=%fused_computation.2 | convolution fusion | flops 404750336 | bytes 794624 | tf_op jit(solution)/shard_map/dot_general | solution.py:42
  74.1 2.9 %fusion.28 = f32[96,1024]{1,0:T(8,128)S(1)} fusion(f32[96,1024]{1,0:T(8,128)} %fusion.7, bf16[96,2048]{1,0:T(8,128)(2,1)} %bitcast_convert_fusion, s32[2048]{0:T(1024)} %copy-done.45), kind=kOutput, calls=%fused_computation.30 | convolution fusion | flops 404848640 | bytes 1187840 | tf_op jit(solution)/shard_map/dot_general | solution.py:42
  77.1 1.8 %fusion.29 = f32[96,1024]{1,0:T(8,128)S(1)} fusion(f32[96,1024]{1,0:T(8,128)S(1)} %fusion.28, bf16[96,2048]{1,0:T(8,128)(2,1)S(1)} %copy-done.27, s32[2048]{0:T(1024)S(1)} %copy-done.48), kind=kOutput, calls=%fused_computation.31 | convolution fusion | flops 404848640 | bytes 1187840 | tf_op jit(solution)/shard_map/dot_general | solution.py:42
  78.9 1.8 %fusion.30 = f32[96,1024]{1,0:T(8,128)S(1)} fusion(f32[96,1024]{1,0:T(8,128)S(1)} %copy-done.55, bf16[96,2048]{1,0:T(8,128)(2,1)S(1)} %copy-done.29, s32[2048]{0:T(1024)S(1)} %copy-done.44), kind=kOutput, calls=%fused_computation.32 | convolution fusion | flops 404848640 | bytes 1187840 | tf_op jit(solution)/shard_map/dot_general | solution.py:42
  80.8 1.8 %fusion.32 = f32[96,1024]{1,0:T(8,128)S(1)} fusion(f32[96,1024]{1,0:T(8,128)S(1)} %fusion.29, f32[96,1024]{1,0:T(8,128)S(1)} %fusion.30, bf16[96,2048]{1,0:T(8,128)(2,1)S(1)} %copy-done.28, s32[2048]{0:T(1024)S(1)} %copy-done.44), kind=kOutput, calls=%fused_computation.34 | convolution fusion | flops 404946944 | bytes 1581056 | tf_op jit(solution)/shard_map/dot_general | solution.py:42
  85.3 6.6 %stack.145 = f32[10]{0:T(128)S(1)} concatenate(f32[1]{0:T(128)} %bitcast.65, f32[1]{0:T(128)} %bitcast.66, f32[1]{0:T(128)} %bitcast.67, f32[1]{0:T(128)} %bitcast.70, f32[1]{0:T(128)} %bitcast.72, f32[1]{0:T(128)} %bitcast.73, f32[1]{0:T(128)} %bitcast.74, f32[1]{0:T(128)} %bitcast.75, f32[1]{0:T(128)} %bitcast.76, f32[1]{0:T(128)} %bitcast.77), dimensions={0} | concatenate | bytes 80 | tf_op jit(solution)/shard_map/stack | solution.py:17
  91.9 6.5 %psum.22 = f32[10]{0:T(128)S(1)} all-reduce(f32[10]{0:T(128)S(1)} %stack.145), channel_id=1, replica_groups=mesh['cells'=8,'slab'=4] {'slab'}, use_global_device_ids=true, to_apply=%region_14.15 | all-reduce | flops 10 | bytes 80 | tf_op jit(solution)/shard_map/psum | solution.py:17
  98.4 2.7 %collective-permute-start.6 = (f32[10]{0:T(128)S(1)}, f32[10]{0:T(128)S(1)}, u32[]{:S(2)}, u32[]{:S(2)}) collective-permute-start(f32[10]{0:T(128)S(1)} %psum.22), channel_id=1, source_target_pairs={{0,4},{4,0},{8,12},{12,8},{16,20},{20,16},{24,28},{28,24},{1,5},{5... | collective-permute-start | bytes 128 | tf_op jit(solution)/shard_map/ppermute | solution.py:24
  101.1 1.5 %collective-permute-done.6 = f32[10]{0:T(128)S(1)} collective-permute-done((f32[10]{0:T(128)S(1)}, f32[10]{0:T(128)S(1)}, u32[]{:S(2)}, u32[]{:S(2)}) %collective-permute-start.6) | collective-permute-done | bytes 72 | tf_op jit(solution)/shard_map/ppermute | solution.py:24
  102.6 2.4 %collective-permute-start.7 = (f32[10]{0:T(128)S(1)}, f32[10]{0:T(128)S(1)}, u32[]{:S(2)}, u32[]{:S(2)}) collective-permute-start(f32[10]{0:T(128)S(1)} %add.236), channel_id=1, source_target_pairs={{0,8},{4,12},{8,0},{12,4},{16,24},{20,28},{24,16},{28,20},{1,9},{5... | collective-permute-start | bytes 128 | tf_op jit(solution)/shard_map/ppermute | solution.py:24
  105.0 1.5 %collective-permute-done.7 = f32[10]{0:T(128)S(1)} collective-permute-done((f32[10]{0:T(128)S(1)}, f32[10]{0:T(128)S(1)}, u32[]{:S(2)}, u32[]{:S(2)}) %collective-permute-start.7) | collective-permute-done | bytes 72 | tf_op jit(solution)/shard_map/ppermute | solution.py:24
  106.5 3.0 %collective-permute-start.8 = (f32[10]{0:T(128)S(1)}, f32[10]{0:T(128)S(1)}, u32[]{:S(2)}, u32[]{:S(2)}) collective-permute-start(f32[10]{0:T(128)S(1)} %add.237), channel_id=1, source_target_pairs={{0,16},{4,20},{8,24},{12,28},{16,0},{20,4},{24,8},{28,12},{1,17},{... | collective-permute-start | bytes 128 | tf_op jit(solution)/shard_map/ppermute | solution.py:24
  109.5 1.5 %collective-permute-done.8 = f32[10]{0:T(128)S(1)} collective-permute-done((f32[10]{0:T(128)S(1)}, f32[10]{0:T(128)S(1)}, u32[]{:S(2)}, u32[]{:S(2)}) %collective-permute-start.8) | collective-permute-done | bytes 72 | tf_op jit(solution)/shard_map/ppermute | solution.py:24
  118.4 2.0 %pad_maximum_fusion.11 = f32[3]{0:T(128)S(1)} fusion(f32[1]{0:T(128)} %bitcast.93, f32[1]{0:T(128)} %bitcast.92, f32[1]{0:T(128)} %bitcast.91), kind=kLoop, calls=%fused_computation.241 | loop fusion | flops 6 | bytes 24 | tf_op jit(solution)/shard_map/stack | solution.py:17
  120.4 5.7 %psum.23 = f32[3]{0:T(128)S(1)} all-reduce(f32[3]{0:T(128)S(1)} %pad_maximum_fusion.11), channel_id=1, replica_groups=mesh['cells'=8,'slab'=4] {'slab'}, use_global_device_ids=true, to_apply=%region_18.19 | all-reduce | flops 3 | bytes 24 | tf_op jit(solution)/shard_map/psum | solution.py:17
  126.1 1.6 %collective-permute-start.9 = (f32[3]{0:T(128)S(1)}, f32[3]{0:T(128)S(1)}, u32[]{:S(2)}, u32[]{:S(2)}) collective-permute-start(f32[3]{0:T(128)S(1)} %psum.23), channel_id=1, source_target_pairs={{0,4},{4,0},{8,12},{12,8},{16,20},{20,16},{24,28},{28,24},{1,5},{5... | collective-permute-start | bytes 44 | tf_op jit(solution)/shard_map/ppermute | solution.py:24
  129.7 1.9 %collective-permute-start.10 = (f32[3]{0:T(128)S(1)}, f32[3]{0:T(128)S(1)}, u32[]{:S(2)}, u32[]{:S(2)}) collective-permute-start(f32[3]{0:T(128)S(1)} %add.249), channel_id=1, source_target_pairs={{0,8},{4,12},{8,0},{12,4},{16,24},{20,28},{24,16},{28,20},{1,9},{5... | collective-permute-start | bytes 44 | tf_op jit(solution)/shard_map/ppermute | solution.py:24
  131.6 1.6 %collective-permute-done.10 = f32[3]{0:T(128)S(1)} collective-permute-done((f32[3]{0:T(128)S(1)}, f32[3]{0:T(128)S(1)}, u32[]{:S(2)}, u32[]{:S(2)}) %collective-permute-start.10) | collective-permute-done | bytes 44 | tf_op jit(solution)/shard_map/ppermute | solution.py:24
  133.2 2.9 %collective-permute-start.11 = (f32[3]{0:T(128)S(1)}, f32[3]{0:T(128)S(1)}, u32[]{:S(2)}, u32[]{:S(2)}) collective-permute-start(f32[3]{0:T(128)S(1)} %add.250), channel_id=1, source_target_pairs={{0,16},{4,20},{8,24},{12,28},{16,0},{20,4},{24,8},{28,12},{1,17},{... | collective-permute-start | bytes 44 | tf_op jit(solution)/shard_map/ppermute | solution.py:24
  136.1 1.5 %collective-permute-done.11 = f32[3]{0:T(128)S(1)} collective-permute-done((f32[3]{0:T(128)S(1)}, f32[3]{0:T(128)S(1)}, u32[]{:S(2)}, u32[]{:S(2)}) %collective-permute-start.11) | collective-permute-done | bytes 44 | tf_op jit(solution)/shard_map/ppermute | solution.py:24
  (214 shorter events, 39.8 us)
Async XLA Ops:
  0.6 13.7 %copy-start.42 = (f32[1,2048]{1,0:T(1,128)S(1)}, f32[1,2048]{1,0:T(1,128)}, u32[]{:S(2)}) copy-start(f32[1,2048]{1,0:T(1,128)} %param.21) | copy-start | bytes 24580
  0.6 12.2 %copy-start.40 = (s32[1,2048]{1,0:T(1,128)S(1)}, s32[1,2048]{1,0:T(1,128)}, u32[]{:S(2)}) copy-start(s32[1,2048]{1,0:T(1,128)} %param.20) | copy-start | bytes 24580
  0.7 13.0 %copy-start.41 = (s32[1,2048]{1,0:T(1,128)S(1)}, s32[1,2048]{1,0:T(1,128)}, u32[]{:S(2)}) copy-start(s32[1,2048]{1,0:T(1,128)} %param.19) | copy-start | bytes 24580
  0.7 13.7 %copy-start = (f32[2,4,16,1024]{3,2,1,0:T(8,128)S(1)}, f32[2,4,16,1024]{3,2,1,0:T(8,128)}, u32[]{:S(2)}) copy-start(f32[2,4,16,1024]{3,2,1,0:T(8,128)} %param.14) | copy-start | bytes 1572868
  2.3 13.2 %copy-start.16 = (f32[16,1024]{1,0:T(8,128)}, f32[16,1024]{1,0:T(8,128)S(1)}, u32[]{:S(2)}) copy-start(f32[16,1024]{1,0:T(8,128)S(1)} %broadcast_select_fusion.1) | copy-start | bytes 196612
  3.2 11.6 %collective-permute-start = (f32[2064]{0:T(1024)S(1)}, f32[2064]{0:T(1024)S(1)}, u32[]{:S(2)}, u32[]{:S(2)}) collective-permute-start(f32[2064]{0:T(1024)S(1)} %pad_maximum_fusion.9), channel_id=1, source_target_pairs={{0,4},{4,8},{8,12},{12,16},{16,20},{20,24},{24,28},{1,5},{5,9},{9,... | collective-permute-start | bytes 24776 | tf_op jit(solution)/shard_map/ppermute | solution.py:13
  9.0 6.4 %copy-start.18 = (f32[16,1024]{1,0:T(8,128)}, f32[16,1024]{1,0:T(8,128)S(1)}, u32[]{:S(2)}) copy-start(f32[16,1024]{1,0:T(8,128)S(1)} %broadcast_select_fusion) | copy-start | bytes 196612
  9.0 5.9 %collective-permute-start.1 = (f32[1024]{0:T(1024)S(1)}, f32[1024]{0:T(1024)S(1)}, u32[]{:S(2)}, u32[]{:S(2)}) collective-permute-start(f32[1024]{0:T(1024)S(1)} %bitcast.389), channel_id=1, source_target_pairs={{0,1},{1,2},{2,3},{4,5},{5,6},{6,7},{8,9},{9,10},{10,11},{12,13},{... | collective-permute-start | bytes 12296 | tf_op jit(solution)/shard_map/ppermute | solution.py:13
  11.2 7.5 %copy-start.51 = (s32[128]{0:T(128)}, s32[128]{0:T(128)S(1)}, u32[]{:S(2)}) copy-start(s32[128]{0:T(128)S(1)} %and_select_fusion.4) | copy-start | bytes 1540
  12.9 16.5 %copy-start.45 = (s32[2048]{0:T(1024)}, s32[2048]{0:T(1024)S(1)}, u32[]{:S(2)}) copy-start(s32[2048]{0:T(1024)S(1)} %add_select_fusion.1) | copy-start | bytes 24580
  13.7 23.6 %copy-start.43 = (s32[2048]{0:T(1024)}, s32[2048]{0:T(1024)S(1)}, u32[]{:S(2)}) copy-start(s32[2048]{0:T(1024)S(1)} %add_select_fusion) | copy-start | bytes 24580
  40.1 5.1 %copy-start.46 = (s32[2048]{0:T(1024)S(1)}, s32[2048]{0:T(1024)}, u32[]{:S(2)}) copy-start(s32[2048]{0:T(1024)} %copy-done.45) | copy-start | bytes 24580
  41.1 7.0 %copy-start.6 = (f32[16,2048]{1,0:T(8,128)S(1)}, f32[16,2048]{1,0:T(8,128)}, u32[]{:S(2)}) copy-start(f32[16,2048]{1,0:T(8,128)} %fusion.68) | copy-start | bytes 393220
  41.1 18.9 %collective-permute-start.3 = (f32[6,2064]{1,0:T(8,128)}, f32[6,2064]{1,0:T(8,128)}, u32[]{:S(2)}, u32[]{:S(2)}) collective-permute-start(f32[6,2064]{1,0:T(8,128)} %pad_maximum_fusion.6), channel_id=1, source_target_pairs={{0,4},{4,8},{8,12},{12,16},{16,20},{20,24},{24,28},{1,5},{5,9},{9,... | collective-permute-start | bytes 148616 | tf_op jit(solution)/shard_map/ppermute | solution.py:13
  48.1 9.0 %copy-start.50 = (f32[2064]{0:T(1024)S(1)}, f32[2064]{0:T(1024)}, u32[]{:S(2)}) copy-start(f32[2064]{0:T(1024)} %copy-done.49) | copy-start | bytes 24772
  48.3 8.8 %copy-start.26 = (f32[6,2048]{1,0:T(8,128)}, f32[6,2048]{1,0:T(8,128)S(1)}, u32[]{:S(2)}) copy-start(f32[6,2048]{1,0:T(8,128)S(1)} %multiply_reduce_fusion.1) | copy-start | bytes 147460
  49.0 14.6 %collective-permute-start.2 = (f32[6,2064]{1,0:T(8,128)}, f32[6,2064]{1,0:T(8,128)}, u32[]{:S(2)}, u32[]{:S(2)}) collective-permute-start(f32[6,2064]{1,0:T(8,128)} %pad_maximum_fusion.5), channel_id=1, source_target_pairs={{4,0},{8,4},{12,8},{16,12},{20,16},{24,20},{28,24},{5,1},{9,5},{13... | collective-permute-start | bytes 148616 | tf_op jit(solution)/shard_map/ppermute | solution.py:13
  50.3 6.9 %collective-permute-start.4 = (f32[6,1024]{1,0:T(8,128)S(1)}, f32[6,1024]{1,0:T(8,128)}, u32[]{:S(2)}, u32[]{:S(2)}) collective-permute-start(f32[6,1024]{1,0:T(8,128)S(1)} %bitcast.380), channel_id=1, source_target_pairs={{1,0},{2,1},{3,2},{5,4},{6,5},{7,6},{9,8},{10,9},{11,10},{13,12},{... | collective-permute-start | bytes 73736 | tf_op jit(solution)/shard_map/ppermute | solution.py:13
  52.2 6.4 %collective-permute-start.5 = (f32[6,1024]{1,0:T(8,128)}, f32[6,1024]{1,0:T(8,128)}, u32[]{:S(2)}, u32[]{:S(2)}) collective-permute-start(f32[6,1024]{1,0:T(8,128)} %bitcast.353), channel_id=1, source_target_pairs={{0,1},{1,2},{2,3},{4,5},{5,6},{6,7},{8,9},{9,10},{10,11},{12,13},{... | collective-permute-start | bytes 73736 | tf_op jit(solution)/shard_map/ppermute | solution.py:13
  74.1 3.0 %copy-start.48 = (s32[2048]{0:T(1024)S(1)}, s32[2048]{0:T(1024)}, u32[]{:S(2)}) copy-start(s32[2048]{0:T(1024)} %copy-done.45) | copy-start | bytes 24580
  83.7 33.8 %copy-start.12 = (f32[16,1024]{1,0:T(8,128)S(1)}, f32[16,1024]{1,0:T(8,128)}, u32[]{:S(2)}) copy-start(f32[16,1024]{1,0:T(8,128)} %copy-done.11) | copy-start | bytes 196612
  83.8 33.8 %copy-start.14 = (f32[16,1024]{1,0:T(8,128)S(1)}, f32[16,1024]{1,0:T(8,128)}, u32[]{:S(2)}) copy-start(f32[16,1024]{1,0:T(8,128)} %copy-done.13) | copy-start | bytes 196612
  83.8 33.8 %copy-start.35 = (f32[2,2,16,1024]{3,2,1,0:T(8,128)S(1)}, f32[2,2,16,1024]{3,2,1,0:T(8,128)}, u32[]{:S(2)}) copy-start(f32[2,2,16,1024]{3,2,1,0:T(8,128)} %param.16) | copy-start | bytes 786436
  85.3 35.0 %copy-start.10 = (f32[16,1024]{1,0:T(8,128)S(1)}, f32[16,1024]{1,0:T(8,128)}, u32[]{:S(2)}) copy-start(f32[16,1024]{1,0:T(8,128)} %copy-done.9) | copy-start | bytes 196612
  85.3 35.0 %copy-start.21 = (f32[16,1024]{1,0:T(8,128)S(1)}, f32[16,1024]{1,0:T(8,128)}, u32[]{:S(2)}) copy-start(f32[16,1024]{1,0:T(8,128)} %copy-done.20) | copy-start | bytes 196612
  85.3 35.0 %copy-start.23 = (f32[16,1024]{1,0:T(8,128)S(1)}, f32[16,1024]{1,0:T(8,128)}, u32[]{:S(2)}) copy-start(f32[16,1024]{1,0:T(8,128)} %copy-done.22) | copy-start | bytes 196612
  98.4 4.2 %collective-permute-start.6 = (f32[10]{0:T(128)S(1)}, f32[10]{0:T(128)S(1)}, u32[]{:S(2)}, u32[]{:S(2)}) collective-permute-start(f32[10]{0:T(128)S(1)} %psum.22), channel_id=1, source_target_pairs={{0,4},{4,0},{8,12},{12,8},{16,20},{20,16},{24,28},{28,24},{1,5},{5... | collective-permute-start | bytes 128 | tf_op jit(solution)/shard_map/ppermute | solution.py:24
  102.6 3.9 %collective-permute-start.7 = (f32[10]{0:T(128)S(1)}, f32[10]{0:T(128)S(1)}, u32[]{:S(2)}, u32[]{:S(2)}) collective-permute-start(f32[10]{0:T(128)S(1)} %add.236), channel_id=1, source_target_pairs={{0,8},{4,12},{8,0},{12,4},{16,24},{20,28},{24,16},{28,20},{1,9},{5... | collective-permute-start | bytes 128 | tf_op jit(solution)/shard_map/ppermute | solution.py:24
  106.5 4.6 %collective-permute-start.8 = (f32[10]{0:T(128)S(1)}, f32[10]{0:T(128)S(1)}, u32[]{:S(2)}, u32[]{:S(2)}) collective-permute-start(f32[10]{0:T(128)S(1)} %add.237), channel_id=1, source_target_pairs={{0,16},{4,20},{8,24},{12,28},{16,0},{20,4},{24,8},{28,12},{1,17},{... | collective-permute-start | bytes 128 | tf_op jit(solution)/shard_map/ppermute | solution.py:24
  126.1 3.6 %collective-permute-start.9 = (f32[3]{0:T(128)S(1)}, f32[3]{0:T(128)S(1)}, u32[]{:S(2)}, u32[]{:S(2)}) collective-permute-start(f32[3]{0:T(128)S(1)} %psum.23), channel_id=1, source_target_pairs={{0,4},{4,0},{8,12},{12,8},{16,20},{20,16},{24,28},{28,24},{1,5},{5... | collective-permute-start | bytes 44 | tf_op jit(solution)/shard_map/ppermute | solution.py:24
  129.7 3.5 %collective-permute-start.10 = (f32[3]{0:T(128)S(1)}, f32[3]{0:T(128)S(1)}, u32[]{:S(2)}, u32[]{:S(2)}) collective-permute-start(f32[3]{0:T(128)S(1)} %add.249), channel_id=1, source_target_pairs={{0,8},{4,12},{8,0},{12,4},{16,24},{20,28},{24,16},{28,20},{1,9},{5... | collective-permute-start | bytes 44 | tf_op jit(solution)/shard_map/ppermute | solution.py:24
  133.2 4.4 %collective-permute-start.11 = (f32[3]{0:T(128)S(1)}, f32[3]{0:T(128)S(1)}, u32[]{:S(2)}, u32[]{:S(2)}) collective-permute-start(f32[3]{0:T(128)S(1)} %add.250), channel_id=1, source_target_pairs={{0,16},{4,20},{8,24},{12,28},{16,0},{20,4},{24,8},{28,12},{1,17},{... | collective-permute-start | bytes 44 | tf_op jit(solution)/shard_map/ppermute | solution.py:24
  (36 other events, 52.4 us)
where the time goes:
time: 141 us; the launch traced here: 140 us
  starting transfers between devices  31.2 us (22%)
  matrix products  30.3 us (21%)
  other arithmetic  20.9 us (15%)
  local copies, waits for them, and re-layouts  20.7 us (15%)
  blocking collectives  19.8 us (14%)
  waiting for transfers between devices  8.96 us (6%)
  between operations  8.26 us (6%)
    dot_general x18, matrix products, onehot_dot(): lax.dot_general(piece, onehot, (dims, ((), ())), preferred_element_type=j...  29.7 us
    ppermute x6, starting transfers between devices, shifted(): return lax.ppermute(value, axis, pairs)  16.7 us
    ppermute x6, starting transfers between devices, global_sum(): lax.ppermute(stacked, 'cells', [(i, i ^ step) for i in range(count)])  14.5 us
    psum x2, blocking collectives, global_sum(): stacked = lax.psum(jnp.stack(values), 'slab')  12.1 us
    ppermute x6, waiting for transfers between devices, global_sum(): lax.ppermute(stacked, 'cells', [(i, i ^ step) for i in range(count)])  8.94 us
    psum x1, blocking collectives, operator(): summed = lax.psum(local, 'slab')  7.71 us
    another operation x1, local copies, waits for them, and re-layouts, global_sum(): stacked = lax.psum(jnp.stack(values), 'slab')  6.58 us
    unnamed x114, local copies, waits for them, and re-layouts  4.08 us
  transfers between devices with their start and end apart: 12, of which 6 were waited for; matrix products, arithmetic and copies ran while one was open for 13% of the time, Pallas kernels for 0%

commit v1 on v0

--- a/solution.py
+++ b/solution.py
@@ -13,8 +13,13 @@
     return lax.ppermute(value, axis, pairs)
 
 
+def stacked_sums(pairs):
+    products = jnp.stack([(left * right).reshape(-1) for left, right in pairs])
+    return jnp.sum(products, axis=1)
+
+
 def global_sum(values):
-    stacked = lax.psum(jnp.stack(values), "slab")
+    stacked = lax.psum(values, "slab")
     count = lax.axis_size("cells")
     if count & (count - 1):
         stacked = lax.psum(stacked, "cells")
@@ -25,7 +30,7 @@
                 stacked, "cells", [(i, i ^ step) for i in range(count)]
             )
             step *= 2
-    return [stacked[i] for i in range(len(values))]
+    return [stacked[i] for i in range(values.shape[0])]
 
 
 def split3(value):
@@ -37,13 +42,12 @@
 
 
 def onehot_dot(value, onehot, dims):
-    total = None
-    for piece in split3(value):
-        part = lax.dot_general(
-            piece, onehot, (dims, ((), ())), preferred_element_type=jnp.float32
-        )
-        total = part if total is None else total + part
-    return total
+    rows = value.shape[0]
+    pieces = jnp.concatenate(split3(value), axis=0)
+    part = lax.dot_general(
+        pieces, onehot, (dims, ((), ())), preferred_element_type=jnp.float32
+    )
+    return (part[:rows] + part[rows : 2 * rows]) + part[2 * rows :]
 
 
 def per_device(
@@ -211,18 +215,20 @@
         direct_coupled,
         coupled_coupled,
     ) = global_sum(
-        [
-            jnp.sum(grad_last * image_last),
-            jnp.sum(image_last * image_last),
-            jnp.sum(grad_last * grad_last),
-            jnp.sum(grad_first * direct),
-            jnp.sum(grad_first * coupled),
-            jnp.sum(carried * direct),
-            jnp.sum(carried * coupled),
-            jnp.sum(direct * direct),
-            jnp.sum(direct * coupled),
-            jnp.sum(coupled * coupled),
-        ]
+        stacked_sums(
+            [
+                (grad_last, image_last),
+                (image_last, image_last),
+                (grad_last, grad_last),
+                (grad_first, direct),
+                (grad_first, coupled),
+                (carried, direct),
+                (carried, coupled),
+                (direct, direct),
+                (direct, coupled),
+                (coupled, coupled),
+            ]
+        )
     )
     alpha_last = along_last / energy_last
     along_first = grad_direct + alpha_last * (grad_coupled + carried_direct) + (
@@ -239,11 +245,13 @@
     image_first = direct + alpha_last * coupled
     closing_first = residual_first - alpha_first * image_first
     norm_first, end_first, end_last = global_sum(
-        [
-            jnp.sum(residual_first * residual_first),
-            jnp.sum(closing_first * closing_first),
-            jnp.sum(residual_last * residual_last),
-        ]
+        stacked_sums(
+            [
+                (residual_first, residual_first),
+                (closing_first, closing_first),
+                (residual_last, residual_last),
+            ]
+        )
     )
     norms = jnp.sqrt(jnp.stack([norm_first, end_first, norm_last, end_last])).reshape(2, 2)
     return (jnp.stack([solution_first, solution_last]), norms)

time: 141 us -> 134 us (0.950)
  matrix products: 30.3 us -> 11 us
  other arithmetic: 20.9 us -> 28.2 us
  local copies, waits for them, and re-layouts: 20.7 us -> 25.7 us
    dot_general x18 -> x6, matrix products: 29.7 us -> 9.2 us  [onehot_dot(): lax.dot_general(pieces, onehot, (dims, ((), ())), preferred_element_type=...]
    mul x0 -> x6, other arithmetic: none -> 4.72 us  [the longest x5 4.64 us: stacked_sums(): products = jnp.stack([(left * right).reshape(-1) for left, right in pairs])]
    select_n x3, other arithmetic: 0.69 us -> 3.78 us  [locate(): onehot = (cells % column_count)[:, None] == column_iota[None, :]]
    unnamed x114 -> x120, local copies, waits for them, and re-layouts: 4.08 us -> 6.32 us
    another operation x1, other arithmetic: 1.98 us -> 0.03 us  [operator(): return jnp.stack([first, second], axis=1)]
    add x1 -> x6, other arithmetic: 0.15 us -> 2.07 us  [the longest x1 0.97 us: per_device(): residual_first = grad_first + store[0] * solution_last]
    convert_element_type x1 -> x5, other arithmetic: 0.05 us -> 1.95 us  [split3(): middle = rest.astype(jnp.bfloat16)]
    convert_element_type x4 -> x0, other arithmetic: 1.72 us -> none  [split3(): low = (rest - middle.astype(value.dtype)).astype(jnp.bfloat16)]
  transfers between devices with their start and end apart: 12 -> 12, of which waited for: 6 -> 6; matrix products, arithmetic and copies ran while one was open for 13% -> 18% of each run, Pallas kernels for 0% -> 0%
where the time goes in v1:
time: 134 us; the launch traced here: 133 us
  starting transfers between devices  30.1 us (22%)
  other arithmetic  28.2 us (21%)
  local copies, waits for them, and re-layouts  25.7 us (19%)
  blocking collectives  19.5 us (15%)
  matrix products  11 us (8%)
  waiting for transfers between devices  9.88 us (7%)
  between operations  8.08 us (6%)
    ppermute x6, starting transfers between devices, shifted(): return lax.ppermute(value, axis, pairs)  17.2 us
    ppermute x6, starting transfers between devices, global_sum(): lax.ppermute(stacked, 'cells', [(i, i ^ step) for i in range(count)])  12.8 us
    psum x2, blocking collectives, global_sum(): stacked = lax.psum(values, 'slab')  11.8 us
    ppermute x6, waiting for transfers between devices, global_sum(): lax.ppermute(stacked, 'cells', [(i, i ^ step) for i in range(count)])  9.87 us
    dot_general x6, matrix products, onehot_dot(): lax.dot_general(pieces, onehot, (dims, ((), ())), preferred_element_type=...  9.2 us
    psum x1, blocking collectives, operator(): summed = lax.psum(local, 'slab')  7.71 us
    unnamed x120, local copies, waits for them, and re-layouts  6.32 us
    another operation x1, local copies, waits for them, and re-layouts, stacked_sums(): products = jnp.stack([(left * right).reshape(-1) for left, right in pairs])  4.82 us
  transfers between devices with their start and end apart: 12, of which 6 were waited for; matrix products, arithmetic and copies ran while one was open for 18% of the time, Pallas kernels for 0%

profile of v1, /device:TPU:0, one launch (start us, length us, event | category | flops | bytes accessed | tf_op | source)
XLA Modules:
  0.0 132.5 jit_solution(11097845798545468266)
XLA Ops:
  3.2 4.9 %collective-permute-start = (f32[2064]{0:T(1024)S(1)}, f32[2064]{0:T(1024)S(1)}, u32[]{:S(2)}, u32[]{:S(2)}) collective-permute-start(f32[2064]{0:T(1024)S(1)} %pad_maximum_fusion.12), channel_id=1, source_target_pairs={{0,4},{4,8},{8,12},{12,16},{16,20},{20,24},{24,28},{1,5},{5,9},{9,... | collective-permute-start | bytes 24776 | tf_op jit(solution)/shard_map/ppermute | solution.py:13
  9.1 1.5 %collective-permute-start.1 = (f32[1024]{0:T(1024)S(1)}, f32[1024]{0:T(1024)S(1)}, u32[]{:S(2)}, u32[]{:S(2)}) collective-permute-start(f32[1024]{0:T(1024)S(1)} %bitcast.366), channel_id=1, source_target_pairs={{0,1},{1,2},{2,3},{4,5},{5,6},{6,7},{8,9},{9,10},{10,11},{12,13},{... | collective-permute-start | bytes 12296 | tf_op jit(solution)/shard_map/ppermute | solution.py:13
  12.4 1.7 %fusion.104 = (f32[1,2,16,1024]{3,2,1,0:T(8,128)S(1)}, f32[1,2,16,1024]{3,2,1,0:T(8,128)}) fusion(f32[2,2,16,1024]{3,2,1,0:T(8,128)} %param.15), kind=kLoop, calls=%fused_computation.247 | loop fusion | bytes 524288 | tf_op jit(solution)/shard_map/slice | solution.py:130
  14.8 1.3 add_select_fusion
  16.9 1.3 add_select_fusion.1
  23.4 1.6 %fusion.51 = (f32[1,16,1024]{2,1,0:T(8,128)S(1)}, f32[16,1024]{1,0:T(8,128)S(1)}, f32[16,1024]{1,0:T(8,128)S(1)}, f32[16,1024]{1,0:T(8,128)S(1)}, f32[16,1024]{1,0:T(8,128)}, /*index=5*/f32[16,1024]{1,0:T(8,128)}) fusion(f32[2,2,16,1024]{3,2,1,0:T(8,128)S(1)} %copy-done.1, f32[2,4,16,1024]{3,2,1,0:T(8,128)S(1)} %copy-done, ...), kind=kLoop, calls=%fused_computation.128 | loop fusion | flops 327680 | bytes 1180688 | tf_op jit(solution)/shard_map/stack | solution.py:143
  26.8 7.7 %psum.21 = f32[4,16]{1,0:T(4,128)S(1)} all-reduce(f32[4,16]{1,0:T(4,128)S(1)} %pad_maximum_fusion.13), channel_id=1, replica_groups=mesh['cells'=8,'slab'=4] {'slab'}, use_global_device_ids=true, to_apply=%region_3.4 | all-reduce | flops 64 | bytes 512 | tf_op jit(solution)/shard_map/psum | solution.py:181
  37.8 1.8 %fusion.1 = f32[288,2048]{1,0:T(8,128)S(1)} fusion(s32[2048]{0:T(1024)S(1)} %copy-done.43, bf16[96,1024]{1,0:T(8,128)(2,1)S(1)} %get-tuple-element.37, bf16[96,1024]{1,0:T(8,128)(2,1)S(1)} %get-tuple-element.36, bf16[96,1024]{1,0:T(8,128)(2,1)S(1)} %bitcast_convert_fusion.2), kind=kOutput, calls=%fused_computation.2 | convolution fusion | flops 1211826176 | bytes 2957312 | tf_op jit(solution)/shard_map/dot_general | solution.py:47
  40.3 1.8 %fusion.3 = f32[288,2048]{1,0:T(8,128)S(1)} fusion(s32[2048]{0:T(1024)S(1)} %copy-done.41, bf16[96,1024]{1,0:T(8,128)(2,1)S(1)} %get-tuple-element.37, bf16[96,1024]{1,0:T(8,128)(2,1)S(1)} %get-tuple-element.36, bf16[96,1024]{1,0:T(8,128)(2,1)S(1)} %bitcast_convert_fusion.2), kind=kOutput, calls=%fused_computation.5 | convolution fusion | flops 1211826176 | bytes 2957312 | tf_op jit(solution)/shard_map/dot_general | solution.py:47
  47.0 3.6 %collective-permute-start.5 = (f32[6,1024]{1,0:T(8,128)}, f32[6,1024]{1,0:T(8,128)}, u32[]{:S(2)}, u32[]{:S(2)}) collective-permute-start(f32[6,1024]{1,0:T(8,128)} %bitcast.311), channel_id=1, source_target_pairs={{0,1},{1,2},{2,3},{4,5},{5,6},{6,7},{8,9},{9,10},{10,11},{12,13},{... | collective-permute-start | bytes 73736 | tf_op jit(solution)/shard_map/ppermute | solution.py:13
  51.9 4.7 %collective-permute-start.3 = (f32[6,2064]{1,0:T(8,128)S(1)}, f32[6,2064]{1,0:T(8,128)S(1)}, u32[]{:S(2)}, u32[]{:S(2)}) collective-permute-start(f32[6,2064]{1,0:T(8,128)S(1)} %pad_maximum_fusion.9), channel_id=1, source_target_pairs={{0,4},{4,8},{8,12},{12,16},{16,20},{20,24},{24,28},{1,5},{5,9},{9,... | collective-permute-start | bytes 148616 | tf_op jit(solution)/shard_map/ppermute | solution.py:13
  56.7 1.7 %stack.98 = f32[1,32768]{1,0:T(1,128)} reshape(f32[2,16,1024]{2,1,0:T(8,128)} %get-tuple-element.58) | data formatting | bytes 262144 | tf_op jit(solution)/shard_map/stack | solution.py:143
  59.2 1.4 %concatenate.105 = f32[3,2,1,1024]{3,2,1,0:T(1,128)} reshape(f32[6,1024]{1,0:T(8,128)} %collective-permute-done.4) | data formatting | bytes 49152 | tf_op jit(solution)/shard_map/concatenate | solution.py:162
  60.6 1.4 %concatenate.106 = f32[3,2,1,1024]{3,2,1,0:T(1,128)} reshape(f32[6,1024]{1,0:T(8,128)} %collective-permute-done.5) | data formatting | bytes 49152 | tf_op jit(solution)/shard_map/concatenate | solution.py:161
  69.4 3.0 %fusion = f32[288,1024]{1,0:T(8,128)S(1)} fusion(s32[2048]{0:T(1024)S(1)} %copy-done.44, bf16[96,2048]{1,0:T(8,128)(2,1)} %get-tuple-element.16, bf16[96,2048]{1,0:T(8,128)(2,1)S(1)} %get-tuple-element.15, bf16[96,2048]{1,0:T(8,128)(2,1)S(1)} %copy-done.30), kind=kOutput, calls=%fused_computation.1 | convolution fusion | flops 1213595648 | bytes 2367488 | tf_op jit(solution)/shard_map/dot_general | solution.py:47
  72.4 1.9 %fusion.2 = f32[288,1024]{1,0:T(8,128)S(1)} fusion(s32[2048]{0:T(1024)S(1)} %copy-done.42, bf16[96,2048]{1,0:T(8,128)(2,1)S(1)} %copy-done.32, bf16[96,2048]{1,0:T(8,128)(2,1)S(1)} %copy-done.31, bf16[96,2048]{1,0:T(8,128)(2,1)S(1)} %copy-done.33), kind=kOutput, calls=%fused_computation.4 | convolution fusion | flops 1213595648 | bytes 2367488 | tf_op jit(solution)/shard_map/dot_general | solution.py:47
  78.6 1.3 %fusion.101 = (f32[1,32768]{1,0:T(1,128)}, f32[1,32768]{1,0:T(1,128)}, f32[1,32768]{1,0:T(1,128)}, f32[1,32768]{1,0:T(1,128)}, f32[1,32768]{1,0:T(1,128)}) fusion(f32[1,32768]{1,0:T(1,128)S(1)} %bitcast.339, f32[1,32768]{1,0:T(1,128)S(1)} %bitcast.325, f32[1,32768]{1,0:T(1,128)S(1)} %bitcast.328, f32[1,32768]{1,0:T(1,128)S(1)} %bitcast.342, ...), kind=kLoop, calls=%fused_computation.244 | loop fusion | flops 196608 | bytes 1310720 | tf_op jit(solution)/shard_map/mul | solution.py:17
  80.0 4.8 %stack.99 = f32[10,32768]{1,0:T(8,128)S(1)} concatenate(f32[1,32768]{1,0:T(1,128)} %get-tuple-element.48, f32[1,32768]{1,0:T(1,128)} %get-tuple-element.49, f32[1,32768]{1,0:T(1,128)} %get-tuple-element.54, f32[1,32768]{1,0:T(1,128)} %get-tuple-element.44, f32[1,32768]{1,0:T(1,128)} %get-tuple-element.55, f32[1,32768]{1,0:T(1,128)} %get-tuple-element.56, ...), dimensions={0} | concatenate | bytes 2621440 | tf_op jit(solution)/shard_map/stack | solution.py:17
  85.2 6.2 %psum.22 = f32[10]{0:T(128)S(1)} all-reduce(f32[10]{0:T(128)S(1)} %reduce_sum.48), channel_id=1, replica_groups=mesh['cells'=8,'slab'=4] {'slab'}, use_global_device_ids=true, to_apply=%region_5.6 | all-reduce | flops 10 | bytes 80 | tf_op jit(solution)/shard_map/psum | solution.py:22
  91.4 2.5 %collective-permute-start.6 = (f32[10]{0:T(128)S(1)}, f32[10]{0:T(128)S(1)}, u32[]{:S(2)}, u32[]{:S(2)}) collective-permute-start(f32[10]{0:T(128)S(1)} %psum.22), channel_id=1, source_target_pairs={{0,4},{4,0},{8,12},{12,8},{16,20},{20,16},{24,28},{28,24},{1,5},{5... | collective-permute-start | bytes 128 | tf_op jit(solution)/shard_map/ppermute | solution.py:29
  93.9 1.5 %collective-permute-done.6 = f32[10]{0:T(128)S(1)} collective-permute-done((f32[10]{0:T(128)S(1)}, f32[10]{0:T(128)S(1)}, u32[]{:S(2)}, u32[]{:S(2)}) %collective-permute-start.6) | collective-permute-done | bytes 72 | tf_op jit(solution)/shard_map/ppermute | solution.py:29
  95.4 1.6 %collective-permute-start.7 = (f32[10]{0:T(128)S(1)}, f32[10]{0:T(128)S(1)}, u32[]{:S(2)}, u32[]{:S(2)}) collective-permute-start(f32[10]{0:T(128)S(1)} %add.256), channel_id=1, source_target_pairs={{0,8},{4,12},{8,0},{12,4},{16,24},{20,28},{24,16},{28,20},{1,9},{5... | collective-permute-start | bytes 128 | tf_op jit(solution)/shard_map/ppermute | solution.py:29
  97.0 2.0 %collective-permute-done.7 = f32[10]{0:T(128)S(1)} collective-permute-done((f32[10]{0:T(128)S(1)}, f32[10]{0:T(128)S(1)}, u32[]{:S(2)}, u32[]{:S(2)}) %collective-permute-start.7) | collective-permute-done | bytes 72 | tf_op jit(solution)/shard_map/ppermute | solution.py:29
  98.9 2.6 %collective-permute-start.8 = (f32[10]{0:T(128)S(1)}, f32[10]{0:T(128)S(1)}, u32[]{:S(2)}, u32[]{:S(2)}) collective-permute-start(f32[10]{0:T(128)S(1)} %add.257), channel_id=1, source_target_pairs={{0,16},{4,20},{8,24},{12,28},{16,0},{20,4},{24,8},{28,12},{1,17},{... | collective-permute-start | bytes 128 | tf_op jit(solution)/shard_map/ppermute | solution.py:29
  101.5 1.9 %collective-permute-done.8 = f32[10]{0:T(128)S(1)} collective-permute-done((f32[10]{0:T(128)S(1)}, f32[10]{0:T(128)S(1)}, u32[]{:S(2)}, u32[]{:S(2)}) %collective-permute-start.8) | collective-permute-done | bytes 72 | tf_op jit(solution)/shard_map/ppermute | solution.py:29
  112.7 5.7 %psum.23 = f32[3]{0:T(128)S(1)} all-reduce(f32[3]{0:T(128)S(1)} %maximum_reduce_fusion), channel_id=1, replica_groups=mesh['cells'=8,'slab'=4] {'slab'}, use_global_device_ids=true, to_apply=%region_7.8 | all-reduce | flops 3 | bytes 24 | tf_op jit(solution)/shard_map/psum | solution.py:22
  118.3 2.1 %collective-permute-start.9 = (f32[3]{0:T(128)S(1)}, f32[3]{0:T(128)S(1)}, u32[]{:S(2)}, u32[]{:S(2)}) collective-permute-start(f32[3]{0:T(128)S(1)} %psum.23), channel_id=1, source_target_pairs={{0,4},{4,0},{8,12},{12,8},{16,20},{20,16},{24,28},{28,24},{1,5},{5... | collective-permute-start | bytes 44 | tf_op jit(solution)/shard_map/ppermute | solution.py:29
  121.9 1.6 %collective-permute-start.10 = (f32[3]{0:T(128)S(1)}, f32[3]{0:T(128)S(1)}, u32[]{:S(2)}, u32[]{:S(2)}) collective-permute-start(f32[3]{0:T(128)S(1)} %add.270), channel_id=1, source_target_pairs={{0,8},{4,12},{8,0},{12,4},{16,24},{20,28},{24,16},{28,20},{1,9},{5... | collective-permute-start | bytes 44 | tf_op jit(solution)/shard_map/ppermute | solution.py:29
  123.5 2.0 %collective-permute-done.10 = f32[3]{0:T(128)S(1)} collective-permute-done((f32[3]{0:T(128)S(1)}, f32[3]{0:T(128)S(1)}, u32[]{:S(2)}, u32[]{:S(2)}) %collective-permute-start.10) | collective-permute-done | bytes 44 | tf_op jit(solution)/shard_map/ppermute | solution.py:29
  125.5 2.6 %collective-permute-start.11 = (f32[3]{0:T(128)S(1)}, f32[3]{0:T(128)S(1)}, u32[]{:S(2)}, u32[]{:S(2)}) collective-permute-start(f32[3]{0:T(128)S(1)} %add.271), channel_id=1, source_target_pairs={{0,16},{4,20},{8,24},{12,28},{16,0},{20,4},{24,8},{28,12},{1,17},{... | collective-permute-start | bytes 44 | tf_op jit(solution)/shard_map/ppermute | solution.py:29
  128.0 1.9 %collective-permute-done.11 = f32[3]{0:T(128)S(1)} collective-permute-done((f32[3]{0:T(128)S(1)}, f32[3]{0:T(128)S(1)}, u32[]{:S(2)}, u32[]{:S(2)}) %collective-permute-start.11) | collective-permute-done | bytes 44 | tf_op jit(solution)/shard_map/ppermute | solution.py:29
  130.5 1.4 %maximum_sqrt_fusion = f32[4]{0:T(128)S(1)} fusion(f32[1]{0:T(128)} %slice.407, f32[1]{0:T(128)} %get-tuple-element.63, f32[2]{0:T(128)S(1)} %bitcast.367), kind=kLoop, calls=%fused_computation.225 | loop fusion | flops 8 | bytes 32 | tf_op jit(solution)/shard_map/sqrt | solution.py:256
  (224 shorter events, 41.8 us)
Async XLA Ops:
  0.6 19.4 %copy-start.1 = (f32[2,2,16,1024]{3,2,1,0:T(8,128)S(1)}, f32[2,2,16,1024]{3,2,1,0:T(8,128)}, u32[]{:S(2)}) copy-start(f32[2,2,16,1024]{3,2,1,0:T(8,128)} %param.13) | copy-start | bytes 786436
  0.6 19.4 %copy-start.52 = (s32[1,128]{1,0:T(1,128)S(1)}, s32[1,128]{1,0:T(1,128)}, u32[]{:S(2)}) copy-start(s32[1,128]{1,0:T(1,128)} %param.24) | copy-start | bytes 1540
  0.7 19.4 %copy-start.54 = (f32[1,128]{1,0:T(1,128)S(1)}, f32[1,128]{1,0:T(1,128)}, u32[]{:S(2)}) copy-start(f32[1,128]{1,0:T(1,128)} %param.25) | copy-start | bytes 1540
  1.6 21.8 %copy-start.17 = (f32[16,1024]{1,0:T(8,128)}, f32[16,1024]{1,0:T(8,128)S(1)}, u32[]{:S(2)}) copy-start(f32[16,1024]{1,0:T(8,128)S(1)} %broadcast_select_fusion.1) | copy-start | bytes 196612
  3.2 19.5 %collective-permute-start = (f32[2064]{0:T(1024)S(1)}, f32[2064]{0:T(1024)S(1)}, u32[]{:S(2)}, u32[]{:S(2)}) collective-permute-start(f32[2064]{0:T(1024)S(1)} %pad_maximum_fusion.12), channel_id=1, source_target_pairs={{0,4},{4,8},{8,12},{12,16},{16,20},{20,24},{24,28},{1,5},{5,9},{9,... | collective-permute-start | bytes 24776 | tf_op jit(solution)/shard_map/ppermute | solution.py:13
  9.0 14.4 %copy-start.19 = (f32[16,1024]{1,0:T(8,128)}, f32[16,1024]{1,0:T(8,128)S(1)}, u32[]{:S(2)}) copy-start(f32[16,1024]{1,0:T(8,128)S(1)} %broadcast_select_fusion) | copy-start | bytes 196612
  9.1 13.8 %collective-permute-start.1 = (f32[1024]{0:T(1024)S(1)}, f32[1024]{0:T(1024)S(1)}, u32[]{:S(2)}, u32[]{:S(2)}) collective-permute-start(f32[1024]{0:T(1024)S(1)} %bitcast.366), channel_id=1, source_target_pairs={{0,1},{1,2},{2,3},{4,5},{5,6},{6,7},{8,9},{9,10},{10,11},{12,13},{... | collective-permute-start | bytes 12296 | tf_op jit(solution)/shard_map/ppermute | solution.py:13
  12.4 9.4 %slice-start = ((f32[2,2,16,1024]{3,2,1,0:T(8,128)}), f32[1,2,16,1024]{3,2,1,0:T(8,128)S(1)}, s32[]{:S(2)}) async-start(f32[2,2,16,1024]{3,2,1,0:T(8,128)} %param.16), calls=%async_computation | async-start | bytes 262144 | tf_op jit(solution)/shard_map/slice | solution.py:198
  18.2 5.3 %copy-start = (f32[2,4,16,1024]{3,2,1,0:T(8,128)S(1)}, f32[2,4,16,1024]{3,2,1,0:T(8,128)}, u32[]{:S(2)}) copy-start(f32[2,4,16,1024]{3,2,1,0:T(8,128)} %param.14) | copy-start | bytes 1572868
  18.2 5.3 %copy-start.2 = (f32[2,2,16,1024]{3,2,1,0:T(8,128)S(1)}, f32[2,2,16,1024]{3,2,1,0:T(8,128)}, u32[]{:S(2)}) copy-start(f32[2,2,16,1024]{3,2,1,0:T(8,128)} %param.15) | copy-start | bytes 786436
  21.0 4.2 %copy-start.25 = (f32[2,2,16,1024]{3,2,1,0:T(8,128)S(1)}, f32[2,2,16,1024]{3,2,1,0:T(8,128)}, u32[]{:S(2)}) copy-start(f32[2,2,16,1024]{3,2,1,0:T(8,128)} %param.16) | copy-start | bytes 786436
  42.2 8.7 %copy-start.51 = (s32[128]{0:T(128)S(1)}, s32[128]{0:T(128)}, u32[]{:S(2)}) copy-start(s32[128]{0:T(128)} %and_select_fusion.4) | copy-start | bytes 1540
  42.5 9.5 %copy-start.26 = (f32[6,2048]{1,0:T(8,128)}, f32[6,2048]{1,0:T(8,128)S(1)}, u32[]{:S(2)}) copy-start(f32[6,2048]{1,0:T(8,128)S(1)} %multiply_reduce_fusion.1) | copy-start | bytes 147460
  43.2 18.8 %collective-permute-start.2 = (f32[6,2064]{1,0:T(8,128)}, f32[6,2064]{1,0:T(8,128)}, u32[]{:S(2)}, u32[]{:S(2)}) collective-permute-start(f32[6,2064]{1,0:T(8,128)} %pad_maximum_fusion.8), channel_id=1, source_target_pairs={{4,0},{8,4},{12,8},{16,12},{20,16},{24,20},{28,24},{5,1},{9,5},{13... | collective-permute-start | bytes 148616 | tf_op jit(solution)/shard_map/ppermute | solution.py:13
  45.1 14.1 %collective-permute-start.4 = (f32[6,1024]{1,0:T(8,128)}, f32[6,1024]{1,0:T(8,128)}, u32[]{:S(2)}, u32[]{:S(2)}) collective-permute-start(f32[6,1024]{1,0:T(8,128)} %bitcast.312), channel_id=1, source_target_pairs={{1,0},{2,1},{3,2},{5,4},{6,5},{7,6},{9,8},{10,9},{11,10},{13,12},{... | collective-permute-start | bytes 73736 | tf_op jit(solution)/shard_map/ppermute | solution.py:13
  47.0 13.6 %collective-permute-start.5 = (f32[6,1024]{1,0:T(8,128)}, f32[6,1024]{1,0:T(8,128)}, u32[]{:S(2)}, u32[]{:S(2)}) collective-permute-start(f32[6,1024]{1,0:T(8,128)} %bitcast.311), channel_id=1, source_target_pairs={{0,1},{1,2},{2,3},{4,5},{5,6},{6,7},{8,9},{9,10},{10,11},{12,13},{... | collective-permute-start | bytes 73736 | tf_op jit(solution)/shard_map/ppermute | solution.py:13
  50.8 5.9 %copy-start.28 = (f32[6,2048]{1,0:T(8,128)}, f32[6,2048]{1,0:T(8,128)S(1)}, u32[]{:S(2)}) copy-start(f32[6,2048]{1,0:T(8,128)S(1)} %multiply_reduce_fusion) | copy-start | bytes 147460
  51.9 12.8 %collective-permute-start.3 = (f32[6,2064]{1,0:T(8,128)S(1)}, f32[6,2064]{1,0:T(8,128)S(1)}, u32[]{:S(2)}, u32[]{:S(2)}) collective-permute-start(f32[6,2064]{1,0:T(8,128)S(1)} %pad_maximum_fusion.9), channel_id=1, source_target_pairs={{0,4},{4,8},{8,12},{12,16},{16,20},{20,24},{24,28},{1,5},{5,9},{9,... | collective-permute-start | bytes 148616 | tf_op jit(solution)/shard_map/ppermute | solution.py:13
  58.4 6.4 %copy-start.27 = (f32[6,2048]{1,0:T(8,128)S(1)}, f32[6,2048]{1,0:T(8,128)}, u32[]{:S(2)}) copy-start(f32[6,2048]{1,0:T(8,128)} %copy-done.26) | copy-start | bytes 147460
  64.7 4.6 %copy-start.44 = (s32[2048]{0:T(1024)S(1)}, s32[2048]{0:T(1024)}, u32[]{:S(2)}) copy-start(s32[2048]{0:T(1024)} %add_select_fusion) | copy-start | bytes 24580
  65.5 3.9 %copy-start.30 = (bf16[96,2048]{1,0:T(8,128)(2,1)S(1)}, bf16[96,2048]{1,0:T(8,128)(2,1)}, u32[]{:S(2)}) copy-start(bf16[96,2048]{1,0:T(8,128)(2,1)} %bitcast_convert_fusion.1) | copy-start | bytes 1179652
  85.2 35.2 %copy-start.11 = (f32[16,1024]{1,0:T(8,128)S(1)}, f32[16,1024]{1,0:T(8,128)}, u32[]{:S(2)}) copy-start(f32[16,1024]{1,0:T(8,128)} %copy-done.10) | copy-start | bytes 196612
  85.2 35.2 %copy-start.22 = (f32[16,1024]{1,0:T(8,128)S(1)}, f32[16,1024]{1,0:T(8,128)}, u32[]{:S(2)}) copy-start(f32[16,1024]{1,0:T(8,128)} %copy-done.21) | copy-start | bytes 196612
  85.2 35.2 %copy-start.24 = (f32[16,1024]{1,0:T(8,128)S(1)}, f32[16,1024]{1,0:T(8,128)}, u32[]{:S(2)}) copy-start(f32[16,1024]{1,0:T(8,128)} %copy-done.23) | copy-start | bytes 196612
  85.2 35.3 %copy-start.13 = (f32[16,1024]{1,0:T(8,128)S(1)}, f32[16,1024]{1,0:T(8,128)}, u32[]{:S(2)}) copy-start(f32[16,1024]{1,0:T(8,128)} %copy-done.12) | copy-start | bytes 196612
  85.2 35.3 %copy-start.15 = (f32[16,1024]{1,0:T(8,128)S(1)}, f32[16,1024]{1,0:T(8,128)}, u32[]{:S(2)}) copy-start(f32[16,1024]{1,0:T(8,128)} %copy-done.14) | copy-start | bytes 196612
  91.4 4.0 %collective-permute-start.6 = (f32[10]{0:T(128)S(1)}, f32[10]{0:T(128)S(1)}, u32[]{:S(2)}, u32[]{:S(2)}) collective-permute-start(f32[10]{0:T(128)S(1)} %psum.22), channel_id=1, source_target_pairs={{0,4},{4,0},{8,12},{12,8},{16,20},{20,16},{24,28},{28,24},{1,5},{5... | collective-permute-start | bytes 128 | tf_op jit(solution)/shard_map/ppermute | solution.py:29
  95.4 3.5 %collective-permute-start.7 = (f32[10]{0:T(128)S(1)}, f32[10]{0:T(128)S(1)}, u32[]{:S(2)}, u32[]{:S(2)}) collective-permute-start(f32[10]{0:T(128)S(1)} %add.256), channel_id=1, source_target_pairs={{0,8},{4,12},{8,0},{12,4},{16,24},{20,28},{24,16},{28,20},{1,9},{5... | collective-permute-start | bytes 128 | tf_op jit(solution)/shard_map/ppermute | solution.py:29
  98.9 4.4 %collective-permute-start.8 = (f32[10]{0:T(128)S(1)}, f32[10]{0:T(128)S(1)}, u32[]{:S(2)}, u32[]{:S(2)}) collective-permute-start(f32[10]{0:T(128)S(1)} %add.257), channel_id=1, source_target_pairs={{0,16},{4,20},{8,24},{12,28},{16,0},{20,4},{24,8},{28,12},{1,17},{... | collective-permute-start | bytes 128 | tf_op jit(solution)/shard_map/ppermute | solution.py:29
  118.3 3.6 %collective-permute-start.9 = (f32[3]{0:T(128)S(1)}, f32[3]{0:T(128)S(1)}, u32[]{:S(2)}, u32[]{:S(2)}) collective-permute-start(f32[3]{0:T(128)S(1)} %psum.23), channel_id=1, source_target_pairs={{0,4},{4,0},{8,12},{12,8},{16,20},{20,16},{24,28},{28,24},{1,5},{5... | collective-permute-start | bytes 44 | tf_op jit(solution)/shard_map/ppermute | solution.py:29
  121.9 3.5 %collective-permute-start.10 = (f32[3]{0:T(128)S(1)}, f32[3]{0:T(128)S(1)}, u32[]{:S(2)}, u32[]{:S(2)}) collective-permute-start(f32[3]{0:T(128)S(1)} %add.270), channel_id=1, source_target_pairs={{0,8},{4,12},{8,0},{12,4},{16,24},{20,28},{24,16},{28,20},{1,9},{5... | collective-permute-start | bytes 44 | tf_op jit(solution)/shard_map/ppermute | solution.py:29
  125.5 4.4 %collective-permute-start.11 = (f32[3]{0:T(128)S(1)}, f32[3]{0:T(128)S(1)}, u32[]{:S(2)}, u32[]{:S(2)}) collective-permute-start(f32[3]{0:T(128)S(1)} %add.271), channel_id=1, source_target_pairs={{0,16},{4,20},{8,24},{12,28},{16,0},{20,4},{24,8},{28,12},{1,17},{... | collective-permute-start | bytes 44 | tf_op jit(solution)/shard_map/ppermute | solution.py:29
  (38 other events, 54.3 us)

commit v2 on v1

--- a/solution.py
+++ b/solution.py
@@ -14,8 +14,19 @@
 
 
 def stacked_sums(pairs):
-    products = jnp.stack([(left * right).reshape(-1) for left, right in pairs])
-    return jnp.sum(products, axis=1)
+    partial = jnp.stack([jnp.sum(left * right, axis=-2) for left, right in pairs])
+    return jnp.sum(partial.reshape(len(pairs), -1), axis=1)
+
+
+def butterfly(value, axis):
+    count = lax.axis_size(axis)
+    if count & (count - 1):
+        return lax.psum(value, axis)
+    step = 1
+    while step < count:
+        value = value + lax.ppermute(value, axis, [(i, i ^ step) for i in range(count)])
+        step *= 2
+    return value
 
 
 def global_sum(values):
@@ -178,7 +189,7 @@
                 jnp.dot(well_index * values, well_onehot, precision=highest),
             ]
         )
-        summed = lax.psum(local, "slab")
+        summed = butterfly(local, "slab")
         back = jnp.dot(summed[1:] / summed[0], well_onehot.T, precision=highest)
         well_term = scatter(well_index * (values - back), well_at)
         first = (

time: 134 us -> 114 us (0.85)
  local copies, waits for them, and re-layouts: 25.7 us -> 15.7 us
  blocking collectives: 19.5 us -> 11.4 us
  other arithmetic: 28.2 us -> 24.7 us
    psum x1 -> x0, blocking collectives: 7.71 us -> none  [operator(): summed = lax.psum(local, 'slab')]
    another operation x2 -> x1, local copies, waits for them, and re-layouts: 6.53 us -> 0.15 us  [stacked_sums(): jnp.stack([jnp.sum(left * right, axis=-2) for left, right in pairs])]
    mul x6 -> x0, other arithmetic: 4.72 us -> none  [the longest x5 4.64 us: stacked_sums(): products = jnp.stack([(left * right).reshape(-1) for left, right in pairs])]
    ppermute x0 -> x2, starting transfers between devices: none -> 4.18 us  [butterfly(): lax.ppermute(value, axis, [(i, i ^ step) for i in range(count)])]
    unnamed x120 -> x121, local copies, waits for them, and re-layouts: 6.32 us -> 3.88 us
    another operation x5 -> x4, other arithmetic: 2.39 us -> 0.85 us  [precondition(): jnp.stack([inverse_aa * residual[0] + inverse_ab * residual[1], inverse_b...]
    ppermute x6, starting transfers between devices: 12.8 us -> 11.3 us  [global_sum(): lax.ppermute(stacked, 'cells', [(i, i ^ step) for i in range(count)])]
  transfers between devices with their start and end apart: 12 -> 14, of which waited for: 6 -> 6; matrix products, arithmetic and copies ran while one was open for 18% -> 21% of each run, Pallas kernels for 0% -> 0%
where the time goes in v2:
time: 114 us; the launch traced here: 113 us
  starting transfers between devices  31.4 us (28%)
  other arithmetic  24.7 us (22%)
  local copies, waits for them, and re-layouts  15.7 us (14%)
  blocking collectives  11.4 us (10%)
  waiting for transfers between devices  11 us (10%)
  matrix products  10.5 us (9%)
  between operations  8.26 us (7%)
    ppermute x6, starting transfers between devices, shifted(): return lax.ppermute(value, axis, pairs)  15.9 us
    psum x2, blocking collectives, global_sum(): stacked = lax.psum(values, 'slab')  11.4 us
    ppermute x6, starting transfers between devices, global_sum(): lax.ppermute(stacked, 'cells', [(i, i ^ step) for i in range(count)])  11.3 us
    ppermute x6, waiting for transfers between devices, global_sum(): lax.ppermute(stacked, 'cells', [(i, i ^ step) for i in range(count)])  11 us
    dot_general x6, matrix products, onehot_dot(): lax.dot_general(pieces, onehot, (dims, ((), ())), preferred_element_type=...  9.4 us
    ppermute x2, starting transfers between devices, butterfly(): lax.ppermute(value, axis, [(i, i ^ step) for i in range(count)])  4.18 us
    unnamed x121, local copies, waits for them, and re-layouts  3.88 us
    select_n x3, other arithmetic, locate(): onehot = (cells % column_count)[:, None] == column_iota[None, :]  3.81 us
  transfers between devices with their start and end apart: 14, of which 6 were waited for; matrix products, arithmetic and copies ran while one was open for 21% of the time, Pallas kernels for 0%

profile of v2, /device:TPU:0, one launch (start us, length us, event | category | flops | bytes accessed | tf_op | source)
XLA Modules:
  0.0 113.1 jit_solution(17196914829028172617)
XLA Ops:
  3.3 4.9 %collective-permute-start = (f32[2064]{0:T(1024)S(1)}, f32[2064]{0:T(1024)S(1)}, u32[]{:S(2)}, u32[]{:S(2)}) collective-permute-start(f32[2064]{0:T(1024)S(1)} %pad_maximum_fusion.12), channel_id=1, source_target_pairs={{0,4},{4,8},{8,12},{12,16},{16,20},{20,24},{24,28},{1,5},{5,9},{9,... | collective-permute-start | bytes 24776 | tf_op jit(solution)/shard_map/ppermute | solution.py:13
  9.1 1.5 %collective-permute-start.1 = (f32[1024]{0:T(1024)S(1)}, f32[1024]{0:T(1024)S(1)}, u32[]{:S(2)}, u32[]{:S(2)}) collective-permute-start(f32[1024]{0:T(1024)S(1)} %bitcast.428), channel_id=1, source_target_pairs={{0,1},{1,2},{2,3},{4,5},{5,6},{6,7},{8,9},{9,10},{10,11},{12,13},{... | collective-permute-start | bytes 12296 | tf_op jit(solution)/shard_map/ppermute | solution.py:13
  10.6 1.2 %and_select_fusion.4 = s32[128]{0:T(128)} fusion(s32[1,128]{1,0:T(1,128)} %param.23), kind=kLoop, calls=%fused_computation.234 | loop fusion | flops 1408 | bytes 1024 | tf_op jit(solution)/shard_map/jit(remainder)/select_n | solution.py:112
  14.2 1.3 %add_select_fusion = s32[2048]{0:T(1024)} fusion(s32[2048]{0:T(1024)} %bitcast.414), kind=kLoop, calls=%fused_computation.212 | loop fusion | flops 22528 | bytes 16384 | tf_op jit(solution)/shard_map/jit(remainder)/select_n | solution.py:112
  16.9 1.3 %add_select_fusion.1 = s32[2048]{0:T(1024)} fusion(s32[2048]{0:T(1024)} %bitcast.415), kind=kLoop, calls=%fused_computation.215 | loop fusion | flops 22528 | bytes 16384 | tf_op jit(solution)/shard_map/jit(remainder)/select_n | solution.py:112
  19.6 1.1 fusion.106
  24.8 1.8 %fusion.1 = f32[288,2048]{1,0:T(8,128)S(1)} fusion(s32[2048]{0:T(1024)S(1)} %copy-done.43, bf16[96,1024]{1,0:T(8,128)(2,1)S(1)} %get-tuple-element.49, bf16[96,1024]{1,0:T(8,128)(2,1)S(1)} %get-tuple-element.48, bf16[96,1024]{1,0:T(8,128)(2,1)S(1)} %bitcast_convert_fusion.2), kind=kOutput, calls=%fused_computation.2 | convolution fusion | flops 1211826176 | bytes 2957312 | tf_op jit(solution)/shard_map/dot_general | solution.py:58
  27.3 1.8 %fusion.3 = f32[288,2048]{1,0:T(8,128)S(1)} fusion(s32[2048]{0:T(1024)S(1)} %copy-done.41, bf16[96,1024]{1,0:T(8,128)(2,1)S(1)} %get-tuple-element.49, bf16[96,1024]{1,0:T(8,128)(2,1)S(1)} %get-tuple-element.48, bf16[96,1024]{1,0:T(8,128)(2,1)S(1)} %bitcast_convert_fusion.2), kind=kOutput, calls=%fused_computation.5 | convolution fusion | flops 1211826176 | bytes 2957312 | tf_op jit(solution)/shard_map/dot_general | solution.py:58
  30.9 1.3 %collective-permute-start.2 = (f32[6,2064]{1,0:T(8,128)}, f32[6,2064]{1,0:T(8,128)}, u32[]{:S(2)}, u32[]{:S(2)}) collective-permute-start(f32[6,2064]{1,0:T(8,128)} %pad_maximum_fusion.8), channel_id=1, source_target_pairs={{4,0},{8,4},{12,8},{16,12},{20,16},{24,20},{28,24},{5,1},{9,5},{13... | collective-permute-start | bytes 148616 | tf_op jit(solution)/shard_map/ppermute | solution.py:13
  32.9 2.1 %collective-permute-start.6 = (f32[4,16]{1,0:T(4,128)S(1)}, f32[4,16]{1,0:T(4,128)S(1)}, u32[]{:S(2)}, u32[]{:S(2)}) collective-permute-start(f32[4,16]{1,0:T(4,128)S(1)} %pad_maximum_fusion.13), channel_id=1, source_target_pairs={{0,1},{1,0},{2,3},{3,2},{4,5},{5,4},{6,7},{7,6},{8,9},{9,8},{10,11... | collective-permute-start | bytes 776 | tf_op jit(solution)/shard_map/ppermute | solution.py:27
  35.9 4.9 %collective-permute-start.3 = (f32[6,2064]{1,0:T(8,128)}, f32[6,2064]{1,0:T(8,128)}, u32[]{:S(2)}, u32[]{:S(2)}) collective-permute-start(f32[6,2064]{1,0:T(8,128)} %pad_maximum_fusion.9), channel_id=1, source_target_pairs={{0,4},{4,8},{8,12},{12,16},{16,20},{20,24},{24,28},{1,5},{5,9},{9,... | collective-permute-start | bytes 148616 | tf_op jit(solution)/shard_map/ppermute | solution.py:13
  40.8 1.3 %collective-permute-start.4 = (f32[6,1024]{1,0:T(8,128)S(1)}, f32[6,1024]{1,0:T(8,128)}, u32[]{:S(2)}, u32[]{:S(2)}) collective-permute-start(f32[6,1024]{1,0:T(8,128)S(1)} %bitcast.407), channel_id=1, source_target_pairs={{1,0},{2,1},{3,2},{5,4},{6,5},{7,6},{9,8},{10,9},{11,10},{13,12},{... | collective-permute-start | bytes 73736 | tf_op jit(solution)/shard_map/ppermute | solution.py:13
  42.1 2.1 %collective-permute-start.7 = (f32[4,16]{1,0:T(4,128)S(1)}, f32[4,16]{1,0:T(4,128)S(1)}, u32[]{:S(2)}, u32[]{:S(2)}) collective-permute-start(f32[4,16]{1,0:T(4,128)S(1)} %fusion.112), channel_id=1, source_target_pairs={{0,2},{1,3},{2,0},{3,1},{4,6},{5,7},{6,4},{7,5},{8,10},{9,11},{10,... | collective-permute-start | bytes 776 | tf_op jit(solution)/shard_map/ppermute | solution.py:27
  44.8 2.1 %collective-permute-start.5 = (f32[6,1024]{1,0:T(8,128)}, f32[6,1024]{1,0:T(8,128)}, u32[]{:S(2)}, u32[]{:S(2)}) collective-permute-start(f32[6,1024]{1,0:T(8,128)} %bitcast.366), channel_id=1, source_target_pairs={{0,1},{1,2},{2,3},{4,5},{5,6},{6,7},{8,9},{9,10},{10,11},{12,13},{... | collective-permute-start | bytes 73736 | tf_op jit(solution)/shard_map/ppermute | solution.py:13
  48.9 1.4 %concatenate.107 = f32[3,2,1,1024]{3,2,1,0:T(1,128)} reshape(f32[6,1024]{1,0:T(8,128)} %collective-permute-done.4) | data formatting | bytes 49152 | tf_op jit(solution)/shard_map/concatenate | solution.py:173
  50.3 1.4 %concatenate.108 = f32[3,2,1,1024]{3,2,1,0:T(1,128)} reshape(f32[6,1024]{1,0:T(8,128)} %collective-permute-done.5) | data formatting | bytes 49152 | tf_op jit(solution)/shard_map/concatenate | solution.py:172
  61.2 3.2 %fusion = f32[288,1024]{1,0:T(8,128)S(1)} fusion(s32[2048]{0:T(1024)S(1)} %copy-done.44, bf16[96,2048]{1,0:T(8,128)(2,1)} %get-tuple-element.31, bf16[96,2048]{1,0:T(8,128)(2,1)} %get-tuple-element.30, bf16[96,2048]{1,0:T(8,128)(2,1)} %bitcast_convert_fusion.1), kind=kOutput, calls=%fused_computation.1 | convolution fusion | flops 1213595648 | bytes 2367488 | tf_op jit(solution)/shard_map/dot_general | solution.py:58
  64.4 1.9 %fusion.2 = f32[288,1024]{1,0:T(8,128)S(1)} fusion(s32[2048]{0:T(1024)S(1)} %copy-done.42, bf16[96,2048]{1,0:T(8,128)(2,1)S(1)} %copy-done.28, bf16[96,2048]{1,0:T(8,128)(2,1)S(1)} %copy-done.27, bf16[96,2048]{1,0:T(8,128)(2,1)S(1)} %copy-done.29), kind=kOutput, calls=%fused_computation.4 | convolution fusion | flops 1213595648 | bytes 2367488 | tf_op jit(solution)/shard_map/dot_general | solution.py:58
  69.0 5.8 %psum.14 = f32[10]{0:T(128)S(1)} all-reduce(f32[10]{0:T(128)S(1)} %reduce_sum.175), channel_id=1, replica_groups=mesh['cells'=8,'slab'=4] {'slab'}, use_global_device_ids=true, to_apply=%region_14.15 | all-reduce | flops 10 | bytes 80 | tf_op jit(solution)/shard_map/psum | solution.py:33
  74.8 1.9 %collective-permute-start.8 = (f32[10]{0:T(128)S(1)}, f32[10]{0:T(128)S(1)}, u32[]{:S(2)}, u32[]{:S(2)}) collective-permute-start(f32[10]{0:T(128)S(1)} %psum.14), channel_id=1, source_target_pairs={{0,4},{4,0},{8,12},{12,8},{16,20},{20,16},{24,28},{28,24},{1,5},{5... | collective-permute-start | bytes 128 | tf_op jit(solution)/shard_map/ppermute | solution.py:40
  76.7 1.7 %collective-permute-done.8 = f32[10]{0:T(128)S(1)} collective-permute-done((f32[10]{0:T(128)S(1)}, f32[10]{0:T(128)S(1)}, u32[]{:S(2)}, u32[]{:S(2)}) %collective-permute-start.8) | collective-permute-done | bytes 72 | tf_op jit(solution)/shard_map/ppermute | solution.py:40
  78.4 1.4 %collective-permute-start.9 = (f32[10]{0:T(128)S(1)}, f32[10]{0:T(128)S(1)}, u32[]{:S(2)}, u32[]{:S(2)}) collective-permute-start(f32[10]{0:T(128)S(1)} %add.242), channel_id=1, source_target_pairs={{0,8},{4,12},{8,0},{12,4},{16,24},{20,28},{24,16},{28,20},{1,9},{5... | collective-permute-start | bytes 128 | tf_op jit(solution)/shard_map/ppermute | solution.py:40
  79.8 2.1 %collective-permute-done.9 = f32[10]{0:T(128)S(1)} collective-permute-done((f32[10]{0:T(128)S(1)}, f32[10]{0:T(128)S(1)}, u32[]{:S(2)}, u32[]{:S(2)}) %collective-permute-start.9) | collective-permute-done | bytes 72 | tf_op jit(solution)/shard_map/ppermute | solution.py:40
  81.9 2.4 %collective-permute-start.10 = (f32[10]{0:T(128)S(1)}, f32[10]{0:T(128)S(1)}, u32[]{:S(2)}, u32[]{:S(2)}) collective-permute-start(f32[10]{0:T(128)S(1)} %add.243), channel_id=1, source_target_pairs={{0,16},{4,20},{8,24},{12,28},{16,0},{20,4},{24,8},{28,12},{1,17},{... | collective-permute-start | bytes 128 | tf_op jit(solution)/shard_map/ppermute | solution.py:40
  84.3 2.0 %collective-permute-done.10 = f32[10]{0:T(128)S(1)} collective-permute-done((f32[10]{0:T(128)S(1)}, f32[10]{0:T(128)S(1)}, u32[]{:S(2)}, u32[]{:S(2)}) %collective-permute-start.10) | collective-permute-done | bytes 72 | tf_op jit(solution)/shard_map/ppermute | solution.py:40
  93.3 5.7 %psum.15 = f32[3]{0:T(128)S(1)} all-reduce(f32[3]{0:T(128)S(1)} %maximum_reduce_fusion), channel_id=1, replica_groups=mesh['cells'=8,'slab'=4] {'slab'}, use_global_device_ids=true, to_apply=%region_19.20 | all-reduce | flops 3 | bytes 24 | tf_op jit(solution)/shard_map/psum | solution.py:33
  99.0 1.9 %collective-permute-start.11 = (f32[3]{0:T(128)S(1)}, f32[3]{0:T(128)S(1)}, u32[]{:S(2)}, u32[]{:S(2)}) collective-permute-start(f32[3]{0:T(128)S(1)} %psum.15), channel_id=1, source_target_pairs={{0,4},{4,0},{8,12},{12,8},{16,20},{20,16},{24,28},{28,24},{1,5},{5... | collective-permute-start | bytes 44 | tf_op jit(solution)/shard_map/ppermute | solution.py:40
  102.5 1.4 %collective-permute-start.12 = (f32[3]{0:T(128)S(1)}, f32[3]{0:T(128)S(1)}, u32[]{:S(2)}, u32[]{:S(2)}) collective-permute-start(f32[3]{0:T(128)S(1)} %add.255), channel_id=1, source_target_pairs={{0,8},{4,12},{8,0},{12,4},{16,24},{20,28},{24,16},{28,20},{1,9},{5... | collective-permute-start | bytes 44 | tf_op jit(solution)/shard_map/ppermute | solution.py:40
  103.9 2.1 %collective-permute-done.12 = f32[3]{0:T(128)S(1)} collective-permute-done((f32[3]{0:T(128)S(1)}, f32[3]{0:T(128)S(1)}, u32[]{:S(2)}, u32[]{:S(2)}) %collective-permute-start.12) | collective-permute-done | bytes 44 | tf_op jit(solution)/shard_map/ppermute | solution.py:40
  106.1 2.4 %collective-permute-start.13 = (f32[3]{0:T(128)S(1)}, f32[3]{0:T(128)S(1)}, u32[]{:S(2)}, u32[]{:S(2)}) collective-permute-start(f32[3]{0:T(128)S(1)} %add.256), channel_id=1, source_target_pairs={{0,16},{4,20},{8,24},{12,28},{16,0},{20,4},{24,8},{28,12},{1,17},{... | collective-permute-start | bytes 44 | tf_op jit(solution)/shard_map/ppermute | solution.py:40
  108.5 2.0 %collective-permute-done.13 = f32[3]{0:T(128)S(1)} collective-permute-done((f32[3]{0:T(128)S(1)}, f32[3]{0:T(128)S(1)}, u32[]{:S(2)}, u32[]{:S(2)}) %collective-permute-start.13) | collective-permute-done | bytes 44 | tf_op jit(solution)/shard_map/ppermute | solution.py:40
  111.1 1.3 %maximum_sqrt_fusion = f32[4]{0:T(128)S(1)} fusion(f32[1]{0:T(128)} %slice.407, f32[1]{0:T(128)} %get-tuple-element.59, f32[2]{0:T(128)S(1)} %bitcast.429), kind=kLoop, calls=%fused_computation.243 | loop fusion | flops 8 | bytes 32 | tf_op jit(solution)/shard_map/sqrt | solution.py:267
  (220 shorter events, 34.2 us)
Async XLA Ops:
  0.6 21.0 %copy-start.32 = (f32[16,1024]{1,0:T(8,128)S(1)}, f32[16,1024]{1,0:T(8,128)}, u32[]{:S(2)}) copy-start(f32[16,1024]{1,0:T(8,128)} %param.17) | copy-start | bytes 196612
  0.6 21.0 %copy-start.33 = (f32[16,1024]{1,0:T(8,128)S(1)}, f32[16,1024]{1,0:T(8,128)}, u32[]{:S(2)}) copy-start(f32[16,1024]{1,0:T(8,128)} %param.18) | copy-start | bytes 196612
  0.7 21.0 %copy-start.2 = (f32[2,2,16,1024]{3,2,1,0:T(8,128)S(1)}, f32[2,2,16,1024]{3,2,1,0:T(8,128)}, u32[]{:S(2)}) copy-start(f32[2,2,16,1024]{3,2,1,0:T(8,128)} %param.15) | copy-start | bytes 786436
  0.7 21.0 %copy-start = (f32[2,4,16,1024]{3,2,1,0:T(8,128)S(1)}, f32[2,4,16,1024]{3,2,1,0:T(8,128)}, u32[]{:S(2)}) copy-start(f32[2,4,16,1024]{3,2,1,0:T(8,128)} %param.14) | copy-start | bytes 1572868
  0.7 20.0 %copy-start.49 = (s32[1,128]{1,0:T(1,128)S(1)}, s32[1,128]{1,0:T(1,128)}, u32[]{:S(2)}) copy-start(s32[1,128]{1,0:T(1,128)} %param.24) | copy-start | bytes 1540
  0.7 20.0 %copy-start.51 = (f32[1,128]{1,0:T(1,128)S(1)}, f32[1,128]{1,0:T(1,128)}, u32[]{:S(2)}) copy-start(f32[1,128]{1,0:T(1,128)} %param.25) | copy-start | bytes 1540
  0.7 21.0 %copy-start.1 = (f32[2,2,16,1024]{3,2,1,0:T(8,128)S(1)}, f32[2,2,16,1024]{3,2,1,0:T(8,128)}, u32[]{:S(2)}) copy-start(f32[2,2,16,1024]{3,2,1,0:T(8,128)} %param.13) | copy-start | bytes 786436
  1.7 20.7 %copy-start.16 = (f32[16,1024]{1,0:T(8,128)}, f32[16,1024]{1,0:T(8,128)S(1)}, u32[]{:S(2)}) copy-start(f32[16,1024]{1,0:T(8,128)S(1)} %broadcast_select_fusion.1) | copy-start | bytes 196612
  3.3 18.2 %collective-permute-start = (f32[2064]{0:T(1024)S(1)}, f32[2064]{0:T(1024)S(1)}, u32[]{:S(2)}, u32[]{:S(2)}) collective-permute-start(f32[2064]{0:T(1024)S(1)} %pad_maximum_fusion.12), channel_id=1, source_target_pairs={{0,4},{4,8},{8,12},{12,16},{16,20},{20,24},{24,28},{1,5},{5,9},{9,... | collective-permute-start | bytes 24776 | tf_op jit(solution)/shard_map/ppermute | solution.py:13
  9.1 13.3 %copy-start.18 = (f32[16,1024]{1,0:T(8,128)}, f32[16,1024]{1,0:T(8,128)S(1)}, u32[]{:S(2)}) copy-start(f32[16,1024]{1,0:T(8,128)S(1)} %broadcast_select_fusion) | copy-start | bytes 196612
  9.1 12.5 %collective-permute-start.1 = (f32[1024]{0:T(1024)S(1)}, f32[1024]{0:T(1024)S(1)}, u32[]{:S(2)}, u32[]{:S(2)}) collective-permute-start(f32[1024]{0:T(1024)S(1)} %bitcast.428), channel_id=1, source_target_pairs={{0,1},{1,2},{2,3},{4,5},{5,6},{6,7},{8,9},{9,10},{10,11},{12,13},{... | collective-permute-start | bytes 12296 | tf_op jit(solution)/shard_map/ppermute | solution.py:13
  29.4 17.6 %copy-start.46 = (f32[2064]{0:T(1024)S(1)}, f32[2064]{0:T(1024)}, u32[]{:S(2)}) copy-start(f32[2064]{0:T(1024)} %copy-done.45) | copy-start | bytes 24772
  30.2 18.7 %copy-start.24 = (f32[6,2048]{1,0:T(8,128)}, f32[6,2048]{1,0:T(8,128)S(1)}, u32[]{:S(2)}) copy-start(f32[6,2048]{1,0:T(8,128)S(1)} %multiply_reduce_fusion.1) | copy-start | bytes 147460
  30.9 20.8 %collective-permute-start.2 = (f32[6,2064]{1,0:T(8,128)}, f32[6,2064]{1,0:T(8,128)}, u32[]{:S(2)}, u32[]{:S(2)}) collective-permute-start(f32[6,2064]{1,0:T(8,128)} %pad_maximum_fusion.8), channel_id=1, source_target_pairs={{4,0},{8,4},{12,8},{16,12},{20,16},{24,20},{28,24},{5,1},{9,5},{13... | collective-permute-start | bytes 148616 | tf_op jit(solution)/shard_map/ppermute | solution.py:13
  32.9 9.2 %collective-permute-start.6 = (f32[4,16]{1,0:T(4,128)S(1)}, f32[4,16]{1,0:T(4,128)S(1)}, u32[]{:S(2)}, u32[]{:S(2)}) collective-permute-start(f32[4,16]{1,0:T(4,128)S(1)} %pad_maximum_fusion.13), channel_id=1, source_target_pairs={{0,1},{1,0},{2,3},{3,2},{4,5},{5,4},{6,7},{7,6},{8,9},{9,8},{10,11... | collective-permute-start | bytes 776 | tf_op jit(solution)/shard_map/ppermute | solution.py:27
  35.2 13.8 %copy-start.26 = (f32[6,2048]{1,0:T(8,128)}, f32[6,2048]{1,0:T(8,128)S(1)}, u32[]{:S(2)}) copy-start(f32[6,2048]{1,0:T(8,128)S(1)} %multiply_reduce_fusion) | copy-start | bytes 147460
  35.9 19.7 %collective-permute-start.3 = (f32[6,2064]{1,0:T(8,128)}, f32[6,2064]{1,0:T(8,128)}, u32[]{:S(2)}, u32[]{:S(2)}) collective-permute-start(f32[6,2064]{1,0:T(8,128)} %pad_maximum_fusion.9), channel_id=1, source_target_pairs={{0,4},{4,8},{8,12},{12,16},{16,20},{20,24},{24,28},{1,5},{5,9},{9,... | collective-permute-start | bytes 148616 | tf_op jit(solution)/shard_map/ppermute | solution.py:13
  40.8 8.2 %collective-permute-start.4 = (f32[6,1024]{1,0:T(8,128)S(1)}, f32[6,1024]{1,0:T(8,128)}, u32[]{:S(2)}, u32[]{:S(2)}) collective-permute-start(f32[6,1024]{1,0:T(8,128)S(1)} %bitcast.407), channel_id=1, source_target_pairs={{1,0},{2,1},{3,2},{5,4},{6,5},{7,6},{9,8},{10,9},{11,10},{13,12},{... | collective-permute-start | bytes 73736 | tf_op jit(solution)/shard_map/ppermute | solution.py:13
  42.1 5.5 %collective-permute-start.7 = (f32[4,16]{1,0:T(4,128)S(1)}, f32[4,16]{1,0:T(4,128)S(1)}, u32[]{:S(2)}, u32[]{:S(2)}) collective-permute-start(f32[4,16]{1,0:T(4,128)S(1)} %fusion.112), channel_id=1, source_target_pairs={{0,2},{1,3},{2,0},{3,1},{4,6},{5,7},{6,4},{7,5},{8,10},{9,11},{10,... | collective-permute-start | bytes 776 | tf_op jit(solution)/shard_map/ppermute | solution.py:27
  44.8 5.6 %collective-permute-start.5 = (f32[6,1024]{1,0:T(8,128)}, f32[6,1024]{1,0:T(8,128)}, u32[]{:S(2)}, u32[]{:S(2)}) collective-permute-start(f32[6,1024]{1,0:T(8,128)} %bitcast.366), channel_id=1, source_target_pairs={{0,1},{1,2},{2,3},{4,5},{5,6},{6,7},{8,9},{9,10},{10,11},{12,13},{... | collective-permute-start | bytes 73736 | tf_op jit(solution)/shard_map/ppermute | solution.py:13
  67.8 25.2 %copy-start.12 = (f32[16,1024]{1,0:T(8,128)S(1)}, f32[16,1024]{1,0:T(8,128)}, u32[]{:S(2)}) copy-start(f32[16,1024]{1,0:T(8,128)} %copy-done.11) | copy-start | bytes 196612
  67.8 25.2 %copy-start.14 = (f32[16,1024]{1,0:T(8,128)S(1)}, f32[16,1024]{1,0:T(8,128)}, u32[]{:S(2)}) copy-start(f32[16,1024]{1,0:T(8,128)} %copy-done.13) | copy-start | bytes 196612
  67.8 25.2 %copy-start.35 = (f32[2,2,16,1024]{3,2,1,0:T(8,128)S(1)}, f32[2,2,16,1024]{3,2,1,0:T(8,128)}, u32[]{:S(2)}) copy-start(f32[2,2,16,1024]{3,2,1,0:T(8,128)} %param.16) | copy-start | bytes 786436
  68.0 32.9 %copy-start.10 = (f32[16,1024]{1,0:T(8,128)S(1)}, f32[16,1024]{1,0:T(8,128)}, u32[]{:S(2)}) copy-start(f32[16,1024]{1,0:T(8,128)} %copy-done.9) | copy-start | bytes 196612
  68.0 32.9 %copy-start.21 = (f32[16,1024]{1,0:T(8,128)S(1)}, f32[16,1024]{1,0:T(8,128)}, u32[]{:S(2)}) copy-start(f32[16,1024]{1,0:T(8,128)} %copy-done.20) | copy-start | bytes 196612
  68.0 32.9 %copy-start.23 = (f32[16,1024]{1,0:T(8,128)S(1)}, f32[16,1024]{1,0:T(8,128)}, u32[]{:S(2)}) copy-start(f32[16,1024]{1,0:T(8,128)} %copy-done.22) | copy-start | bytes 196612
  74.8 3.6 %collective-permute-start.8 = (f32[10]{0:T(128)S(1)}, f32[10]{0:T(128)S(1)}, u32[]{:S(2)}, u32[]{:S(2)}) collective-permute-start(f32[10]{0:T(128)S(1)} %psum.14), channel_id=1, source_target_pairs={{0,4},{4,0},{8,12},{12,8},{16,20},{20,16},{24,28},{28,24},{1,5},{5... | collective-permute-start | bytes 128 | tf_op jit(solution)/shard_map/ppermute | solution.py:40
  78.4 3.5 %collective-permute-start.9 = (f32[10]{0:T(128)S(1)}, f32[10]{0:T(128)S(1)}, u32[]{:S(2)}, u32[]{:S(2)}) collective-permute-start(f32[10]{0:T(128)S(1)} %add.242), channel_id=1, source_target_pairs={{0,8},{4,12},{8,0},{12,4},{16,24},{20,28},{24,16},{28,20},{1,9},{5... | collective-permute-start | bytes 128 | tf_op jit(solution)/shard_map/ppermute | solution.py:40
  81.9 4.4 %collective-permute-start.10 = (f32[10]{0:T(128)S(1)}, f32[10]{0:T(128)S(1)}, u32[]{:S(2)}, u32[]{:S(2)}) collective-permute-start(f32[10]{0:T(128)S(1)} %add.243), channel_id=1, source_target_pairs={{0,16},{4,20},{8,24},{12,28},{16,0},{20,4},{24,8},{28,12},{1,17},{... | collective-permute-start | bytes 128 | tf_op jit(solution)/shard_map/ppermute | solution.py:40
  99.0 3.6 %collective-permute-start.11 = (f32[3]{0:T(128)S(1)}, f32[3]{0:T(128)S(1)}, u32[]{:S(2)}, u32[]{:S(2)}) collective-permute-start(f32[3]{0:T(128)S(1)} %psum.15), channel_id=1, source_target_pairs={{0,4},{4,0},{8,12},{12,8},{16,20},{20,16},{24,28},{28,24},{1,5},{5... | collective-permute-start | bytes 44 | tf_op jit(solution)/shard_map/ppermute | solution.py:40
  102.5 3.5 %collective-permute-start.12 = (f32[3]{0:T(128)S(1)}, f32[3]{0:T(128)S(1)}, u32[]{:S(2)}, u32[]{:S(2)}) collective-permute-start(f32[3]{0:T(128)S(1)} %add.255), channel_id=1, source_target_pairs={{0,8},{4,12},{8,0},{12,4},{16,24},{20,28},{24,16},{28,20},{1,9},{5... | collective-permute-start | bytes 44 | tf_op jit(solution)/shard_map/ppermute | solution.py:40
  106.1 4.4 %collective-permute-start.13 = (f32[3]{0:T(128)S(1)}, f32[3]{0:T(128)S(1)}, u32[]{:S(2)}, u32[]{:S(2)}) collective-permute-start(f32[3]{0:T(128)S(1)} %add.256), channel_id=1, source_target_pairs={{0,16},{4,20},{8,24},{12,28},{16,0},{20,4},{24,8},{28,12},{1,17},{... | collective-permute-start | bytes 44 | tf_op jit(solution)/shard_map/ppermute | solution.py:40
  (35 other events, 74.6 us)

commit v3 on v2

--- a/solution.py
+++ b/solution.py
@@ -30,17 +30,11 @@
 
 
 def global_sum(values):
-    stacked = lax.psum(values, "slab")
-    count = lax.axis_size("cells")
-    if count & (count - 1):
-        stacked = lax.psum(stacked, "cells")
-    else:
-        step = 1
-        while step < count:
-            stacked = stacked + lax.ppermute(
-                stacked, "cells", [(i, i ^ step) for i in range(count)]
-            )
-            step *= 2
+    axes = ("cells", "slab")
+    count = lax.axis_size("cells") * lax.axis_size("slab")
+    copies = jnp.broadcast_to(values[None], (count,) + values.shape)
+    gathered = lax.all_to_all(copies, axes, 0, 0, tiled=True)
+    stacked = jnp.sum(gathered, axis=0)
     return [stacked[i] for i in range(values.shape[0])]
 
 

time: 114 us -> 102 us (0.89)
  starting transfers between devices: 31.4 us -> 22.6 us
  waiting for transfers between devices: 11 us -> 6.34 us
    all_to_all x0 -> x1, blocking collectives: none -> 11.4 us  [global_sum(): gathered = lax.all_to_all(copies, axes, 0, 0, tiled=True)]
    psum x2 -> x0, blocking collectives: 11.4 us -> none  [global_sum(): stacked = lax.psum(values, 'slab')]
    ppermute x6 -> x0, starting transfers between devices: 11.3 us -> none  [global_sum(): lax.ppermute(stacked, 'cells', [(i, i ^ step) for i in range(count)])]
    ppermute x6 -> x0, waiting for transfers between devices: 11 us -> none  [global_sum(): lax.ppermute(stacked, 'cells', [(i, i ^ step) for i in range(count)])]
    all_to_all x0 -> x1, waiting for transfers between devices: none -> 6.31 us  [global_sum(): gathered = lax.all_to_all(copies, axes, 0, 0, tiled=True)]
    all_to_all x0 -> x1, starting transfers between devices: none -> 2.51 us  [global_sum(): gathered = lax.all_to_all(copies, axes, 0, 0, tiled=True)]
  transfers between devices with their start and end apart: 14 -> 9, of which waited for: 6 -> 1; matrix products, arithmetic and copies ran while one was open for 21% -> 23% of each run, Pallas kernels for 0% -> 0%
where the time goes in v3:
time: 102 us; the launch traced here: 100 us
  other arithmetic  24.9 us (24%)
  starting transfers between devices  22.6 us (22%)
  local copies, waits for them, and re-layouts  16.3 us (16%)
  blocking collectives  11.4 us (11%)
  matrix products  10.5 us (10%)
  between operations  8.23 us (8%)
  waiting for transfers between devices  6.34 us (6%)
    ppermute x6, starting transfers between devices, shifted(): return lax.ppermute(value, axis, pairs)  15.9 us
    all_to_all x1, blocking collectives, global_sum(): gathered = lax.all_to_all(copies, axes, 0, 0, tiled=True)  11.4 us
    dot_general x6, matrix products, onehot_dot(): lax.dot_general(pieces, onehot, (dims, ((), ())), preferred_element_type=...  9.41 us
    all_to_all x1, waiting for transfers between devices, global_sum(): gathered = lax.all_to_all(copies, axes, 0, 0, tiled=True)  6.31 us
    ppermute x2, starting transfers between devices, butterfly(): lax.ppermute(value, axis, [(i, i ^ step) for i in range(count)])  4.18 us
    unnamed x121, local copies, waits for them, and re-layouts  3.88 us
    select_n x3, other arithmetic, locate(): onehot = (cells % column_count)[:, None] == column_iota[None, :]  3.85 us
    all_to_all x1, starting transfers between devices, global_sum(): gathered = lax.all_to_all(copies, axes, 0, 0, tiled=True)  2.51 us
  transfers between devices with their start and end apart: 9, of which 1 were waited for; matrix products, arithmetic and copies ran while one was open for 23% of the time, Pallas kernels for 0%

profile of v3, /device:TPU:0, one launch (start us, length us, event | category | flops | bytes accessed | tf_op | source)
XLA Modules:
  0.0 100.4 jit_solution(14986214141710849436)
XLA Ops:
  0.7 1.0 broadcast_select_fusion.1
  3.3 4.9 %collective-permute-start = (f32[2064]{0:T(1024)S(1)}, f32[2064]{0:T(1024)S(1)}, u32[]{:S(2)}, u32[]{:S(2)}) collective-permute-start(f32[2064]{0:T(1024)S(1)} %pad_maximum_fusion.12), channel_id=1, source_target_pairs={{0,4},{4,8},{8,12},{12,16},{16,20},{20,24},{24,28},{1,5},{5,9},{9,... | collective-permute-start | bytes 24776 | tf_op jit(solution)/shard_map/ppermute | solution.py:13
  8.2 0.9 broadcast_select_fusion
  9.1 1.5 %collective-permute-start.1 = (f32[1024]{0:T(1024)S(1)}, f32[1024]{0:T(1024)S(1)}, u32[]{:S(2)}, u32[]{:S(2)}) collective-permute-start(f32[1024]{0:T(1024)S(1)} %bitcast.428), channel_id=1, source_target_pairs={{0,1},{1,2},{2,3},{4,5},{5,6},{6,7},{8,9},{9,10},{10,11},{12,13},{... | collective-permute-start | bytes 12296 | tf_op jit(solution)/shard_map/ppermute | solution.py:13
  10.6 1.2 %and_select_fusion.4 = s32[128]{0:T(128)} fusion(s32[1,128]{1,0:T(1,128)} %param.23), kind=kLoop, calls=%fused_computation.234 | loop fusion | flops 1408 | bytes 1024 | tf_op jit(solution)/shard_map/jit(remainder)/select_n | solution.py:106
  12.5 1.0 fusion.110
  14.2 1.3 %add_select_fusion = s32[2048]{0:T(1024)} fusion(s32[2048]{0:T(1024)} %bitcast.414), kind=kLoop, calls=%fused_computation.212 | loop fusion | flops 22528 | bytes 16384 | tf_op jit(solution)/shard_map/jit(remainder)/select_n | solution.py:106
  16.9 1.3 %add_select_fusion.1 = s32[2048]{0:T(1024)} fusion(s32[2048]{0:T(1024)} %bitcast.415), kind=kLoop, calls=%fused_computation.215 | loop fusion | flops 22528 | bytes 16384 | tf_op jit(solution)/shard_map/jit(remainder)/select_n | solution.py:106
  19.6 1.1 %fusion.106 = (f32[1,4,16,1024]{3,2,1,0:T(8,128)S(1)}, f32[1,4,16,1024]{3,2,1,0:T(8,128)S(1)}) fusion(f32[2,4,16,1024]{3,2,1,0:T(8,128)} %param.14), kind=kLoop, calls=%fused_computation.255 | loop fusion | bytes 1048576 | tf_op jit(solution)/shard_map/slice | solution.py:208
  23.9 0.8 fusion.108
  24.8 1.8 %fusion.1 = f32[288,2048]{1,0:T(8,128)S(1)} fusion(s32[2048]{0:T(1024)S(1)} %copy-done.43, bf16[96,1024]{1,0:T(8,128)(2,1)S(1)} %get-tuple-element.49, bf16[96,1024]{1,0:T(8,128)(2,1)S(1)} %get-tuple-element.48, bf16[96,1024]{1,0:T(8,128)(2,1)S(1)} %bitcast_convert_fusion.2), kind=kOutput, calls=%fused_computation.2 | convolution fusion | flops 1211826176 | bytes 2957312 | tf_op jit(solution)/shard_map/dot_general | solution.py:52
  27.4 1.8 %fusion.3 = f32[288,2048]{1,0:T(8,128)S(1)} fusion(s32[2048]{0:T(1024)S(1)} %copy-done.41, bf16[96,1024]{1,0:T(8,128)(2,1)S(1)} %get-tuple-element.49, bf16[96,1024]{1,0:T(8,128)(2,1)S(1)} %get-tuple-element.48, bf16[96,1024]{1,0:T(8,128)(2,1)S(1)} %bitcast_convert_fusion.2), kind=kOutput, calls=%fused_computation.5 | convolution fusion | flops 1211826176 | bytes 2957312 | tf_op jit(solution)/shard_map/dot_general | solution.py:52
  31.0 1.3 %collective-permute-start.2 = (f32[6,2064]{1,0:T(8,128)}, f32[6,2064]{1,0:T(8,128)}, u32[]{:S(2)}, u32[]{:S(2)}) collective-permute-start(f32[6,2064]{1,0:T(8,128)} %pad_maximum_fusion.8), channel_id=1, source_target_pairs={{4,0},{8,4},{12,8},{16,12},{20,16},{24,20},{28,24},{5,1},{9,5},{13... | collective-permute-start | bytes 148616 | tf_op jit(solution)/shard_map/ppermute | solution.py:13
  32.9 2.1 %collective-permute-start.6 = (f32[4,16]{1,0:T(4,128)S(1)}, f32[4,16]{1,0:T(4,128)S(1)}, u32[]{:S(2)}, u32[]{:S(2)}) collective-permute-start(f32[4,16]{1,0:T(4,128)S(1)} %pad_maximum_fusion.13), channel_id=1, source_target_pairs={{0,1},{1,0},{2,3},{3,2},{4,5},{5,4},{6,7},{7,6},{8,9},{9,8},{10,11... | collective-permute-start | bytes 776 | tf_op jit(solution)/shard_map/ppermute | solution.py:27
  35.9 4.9 %collective-permute-start.3 = (f32[6,2064]{1,0:T(8,128)}, f32[6,2064]{1,0:T(8,128)}, u32[]{:S(2)}, u32[]{:S(2)}) collective-permute-start(f32[6,2064]{1,0:T(8,128)} %pad_maximum_fusion.9), channel_id=1, source_target_pairs={{0,4},{4,8},{8,12},{12,16},{16,20},{20,24},{24,28},{1,5},{5,9},{9,... | collective-permute-start | bytes 148616 | tf_op jit(solution)/shard_map/ppermute | solution.py:13
  40.8 1.3 %collective-permute-start.4 = (f32[6,1024]{1,0:T(8,128)S(1)}, f32[6,1024]{1,0:T(8,128)}, u32[]{:S(2)}, u32[]{:S(2)}) collective-permute-start(f32[6,1024]{1,0:T(8,128)S(1)} %bitcast.407), channel_id=1, source_target_pairs={{1,0},{2,1},{3,2},{5,4},{6,5},{7,6},{9,8},{10,9},{11,10},{13,12},{... | collective-permute-start | bytes 73736 | tf_op jit(solution)/shard_map/ppermute | solution.py:13
  42.1 2.1 %collective-permute-start.7 = (f32[4,16]{1,0:T(4,128)S(1)}, f32[4,16]{1,0:T(4,128)S(1)}, u32[]{:S(2)}, u32[]{:S(2)}) collective-permute-start(f32[4,16]{1,0:T(4,128)S(1)} %fusion.112), channel_id=1, source_target_pairs={{0,2},{1,3},{2,0},{3,1},{4,6},{5,7},{6,4},{7,5},{8,10},{9,11},{10,... | collective-permute-start | bytes 776 | tf_op jit(solution)/shard_map/ppermute | solution.py:27
  44.8 2.1 %collective-permute-start.5 = (f32[6,1024]{1,0:T(8,128)}, f32[6,1024]{1,0:T(8,128)}, u32[]{:S(2)}, u32[]{:S(2)}) collective-permute-start(f32[6,1024]{1,0:T(8,128)} %bitcast.366), channel_id=1, source_target_pairs={{0,1},{1,2},{2,3},{4,5},{5,6},{6,7},{8,9},{9,10},{10,11},{12,13},{... | collective-permute-start | bytes 73736 | tf_op jit(solution)/shard_map/ppermute | solution.py:13
  49.0 1.4 %concatenate.107 = f32[3,2,1,1024]{3,2,1,0:T(1,128)} reshape(f32[6,1024]{1,0:T(8,128)} %collective-permute-done.4) | data formatting | bytes 49152 | tf_op jit(solution)/shard_map/concatenate | solution.py:167
  50.4 1.4 %concatenate.108 = f32[3,2,1,1024]{3,2,1,0:T(1,128)} reshape(f32[6,1024]{1,0:T(8,128)} %collective-permute-done.5) | data formatting | bytes 49152 | tf_op jit(solution)/shard_map/concatenate | solution.py:166
  51.8 1.0 %fusion.59 = f32[6,2048]{1,0:T(8,128)S(1)} fusion(f32[6,2048]{1,0:T(8,128)} %copy-done.26, f32[6,2064]{1,0:T(8,128)} %collective-permute-done.2, f32[2048]{0:T(1024)S(1)} %bitcast.408), kind=kLoop, calls=%fused_computation.138 | loop fusion | flops 24576 | bytes 155648 | tf_op jit(solution)/shard_map/mul | solution.py:174
  52.8 1.0 broadcast_multiply_fusion.1
  53.8 1.0 fusion.19
  54.8 0.8 bitcast_convert_fusion.1
  55.6 1.0 fusion.58
  56.7 1.0 %fusion.20 = (bf16[96,2048]{1,0:T(8,128)(2,1)}, bf16[96,2048]{1,0:T(8,128)(2,1)}) fusion(f32[6,16,2048]{2,1,0:T(8,128)S(1)} %broadcast_multiply_fusion), kind=kLoop, calls=%fused_computation.37 | loop fusion | flops 1376256 | bytes 1572864 | tf_op jit(solution)/shard_map/convert_element_type | solution.py:44
  61.2 3.2 %fusion = f32[288,1024]{1,0:T(8,128)S(1)} fusion(s32[2048]{0:T(1024)S(1)} %copy-done.44, bf16[96,2048]{1,0:T(8,128)(2,1)} %get-tuple-element.31, bf16[96,2048]{1,0:T(8,128)(2,1)} %get-tuple-element.30, bf16[96,2048]{1,0:T(8,128)(2,1)} %bitcast_convert_fusion.1), kind=kOutput, calls=%fused_computation.1 | convolution fusion | flops 1213595648 | bytes 2367488 | tf_op jit(solution)/shard_map/dot_general | solution.py:52
  64.5 1.9 %fusion.2 = f32[288,1024]{1,0:T(8,128)S(1)} fusion(s32[2048]{0:T(1024)S(1)} %copy-done.42, bf16[96,2048]{1,0:T(8,128)(2,1)S(1)} %copy-done.28, bf16[96,2048]{1,0:T(8,128)(2,1)S(1)} %copy-done.27, bf16[96,2048]{1,0:T(8,128)(2,1)S(1)} %copy-done.29), kind=kOutput, calls=%fused_computation.4 | convolution fusion | flops 1213595648 | bytes 2367488 | tf_op jit(solution)/shard_map/dot_general | solution.py:52
  69.1 11.4 %all_to_all.12 = f32[32,1,10]{2,1,0:T(1,128)S(1)} all-to-all(f32[32,1,10]{2,1,0:T(1,128)S(1)} %broadcast_in_dim.27), channel_id=1, replica_groups=mesh['cells'=8,'slab'=4] {'cells','slab'}, dimensions={0} | all-to-all | bytes 2560 | tf_op jit(solution)/shard_map/all_to_all | solution.py:36
  88.1 2.5 %all-to-all-start.1 = ((f32[32,1,3]{2,1,0:T(1,128)}), f32[32,1,3]{2,1,0:T(1,128)S(1)}, u32[]{:S(2)}, u32[]{:S(2)}) async-start(f32[32,1,3]{2,1,0:T(1,128)} %broadcast_in_dim.28), calls=%async_computation.1 | async-start | bytes 32768 | tf_op jit(solution)/shard_map/all_to_all | solution.py:36
  91.4 6.3 %all-to-all-done.1 = f32[32,1,3]{2,1,0:T(1,128)S(1)} async-done(((f32[32,1,3]{2,1,0:T(1,128)}), f32[32,1,3]{2,1,0:T(1,128)S(1)}, u32[]{:S(2)}, u32[]{:S(2)}) %all-to-all-start.1) | async-done | bytes 416 | tf_op jit(solution)/shard_map/all_to_all | solution.py:36
  98.4 1.4 %maximum_sqrt_fusion = f32[4]{0:T(128)S(1)} fusion(f32[1]{0:T(128)} %slice.407, f32[1]{0:T(128)} %get-tuple-element.59, f32[2]{0:T(128)S(1)} %bitcast.429), kind=kLoop, calls=%fused_computation.243 | loop fusion | flops 8 | bytes 32 | tf_op jit(solution)/shard_map/sqrt | solution.py:261
  (207 shorter events, 24.6 us)
Async XLA Ops:
  0.6 21.0 %copy-start.32 = (f32[16,1024]{1,0:T(8,128)S(1)}, f32[16,1024]{1,0:T(8,128)}, u32[]{:S(2)}) copy-start(f32[16,1024]{1,0:T(8,128)} %param.17) | copy-start | bytes 196612
  0.6 21.0 %copy-start.33 = (f32[16,1024]{1,0:T(8,128)S(1)}, f32[16,1024]{1,0:T(8,128)}, u32[]{:S(2)}) copy-start(f32[16,1024]{1,0:T(8,128)} %param.18) | copy-start | bytes 196612
  0.7 21.0 %copy-start.2 = (f32[2,2,16,1024]{3,2,1,0:T(8,128)S(1)}, f32[2,2,16,1024]{3,2,1,0:T(8,128)}, u32[]{:S(2)}) copy-start(f32[2,2,16,1024]{3,2,1,0:T(8,128)} %param.15) | copy-start | bytes 786436
  0.7 21.0 %copy-start = (f32[2,4,16,1024]{3,2,1,0:T(8,128)S(1)}, f32[2,4,16,1024]{3,2,1,0:T(8,128)}, u32[]{:S(2)}) copy-start(f32[2,4,16,1024]{3,2,1,0:T(8,128)} %param.14) | copy-start | bytes 1572868
  0.7 20.0 %copy-start.49 = (s32[1,128]{1,0:T(1,128)S(1)}, s32[1,128]{1,0:T(1,128)}, u32[]{:S(2)}) copy-start(s32[1,128]{1,0:T(1,128)} %param.24) | copy-start | bytes 1540
  0.7 20.0 %copy-start.51 = (f32[1,128]{1,0:T(1,128)S(1)}, f32[1,128]{1,0:T(1,128)}, u32[]{:S(2)}) copy-start(f32[1,128]{1,0:T(1,128)} %param.25) | copy-start | bytes 1540
  0.7 21.0 %copy-start.1 = (f32[2,2,16,1024]{3,2,1,0:T(8,128)S(1)}, f32[2,2,16,1024]{3,2,1,0:T(8,128)}, u32[]{:S(2)}) copy-start(f32[2,2,16,1024]{3,2,1,0:T(8,128)} %param.13) | copy-start | bytes 786436
  1.7 20.7 %copy-start.16 = (f32[16,1024]{1,0:T(8,128)}, f32[16,1024]{1,0:T(8,128)S(1)}, u32[]{:S(2)}) copy-start(f32[16,1024]{1,0:T(8,128)S(1)} %broadcast_select_fusion.1) | copy-start | bytes 196612
  3.3 18.2 %collective-permute-start = (f32[2064]{0:T(1024)S(1)}, f32[2064]{0:T(1024)S(1)}, u32[]{:S(2)}, u32[]{:S(2)}) collective-permute-start(f32[2064]{0:T(1024)S(1)} %pad_maximum_fusion.12), channel_id=1, source_target_pairs={{0,4},{4,8},{8,12},{12,16},{16,20},{20,24},{24,28},{1,5},{5,9},{9,... | collective-permute-start | bytes 24776 | tf_op jit(solution)/shard_map/ppermute | solution.py:13
  9.1 13.3 %copy-start.18 = (f32[16,1024]{1,0:T(8,128)}, f32[16,1024]{1,0:T(8,128)S(1)}, u32[]{:S(2)}) copy-start(f32[16,1024]{1,0:T(8,128)S(1)} %broadcast_select_fusion) | copy-start | bytes 196612
  9.1 12.5 %collective-permute-start.1 = (f32[1024]{0:T(1024)S(1)}, f32[1024]{0:T(1024)S(1)}, u32[]{:S(2)}, u32[]{:S(2)}) collective-permute-start(f32[1024]{0:T(1024)S(1)} %bitcast.428), channel_id=1, source_target_pairs={{0,1},{1,2},{2,3},{4,5},{5,6},{6,7},{8,9},{9,10},{10,11},{12,13},{... | collective-permute-start | bytes 12296 | tf_op jit(solution)/shard_map/ppermute | solution.py:13
  29.2 5.8 %copy-start.6 = (f32[16,2048]{1,0:T(8,128)S(1)}, f32[16,2048]{1,0:T(8,128)}, u32[]{:S(2)}) copy-start(f32[16,2048]{1,0:T(8,128)} %fusion.56) | copy-start | bytes 393220
  29.4 17.6 %copy-start.46 = (f32[2064]{0:T(1024)S(1)}, f32[2064]{0:T(1024)}, u32[]{:S(2)}) copy-start(f32[2064]{0:T(1024)} %copy-done.45) | copy-start | bytes 24772
  30.3 18.7 %copy-start.24 = (f32[6,2048]{1,0:T(8,128)}, f32[6,2048]{1,0:T(8,128)S(1)}, u32[]{:S(2)}) copy-start(f32[6,2048]{1,0:T(8,128)S(1)} %multiply_reduce_fusion.1) | copy-start | bytes 147460
  31.0 20.8 %collective-permute-start.2 = (f32[6,2064]{1,0:T(8,128)}, f32[6,2064]{1,0:T(8,128)}, u32[]{:S(2)}, u32[]{:S(2)}) collective-permute-start(f32[6,2064]{1,0:T(8,128)} %pad_maximum_fusion.8), channel_id=1, source_target_pairs={{4,0},{8,4},{12,8},{16,12},{20,16},{24,20},{28,24},{5,1},{9,5},{13... | collective-permute-start | bytes 148616 | tf_op jit(solution)/shard_map/ppermute | solution.py:13
  32.9 9.2 %collective-permute-start.6 = (f32[4,16]{1,0:T(4,128)S(1)}, f32[4,16]{1,0:T(4,128)S(1)}, u32[]{:S(2)}, u32[]{:S(2)}) collective-permute-start(f32[4,16]{1,0:T(4,128)S(1)} %pad_maximum_fusion.13), channel_id=1, source_target_pairs={{0,1},{1,0},{2,3},{3,2},{4,5},{5,4},{6,7},{7,6},{8,9},{9,8},{10,11... | collective-permute-start | bytes 776 | tf_op jit(solution)/shard_map/ppermute | solution.py:27
  35.2 13.8 %copy-start.26 = (f32[6,2048]{1,0:T(8,128)}, f32[6,2048]{1,0:T(8,128)S(1)}, u32[]{:S(2)}) copy-start(f32[6,2048]{1,0:T(8,128)S(1)} %multiply_reduce_fusion) | copy-start | bytes 147460
  35.9 19.7 %collective-permute-start.3 = (f32[6,2064]{1,0:T(8,128)}, f32[6,2064]{1,0:T(8,128)}, u32[]{:S(2)}, u32[]{:S(2)}) collective-permute-start(f32[6,2064]{1,0:T(8,128)} %pad_maximum_fusion.9), channel_id=1, source_target_pairs={{0,4},{4,8},{8,12},{12,16},{16,20},{20,24},{24,28},{1,5},{5,9},{9,... | collective-permute-start | bytes 148616 | tf_op jit(solution)/shard_map/ppermute | solution.py:13
  40.8 8.2 %collective-permute-start.4 = (f32[6,1024]{1,0:T(8,128)S(1)}, f32[6,1024]{1,0:T(8,128)}, u32[]{:S(2)}, u32[]{:S(2)}) collective-permute-start(f32[6,1024]{1,0:T(8,128)S(1)} %bitcast.407), channel_id=1, source_target_pairs={{1,0},{2,1},{3,2},{5,4},{6,5},{7,6},{9,8},{10,9},{11,10},{13,12},{... | collective-permute-start | bytes 73736 | tf_op jit(solution)/shard_map/ppermute | solution.py:13
  42.1 5.5 %collective-permute-start.7 = (f32[4,16]{1,0:T(4,128)S(1)}, f32[4,16]{1,0:T(4,128)S(1)}, u32[]{:S(2)}, u32[]{:S(2)}) collective-permute-start(f32[4,16]{1,0:T(4,128)S(1)} %fusion.112), channel_id=1, source_target_pairs={{0,2},{1,3},{2,0},{3,1},{4,6},{5,7},{6,4},{7,5},{8,10},{9,11},{10,... | collective-permute-start | bytes 776 | tf_op jit(solution)/shard_map/ppermute | solution.py:27
  44.8 5.6 %collective-permute-start.5 = (f32[6,1024]{1,0:T(8,128)}, f32[6,1024]{1,0:T(8,128)}, u32[]{:S(2)}, u32[]{:S(2)}) collective-permute-start(f32[6,1024]{1,0:T(8,128)} %bitcast.366), channel_id=1, source_target_pairs={{0,1},{1,2},{2,3},{4,5},{5,6},{6,7},{8,9},{9,10},{10,11},{12,13},{... | collective-permute-start | bytes 73736 | tf_op jit(solution)/shard_map/ppermute | solution.py:13
  49.0 6.6 %copy-start.40 = (f32[2048]{0:T(1024)S(1)}, f32[2048]{0:T(1024)}, u32[]{:S(2)}) copy-start(f32[2048]{0:T(1024)} %slice.439) | copy-start | bytes 24580
  51.8 3.8 %copy-start.25 = (f32[6,2048]{1,0:T(8,128)S(1)}, f32[6,2048]{1,0:T(8,128)}, u32[]{:S(2)}) copy-start(f32[6,2048]{1,0:T(8,128)} %copy-done.24) | copy-start | bytes 147460
  51.8 4.8 %copy-start.5 = (f32[16,2048]{1,0:T(8,128)S(1)}, f32[16,2048]{1,0:T(8,128)}, u32[]{:S(2)}) copy-start(f32[16,2048]{1,0:T(8,128)} %fusion.55) | copy-start | bytes 393220
  55.6 5.6 %copy-start.44 = (s32[2048]{0:T(1024)S(1)}, s32[2048]{0:T(1024)}, u32[]{:S(2)}) copy-start(s32[2048]{0:T(1024)} %add_select_fusion) | copy-start | bytes 24580
  67.8 19.3 %copy-start.12 = (f32[16,1024]{1,0:T(8,128)S(1)}, f32[16,1024]{1,0:T(8,128)}, u32[]{:S(2)}) copy-start(f32[16,1024]{1,0:T(8,128)} %copy-done.11) | copy-start | bytes 196612
  67.8 19.3 %copy-start.14 = (f32[16,1024]{1,0:T(8,128)S(1)}, f32[16,1024]{1,0:T(8,128)}, u32[]{:S(2)}) copy-start(f32[16,1024]{1,0:T(8,128)} %copy-done.13) | copy-start | bytes 196612
  67.9 19.3 %copy-start.35 = (f32[2,2,16,1024]{3,2,1,0:T(8,128)S(1)}, f32[2,2,16,1024]{3,2,1,0:T(8,128)}, u32[]{:S(2)}) copy-start(f32[2,2,16,1024]{3,2,1,0:T(8,128)} %param.16) | copy-start | bytes 786436
  68.0 22.6 %copy-start.10 = (f32[16,1024]{1,0:T(8,128)S(1)}, f32[16,1024]{1,0:T(8,128)}, u32[]{:S(2)}) copy-start(f32[16,1024]{1,0:T(8,128)} %copy-done.9) | copy-start | bytes 196612
  68.0 22.6 %copy-start.21 = (f32[16,1024]{1,0:T(8,128)S(1)}, f32[16,1024]{1,0:T(8,128)}, u32[]{:S(2)}) copy-start(f32[16,1024]{1,0:T(8,128)} %copy-done.20) | copy-start | bytes 196612
  68.0 22.6 %copy-start.23 = (f32[16,1024]{1,0:T(8,128)S(1)}, f32[16,1024]{1,0:T(8,128)}, u32[]{:S(2)}) copy-start(f32[16,1024]{1,0:T(8,128)} %copy-done.22) | copy-start | bytes 196612
  88.1 9.7 %all-to-all-start.1 = ((f32[32,1,3]{2,1,0:T(1,128)}), f32[32,1,3]{2,1,0:T(1,128)S(1)}, u32[]{:S(2)}, u32[]{:S(2)}) async-start(f32[32,1,3]{2,1,0:T(1,128)} %broadcast_in_dim.28), calls=%async_computation.1 | async-start | bytes 32768 | tf_op jit(solution)/shard_map/all_to_all | solution.py:36
  (30 other events, 47.9 us)

commit v4 on v3

--- a/solution.py
+++ b/solution.py
@@ -34,8 +34,7 @@
     count = lax.axis_size("cells") * lax.axis_size("slab")
     copies = jnp.broadcast_to(values[None], (count,) + values.shape)
     gathered = lax.all_to_all(copies, axes, 0, 0, tiled=True)
-    stacked = jnp.sum(gathered, axis=0)
-    return [stacked[i] for i in range(values.shape[0])]
+    return jnp.sum(gathered, axis=0)
 
 
 def split3(value):
@@ -208,6 +207,25 @@
     block = jnp.stack([acc_block[1], acc_block[0], acc_block[0]])
     images = operator(fields, mobile, block)
     image_last, direct, coupled = images[0], images[1], images[2]
+    first_sums = global_sum(
+        stacked_sums(
+            [
+                (grad_last, image_last),
+                (image_last, image_last),
+                (grad_last, grad_last),
+                (grad_first, direct),
+                (grad_first, coupled),
+                (carried, direct),
+                (carried, coupled),
+                (direct, direct),
+                (direct, coupled),
+                (coupled, coupled),
+            ]
+        )
+    )
+    lanes = lax.optimization_barrier(
+        jnp.broadcast_to(first_sums[:, None], (first_sums.shape[0], column_count))
+    )
     (
         along_last,
         energy_last,
@@ -219,22 +237,7 @@
         direct_direct,
         direct_coupled,
         coupled_coupled,
-    ) = global_sum(
-        stacked_sums(
-            [
-                (grad_last, image_last),
-                (image_last, image_last),
-                (grad_last, grad_last),
-                (grad_first, direct),
-                (grad_first, coupled),
-                (carried, direct),
-                (carried, coupled),
-                (direct, direct),
-                (direct, coupled),
-                (coupled, coupled),
-            ]
-        )
-    )
+    ) = [lanes[i] for i in range(first_sums.shape[0])]
     alpha_last = along_last / energy_last
     along_first = grad_direct + alpha_last * (grad_coupled + carried_direct) + (
         alpha_last * alpha_last
@@ -249,7 +252,7 @@
     solution_first = alpha_first * precondition(inverse_first, residual_first)
     image_first = direct + alpha_last * coupled
     closing_first = residual_first - alpha_first * image_first
-    norm_first, end_first, end_last = global_sum(
+    second_sums = global_sum(
         stacked_sums(
             [
                 (residual_first, residual_first),
@@ -258,7 +261,9 @@
             ]
         )
     )
-    norms = jnp.sqrt(jnp.stack([norm_first, end_first, norm_last, end_last])).reshape(2, 2)
+    norms = jnp.sqrt(
+        jnp.concatenate([second_sums[0:2], first_sums[2:3], second_sums[2:3]])
+    ).reshape(2, 2)
     return (jnp.stack([solution_first, solution_last]), norms)
 
 

time: 102 us -> 95 us (0.931)
  between operations: 8.23 us -> 2.44 us
  transfers between devices with their start and end apart: 9 -> 9, of which waited for: 1 -> 1; matrix products, arithmetic and copies ran while one was open for 23% -> 25% of each run, Pallas kernels for 0% -> 0%
where the time goes in v4:
time: 95 us; the launch traced here: 93.9 us
  other arithmetic  24.9 us (26%)
  starting transfers between devices  22.6 us (24%)
  local copies, waits for them, and re-layouts  16.3 us (17%)
  blocking collectives  11.4 us (12%)
  matrix products  10.5 us (11%)
  waiting for transfers between devices  5.78 us (6%)
  between operations  2.44 us (3%)
    ppermute x6, starting transfers between devices, shifted(): return lax.ppermute(value, axis, pairs)  15.9 us
    all_to_all x1, blocking collectives, global_sum(): gathered = lax.all_to_all(copies, axes, 0, 0, tiled=True)  11.4 us
    dot_general x6, matrix products, onehot_dot(): lax.dot_general(pieces, onehot, (dims, ((), ())), preferred_element_type=...  9.41 us
    all_to_all x1, waiting for transfers between devices, global_sum(): gathered = lax.all_to_all(copies, axes, 0, 0, tiled=True)  5.76 us
    ppermute x2, starting transfers between devices, butterfly(): lax.ppermute(value, axis, [(i, i ^ step) for i in range(count)])  4.18 us
    unnamed x121, local copies, waits for them, and re-layouts  3.88 us
    select_n x3, other arithmetic, locate(): onehot = (cells % column_count)[:, None] == column_iota[None, :]  3.85 us
    all_to_all x1, starting transfers between devices, global_sum(): gathered = lax.all_to_all(copies, axes, 0, 0, tiled=True)  2.51 us
  transfers between devices with their start and end apart: 9, of which 1 were waited for; matrix products, arithmetic and copies ran while one was open for 25% of the time, Pallas kernels for 0%

profile of v4, /device:TPU:0, one launch (start us, length us, event | category | flops | bytes accessed | tf_op | source)
XLA Modules:
  0.0 93.9 jit_solution(17750870170833004516)
XLA Ops:
  0.7 1.0 %broadcast_select_fusion.1 = f32[16,1024]{1,0:T(8,128)S(1)} fusion(f32[16,1024]{1,0:T(8,128)} %param.17, pred[1024]{0:T(1024)(128)(4,1)S(1)} %fusion.87), kind=kLoop, calls=%fused_computation.193 | loop fusion | flops 16384 | bytes 132096 | tf_op jit(solution)/shard_map/jit(_where)/select_n | solution.py:81
  3.3 4.9 %collective-permute-start = (f32[2064]{0:T(1024)S(1)}, f32[2064]{0:T(1024)S(1)}, u32[]{:S(2)}, u32[]{:S(2)}) collective-permute-start(f32[2064]{0:T(1024)S(1)} %pad_maximum_fusion.12), channel_id=1, source_target_pairs={{0,4},{4,8},{8,12},{12,16},{16,20},{20,24},{24,28},{1,5},{5,9},{9,... | collective-permute-start | bytes 24776 | tf_op jit(solution)/shard_map/ppermute | solution.py:13
  8.2 0.9 broadcast_select_fusion
  9.1 1.5 %collective-permute-start.1 = (f32[1024]{0:T(1024)S(1)}, f32[1024]{0:T(1024)S(1)}, u32[]{:S(2)}, u32[]{:S(2)}) collective-permute-start(f32[1024]{0:T(1024)S(1)} %bitcast.437), channel_id=1, source_target_pairs={{0,1},{1,2},{2,3},{4,5},{5,6},{6,7},{8,9},{9,10},{10,11},{12,13},{... | collective-permute-start | bytes 12296 | tf_op jit(solution)/shard_map/ppermute | solution.py:13
  10.6 1.2 %and_select_fusion.4 = s32[128]{0:T(128)} fusion(s32[1,128]{1,0:T(1,128)} %param.23), kind=kLoop, calls=%fused_computation.237 | loop fusion | flops 1408 | bytes 1024 | tf_op jit(solution)/shard_map/jit(remainder)/select_n | solution.py:105
  12.5 1.0 %fusion.110 = (f32[1,2,16,1024]{3,2,1,0:T(8,128)S(1)}, f32[1,2,16,1024]{3,2,1,0:T(8,128)S(1)}) fusion(f32[2,2,16,1024]{3,2,1,0:T(8,128)} %param.15), kind=kLoop, calls=%fused_computation.262 | loop fusion | bytes 524288 | tf_op jit(solution)/shard_map/slice | solution.py:134
  14.2 1.3 %add_select_fusion = s32[2048]{0:T(1024)} fusion(s32[2048]{0:T(1024)} %bitcast.417), kind=kLoop, calls=%fused_computation.212 | loop fusion | flops 22528 | bytes 16384 | tf_op jit(solution)/shard_map/jit(remainder)/select_n | solution.py:105
  16.9 1.3 %add_select_fusion.1 = s32[2048]{0:T(1024)} fusion(s32[2048]{0:T(1024)} %bitcast.418), kind=kLoop, calls=%fused_computation.215 | loop fusion | flops 22528 | bytes 16384 | tf_op jit(solution)/shard_map/jit(remainder)/select_n | solution.py:105
  19.6 1.1 %fusion.106 = (f32[1,4,16,1024]{3,2,1,0:T(8,128)S(1)}, f32[1,4,16,1024]{3,2,1,0:T(8,128)S(1)}) fusion(f32[2,4,16,1024]{3,2,1,0:T(8,128)} %param.14), kind=kLoop, calls=%fused_computation.258 | loop fusion | bytes 1048576 | tf_op jit(solution)/shard_map/slice | solution.py:207
  23.9 0.8 fusion.108
  24.8 1.8 %fusion.1 = f32[288,2048]{1,0:T(8,128)S(1)} fusion(s32[2048]{0:T(1024)S(1)} %copy-done.43, bf16[96,1024]{1,0:T(8,128)(2,1)S(1)} %get-tuple-element.50, bf16[96,1024]{1,0:T(8,128)(2,1)S(1)} %get-tuple-element.49, bf16[96,1024]{1,0:T(8,128)(2,1)S(1)} %bitcast_convert_fusion.2), kind=kOutput, calls=%fused_computation.2 | convolution fusion | flops 1211826176 | bytes 2957312 | tf_op jit(solution)/shard_map/dot_general | solution.py:51
  27.4 1.8 %fusion.3 = f32[288,2048]{1,0:T(8,128)S(1)} fusion(s32[2048]{0:T(1024)S(1)} %copy-done.41, bf16[96,1024]{1,0:T(8,128)(2,1)S(1)} %get-tuple-element.50, bf16[96,1024]{1,0:T(8,128)(2,1)S(1)} %get-tuple-element.49, bf16[96,1024]{1,0:T(8,128)(2,1)S(1)} %bitcast_convert_fusion.2), kind=kOutput, calls=%fused_computation.5 | convolution fusion | flops 1211826176 | bytes 2957312 | tf_op jit(solution)/shard_map/dot_general | solution.py:51
  31.0 1.3 %collective-permute-start.2 = (f32[6,2064]{1,0:T(8,128)}, f32[6,2064]{1,0:T(8,128)}, u32[]{:S(2)}, u32[]{:S(2)}) collective-permute-start(f32[6,2064]{1,0:T(8,128)} %pad_maximum_fusion.8), channel_id=1, source_target_pairs={{4,0},{8,4},{12,8},{16,12},{20,16},{24,20},{28,24},{5,1},{9,5},{13... | collective-permute-start | bytes 148616 | tf_op jit(solution)/shard_map/ppermute | solution.py:13
  32.9 2.1 %collective-permute-start.6 = (f32[4,16]{1,0:T(4,128)S(1)}, f32[4,16]{1,0:T(4,128)S(1)}, u32[]{:S(2)}, u32[]{:S(2)}) collective-permute-start(f32[4,16]{1,0:T(4,128)S(1)} %pad_maximum_fusion.13), channel_id=1, source_target_pairs={{0,1},{1,0},{2,3},{3,2},{4,5},{5,4},{6,7},{7,6},{8,9},{9,8},{10,11... | collective-permute-start | bytes 776 | tf_op jit(solution)/shard_map/ppermute | solution.py:27
  35.9 4.9 %collective-permute-start.3 = (f32[6,2064]{1,0:T(8,128)}, f32[6,2064]{1,0:T(8,128)}, u32[]{:S(2)}, u32[]{:S(2)}) collective-permute-start(f32[6,2064]{1,0:T(8,128)} %pad_maximum_fusion.9), channel_id=1, source_target_pairs={{0,4},{4,8},{8,12},{12,16},{16,20},{20,24},{24,28},{1,5},{5,9},{9,... | collective-permute-start | bytes 148616 | tf_op jit(solution)/shard_map/ppermute | solution.py:13
  40.8 1.3 %collective-permute-start.4 = (f32[6,1024]{1,0:T(8,128)S(1)}, f32[6,1024]{1,0:T(8,128)}, u32[]{:S(2)}, u32[]{:S(2)}) collective-permute-start(f32[6,1024]{1,0:T(8,128)S(1)} %bitcast.410), channel_id=1, source_target_pairs={{1,0},{2,1},{3,2},{5,4},{6,5},{7,6},{9,8},{10,9},{11,10},{13,12},{... | collective-permute-start | bytes 73736 | tf_op jit(solution)/shard_map/ppermute | solution.py:13
  42.1 2.1 %collective-permute-start.7 = (f32[4,16]{1,0:T(4,128)S(1)}, f32[4,16]{1,0:T(4,128)S(1)}, u32[]{:S(2)}, u32[]{:S(2)}) collective-permute-start(f32[4,16]{1,0:T(4,128)S(1)} %fusion.111), channel_id=1, source_target_pairs={{0,2},{1,3},{2,0},{3,1},{4,6},{5,7},{6,4},{7,5},{8,10},{9,11},{10,... | collective-permute-start | bytes 776 | tf_op jit(solution)/shard_map/ppermute | solution.py:27
  44.8 2.1 %collective-permute-start.5 = (f32[6,1024]{1,0:T(8,128)}, f32[6,1024]{1,0:T(8,128)}, u32[]{:S(2)}, u32[]{:S(2)}) collective-permute-start(f32[6,1024]{1,0:T(8,128)} %bitcast.366), channel_id=1, source_target_pairs={{0,1},{1,2},{2,3},{4,5},{5,6},{6,7},{8,9},{9,10},{10,11},{12,13},{... | collective-permute-start | bytes 73736 | tf_op jit(solution)/shard_map/ppermute | solution.py:13
  49.0 1.4 %concatenate.111 = f32[3,2,1,1024]{3,2,1,0:T(1,128)} reshape(f32[6,1024]{1,0:T(8,128)} %collective-permute-done.4) | data formatting | bytes 49152 | tf_op jit(solution)/shard_map/concatenate | solution.py:166
  50.4 1.4 %concatenate.112 = f32[3,2,1,1024]{3,2,1,0:T(1,128)} reshape(f32[6,1024]{1,0:T(8,128)} %collective-permute-done.5) | data formatting | bytes 49152 | tf_op jit(solution)/shard_map/concatenate | solution.py:165
  51.8 1.0 %fusion.59 = f32[6,2048]{1,0:T(8,128)S(1)} fusion(f32[6,2048]{1,0:T(8,128)} %copy-done.26, f32[6,2064]{1,0:T(8,128)} %collective-permute-done.2, f32[2048]{0:T(1024)S(1)} %bitcast.411), kind=kLoop, calls=%fused_computation.138 | loop fusion | flops 24576 | bytes 155648 | tf_op jit(solution)/shard_map/mul | solution.py:173
  52.8 1.0 %broadcast_multiply_fusion.1 = f32[6,16,2048]{2,1,0:T(8,128)S(1)} fusion(f32[6,2048]{1,0:T(8,128)S(1)} %fusion.59, f32[16,2048]{1,0:T(8,128)} %fusion.56), kind=kLoop, calls=%fused_computation.67 | loop fusion | flops 196608 | bytes 966656 | tf_op jit(solution)/shard_map/mul | solution.py:120
  53.8 1.0 %fusion.19 = (bf16[96,2048]{1,0:T(8,128)(2,1)}, bf16[96,2048]{1,0:T(8,128)(2,1)}) fusion(f32[6,16,2048]{2,1,0:T(8,128)S(1)} %broadcast_multiply_fusion.1), kind=kLoop, calls=%fused_computation.36 | loop fusion | flops 1376256 | bytes 1572864 | tf_op jit(solution)/shard_map/convert_element_type | solution.py:43
  54.8 0.8 bitcast_convert_fusion.1
  55.6 1.0 %fusion.58 = f32[6,2048]{1,0:T(8,128)S(1)} fusion(f32[6,2048]{1,0:T(8,128)S(1)} %copy-done.25, f32[6,2064]{1,0:T(8,128)} %collective-permute-done.3, f32[2048]{0:T(1024)S(1)} %copy-done.40), kind=kLoop, calls=%fused_computation.136 | loop fusion | flops 24576 | bytes 155648 | tf_op jit(solution)/shard_map/mul | solution.py:174
  56.7 1.0 %fusion.20 = (bf16[96,2048]{1,0:T(8,128)(2,1)}, bf16[96,2048]{1,0:T(8,128)(2,1)}) fusion(f32[6,16,2048]{2,1,0:T(8,128)S(1)} %broadcast_multiply_fusion), kind=kLoop, calls=%fused_computation.37 | loop fusion | flops 1376256 | bytes 1572864 | tf_op jit(solution)/shard_map/convert_element_type | solution.py:43
  61.2 3.2 %fusion = f32[288,1024]{1,0:T(8,128)S(1)} fusion(s32[2048]{0:T(1024)S(1)} %copy-done.44, bf16[96,2048]{1,0:T(8,128)(2,1)} %get-tuple-element.32, bf16[96,2048]{1,0:T(8,128)(2,1)} %get-tuple-element.31, bf16[96,2048]{1,0:T(8,128)(2,1)} %bitcast_convert_fusion.1), kind=kOutput, calls=%fused_computation.1 | convolution fusion | flops 1213595648 | bytes 2367488 | tf_op jit(solution)/shard_map/dot_general | solution.py:51
  64.5 1.9 %fusion.2 = f32[288,1024]{1,0:T(8,128)S(1)} fusion(s32[2048]{0:T(1024)S(1)} %copy-done.42, bf16[96,2048]{1,0:T(8,128)(2,1)S(1)} %copy-done.28, bf16[96,2048]{1,0:T(8,128)(2,1)S(1)} %copy-done.27, bf16[96,2048]{1,0:T(8,128)(2,1)S(1)} %copy-done.29), kind=kOutput, calls=%fused_computation.4 | convolution fusion | flops 1213595648 | bytes 2367488 | tf_op jit(solution)/shard_map/dot_general | solution.py:51
  69.1 11.4 %all_to_all.12 = f32[32,1,10]{2,1,0:T(1,128)S(1)} all-to-all(f32[32,1,10]{2,1,0:T(1,128)S(1)} %broadcast_in_dim.29), channel_id=1, replica_groups=mesh['cells'=8,'slab'=4] {'cells','slab'}, dimensions={0} | all-to-all | bytes 2560 | tf_op jit(solution)/shard_map/all_to_all | solution.py:36
  81.7 2.5 %all-to-all-start.1 = ((f32[32,1,3]{2,1,0:T(1,128)}), f32[32,1,3]{2,1,0:T(1,128)S(1)}, u32[]{:S(2)}, u32[]{:S(2)}) async-start(f32[32,1,3]{2,1,0:T(1,128)} %broadcast_in_dim.31), calls=%async_computation.1 | async-start | bytes 32768 | tf_op jit(solution)/shard_map/all_to_all | solution.py:36
  85.6 5.8 %all-to-all-done.1 = f32[32,1,3]{2,1,0:T(1,128)S(1)} async-done(((f32[32,1,3]{2,1,0:T(1,128)}), f32[32,1,3]{2,1,0:T(1,128)S(1)}, u32[]{:S(2)}, u32[]{:S(2)}) %all-to-all-start.1) | async-done | bytes 416 | tf_op jit(solution)/shard_map/all_to_all | solution.py:36
  92.0 1.3 %maximum_sqrt_fusion = f32[4]{0:T(128)S(1)} fusion(f32[1]{0:T(128)} %slice.405, f32[1]{0:T(128)} %slice.404, f32[2]{0:T(128)S(1)} %bitcast.438), kind=kLoop, calls=%fused_computation.246 | loop fusion | flops 8 | bytes 32 | tf_op jit(solution)/shard_map/sqrt | solution.py:264
  (210 shorter events, 24.5 us)
Async XLA Ops:
  0.6 21.0 %copy-start.32 = (f32[16,1024]{1,0:T(8,128)S(1)}, f32[16,1024]{1,0:T(8,128)}, u32[]{:S(2)}) copy-start(f32[16,1024]{1,0:T(8,128)} %param.17) | copy-start | bytes 196612
  0.6 21.0 %copy-start.33 = (f32[16,1024]{1,0:T(8,128)S(1)}, f32[16,1024]{1,0:T(8,128)}, u32[]{:S(2)}) copy-start(f32[16,1024]{1,0:T(8,128)} %param.18) | copy-start | bytes 196612
  0.7 21.0 %copy-start.2 = (f32[2,2,16,1024]{3,2,1,0:T(8,128)S(1)}, f32[2,2,16,1024]{3,2,1,0:T(8,128)}, u32[]{:S(2)}) copy-start(f32[2,2,16,1024]{3,2,1,0:T(8,128)} %param.15) | copy-start | bytes 786436
  0.7 21.0 %copy-start = (f32[2,4,16,1024]{3,2,1,0:T(8,128)S(1)}, f32[2,4,16,1024]{3,2,1,0:T(8,128)}, u32[]{:S(2)}) copy-start(f32[2,4,16,1024]{3,2,1,0:T(8,128)} %param.14) | copy-start | bytes 1572868
  0.7 20.0 %copy-start.49 = (s32[1,128]{1,0:T(1,128)S(1)}, s32[1,128]{1,0:T(1,128)}, u32[]{:S(2)}) copy-start(s32[1,128]{1,0:T(1,128)} %param.24) | copy-start | bytes 1540
  0.7 20.0 %copy-start.51 = (f32[1,128]{1,0:T(1,128)S(1)}, f32[1,128]{1,0:T(1,128)}, u32[]{:S(2)}) copy-start(f32[1,128]{1,0:T(1,128)} %param.25) | copy-start | bytes 1540
  0.7 21.0 %copy-start.1 = (f32[2,2,16,1024]{3,2,1,0:T(8,128)S(1)}, f32[2,2,16,1024]{3,2,1,0:T(8,128)}, u32[]{:S(2)}) copy-start(f32[2,2,16,1024]{3,2,1,0:T(8,128)} %param.13) | copy-start | bytes 786436
  1.7 20.7 %copy-start.16 = (f32[16,1024]{1,0:T(8,128)}, f32[16,1024]{1,0:T(8,128)S(1)}, u32[]{:S(2)}) copy-start(f32[16,1024]{1,0:T(8,128)S(1)} %broadcast_select_fusion.1) | copy-start | bytes 196612
  3.3 18.2 %collective-permute-start = (f32[2064]{0:T(1024)S(1)}, f32[2064]{0:T(1024)S(1)}, u32[]{:S(2)}, u32[]{:S(2)}) collective-permute-start(f32[2064]{0:T(1024)S(1)} %pad_maximum_fusion.12), channel_id=1, source_target_pairs={{0,4},{4,8},{8,12},{12,16},{16,20},{20,24},{24,28},{1,5},{5,9},{9,... | collective-permute-start | bytes 24776 | tf_op jit(solution)/shard_map/ppermute | solution.py:13
  9.1 13.3 %copy-start.18 = (f32[16,1024]{1,0:T(8,128)}, f32[16,1024]{1,0:T(8,128)S(1)}, u32[]{:S(2)}) copy-start(f32[16,1024]{1,0:T(8,128)S(1)} %broadcast_select_fusion) | copy-start | bytes 196612
  9.1 12.5 %collective-permute-start.1 = (f32[1024]{0:T(1024)S(1)}, f32[1024]{0:T(1024)S(1)}, u32[]{:S(2)}, u32[]{:S(2)}) collective-permute-start(f32[1024]{0:T(1024)S(1)} %bitcast.437), channel_id=1, source_target_pairs={{0,1},{1,2},{2,3},{4,5},{5,6},{6,7},{8,9},{9,10},{10,11},{12,13},{... | collective-permute-start | bytes 12296 | tf_op jit(solution)/shard_map/ppermute | solution.py:13
  29.3 5.8 %copy-start.6 = (f32[16,2048]{1,0:T(8,128)S(1)}, f32[16,2048]{1,0:T(8,128)}, u32[]{:S(2)}) copy-start(f32[16,2048]{1,0:T(8,128)} %fusion.56) | copy-start | bytes 393220
  29.4 17.6 %copy-start.46 = (f32[2064]{0:T(1024)S(1)}, f32[2064]{0:T(1024)}, u32[]{:S(2)}) copy-start(f32[2064]{0:T(1024)} %copy-done.45) | copy-start | bytes 24772
  30.3 18.7 %copy-start.24 = (f32[6,2048]{1,0:T(8,128)}, f32[6,2048]{1,0:T(8,128)S(1)}, u32[]{:S(2)}) copy-start(f32[6,2048]{1,0:T(8,128)S(1)} %multiply_reduce_fusion.1) | copy-start | bytes 147460
  31.0 20.8 %collective-permute-start.2 = (f32[6,2064]{1,0:T(8,128)}, f32[6,2064]{1,0:T(8,128)}, u32[]{:S(2)}, u32[]{:S(2)}) collective-permute-start(f32[6,2064]{1,0:T(8,128)} %pad_maximum_fusion.8), channel_id=1, source_target_pairs={{4,0},{8,4},{12,8},{16,12},{20,16},{24,20},{28,24},{5,1},{9,5},{13... | collective-permute-start | bytes 148616 | tf_op jit(solution)/shard_map/ppermute | solution.py:13
  32.9 9.2 %collective-permute-start.6 = (f32[4,16]{1,0:T(4,128)S(1)}, f32[4,16]{1,0:T(4,128)S(1)}, u32[]{:S(2)}, u32[]{:S(2)}) collective-permute-start(f32[4,16]{1,0:T(4,128)S(1)} %pad_maximum_fusion.13), channel_id=1, source_target_pairs={{0,1},{1,0},{2,3},{3,2},{4,5},{5,4},{6,7},{7,6},{8,9},{9,8},{10,11... | collective-permute-start | bytes 776 | tf_op jit(solution)/shard_map/ppermute | solution.py:27
  35.2 13.8 %copy-start.26 = (f32[6,2048]{1,0:T(8,128)}, f32[6,2048]{1,0:T(8,128)S(1)}, u32[]{:S(2)}) copy-start(f32[6,2048]{1,0:T(8,128)S(1)} %multiply_reduce_fusion) | copy-start | bytes 147460
  35.9 19.7 %collective-permute-start.3 = (f32[6,2064]{1,0:T(8,128)}, f32[6,2064]{1,0:T(8,128)}, u32[]{:S(2)}, u32[]{:S(2)}) collective-permute-start(f32[6,2064]{1,0:T(8,128)} %pad_maximum_fusion.9), channel_id=1, source_target_pairs={{0,4},{4,8},{8,12},{12,16},{16,20},{20,24},{24,28},{1,5},{5,9},{9,... | collective-permute-start | bytes 148616 | tf_op jit(solution)/shard_map/ppermute | solution.py:13
  40.8 8.2 %collective-permute-start.4 = (f32[6,1024]{1,0:T(8,128)S(1)}, f32[6,1024]{1,0:T(8,128)}, u32[]{:S(2)}, u32[]{:S(2)}) collective-permute-start(f32[6,1024]{1,0:T(8,128)S(1)} %bitcast.410), channel_id=1, source_target_pairs={{1,0},{2,1},{3,2},{5,4},{6,5},{7,6},{9,8},{10,9},{11,10},{13,12},{... | collective-permute-start | bytes 73736 | tf_op jit(solution)/shard_map/ppermute | solution.py:13
  42.1 5.5 %collective-permute-start.7 = (f32[4,16]{1,0:T(4,128)S(1)}, f32[4,16]{1,0:T(4,128)S(1)}, u32[]{:S(2)}, u32[]{:S(2)}) collective-permute-start(f32[4,16]{1,0:T(4,128)S(1)} %fusion.111), channel_id=1, source_target_pairs={{0,2},{1,3},{2,0},{3,1},{4,6},{5,7},{6,4},{7,5},{8,10},{9,11},{10,... | collective-permute-start | bytes 776 | tf_op jit(solution)/shard_map/ppermute | solution.py:27
  44.8 5.6 %collective-permute-start.5 = (f32[6,1024]{1,0:T(8,128)}, f32[6,1024]{1,0:T(8,128)}, u32[]{:S(2)}, u32[]{:S(2)}) collective-permute-start(f32[6,1024]{1,0:T(8,128)} %bitcast.366), channel_id=1, source_target_pairs={{0,1},{1,2},{2,3},{4,5},{5,6},{6,7},{8,9},{9,10},{10,11},{12,13},{... | collective-permute-start | bytes 73736 | tf_op jit(solution)/shard_map/ppermute | solution.py:13
  49.0 6.6 %copy-start.40 = (f32[2048]{0:T(1024)S(1)}, f32[2048]{0:T(1024)}, u32[]{:S(2)}) copy-start(f32[2048]{0:T(1024)} %slice.437) | copy-start | bytes 24580
  51.8 3.8 %copy-start.25 = (f32[6,2048]{1,0:T(8,128)S(1)}, f32[6,2048]{1,0:T(8,128)}, u32[]{:S(2)}) copy-start(f32[6,2048]{1,0:T(8,128)} %copy-done.24) | copy-start | bytes 147460
  51.8 4.8 %copy-start.5 = (f32[16,2048]{1,0:T(8,128)S(1)}, f32[16,2048]{1,0:T(8,128)}, u32[]{:S(2)}) copy-start(f32[16,2048]{1,0:T(8,128)} %fusion.55) | copy-start | bytes 393220
  55.6 5.6 %copy-start.44 = (s32[2048]{0:T(1024)S(1)}, s32[2048]{0:T(1024)}, u32[]{:S(2)}) copy-start(s32[2048]{0:T(1024)} %add_select_fusion) | copy-start | bytes 24580
  67.8 12.9 %copy-start.12 = (f32[16,1024]{1,0:T(8,128)S(1)}, f32[16,1024]{1,0:T(8,128)}, u32[]{:S(2)}) copy-start(f32[16,1024]{1,0:T(8,128)} %copy-done.11) | copy-start | bytes 196612
  67.8 12.9 %copy-start.14 = (f32[16,1024]{1,0:T(8,128)S(1)}, f32[16,1024]{1,0:T(8,128)}, u32[]{:S(2)}) copy-start(f32[16,1024]{1,0:T(8,128)} %copy-done.13) | copy-start | bytes 196612
  67.9 12.9 %copy-start.35 = (f32[2,2,16,1024]{3,2,1,0:T(8,128)S(1)}, f32[2,2,16,1024]{3,2,1,0:T(8,128)}, u32[]{:S(2)}) copy-start(f32[2,2,16,1024]{3,2,1,0:T(8,128)} %param.16) | copy-start | bytes 786436
  68.0 16.2 %copy-start.10 = (f32[16,1024]{1,0:T(8,128)S(1)}, f32[16,1024]{1,0:T(8,128)}, u32[]{:S(2)}) copy-start(f32[16,1024]{1,0:T(8,128)} %copy-done.9) | copy-start | bytes 196612
  68.0 16.2 %copy-start.21 = (f32[16,1024]{1,0:T(8,128)S(1)}, f32[16,1024]{1,0:T(8,128)}, u32[]{:S(2)}) copy-start(f32[16,1024]{1,0:T(8,128)} %copy-done.20) | copy-start | bytes 196612
  68.0 16.2 %copy-start.23 = (f32[16,1024]{1,0:T(8,128)S(1)}, f32[16,1024]{1,0:T(8,128)}, u32[]{:S(2)}) copy-start(f32[16,1024]{1,0:T(8,128)} %copy-done.22) | copy-start | bytes 196612
  81.7 9.7 %all-to-all-start.1 = ((f32[32,1,3]{2,1,0:T(1,128)}), f32[32,1,3]{2,1,0:T(1,128)S(1)}, u32[]{:S(2)}, u32[]{:S(2)}) async-start(f32[32,1,3]{2,1,0:T(1,128)} %broadcast_in_dim.31), calls=%async_computation.1 | async-start | bytes 32768 | tf_op jit(solution)/shard_map/all_to_all | solution.py:36
  (30 other events, 48.0 us)

commit v5 on v4

--- a/solution.py
+++ b/solution.py
@@ -121,8 +121,7 @@
         placed = onehot_dot(spread, onehot, ((1,), (0,)))
         return placed.reshape(parts, layer_count, column_count)
 
-    near_at = locate(fault_near)
-    far_at = locate(fault_far)
+    fault_at = locate(jnp.concatenate([fault_near.reshape(-1), fault_far.reshape(-1)]))
     well_at = locate(compl_cell)
     well_index = compl_wi.reshape(-1)
     well_onehot = (
@@ -151,15 +150,42 @@
             ]
         )
 
+    def slab_shift(value, by):
+        count = lax.axis_size("slab")
+        return lax.ppermute(value, "slab", [(i, (i + by) % count) for i in range(count)])
+
     def operator(fields, mobile, block):
         count = fields.shape[0]
         scaled = (mobile * fields).reshape(count * 2, layer_count, column_count)
-        picks_near = gather(scaled, near_at)
-        picks_far = gather(scaled, far_at)
+        picks = gather(scaled, fault_at)
+        picks_near = picks[:, :slot_count]
+        picks_far = picks[:, slot_count:]
         from_left = shifted(jnp.concatenate([scaled[:, :, -1], picks_near], axis=1), "cells", 1)
         from_right = shifted(jnp.concatenate([scaled[:, :, 0], picks_far], axis=1), "cells", -1)
-        from_above = shifted(scaled[:, -1, :], "slab", 1)
-        from_below = shifted(scaled[:, 0, :], "slab", -1)
+        pressure = fields[:, 0]
+        values = gather(pressure, well_at)
+        local = jnp.concatenate(
+            [
+                jnp.dot(well_index, well_onehot, precision=highest)[None],
+                jnp.dot(well_index * values, well_onehot, precision=highest),
+            ]
+        )
+        halo_size = count * 2 * column_count
+        from_above = slab_shift(
+            jnp.concatenate([scaled[:, -1, :].reshape(-1), local.reshape(-1)]), 1
+        )
+        from_below = slab_shift(
+            jnp.concatenate([scaled[:, 0, :].reshape(-1), local.reshape(-1)]), -1
+        )
+        summed = local
+        if slab_size > 1:
+            summed = summed + from_above[halo_size:].reshape(local.shape)
+        if slab_size > 2:
+            summed = summed + from_below[halo_size:].reshape(local.shape)
+        for by in range(2, slab_size - 1):
+            summed = summed + slab_shift(local, by)
+        from_above = from_above[:halo_size].reshape(count * 2, column_count)
+        from_below = from_below[:halo_size].reshape(count * 2, column_count)
         west = jnp.concatenate([from_left[:, :layer_count, None], scaled[:, :, :-1]], axis=2)
         east = jnp.concatenate([scaled[:, :, 1:], from_right[:, :layer_count, None]], axis=2)
         above = jnp.concatenate([from_above[:, None, :], scaled[:, :-1, :]], axis=1)
@@ -172,17 +198,8 @@
         )
         flux_right = weight_here * (picks_near - from_right[:, layer_count:])
         flux_left = weight_left * (from_left[:, layer_count:] - picks_far)
-        fault_term = scatter(flux_right, near_at) - scatter(flux_left, far_at)
+        fault_term = scatter(jnp.concatenate([flux_right, -flux_left], axis=1), fault_at)
         laplace = (laplace + fault_term).reshape(count, 2, layer_count, column_count)
-        pressure = fields[:, 0]
-        values = gather(pressure, well_at)
-        local = jnp.concatenate(
-            [
-                jnp.dot(well_index, well_onehot, precision=highest)[None],
-                jnp.dot(well_index * values, well_onehot, precision=highest),
-            ]
-        )
-        summed = butterfly(local, "slab")
         back = jnp.dot(summed[1:] / summed[0], well_onehot.T, precision=highest)
         well_term = scatter(well_index * (values - back), well_at)
         first = (

time: 95 us -> 93.1 us (0.980)
  local copies, waits for them, and re-layouts: 16.3 us -> 21.6 us
  starting transfers between devices: 22.6 us -> 17.5 us
  other arithmetic: 24.9 us -> 20.9 us
  blocking collectives: 11.4 us -> 12.8 us
    slice x1 -> x6, local copies, waits for them, and re-layouts: 0.04 us -> 4.42 us  [the longest x1 1.33 us: operator(): from_below = from_below[:halo_size].reshape(count * 2, column_count)]
    ppermute x6 -> x4, starting transfers between devices: 15.9 us -> 11.8 us  [shifted(): return lax.ppermute(value, axis, pairs)]
    reshape x0 -> x3, local copies, waits for them, and re-layouts: none -> 3.96 us  [the longest x1 1.33 us: operator(): local.reshape(-1)]
    concatenate x2 -> x0, local copies, waits for them, and re-layouts: 2.79 us -> none  [the longest x1 1.4 us: operator(): below = jnp.concatenate([scaled[:, 1:, :], from_below[:, None, :]], axis=1)]
    select_n x3 -> x1, other arithmetic: 3.85 us -> 1.24 us  [locate(): onehot = (cells % column_count)[:, None] == column_iota[None, :]]
    all_to_all x1, blocking collectives: 11.4 us -> 12.8 us  [global_sum(): gathered = lax.all_to_all(copies, axes, 0, 0, tiled=True)]
    convert_element_type x3 -> x2, other arithmetic: 1.33 us -> 0.03 us  [locate(): (layer_iota[:, None] == (cells // column_count)[None, :]).astype(jnp.floa...]
    add x1, other arithmetic: 0.37 us -> 1.63 us  [operator(): laplace + fault_term]
  transfers between devices with their start and end apart: 9 -> 8, of which waited for: 1 -> 2; matrix products, arithmetic and copies ran while one was open for 25% -> 28% of each run, Pallas kernels for 0% -> 0%
where the time goes in v5:
time: 93.1 us; the launch traced here: 92.2 us
  local copies, waits for them, and re-layouts  21.6 us (23%)
  other arithmetic  20.9 us (22%)
  starting transfers between devices  17.5 us (19%)
  blocking collectives  12.8 us (14%)
  matrix products  11 us (12%)
  waiting for transfers between devices  6.12 us (7%)
  between operations  2.23 us (2%)
    all_to_all x1, blocking collectives, global_sum(): gathered = lax.all_to_all(copies, axes, 0, 0, tiled=True)  12.8 us
    ppermute x4, starting transfers between devices, shifted(): return lax.ppermute(value, axis, pairs)  11.8 us
    dot_general x4, matrix products, onehot_dot(): lax.dot_general(pieces, onehot, (dims, ((), ())), preferred_element_type=...  9.18 us
    all_to_all x1, waiting for transfers between devices, global_sum(): gathered = lax.all_to_all(copies, axes, 0, 0, tiled=True)  5.68 us
    unnamed x103, local copies, waits for them, and re-layouts  3.89 us
    ppermute x3, starting transfers between devices, slab_shift(): lax.ppermute(value, 'slab', [(i, (i + by) % count) for i in range(count)])  3.14 us
    all_to_all x1, starting transfers between devices, global_sum(): gathered = lax.all_to_all(copies, axes, 0, 0, tiled=True)  2.49 us
    select_n x2, other arithmetic, locate(): cells // column_count  1.99 us
  transfers between devices with their start and end apart: 8, of which 2 were waited for; matrix products, arithmetic and copies ran while one was open for 28% of the time, Pallas kernels for 0%

profile of v5, /device:TPU:0, one launch (start us, length us, event | category | flops | bytes accessed | tf_op | source)
XLA Modules:
  0.0 92.2 jit_solution(7843503339394239278)
XLA Ops:
  0.7 0.9 broadcast_select_fusion.1
  3.2 4.9 %collective-permute-start = (f32[2064]{0:T(1024)S(1)}, f32[2064]{0:T(1024)S(1)}, u32[]{:S(2)}, u32[]{:S(2)}) collective-permute-start(f32[2064]{0:T(1024)S(1)} %pad_maximum_fusion.12), channel_id=1, source_target_pairs={{0,4},{4,8},{8,12},{12,16},{16,20},{20,24},{24,28},{1,5},{5,9},{9,... | collective-permute-start | bytes 24776 | tf_op jit(solution)/shard_map/ppermute | solution.py:13
  8.1 0.9 broadcast_select_fusion
  9.0 1.5 %collective-permute-start.1 = (f32[1024]{0:T(1024)S(1)}, f32[1024]{0:T(1024)S(1)}, u32[]{:S(2)}, u32[]{:S(2)}) collective-permute-start(f32[1024]{0:T(1024)S(1)} %bitcast.419), channel_id=1, source_target_pairs={{0,1},{1,2},{2,3},{4,5},{5,6},{6,7},{8,9},{9,10},{10,11},{12,13},{... | collective-permute-start | bytes 12296 | tf_op jit(solution)/shard_map/ppermute | solution.py:13
  10.5 1.2 %and_select_fusion.2 = s32[128]{0:T(128)} fusion(s32[1,128]{1,0:T(1,128)} %param.23), kind=kLoop, calls=%fused_computation.214 | loop fusion | flops 1408 | bytes 1024 | tf_op jit(solution)/shard_map/jit(remainder)/select_n | solution.py:105
  12.4 1.0 %fusion.101 = (f32[1,2,16,1024]{3,2,1,0:T(8,128)S(1)}, f32[1,2,16,1024]{3,2,1,0:T(8,128)S(1)}) fusion(f32[2,2,16,1024]{3,2,1,0:T(8,128)} %param.15), kind=kLoop, calls=%fused_computation.237 | loop fusion | bytes 524288 | tf_op jit(solution)/shard_map/slice | solution.py:133
  13.5 1.3 %add_select_fusion = (s32[4096]{0:T(1024)S(1)}, s32[4096]{0:T(1024)}) fusion(s32[2048]{0:T(1024)} %bitcast.416, s32[2048]{0:T(1024)} %bitcast.417), kind=kLoop, calls=%fused_computation.184 | loop fusion | flops 81920 | bytes 49152 | tf_op jit(solution)/shard_map/jit(floor_divide)/jit(_where)/select_n | solution.py:106
  15.6 0.7 fusion.66
  18.2 0.8 fusion.31
  19.7 0.8 slice_reduce_fusion.1
  20.7 1.0 %fusion.99 = (f32[6,15,1024]{2,1,0:T(8,128)}, f32[6,15,1024]{2,1,0:T(8,128)}) fusion(f32[6,16,1024]{2,1,0:T(8,128)S(1)} %bitcast.357), kind=kLoop, calls=%fused_computation.235 | loop fusion | bytes 1474560 | tf_op jit(solution)/shard_map/slice | solution.py:191
  24.7 1.3 %reshape.486 = f32[64]{0:T(128)} reshape(f32[4,16]{1,0:T(4,128)} %pad_maximum_fusion.13) | data formatting | bytes 512 | tf_op jit(solution)/shard_map/reshape | solution.py:178
  26.1 2.0 %collective-permute-start.6 = (f32[4,16]{1,0:T(4,128)}, f32[4,16]{1,0:T(4,128)}, u32[]{:S(2)}, u32[]{:S(2)}) collective-permute-start(f32[4,16]{1,0:T(4,128)} %pad_maximum_fusion.13), channel_id=1, source_target_pairs={{0,2},{1,3},{2,0},{3,1},{4,6},{5,7},{6,4},{7,5},{8,10},{9,11},{10,... | collective-permute-start | bytes 776 | tf_op jit(solution)/shard_map/ppermute | solution.py:155
  28.0 4.4 %fusion.1 = f32[288,4096]{1,0:T(8,128)S(1)} fusion(s32[4096]{0:T(1024)} %get-tuple-element.69, bf16[96,1024]{1,0:T(8,128)(2,1)} %get-tuple-element.48, bf16[96,1024]{1,0:T(8,128)(2,1)} %get-tuple-element.47, bf16[96,1024]{1,0:T(8,128)(2,1)} %bitcast_convert_fusion.1), kind=kOutput, calls=%fused_computation.2 | convolution fusion | flops 2421882880 | bytes 5324800 | tf_op jit(solution)/shard_map/dot_general | solution.py:51
  34.5 4.0 %collective-permute-start.3 = (f32[6,2064]{1,0:T(8,128)}, f32[6,2064]{1,0:T(8,128)}, u32[]{:S(2)}, u32[]{:S(2)}) collective-permute-start(f32[6,2064]{1,0:T(8,128)} %pad_maximum_fusion.7), channel_id=1, source_target_pairs={{0,4},{4,8},{8,12},{12,16},{16,20},{20,24},{24,28},{1,5},{5,9},{9,... | collective-permute-start | bytes 148616 | tf_op jit(solution)/shard_map/ppermute | solution.py:13
  39.1 1.2 %collective-permute-start.4 = (f32[6208]{0:T(1024)}, f32[6208]{0:T(1024)}, u32[]{:S(2)}, u32[]{:S(2)}) collective-permute-start(f32[6208]{0:T(1024)} %get-tuple-element.71), channel_id=1, source_target_pairs={{0,3},{1,0},{2,1},{3,2},{4,7},{5,4},{6,5},{7,6},{8,11},{9,8},{10,9... | collective-permute-start | bytes 74504 | tf_op jit(solution)/shard_map/ppermute | solution.py:155
  41.0 1.5 %collective-permute-start.2 = (f32[6,2064]{1,0:T(8,128)}, f32[6,2064]{1,0:T(8,128)}, u32[]{:S(2)}, u32[]{:S(2)}) collective-permute-start(f32[6,2064]{1,0:T(8,128)} %pad_maximum_fusion.6), channel_id=1, source_target_pairs={{4,0},{8,4},{12,8},{16,12},{20,16},{24,20},{28,24},{5,1},{9,5},{13... | collective-permute-start | bytes 148616 | tf_op jit(solution)/shard_map/ppermute | solution.py:13
  44.8 1.3 %reshape.488 = f32[4,16]{1,0:T(4,128)} reshape(f32[64]{0:T(128)} %slice.460) | data formatting | bytes 512 | tf_op jit(solution)/shard_map/reshape | solution.py:182
  46.1 1.2 %slice.461 = f32[64]{0:T(128)} slice(f32[6208]{0:T(1024)} %collective-permute-done.4), slice={[6144:6208]} | slice | bytes 512 | tf_op jit(solution)/shard_map/slice | solution.py:184
  47.3 1.3 %reshape.489 = f32[4,16]{1,0:T(4,128)} reshape(f32[64]{0:T(128)} %slice.461) | data formatting | bytes 512 | tf_op jit(solution)/shard_map/reshape | solution.py:184
  48.7 0.8 add_add_fusion.1
  49.4 0.9 fusion.9
  50.4 1.0 %fusion.16 = f32[144,1024]{1,0:T(8,128)S(1)} fusion(s32[128]{0:T(128)} %and_select_fusion.2, bf16[48,128]{1,0:T(8,128)(2,1)S(1)} %get-tuple-element.67, bf16[48,128]{1,0:T(8,128)(2,1)S(1)} %get-tuple-element.66, bf16[48,128]{1,0:T(8,128)(2,1)S(1)} %bitcast_convert_fusion.3), kind=kOutput, calls=%fused_computation.27 | convolution fusion | flops 37990400 | bytes 627200 | tf_op jit(solution)/shard_map/dot_general | solution.py:51
  52.1 1.3 %slice.449 = f32[6144]{0:T(1024)} slice(f32[6208]{0:T(1024)} %collective-permute-done.4), slice={[0:6144]} | slice | bytes 49152 | tf_op jit(solution)/shard_map/slice | solution.py:188
  54.1 1.0 %fusion.53 = (f32[6,2048]{1,0:T(8,128)S(1)}, f32[6,2048]{1,0:T(8,128)S(1)}) fusion(f32[6,2064]{1,0:T(8,128)} %collective-permute-done.2, f32[2048]{0:T(1024)S(1)} %bitcast.395, f32[6,4096]{1,0:T(8,128)S(1)} %copy-done.4, f32[6,2064]{1,0:T(8,128)} %collective-permute-done.3, f32[2048]{0:T(1024)S(1)} %copy-done.28), kind=kLoop, calls=%fused_computation.121 | loop fusion | flops 61440 | bytes 311296 | tf_op jit(solution)/shard_map/mul | solution.py:199
  56.2 3.4 %fusion = f32[288,1024]{1,0:T(8,128)S(1)} fusion(s32[4096]{0:T(1024)S(1)} %copy-done.31, bf16[96,4096]{1,0:T(8,128)(2,1)S(1)} %get-tuple-element.31, bf16[96,4096]{1,0:T(8,128)(2,1)S(1)} %get-tuple-element.30, bf16[96,4096]{1,0:T(8,128)(2,1)S(1)} %bitcast_convert_fusion), kind=kOutput, calls=%fused_computation.1 | convolution fusion | flops 2427191296 | bytes 3555328 | tf_op jit(solution)/shard_map/dot_general | solution.py:51
  59.7 0.8 slice_add_fusion.2
  63.3 1.6 %fusion.22 = f32[3,2,16,1024]{3,2,1,0:T(8,128)S(1)} fusion(f32[3,2,16,1024]{3,2,1,0:T(8,128)} %bitcast.364, f32[3,2,16,1024]{3,2,1,0:T(8,128)S(1)} %get-tuple-element.44, f32[3,2,16,1]{3,2,1,0:T(8,128)} %concatenate.149, f32[3,2,16,1023]{3,2,1,0:T(8,128)S(1)} %bitcast.361, f32[3,2,16,1023]{3,2,1,0:T(8,128)S(1)} %bitcast.360, ...), kind=kLoop, calls=%fused_computation.42 | loop fusion | flops 1572864 | bytes 3014656 | tf_op jit(solution)/shard_map/add | solution.py:202
  65.9 12.8 %all_to_all.12 = f32[32,1,10]{2,1,0:T(1,128)S(1)} all-to-all(f32[32,1,10]{2,1,0:T(1,128)S(1)} %broadcast_in_dim.29), channel_id=1, replica_groups=mesh['cells'=8,'slab'=4] {'cells','slab'}, dimensions={0} | all-to-all | bytes 2560 | tf_op jit(solution)/shard_map/all_to_all | solution.py:36
  79.9 2.5 %all-to-all-start.1 = ((f32[32,1,3]{2,1,0:T(1,128)}), f32[32,1,3]{2,1,0:T(1,128)S(1)}, u32[]{:S(2)}, u32[]{:S(2)}) async-start(f32[32,1,3]{2,1,0:T(1,128)} %broadcast_in_dim.31), calls=%async_computation.1 | async-start | bytes 32768 | tf_op jit(solution)/shard_map/all_to_all | solution.py:36
  83.8 5.7 %all-to-all-done.1 = f32[32,1,3]{2,1,0:T(1,128)S(1)} async-done(((f32[32,1,3]{2,1,0:T(1,128)}), f32[32,1,3]{2,1,0:T(1,128)S(1)}, u32[]{:S(2)}, u32[]{:S(2)}) %all-to-all-start.1) | async-done | bytes 416 | tf_op jit(solution)/shard_map/all_to_all | solution.py:36
  90.2 1.4 %maximum_sqrt_fusion = f32[4]{0:T(128)S(1)} fusion(f32[1]{0:T(128)} %slice.421, f32[1]{0:T(128)} %slice.420, f32[2]{0:T(128)S(1)} %bitcast.420), kind=kLoop, calls=%fused_computation.223 | loop fusion | flops 8 | bytes 32 | tf_op jit(solution)/shard_map/sqrt | solution.py:281
  (185 shorter events, 23.5 us)
Async XLA Ops:
  0.6 14.9 %copy-start = (f32[2,4,16,1024]{3,2,1,0:T(8,128)S(1)}, f32[2,4,16,1024]{3,2,1,0:T(8,128)}, u32[]{:S(2)}) copy-start(f32[2,4,16,1024]{3,2,1,0:T(8,128)} %param.14) | copy-start | bytes 1572868
  0.6 15.0 %copy-start.41 = (s32[1,128]{1,0:T(1,128)S(1)}, s32[1,128]{1,0:T(1,128)}, u32[]{:S(2)}) copy-start(s32[1,128]{1,0:T(1,128)} %param.24) | copy-start | bytes 1540
  0.7 15.0 %copy-start.43 = (f32[1,128]{1,0:T(1,128)S(1)}, f32[1,128]{1,0:T(1,128)}, u32[]{:S(2)}) copy-start(f32[1,128]{1,0:T(1,128)} %param.25) | copy-start | bytes 1540
  1.6 15.0 %copy-start.12 = (f32[16,1024]{1,0:T(8,128)}, f32[16,1024]{1,0:T(8,128)S(1)}, u32[]{:S(2)}) copy-start(f32[16,1024]{1,0:T(8,128)S(1)} %broadcast_select_fusion.1) | copy-start | bytes 196612
  3.2 13.3 %collective-permute-start = (f32[2064]{0:T(1024)S(1)}, f32[2064]{0:T(1024)S(1)}, u32[]{:S(2)}, u32[]{:S(2)}) collective-permute-start(f32[2064]{0:T(1024)S(1)} %pad_maximum_fusion.12), channel_id=1, source_target_pairs={{0,4},{4,8},{8,12},{12,16},{16,20},{20,24},{24,28},{1,5},{5,9},{9,... | collective-permute-start | bytes 24776 | tf_op jit(solution)/shard_map/ppermute | solution.py:13
  9.0 7.6 %copy-start.14 = (f32[16,1024]{1,0:T(8,128)}, f32[16,1024]{1,0:T(8,128)S(1)}, u32[]{:S(2)}) copy-start(f32[16,1024]{1,0:T(8,128)S(1)} %broadcast_select_fusion) | copy-start | bytes 196612
  9.0 7.6 %collective-permute-start.1 = (f32[1024]{0:T(1024)S(1)}, f32[1024]{0:T(1024)S(1)}, u32[]{:S(2)}, u32[]{:S(2)}) collective-permute-start(f32[1024]{0:T(1024)S(1)} %bitcast.419), channel_id=1, source_target_pairs={{0,1},{1,2},{2,3},{4,5},{5,6},{6,7},{8,9},{9,10},{10,11},{12,13},{... | collective-permute-start | bytes 12296 | tf_op jit(solution)/shard_map/ppermute | solution.py:13
  12.4 4.2 %copy-start.1 = (f32[2,2,16,1024]{3,2,1,0:T(8,128)S(1)}, f32[2,2,16,1024]{3,2,1,0:T(8,128)}, u32[]{:S(2)}) copy-start(f32[2,2,16,1024]{3,2,1,0:T(8,128)} %param.13) | copy-start | bytes 786436
  12.4 4.2 %copy-start.2 = (f32[2,2,16,1024]{3,2,1,0:T(8,128)S(1)}, f32[2,2,16,1024]{3,2,1,0:T(8,128)}, u32[]{:S(2)}) copy-start(f32[2,2,16,1024]{3,2,1,0:T(8,128)} %param.15) | copy-start | bytes 786436
  12.4 4.2 %copy-start.22 = (f32[16,1024]{1,0:T(8,128)S(1)}, f32[16,1024]{1,0:T(8,128)}, u32[]{:S(2)}) copy-start(f32[16,1024]{1,0:T(8,128)} %param.17) | copy-start | bytes 196612
  12.4 4.2 %copy-start.23 = (f32[16,1024]{1,0:T(8,128)S(1)}, f32[16,1024]{1,0:T(8,128)}, u32[]{:S(2)}) copy-start(f32[16,1024]{1,0:T(8,128)} %param.18) | copy-start | bytes 196612
  26.1 22.6 %collective-permute-start.6 = (f32[4,16]{1,0:T(4,128)}, f32[4,16]{1,0:T(4,128)}, u32[]{:S(2)}, u32[]{:S(2)}) collective-permute-start(f32[4,16]{1,0:T(4,128)} %pad_maximum_fusion.13), channel_id=1, source_target_pairs={{0,2},{1,3},{2,0},{3,1},{4,6},{5,7},{6,4},{7,5},{8,10},{9,11},{10,... | collective-permute-start | bytes 776 | tf_op jit(solution)/shard_map/ppermute | solution.py:155
  32.7 5.8 %copy-start.26 = (f32[6,1,1024]{2,1,0:T(1,128)S(1)}, f32[6,1,1024]{2,1,0:T(1,128)}, u32[]{:S(2)}) copy-start(f32[6,1,1024]{2,1,0:T(1,128)} %get-tuple-element.39) | copy-start | bytes 73732
  32.7 5.8 %copy-start.27 = (f32[6,1,1024]{2,1,0:T(1,128)S(1)}, f32[6,1,1024]{2,1,0:T(1,128)}, u32[]{:S(2)}) copy-start(f32[6,1,1024]{2,1,0:T(1,128)} %get-tuple-element.40) | copy-start | bytes 73732
  32.7 5.8 %copy-start.37 = (f32[64]{0:T(128)S(1)}, f32[64]{0:T(128)}, u32[]{:S(2)}) copy-start(f32[64]{0:T(128)} %reshape.486) | copy-start | bytes 772
  32.7 7.6 %copy-start.32 = (f32[6,16]{1,0:T(8,128)S(1)}, f32[6,16]{1,0:T(8,128)}, u32[]{:S(2)}) copy-start(f32[6,16]{1,0:T(8,128)} %get-tuple-element.4) | copy-start | bytes 1156
  32.7 9.8 %copy-start.36 = (f32[2064]{0:T(1024)S(1)}, f32[2064]{0:T(1024)}, u32[]{:S(2)}) copy-start(f32[2064]{0:T(1024)} %copy-done.35) | copy-start | bytes 24772
  34.5 19.6 %collective-permute-start.3 = (f32[6,2064]{1,0:T(8,128)}, f32[6,2064]{1,0:T(8,128)}, u32[]{:S(2)}, u32[]{:S(2)}) collective-permute-start(f32[6,2064]{1,0:T(8,128)} %pad_maximum_fusion.7), channel_id=1, source_target_pairs={{0,4},{4,8},{8,12},{12,16},{16,20},{20,24},{24,28},{1,5},{5,9},{9,... | collective-permute-start | bytes 148616 | tf_op jit(solution)/shard_map/ppermute | solution.py:13
  39.1 7.0 %collective-permute-start.4 = (f32[6208]{0:T(1024)}, f32[6208]{0:T(1024)}, u32[]{:S(2)}, u32[]{:S(2)}) collective-permute-start(f32[6208]{0:T(1024)} %get-tuple-element.71), channel_id=1, source_target_pairs={{0,3},{1,0},{2,1},{3,2},{4,7},{5,4},{6,5},{7,6},{8,11},{9,8},{10,9... | collective-permute-start | bytes 74504 | tf_op jit(solution)/shard_map/ppermute | solution.py:155
  40.3 3.3 %collective-permute-start.5 = (f32[6208]{0:T(1024)S(1)}, f32[6208]{0:T(1024)S(1)}, u32[]{:S(2)}, u32[]{:S(2)}) collective-permute-start(f32[6208]{0:T(1024)S(1)} %get-tuple-element.70), channel_id=1, source_target_pairs={{0,1},{1,2},{2,3},{3,0},{4,5},{5,6},{6,7},{7,4},{8,9},{9,10},{10,1... | collective-permute-start | bytes 74504 | tf_op jit(solution)/shard_map/ppermute | solution.py:155
  41.0 13.0 %collective-permute-start.2 = (f32[6,2064]{1,0:T(8,128)}, f32[6,2064]{1,0:T(8,128)}, u32[]{:S(2)}, u32[]{:S(2)}) collective-permute-start(f32[6,2064]{1,0:T(8,128)} %pad_maximum_fusion.6), channel_id=1, source_target_pairs={{4,0},{8,4},{12,8},{16,12},{20,16},{24,20},{28,24},{5,1},{9,5},{13... | collective-permute-start | bytes 148616 | tf_op jit(solution)/shard_map/ppermute | solution.py:13
  48.7 4.8 %copy-start.30 = (f32[6208]{0:T(1024)S(1)}, f32[6208]{0:T(1024)}, u32[]{:S(2)}) copy-start(f32[6208]{0:T(1024)} %copy-done.29) | copy-start | bytes 74500
  48.7 5.4 %copy-start.4 = (f32[6,4096]{1,0:T(8,128)S(1)}, f32[6,4096]{1,0:T(8,128)}, u32[]{:S(2)}) copy-start(f32[6,4096]{1,0:T(8,128)} %copy-done.3) | copy-start | bytes 294916
  48.7 5.4 %copy-start.28 = (f32[2048]{0:T(1024)S(1)}, f32[2048]{0:T(1024)}, u32[]{:S(2)}) copy-start(f32[2048]{0:T(1024)} %slice.454) | copy-start | bytes 24580
  59.7 3.6 %copy-start.13 = (f32[16,1024]{1,0:T(8,128)S(1)}, f32[16,1024]{1,0:T(8,128)}, u32[]{:S(2)}) copy-start(f32[16,1024]{1,0:T(8,128)} %copy-done.12) | copy-start | bytes 196612
  64.9 14.0 %copy-start.8 = (f32[16,1024]{1,0:T(8,128)S(1)}, f32[16,1024]{1,0:T(8,128)}, u32[]{:S(2)}) copy-start(f32[16,1024]{1,0:T(8,128)} %copy-done.7) | copy-start | bytes 196612
  64.9 14.0 %copy-start.10 = (f32[16,1024]{1,0:T(8,128)S(1)}, f32[16,1024]{1,0:T(8,128)}, u32[]{:S(2)}) copy-start(f32[16,1024]{1,0:T(8,128)} %copy-done.9) | copy-start | bytes 196612
  65.0 14.0 %copy-start.25 = (f32[2,2,16,1024]{3,2,1,0:T(8,128)S(1)}, f32[2,2,16,1024]{3,2,1,0:T(8,128)}, u32[]{:S(2)}) copy-start(f32[2,2,16,1024]{3,2,1,0:T(8,128)} %param.16) | copy-start | bytes 786436
  65.1 17.3 %copy-start.6 = (f32[16,1024]{1,0:T(8,128)S(1)}, f32[16,1024]{1,0:T(8,128)}, u32[]{:S(2)}) copy-start(f32[16,1024]{1,0:T(8,128)} %copy-done.5) | copy-start | bytes 196612
  65.1 17.3 %copy-start.17 = (f32[16,1024]{1,0:T(8,128)S(1)}, f32[16,1024]{1,0:T(8,128)}, u32[]{:S(2)}) copy-start(f32[16,1024]{1,0:T(8,128)} %copy-done.16) | copy-start | bytes 196612
  65.1 17.3 %copy-start.19 = (f32[16,1024]{1,0:T(8,128)S(1)}, f32[16,1024]{1,0:T(8,128)}, u32[]{:S(2)}) copy-start(f32[16,1024]{1,0:T(8,128)} %copy-done.18) | copy-start | bytes 196612
  79.9 9.6 %all-to-all-start.1 = ((f32[32,1,3]{2,1,0:T(1,128)}), f32[32,1,3]{2,1,0:T(1,128)S(1)}, u32[]{:S(2)}, u32[]{:S(2)}) async-start(f32[32,1,3]{2,1,0:T(1,128)} %broadcast_in_dim.31), calls=%async_computation.1 | async-start | bytes 32768 | tf_op jit(solution)/shard_map/all_to_all | solution.py:36
  (21 other events, 31.4 us)

commit v6 on v5

--- a/solution.py
+++ b/solution.py
@@ -160,8 +160,8 @@
         picks = gather(scaled, fault_at)
         picks_near = picks[:, :slot_count]
         picks_far = picks[:, slot_count:]
-        from_left = shifted(jnp.concatenate([scaled[:, :, -1], picks_near], axis=1), "cells", 1)
-        from_right = shifted(jnp.concatenate([scaled[:, :, 0], picks_far], axis=1), "cells", -1)
+        from_left = shifted(jnp.concatenate([picks_near, scaled[:, :, -1]], axis=1), "cells", 1)
+        from_right = shifted(jnp.concatenate([picks_far, scaled[:, :, 0]], axis=1), "cells", -1)
         pressure = fields[:, 0]
         values = gather(pressure, well_at)
         local = jnp.concatenate(
@@ -170,24 +170,28 @@
                 jnp.dot(well_index * values, well_onehot, precision=highest),
             ]
         )
-        halo_size = count * 2 * column_count
-        from_above = slab_shift(
-            jnp.concatenate([scaled[:, -1, :].reshape(-1), local.reshape(-1)]), 1
-        )
-        from_below = slab_shift(
-            jnp.concatenate([scaled[:, 0, :].reshape(-1), local.reshape(-1)]), -1
-        )
+        halo_rows = count * 2
+        well_rows = -(-local.size // column_count)
+        well_block = jnp.pad(
+            local.reshape(-1), (0, well_rows * column_count - local.size)
+        ).reshape(well_rows, column_count)
+        from_above = slab_shift(jnp.concatenate([scaled[:, -1, :], well_block]), 1)
+        from_below = slab_shift(jnp.concatenate([scaled[:, 0, :], well_block]), -1)
+
+        def wells_of(message):
+            return message[halo_rows:].reshape(-1)[: local.size].reshape(local.shape)
+
         summed = local
         if slab_size > 1:
-            summed = summed + from_above[halo_size:].reshape(local.shape)
+            summed = summed + wells_of(from_above)
         if slab_size > 2:
-            summed = summed + from_below[halo_size:].reshape(local.shape)
+            summed = summed + wells_of(from_below)
         for by in range(2, slab_size - 1):
             summed = summed + slab_shift(local, by)
-        from_above = from_above[:halo_size].reshape(count * 2, column_count)
-        from_below = from_below[:halo_size].reshape(count * 2, column_count)
-        west = jnp.concatenate([from_left[:, :layer_count, None], scaled[:, :, :-1]], axis=2)
-        east = jnp.concatenate([scaled[:, :, 1:], from_right[:, :layer_count, None]], axis=2)
+        from_above = from_above[:halo_rows]
+        from_below = from_below[:halo_rows]
+        west = jnp.concatenate([from_left[:, slot_count:, None], scaled[:, :, :-1]], axis=2)
+        east = jnp.concatenate([scaled[:, :, 1:], from_right[:, slot_count:, None]], axis=2)
         above = jnp.concatenate([from_above[:, None, :], scaled[:, :-1, :]], axis=1)
         below = jnp.concatenate([scaled[:, 1:, :], from_below[:, None, :]], axis=1)
         laplace = (
@@ -196,8 +200,8 @@
             + trans_down * (scaled - below)
             + trans_up * (scaled - above)
         )
-        flux_right = weight_here * (picks_near - from_right[:, layer_count:])
-        flux_left = weight_left * (from_left[:, layer_count:] - picks_far)
+        flux_right = weight_here * (picks_near - from_right[:, :slot_count])
+        flux_left = weight_left * (from_left[:, :slot_count] - picks_far)
         fault_term = scatter(jnp.concatenate([flux_right, -flux_left], axis=1), fault_at)
         laplace = (laplace + fault_term).reshape(count, 2, layer_count, column_count)
         back = jnp.dot(summed[1:] / summed[0], well_onehot.T, precision=highest)

time: 93.1 us -> 93.8 us (level)
  local copies, waits for them, and re-layouts: 21.6 us -> 22.6 us
    concatenate x2 -> x4, local copies, waits for them, and re-layouts: 1.4 us -> 4.19 us  [the longest x1 1.4 us: operator(): below = jnp.concatenate([scaled[:, 1:, :], from_below[:, None, :]], axis=1)]
    slice x7 -> x5, local copies, waits for them, and re-layouts: 5.77 us -> 3.04 us  [the longest x2 1.03 us: wells_of(): return message[halo_rows:].reshape(-1)[:local.size].reshape(local.shape)]
    unnamed x103, local copies, waits for them, and re-layouts: 3.89 us -> 4.9 us
  transfers between devices with their start and end apart: 8 -> 8, of which waited for: 2 -> 1; matrix products, arithmetic and copies ran while one was open for 28% -> 27% of each run, Pallas kernels for 0% -> 0%
where the time goes in v6:
time: 93.8 us; the launch traced here: 92.8 us
  local copies, waits for them, and re-layouts  22.6 us (24%)
  other arithmetic  20 us (21%)
  starting transfers between devices  18.2 us (19%)
  blocking collectives  13 us (14%)
  matrix products  11 us (12%)
  waiting for transfers between devices  5.75 us (6%)
  between operations  2.25 us (2%)
    all_to_all x1, blocking collectives, global_sum(): gathered = lax.all_to_all(copies, axes, 0, 0, tiled=True)  13 us
    ppermute x4, starting transfers between devices, shifted(): return lax.ppermute(value, axis, pairs)  11.6 us
    dot_general x4, matrix products, onehot_dot(): lax.dot_general(pieces, onehot, (dims, ((), ())), preferred_element_type=...  9.17 us
    all_to_all x1, waiting for transfers between devices, global_sum(): gathered = lax.all_to_all(copies, axes, 0, 0, tiled=True)  5.73 us
    unnamed x103, local copies, waits for them, and re-layouts  4.9 us
    ppermute x3, starting transfers between devices, slab_shift(): lax.ppermute(value, 'slab', [(i, (i + by) % count) for i in range(count)])  3.97 us
    all_to_all x1, starting transfers between devices, global_sum(): gathered = lax.all_to_all(copies, axes, 0, 0, tiled=True)  2.57 us
    reshape x2, local copies, waits for them, and re-layouts, wells_of(): return message[halo_rows:].reshape(-1)[:local.size].reshape(local.shape)  2.56 us
  transfers between devices with their start and end apart: 8, of which 1 were waited for; matrix products, arithmetic and copies ran while one was open for 27% of the time, Pallas kernels for 0%

profile of v6, /device:TPU:0, one launch (start us, length us, event | category | flops | bytes accessed | tf_op | source)
XLA Modules:
  0.0 92.8 jit_solution(16746310449666553342)
XLA Ops:
  0.7 0.9 broadcast_select_fusion.1
  3.2 4.9 %collective-permute-start = (f32[2064]{0:T(1024)S(1)}, f32[2064]{0:T(1024)S(1)}, u32[]{:S(2)}, u32[]{:S(2)}) collective-permute-start(f32[2064]{0:T(1024)S(1)} %pad_maximum_fusion.12), channel_id=1, source_target_pairs={{0,4},{4,8},{8,12},{12,16},{16,20},{20,24},{24,28},{1,5},{5,9},{9,... | collective-permute-start | bytes 24776 | tf_op jit(solution)/shard_map/ppermute | solution.py:13
  8.1 0.9 broadcast_select_fusion
  9.0 1.5 %collective-permute-start.1 = (f32[1024]{0:T(1024)S(1)}, f32[1024]{0:T(1024)S(1)}, u32[]{:S(2)}, u32[]{:S(2)}) collective-permute-start(f32[1024]{0:T(1024)S(1)} %bitcast.425), channel_id=1, source_target_pairs={{0,1},{1,2},{2,3},{4,5},{5,6},{6,7},{8,9},{9,10},{10,11},{12,13},{... | collective-permute-start | bytes 12296 | tf_op jit(solution)/shard_map/ppermute | solution.py:13
  10.5 1.2 %and_select_fusion.2 = s32[128]{0:T(128)} fusion(s32[1,128]{1,0:T(1,128)} %param.23), kind=kLoop, calls=%fused_computation.216 | loop fusion | flops 1408 | bytes 1024 | tf_op jit(solution)/shard_map/jit(remainder)/select_n | solution.py:105
  12.4 1.0 %fusion.101 = (f32[1,2,16,1024]{3,2,1,0:T(8,128)S(1)}, f32[1,2,16,1024]{3,2,1,0:T(8,128)S(1)}) fusion(f32[2,2,16,1024]{3,2,1,0:T(8,128)} %param.15), kind=kLoop, calls=%fused_computation.241 | loop fusion | bytes 524288 | tf_op jit(solution)/shard_map/slice | solution.py:133
  13.5 1.3 %add_select_fusion = (s32[4096]{0:T(1024)S(1)}, s32[4096]{0:T(1024)}) fusion(s32[2048]{0:T(1024)} %bitcast.422, s32[2048]{0:T(1024)} %bitcast.423), kind=kLoop, calls=%fused_computation.186 | loop fusion | flops 81920 | bytes 49152 | tf_op jit(solution)/shard_map/jit(floor_divide)/jit(_where)/select_n | solution.py:106
  15.6 0.7 fusion.66
  17.1 0.7 fusion.55
  18.6 0.8 fusion.31
  20.2 0.8 slice_reduce_fusion.1
  21.8 0.9 %fusion.99 = (f32[6,15,1024]{2,1,0:T(8,128)}, f32[6,15,1024]{2,1,0:T(8,128)}) fusion(f32[6,16,1024]{2,1,0:T(8,128)S(1)} %bitcast.363), kind=kLoop, calls=%fused_computation.239 | loop fusion | bytes 1474560 | tf_op jit(solution)/shard_map/slice | solution.py:195
  25.1 1.3 %reshape.478 = f32[64]{0:T(128)} reshape(f32[4,16]{1,0:T(4,128)} %pad_maximum_fusion.13) | data formatting | bytes 512 | tf_op jit(solution)/shard_map/reshape | solution.py:176
  26.4 2.0 %collective-permute-start.6 = (f32[4,16]{1,0:T(4,128)}, f32[4,16]{1,0:T(4,128)}, u32[]{:S(2)}, u32[]{:S(2)}) collective-permute-start(f32[4,16]{1,0:T(4,128)} %pad_maximum_fusion.13), channel_id=1, source_target_pairs={{0,2},{1,3},{2,0},{3,1},{4,6},{5,7},{6,4},{7,5},{8,10},{9,11},{10,... | collective-permute-start | bytes 776 | tf_op jit(solution)/shard_map/ppermute | solution.py:155
  28.4 4.4 %fusion.1 = f32[288,4096]{1,0:T(8,128)S(1)} fusion(s32[4096]{0:T(1024)} %get-tuple-element.69, bf16[96,1024]{1,0:T(8,128)(2,1)} %get-tuple-element.48, bf16[96,1024]{1,0:T(8,128)(2,1)} %get-tuple-element.47, bf16[96,1024]{1,0:T(8,128)(2,1)} %bitcast_convert_fusion.1), kind=kOutput, calls=%fused_computation.2 | convolution fusion | flops 2421882880 | bytes 5324800 | tf_op jit(solution)/shard_map/dot_general | solution.py:51
  34.7 4.0 %collective-permute-start.3 = (f32[6,2064]{1,0:T(8,128)}, f32[6,2064]{1,0:T(8,128)}, u32[]{:S(2)}, u32[]{:S(2)}) collective-permute-start(f32[6,2064]{1,0:T(8,128)} %pad_maximum_fusion.7), channel_id=1, source_target_pairs={{0,4},{4,8},{8,12},{12,16},{16,20},{20,24},{24,28},{1,5},{5,9},{9,... | collective-permute-start | bytes 148616 | tf_op jit(solution)/shard_map/ppermute | solution.py:13
  39.5 1.3 %collective-permute-start.2 = (f32[6,2064]{1,0:T(8,128)}, f32[6,2064]{1,0:T(8,128)}, u32[]{:S(2)}, u32[]{:S(2)}) collective-permute-start(f32[6,2064]{1,0:T(8,128)} %pad_maximum_fusion.6), channel_id=1, source_target_pairs={{4,0},{8,4},{12,8},{16,12},{20,16},{24,20},{28,24},{5,1},{9,5},{13... | collective-permute-start | bytes 148616 | tf_op jit(solution)/shard_map/ppermute | solution.py:13
  40.8 2.0 %collective-permute-start.4 = (f32[7,1024]{1,0:T(8,128)S(1)}, f32[7,1024]{1,0:T(8,128)S(1)}, u32[]{:S(2)}, u32[]{:S(2)}) collective-permute-start(f32[7,1024]{1,0:T(8,128)S(1)} %get-tuple-element.71), channel_id=1, source_target_pairs={{0,3},{1,0},{2,1},{3,2},{4,7},{5,4},{6,5},{7,6},{8,11},{9,8},{10,9... | collective-permute-start | bytes 86024 | tf_op jit(solution)/shard_map/ppermute | solution.py:155
  45.7 1.3 %reshape.481 = f32[4,16]{1,0:T(4,128)} reshape(f32[64]{0:T(128)} %slice_reduce_fusion.4) | data formatting | bytes 512 | tf_op jit(solution)/shard_map/reshape | solution.py:182
  47.0 1.2 %reshape.482 = f32[4,16]{1,0:T(4,128)} reshape(f32[64]{0:T(128)} %slice_reduce_fusion.3) | data formatting | bytes 512 | tf_op jit(solution)/shard_map/reshape | solution.py:182
  49.0 0.9 fusion.9
  50.0 1.0 %fusion.16 = f32[144,1024]{1,0:T(8,128)S(1)} fusion(s32[128]{0:T(128)} %and_select_fusion.2, bf16[48,128]{1,0:T(8,128)(2,1)S(1)} %get-tuple-element.67, bf16[48,128]{1,0:T(8,128)(2,1)S(1)} %get-tuple-element.66, bf16[48,128]{1,0:T(8,128)(2,1)S(1)} %bitcast_convert_fusion.3), kind=kOutput, calls=%fused_computation.27 | convolution fusion | flops 37990400 | bytes 627200 | tf_op jit(solution)/shard_map/dot_general | solution.py:51
  51.7 1.4 %concatenate.151 = f32[3,2,1,1024]{3,2,1,0:T(1,128)} reshape(f32[6,1024]{1,0:T(8,128)} %bitcast.399) | data formatting | bytes 49152 | tf_op jit(solution)/shard_map/concatenate | solution.py:196
  53.1 1.4 %concatenate.152 = f32[3,2,1,1024]{3,2,1,0:T(1,128)} reshape(f32[6,1024]{1,0:T(8,128)} %bitcast.398) | data formatting | bytes 49152 | tf_op jit(solution)/shard_map/concatenate | solution.py:195
  54.5 1.0 %fusion.53 = (f32[6,2048]{1,0:T(8,128)S(1)}, f32[6,2048]{1,0:T(8,128)S(1)}) fusion(f32[6,2064]{1,0:T(8,128)} %collective-permute-done.2, f32[2048]{0:T(1024)S(1)} %bitcast.400, f32[6,4096]{1,0:T(8,128)} %copy-done.3, f32[6,2064]{1,0:T(8,128)} %collective-permute-done.3, f32[2048]{0:T(1024)S(1)} %copy-done.29), kind=kLoop, calls=%fused_computation.121 | loop fusion | flops 61440 | bytes 311296 | tf_op jit(solution)/shard_map/mul | solution.py:203
  56.6 3.4 %fusion = f32[288,1024]{1,0:T(8,128)S(1)} fusion(s32[4096]{0:T(1024)S(1)} %copy-done.30, bf16[96,4096]{1,0:T(8,128)(2,1)S(1)} %get-tuple-element.31, bf16[96,4096]{1,0:T(8,128)(2,1)S(1)} %get-tuple-element.30, bf16[96,4096]{1,0:T(8,128)(2,1)S(1)} %bitcast_convert_fusion), kind=kOutput, calls=%fused_computation.1 | convolution fusion | flops 2427191296 | bytes 3555328 | tf_op jit(solution)/shard_map/dot_general | solution.py:51
  60.0 0.8 slice_add_fusion.2
  63.7 1.6 %fusion.22 = f32[3,2,16,1024]{3,2,1,0:T(8,128)S(1)} fusion(f32[3,2,16,1024]{3,2,1,0:T(8,128)} %bitcast.369, f32[3,2,16,1024]{3,2,1,0:T(8,128)S(1)} %get-tuple-element.44, f32[3,2,16,1]{3,2,1,0:T(8,128)} %concatenate.149, f32[3,2,16,1023]{3,2,1,0:T(8,128)S(1)} %bitcast.366, f32[3,2,16,1023]{3,2,1,0:T(8,128)S(1)} %bitcast.365, ...), kind=kLoop, calls=%fused_computation.42 | loop fusion | flops 1572864 | bytes 3014656 | tf_op jit(solution)/shard_map/add | solution.py:206
  66.3 13.0 %all_to_all.12 = f32[32,1,10]{2,1,0:T(1,128)S(1)} all-to-all(f32[32,1,10]{2,1,0:T(1,128)S(1)} %broadcast_in_dim.29), channel_id=1, replica_groups=mesh['cells'=8,'slab'=4] {'cells','slab'}, dimensions={0} | all-to-all | bytes 2560 | tf_op jit(solution)/shard_map/all_to_all | solution.py:36
  80.5 2.6 %all-to-all-start.1 = ((f32[32,1,3]{2,1,0:T(1,128)}), f32[32,1,3]{2,1,0:T(1,128)S(1)}, u32[]{:S(2)}, u32[]{:S(2)}) async-start(f32[32,1,3]{2,1,0:T(1,128)} %broadcast_in_dim.31), calls=%async_computation.1 | async-start | bytes 32768 | tf_op jit(solution)/shard_map/all_to_all | solution.py:36
  84.5 5.7 %all-to-all-done.1 = f32[32,1,3]{2,1,0:T(1,128)S(1)} async-done(((f32[32,1,3]{2,1,0:T(1,128)}), f32[32,1,3]{2,1,0:T(1,128)S(1)}, u32[]{:S(2)}, u32[]{:S(2)}) %all-to-all-start.1) | async-done | bytes 416 | tf_op jit(solution)/shard_map/all_to_all | solution.py:36
  90.8 1.3 %maximum_sqrt_fusion = f32[4]{0:T(128)S(1)} fusion(f32[1]{0:T(128)} %slice.411, f32[1]{0:T(128)} %slice.410, f32[2]{0:T(128)S(1)} %bitcast.426), kind=kLoop, calls=%fused_computation.227 | loop fusion | flops 8 | bytes 32 | tf_op jit(solution)/shard_map/sqrt | solution.py:285
  (186 shorter events, 23.2 us)
Async XLA Ops:
  0.6 14.9 %copy-start = (f32[2,4,16,1024]{3,2,1,0:T(8,128)S(1)}, f32[2,4,16,1024]{3,2,1,0:T(8,128)}, u32[]{:S(2)}) copy-start(f32[2,4,16,1024]{3,2,1,0:T(8,128)} %param.14) | copy-start | bytes 1572868
  0.6 15.0 %copy-start.40 = (s32[1,128]{1,0:T(1,128)S(1)}, s32[1,128]{1,0:T(1,128)}, u32[]{:S(2)}) copy-start(s32[1,128]{1,0:T(1,128)} %param.24) | copy-start | bytes 1540
  0.7 15.0 %copy-start.42 = (f32[1,128]{1,0:T(1,128)S(1)}, f32[1,128]{1,0:T(1,128)}, u32[]{:S(2)}) copy-start(f32[1,128]{1,0:T(1,128)} %param.25) | copy-start | bytes 1540
  1.6 15.5 %copy-start.11 = (f32[16,1024]{1,0:T(8,128)}, f32[16,1024]{1,0:T(8,128)S(1)}, u32[]{:S(2)}) copy-start(f32[16,1024]{1,0:T(8,128)S(1)} %broadcast_select_fusion.1) | copy-start | bytes 196612
  3.2 13.3 %collective-permute-start = (f32[2064]{0:T(1024)S(1)}, f32[2064]{0:T(1024)S(1)}, u32[]{:S(2)}, u32[]{:S(2)}) collective-permute-start(f32[2064]{0:T(1024)S(1)} %pad_maximum_fusion.12), channel_id=1, source_target_pairs={{0,4},{4,8},{8,12},{12,16},{16,20},{20,24},{24,28},{1,5},{5,9},{9,... | collective-permute-start | bytes 24776 | tf_op jit(solution)/shard_map/ppermute | solution.py:13
  9.0 8.1 %copy-start.13 = (f32[16,1024]{1,0:T(8,128)}, f32[16,1024]{1,0:T(8,128)S(1)}, u32[]{:S(2)}) copy-start(f32[16,1024]{1,0:T(8,128)S(1)} %broadcast_select_fusion) | copy-start | bytes 196612
  9.0 7.6 %collective-permute-start.1 = (f32[1024]{0:T(1024)S(1)}, f32[1024]{0:T(1024)S(1)}, u32[]{:S(2)}, u32[]{:S(2)}) collective-permute-start(f32[1024]{0:T(1024)S(1)} %bitcast.425), channel_id=1, source_target_pairs={{0,1},{1,2},{2,3},{4,5},{5,6},{6,7},{8,9},{9,10},{10,11},{12,13},{... | collective-permute-start | bytes 12296 | tf_op jit(solution)/shard_map/ppermute | solution.py:13
  12.4 4.7 %copy-start.1 = (f32[2,2,16,1024]{3,2,1,0:T(8,128)S(1)}, f32[2,2,16,1024]{3,2,1,0:T(8,128)}, u32[]{:S(2)}) copy-start(f32[2,2,16,1024]{3,2,1,0:T(8,128)} %param.13) | copy-start | bytes 786436
  12.4 4.7 %copy-start.2 = (f32[2,2,16,1024]{3,2,1,0:T(8,128)S(1)}, f32[2,2,16,1024]{3,2,1,0:T(8,128)}, u32[]{:S(2)}) copy-start(f32[2,2,16,1024]{3,2,1,0:T(8,128)} %param.15) | copy-start | bytes 786436
  12.4 4.7 %copy-start.21 = (f32[16,1024]{1,0:T(8,128)S(1)}, f32[16,1024]{1,0:T(8,128)}, u32[]{:S(2)}) copy-start(f32[16,1024]{1,0:T(8,128)} %param.17) | copy-start | bytes 196612
  12.4 4.7 %copy-start.22 = (f32[16,1024]{1,0:T(8,128)S(1)}, f32[16,1024]{1,0:T(8,128)}, u32[]{:S(2)}) copy-start(f32[16,1024]{1,0:T(8,128)} %param.18) | copy-start | bytes 196612
  26.4 21.9 %collective-permute-start.6 = (f32[4,16]{1,0:T(4,128)}, f32[4,16]{1,0:T(4,128)}, u32[]{:S(2)}, u32[]{:S(2)}) collective-permute-start(f32[4,16]{1,0:T(4,128)} %pad_maximum_fusion.13), channel_id=1, source_target_pairs={{0,2},{1,3},{2,0},{3,1},{4,6},{5,7},{6,4},{7,5},{8,10},{9,11},{10,... | collective-permute-start | bytes 776 | tf_op jit(solution)/shard_map/ppermute | solution.py:155
  33.0 5.7 %copy-start.26 = (f32[6,1,1024]{2,1,0:T(1,128)S(1)}, f32[6,1,1024]{2,1,0:T(1,128)}, u32[]{:S(2)}) copy-start(f32[6,1,1024]{2,1,0:T(1,128)} %get-tuple-element.39) | copy-start | bytes 73732
  33.1 5.7 %copy-start.25 = (f32[6,1,1024]{2,1,0:T(1,128)S(1)}, f32[6,1,1024]{2,1,0:T(1,128)}, u32[]{:S(2)}) copy-start(f32[6,1,1024]{2,1,0:T(1,128)} %get-tuple-element.40) | copy-start | bytes 73732
  33.1 5.7 %copy-start.37 = (f32[64]{0:T(128)S(1)}, f32[64]{0:T(128)}, u32[]{:S(2)}) copy-start(f32[64]{0:T(128)} %reshape.478) | copy-start | bytes 772
  33.1 5.8 %copy-start.31 = (f32[6,16]{1,0:T(8,128)S(1)}, f32[6,16]{1,0:T(8,128)}, u32[]{:S(2)}) copy-start(f32[6,16]{1,0:T(8,128)} %get-tuple-element.4) | copy-start | bytes 1156
  33.1 9.7 %copy-start.35 = (f32[2064]{0:T(1024)S(1)}, f32[2064]{0:T(1024)}, u32[]{:S(2)}) copy-start(f32[2064]{0:T(1024)} %copy-done.34) | copy-start | bytes 24772
  34.7 19.8 %collective-permute-start.3 = (f32[6,2064]{1,0:T(8,128)}, f32[6,2064]{1,0:T(8,128)}, u32[]{:S(2)}, u32[]{:S(2)}) collective-permute-start(f32[6,2064]{1,0:T(8,128)} %pad_maximum_fusion.7), channel_id=1, source_target_pairs={{0,4},{4,8},{8,12},{12,16},{16,20},{20,24},{24,28},{1,5},{5,9},{9,... | collective-permute-start | bytes 148616 | tf_op jit(solution)/shard_map/ppermute | solution.py:13
  38.8 4.6 %collective-permute-start.5 = (f32[7,1024]{1,0:T(8,128)S(1)}, f32[7,1024]{1,0:T(8,128)S(1)}, u32[]{:S(2)}, u32[]{:S(2)}) collective-permute-start(f32[7,1024]{1,0:T(8,128)S(1)} %get-tuple-element.70), channel_id=1, source_target_pairs={{0,1},{1,2},{2,3},{3,0},{4,5},{5,6},{6,7},{7,4},{8,9},{9,10},{10,1... | collective-permute-start | bytes 86024 | tf_op jit(solution)/shard_map/ppermute | solution.py:155
  39.5 14.9 %collective-permute-start.2 = (f32[6,2064]{1,0:T(8,128)}, f32[6,2064]{1,0:T(8,128)}, u32[]{:S(2)}, u32[]{:S(2)}) collective-permute-start(f32[6,2064]{1,0:T(8,128)} %pad_maximum_fusion.6), channel_id=1, source_target_pairs={{4,0},{8,4},{12,8},{16,12},{20,16},{24,20},{28,24},{5,1},{9,5},{13... | collective-permute-start | bytes 148616 | tf_op jit(solution)/shard_map/ppermute | solution.py:13
  40.8 3.8 %collective-permute-start.4 = (f32[7,1024]{1,0:T(8,128)S(1)}, f32[7,1024]{1,0:T(8,128)S(1)}, u32[]{:S(2)}, u32[]{:S(2)}) collective-permute-start(f32[7,1024]{1,0:T(8,128)S(1)} %get-tuple-element.71), channel_id=1, source_target_pairs={{0,3},{1,0},{2,1},{3,2},{4,7},{5,4},{6,5},{7,6},{8,11},{9,8},{10,9... | collective-permute-start | bytes 86024 | tf_op jit(solution)/shard_map/ppermute | solution.py:155
  49.9 4.5 %copy-start.29 = (f32[2048]{0:T(1024)S(1)}, f32[2048]{0:T(1024)}, u32[]{:S(2)}) copy-start(f32[2048]{0:T(1024)} %slice.444) | copy-start | bytes 24580
  60.0 3.6 %copy-start.12 = (f32[16,1024]{1,0:T(8,128)S(1)}, f32[16,1024]{1,0:T(8,128)}, u32[]{:S(2)}) copy-start(f32[16,1024]{1,0:T(8,128)} %copy-done.11) | copy-start | bytes 196612
  60.0 3.6 %copy-start.14 = (f32[16,1024]{1,0:T(8,128)S(1)}, f32[16,1024]{1,0:T(8,128)}, u32[]{:S(2)}) copy-start(f32[16,1024]{1,0:T(8,128)} %copy-done.13) | copy-start | bytes 196612
  60.0 3.6 %copy-start.19 = (f32[16,1024]{1,0:T(8,128)S(1)}, f32[16,1024]{1,0:T(8,128)}, u32[]{:S(2)}) copy-start(f32[16,1024]{1,0:T(8,128)} %get-tuple-element.24) | copy-start | bytes 196612
  65.3 14.2 %copy-start.7 = (f32[16,1024]{1,0:T(8,128)S(1)}, f32[16,1024]{1,0:T(8,128)}, u32[]{:S(2)}) copy-start(f32[16,1024]{1,0:T(8,128)} %copy-done.6) | copy-start | bytes 196612
  65.3 14.2 %copy-start.9 = (f32[16,1024]{1,0:T(8,128)S(1)}, f32[16,1024]{1,0:T(8,128)}, u32[]{:S(2)}) copy-start(f32[16,1024]{1,0:T(8,128)} %copy-done.8) | copy-start | bytes 196612
  65.3 14.2 %copy-start.24 = (f32[2,2,16,1024]{3,2,1,0:T(8,128)S(1)}, f32[2,2,16,1024]{3,2,1,0:T(8,128)}, u32[]{:S(2)}) copy-start(f32[2,2,16,1024]{3,2,1,0:T(8,128)} %param.16) | copy-start | bytes 786436
  65.5 17.6 %copy-start.5 = (f32[16,1024]{1,0:T(8,128)S(1)}, f32[16,1024]{1,0:T(8,128)}, u32[]{:S(2)}) copy-start(f32[16,1024]{1,0:T(8,128)} %copy-done.4) | copy-start | bytes 196612
  65.5 17.6 %copy-start.16 = (f32[16,1024]{1,0:T(8,128)S(1)}, f32[16,1024]{1,0:T(8,128)}, u32[]{:S(2)}) copy-start(f32[16,1024]{1,0:T(8,128)} %copy-done.15) | copy-start | bytes 196612
  65.5 17.6 %copy-start.18 = (f32[16,1024]{1,0:T(8,128)S(1)}, f32[16,1024]{1,0:T(8,128)}, u32[]{:S(2)}) copy-start(f32[16,1024]{1,0:T(8,128)} %copy-done.17) | copy-start | bytes 196612
  80.5 9.7 %all-to-all-start.1 = ((f32[32,1,3]{2,1,0:T(1,128)}), f32[32,1,3]{2,1,0:T(1,128)S(1)}, u32[]{:S(2)}, u32[]{:S(2)}) async-start(f32[32,1,3]{2,1,0:T(1,128)} %broadcast_in_dim.31), calls=%async_computation.1 | async-start | bytes 32768 | tf_op jit(solution)/shard_map/all_to_all | solution.py:36
  (20 other events, 24.9 us)

commit v7 on v5

--- a/solution.py
+++ b/solution.py
@@ -45,13 +45,23 @@
     return high, middle, low
 
 
-def onehot_dot(value, onehot, dims):
+def split2(value):
+    high = value.astype(jnp.bfloat16)
+    low = (value - high.astype(value.dtype)).astype(jnp.bfloat16)
+    return high, low
+
+
+def onehot_dot(value, onehot, dims, split=split3):
     rows = value.shape[0]
-    pieces = jnp.concatenate(split3(value), axis=0)
+    parts = split(value)
+    pieces = jnp.concatenate(parts, axis=0)
     part = lax.dot_general(
         pieces, onehot, (dims, ((), ())), preferred_element_type=jnp.float32
     )
-    return (part[:rows] + part[rows : 2 * rows]) + part[2 * rows :]
+    total = part[:rows]
+    for index in range(1, len(parts)):
+        total = total + part[index * rows : (index + 1) * rows]
+    return total
 
 
 def per_device(
@@ -106,19 +116,19 @@
         rows = (layer_iota[:, None] == (cells // column_count)[None, :]).astype(jnp.float32)
         return onehot.astype(jnp.bfloat16), rows
 
-    def gather(field, where):
+    def gather(field, where, split=split3):
         onehot, rows = where
         parts = field.shape[0]
         flat = field.reshape(parts * layer_count, column_count)
-        picked = onehot_dot(flat, onehot, ((1,), (1,)))
+        picked = onehot_dot(flat, onehot, ((1,), (1,)), split)
         picked = picked.reshape(parts, layer_count, -1) * rows[None]
         return jnp.sum(picked, axis=1)
 
-    def scatter(values, where):
+    def scatter(values, where, split=split3):
         onehot, rows = where
         parts = values.shape[0]
         spread = (values[:, None, :] * rows[None]).reshape(parts * layer_count, -1)
-        placed = onehot_dot(spread, onehot, ((1,), (0,)))
+        placed = onehot_dot(spread, onehot, ((1,), (0,)), split)
         return placed.reshape(parts, layer_count, column_count)
 
     fault_at = locate(jnp.concatenate([fault_near.reshape(-1), fault_far.reshape(-1)]))
@@ -157,7 +167,7 @@
     def operator(fields, mobile, block):
         count = fields.shape[0]
         scaled = (mobile * fields).reshape(count * 2, layer_count, column_count)
-        picks = gather(scaled, fault_at)
+        picks = gather(scaled, fault_at, split2)
         picks_near = picks[:, :slot_count]
         picks_far = picks[:, slot_count:]
         from_left = shifted(jnp.concatenate([scaled[:, :, -1], picks_near], axis=1), "cells", 1)
@@ -198,7 +208,9 @@
         )
         flux_right = weight_here * (picks_near - from_right[:, layer_count:])
         flux_left = weight_left * (from_left[:, layer_count:] - picks_far)
-        fault_term = scatter(jnp.concatenate([flux_right, -flux_left], axis=1), fault_at)
+        fault_term = scatter(
+            jnp.concatenate([flux_right, -flux_left], axis=1), fault_at, split2
+        )
         laplace = (laplace + fault_term).reshape(count, 2, layer_count, column_count)
         back = jnp.dot(summed[1:] / summed[0], well_onehot.T, precision=highest)
         well_term = scatter(well_index * (values - back), well_at)

time: 93.1 us -> 92.4 us (level)
    convert_element_type x4 -> x2, other arithmetic: 1.05 us -> 0.04 us  [split3(): middle = rest.astype(jnp.bfloat16)]
  transfers between devices with their start and end apart: 8 -> 8, of which waited for: 2 -> 2; matrix products, arithmetic and copies ran while one was open for 28% -> 29% of each run, Pallas kernels for 0% -> 0%
where the time goes in v7:
time: 92.4 us; the launch traced here: 91.5 us
  local copies, waits for them, and re-layouts  21.6 us (23%)
  other arithmetic  20 us (22%)
  starting transfers between devices  17.3 us (19%)
  blocking collectives  12.6 us (14%)
  matrix products  11.5 us (12%)
  waiting for transfers between devices  6.3 us (7%)
  between operations  2.19 us (2%)
    all_to_all x1, blocking collectives, global_sum(): gathered = lax.all_to_all(copies, axes, 0, 0, tiled=True)  12.6 us
    ppermute x4, starting transfers between devices, shifted(): return lax.ppermute(value, axis, pairs)  11.6 us
    dot_general x4, matrix products, onehot_dot(): lax.dot_general(pieces, onehot, (dims, ((), ())), preferred_element_type=...  9.7 us
    all_to_all x1, waiting for transfers between devices, global_sum(): gathered = lax.all_to_all(copies, axes, 0, 0, tiled=True)  5.68 us
    unnamed x103, local copies, waits for them, and re-layouts  3.8 us
    ppermute x3, starting transfers between devices, slab_shift(): lax.ppermute(value, 'slab', [(i, (i + by) % count) for i in range(count)])  3.14 us
    all_to_all x1, starting transfers between devices, global_sum(): gathered = lax.all_to_all(copies, axes, 0, 0, tiled=True)  2.49 us
    select_n x2, other arithmetic, locate(): cells // column_count  2 us
  transfers between devices with their start and end apart: 8, of which 2 were waited for; matrix products, arithmetic and copies ran while one was open for 29% of the time, Pallas kernels for 0%

profile of v7, /device:TPU:0, one launch (start us, length us, event | category | flops | bytes accessed | tf_op | source)
XLA Modules:
  0.0 91.5 jit_solution(7966570307976983944)
XLA Ops:
  0.7 0.9 broadcast_select_fusion.1
  3.2 4.9 %collective-permute-start = (f32[2064]{0:T(1024)S(1)}, f32[2064]{0:T(1024)S(1)}, u32[]{:S(2)}, u32[]{:S(2)}) collective-permute-start(f32[2064]{0:T(1024)S(1)} %pad_maximum_fusion.12), channel_id=1, source_target_pairs={{0,4},{4,8},{8,12},{12,16},{16,20},{20,24},{24,28},{1,5},{5,9},{9,... | collective-permute-start | bytes 24776 | tf_op jit(solution)/shard_map/ppermute | solution.py:13
  8.1 0.9 %broadcast_select_fusion = f32[16,1024]{1,0:T(8,128)S(1)} fusion(f32[16,1024]{1,0:T(8,128)} %param.18, pred[16]{0:T(512)(128)(4,1)S(1)} %compare_and_fusion), kind=kLoop, calls=%fused_computation.167 | loop fusion | flops 16384 | bytes 131088 | tf_op jit(solution)/shard_map/jit(_where)/select_n | solution.py:94
  9.0 1.5 %collective-permute-start.1 = (f32[1024]{0:T(1024)S(1)}, f32[1024]{0:T(1024)S(1)}, u32[]{:S(2)}, u32[]{:S(2)}) collective-permute-start(f32[1024]{0:T(1024)S(1)} %bitcast.405), channel_id=1, source_target_pairs={{0,1},{1,2},{2,3},{4,5},{5,6},{6,7},{8,9},{9,10},{10,11},{12,13},{... | collective-permute-start | bytes 12296 | tf_op jit(solution)/shard_map/ppermute | solution.py:13
  10.5 1.2 %and_select_fusion.2 = s32[128]{0:T(128)} fusion(s32[1,128]{1,0:T(1,128)} %param.23), kind=kLoop, calls=%fused_computation.206 | loop fusion | flops 1408 | bytes 1024 | tf_op jit(solution)/shard_map/jit(remainder)/select_n | solution.py:115
  12.4 1.0 %fusion.97 = (f32[1,2,16,1024]{3,2,1,0:T(8,128)S(1)}, f32[1,2,16,1024]{3,2,1,0:T(8,128)S(1)}) fusion(f32[2,2,16,1024]{3,2,1,0:T(8,128)} %param.15), kind=kLoop, calls=%fused_computation.229 | loop fusion | bytes 524288 | tf_op jit(solution)/shard_map/slice | solution.py:143
  13.5 1.3 %add_select_fusion = (s32[4096]{0:T(1024)S(1)}, s32[4096]{0:T(1024)}) fusion(s32[2048]{0:T(1024)} %bitcast.402, s32[2048]{0:T(1024)} %bitcast.403), kind=kLoop, calls=%fused_computation.176 | loop fusion | flops 81920 | bytes 49152 | tf_op jit(solution)/shard_map/jit(floor_divide)/jit(_where)/select_n | solution.py:116
  15.6 0.7 fusion.62
  18.2 0.8 fusion.22
  19.0 0.8 slice_reduce_fusion.1
  20.0 1.0 %fusion.95 = (f32[6,15,1024]{2,1,0:T(8,128)}, f32[6,15,1024]{2,1,0:T(8,128)}) fusion(f32[6,16,1024]{2,1,0:T(8,128)S(1)} %bitcast.343), kind=kLoop, calls=%fused_computation.227 | loop fusion | bytes 1474560 | tf_op jit(solution)/shard_map/slice | solution.py:201
  24.0 1.3 %reshape.486 = f32[64]{0:T(128)} reshape(f32[4,16]{1,0:T(4,128)} %pad_maximum_fusion.13) | data formatting | bytes 512 | tf_op jit(solution)/shard_map/reshape | solution.py:188
  25.4 2.0 %collective-permute-start.6 = (f32[4,16]{1,0:T(4,128)}, f32[4,16]{1,0:T(4,128)}, u32[]{:S(2)}, u32[]{:S(2)}) collective-permute-start(f32[4,16]{1,0:T(4,128)} %pad_maximum_fusion.13), channel_id=1, source_target_pairs={{0,2},{1,3},{2,0},{3,1},{4,6},{5,7},{6,4},{7,5},{8,10},{9,11},{10,... | collective-permute-start | bytes 776 | tf_op jit(solution)/shard_map/ppermute | solution.py:165
  27.3 4.9 %fusion.1 = f32[192,4096]{1,0:T(8,128)S(1)} fusion(s32[4096]{0:T(1024)} %get-tuple-element.69, bf16[96,1024]{1,0:T(8,128)(2,1)} %get-tuple-element.22, bf16[96,1024]{1,0:T(8,128)(2,1)} %get-tuple-element.23), kind=kOutput, calls=%fused_computation.2 | convolution fusion | flops 1615593472 | bytes 3555328 | tf_op jit(solution)/shard_map/dot_general | solution.py:58
  34.2 4.0 %collective-permute-start.3 = (f32[6,2064]{1,0:T(8,128)}, f32[6,2064]{1,0:T(8,128)}, u32[]{:S(2)}, u32[]{:S(2)}) collective-permute-start(f32[6,2064]{1,0:T(8,128)} %pad_maximum_fusion.7), channel_id=1, source_target_pairs={{0,4},{4,8},{8,12},{12,16},{16,20},{20,24},{24,28},{1,5},{5,9},{9,... | collective-permute-start | bytes 148616 | tf_op jit(solution)/shard_map/ppermute | solution.py:13
  38.9 1.2 %collective-permute-start.4 = (f32[6208]{0:T(1024)}, f32[6208]{0:T(1024)}, u32[]{:S(2)}, u32[]{:S(2)}) collective-permute-start(f32[6208]{0:T(1024)} %get-tuple-element.71), channel_id=1, source_target_pairs={{0,3},{1,0},{2,1},{3,2},{4,7},{5,4},{6,5},{7,6},{8,11},{9,8},{10,9... | collective-permute-start | bytes 74504 | tf_op jit(solution)/shard_map/ppermute | solution.py:165
  40.8 1.3 %collective-permute-start.2 = (f32[6,2064]{1,0:T(8,128)}, f32[6,2064]{1,0:T(8,128)}, u32[]{:S(2)}, u32[]{:S(2)}) collective-permute-start(f32[6,2064]{1,0:T(8,128)} %pad_maximum_fusion.6), channel_id=1, source_target_pairs={{4,0},{8,4},{12,8},{16,12},{20,16},{24,20},{28,24},{5,1},{9,5},{13... | collective-permute-start | bytes 148616 | tf_op jit(solution)/shard_map/ppermute | solution.py:13
  44.5 1.3 %reshape.488 = f32[4,16]{1,0:T(4,128)} reshape(f32[64]{0:T(128)} %slice.450) | data formatting | bytes 512 | tf_op jit(solution)/shard_map/reshape | solution.py:192
  45.9 1.2 %slice.451 = f32[64]{0:T(128)} slice(f32[6208]{0:T(1024)} %collective-permute-done.4), slice={[6144:6208]} | slice | bytes 512 | tf_op jit(solution)/shard_map/slice | solution.py:194
  47.1 1.3 %reshape.489 = f32[4,16]{1,0:T(4,128)} reshape(f32[64]{0:T(128)} %slice.451) | data formatting | bytes 512 | tf_op jit(solution)/shard_map/reshape | solution.py:194
  48.4 0.8 add_add_fusion.1
  49.2 0.9 fusion.8
  50.2 1.0 %fusion.9 = f32[144,1024]{1,0:T(8,128)S(1)} fusion(s32[128]{0:T(128)} %and_select_fusion.2, bf16[48,128]{1,0:T(8,128)(2,1)S(1)} %get-tuple-element.67, bf16[48,128]{1,0:T(8,128)(2,1)S(1)} %get-tuple-element.66, bf16[48,128]{1,0:T(8,128)(2,1)S(1)} %bitcast_convert_fusion.3), kind=kOutput, calls=%fused_computation.18 | convolution fusion | flops 37990400 | bytes 627200 | tf_op jit(solution)/shard_map/dot_general | solution.py:58
  51.9 1.3 %slice.440 = f32[6144]{0:T(1024)} slice(f32[6208]{0:T(1024)} %collective-permute-done.4), slice={[0:6144]} | slice | bytes 49152 | tf_op jit(solution)/shard_map/slice | solution.py:198
  53.8 1.0 %fusion.49 = (f32[6,2048]{1,0:T(8,128)S(1)}, f32[6,2048]{1,0:T(8,128)S(1)}) fusion(f32[6,2064]{1,0:T(8,128)} %collective-permute-done.2, f32[2048]{0:T(1024)S(1)} %bitcast.381, f32[6,4096]{1,0:T(8,128)S(1)} %copy-done.4, f32[6,2064]{1,0:T(8,128)} %collective-permute-done.3, f32[2048]{0:T(1024)S(1)} %copy-done.28), kind=kLoop, calls=%fused_computation.113 | loop fusion | flops 61440 | bytes 311296 | tf_op jit(solution)/shard_map/mul | solution.py:209
  55.8 3.4 %fusion = f32[192,1024]{1,0:T(8,128)S(1)} fusion(s32[4096]{0:T(1024)S(1)} %copy-done.31, bf16[96,4096]{1,0:T(8,128)(2,1)S(1)} %get-tuple-element.20, bf16[96,4096]{1,0:T(8,128)(2,1)S(1)} %get-tuple-element.21), kind=kOutput, calls=%fused_computation.1 | convolution fusion | flops 1617952768 | bytes 2375680 | tf_op jit(solution)/shard_map/dot_general | solution.py:58
  59.2 0.8 slice_add_fusion.1
  62.8 1.6 %fusion.18 = f32[3,2,16,1024]{3,2,1,0:T(8,128)S(1)} fusion(f32[3,2,16,1024]{3,2,1,0:T(8,128)} %bitcast.350, f32[3,2,16,1024]{3,2,1,0:T(8,128)S(1)} %get-tuple-element.46, f32[3,2,16,1]{3,2,1,0:T(8,128)} %concatenate.149, f32[3,2,16,1023]{3,2,1,0:T(8,128)S(1)} %bitcast.347, f32[3,2,16,1023]{3,2,1,0:T(8,128)S(1)} %bitcast.346, ...), kind=kLoop, calls=%fused_computation.35 | loop fusion | flops 1572864 | bytes 3014656 | tf_op jit(solution)/shard_map/add | solution.py:214
  65.4 12.6 %all_to_all.12 = f32[32,1,10]{2,1,0:T(1,128)S(1)} all-to-all(f32[32,1,10]{2,1,0:T(1,128)S(1)} %broadcast_in_dim.29), channel_id=1, replica_groups=mesh['cells'=8,'slab'=4] {'cells','slab'}, dimensions={0} | all-to-all | bytes 2560 | tf_op jit(solution)/shard_map/all_to_all | solution.py:36
  79.2 2.5 %all-to-all-start.1 = ((f32[32,1,3]{2,1,0:T(1,128)}), f32[32,1,3]{2,1,0:T(1,128)S(1)}, u32[]{:S(2)}, u32[]{:S(2)}) async-start(f32[32,1,3]{2,1,0:T(1,128)} %broadcast_in_dim.31), calls=%async_computation.1 | async-start | bytes 32768 | tf_op jit(solution)/shard_map/all_to_all | solution.py:36
  83.2 5.7 %all-to-all-done.1 = f32[32,1,3]{2,1,0:T(1,128)S(1)} async-done(((f32[32,1,3]{2,1,0:T(1,128)}), f32[32,1,3]{2,1,0:T(1,128)S(1)}, u32[]{:S(2)}, u32[]{:S(2)}) %all-to-all-start.1) | async-done | bytes 416 | tf_op jit(solution)/shard_map/all_to_all | solution.py:36
  89.5 1.4 %maximum_sqrt_fusion = f32[4]{0:T(128)S(1)} fusion(f32[1]{0:T(128)} %slice.413, f32[1]{0:T(128)} %slice.412, f32[2]{0:T(128)S(1)} %bitcast.406), kind=kLoop, calls=%fused_computation.215 | loop fusion | flops 8 | bytes 32 | tf_op jit(solution)/shard_map/sqrt | solution.py:293
  (183 shorter events, 22.7 us)
Async XLA Ops:
  0.6 14.9 %copy-start = (f32[2,4,16,1024]{3,2,1,0:T(8,128)S(1)}, f32[2,4,16,1024]{3,2,1,0:T(8,128)}, u32[]{:S(2)}) copy-start(f32[2,4,16,1024]{3,2,1,0:T(8,128)} %param.14) | copy-start | bytes 1572868
  0.6 15.0 %copy-start.41 = (s32[1,128]{1,0:T(1,128)S(1)}, s32[1,128]{1,0:T(1,128)}, u32[]{:S(2)}) copy-start(s32[1,128]{1,0:T(1,128)} %param.24) | copy-start | bytes 1540
  0.7 15.0 %copy-start.43 = (f32[1,128]{1,0:T(1,128)S(1)}, f32[1,128]{1,0:T(1,128)}, u32[]{:S(2)}) copy-start(f32[1,128]{1,0:T(1,128)} %param.25) | copy-start | bytes 1540
  1.6 15.0 %copy-start.12 = (f32[16,1024]{1,0:T(8,128)}, f32[16,1024]{1,0:T(8,128)S(1)}, u32[]{:S(2)}) copy-start(f32[16,1024]{1,0:T(8,128)S(1)} %broadcast_select_fusion.1) | copy-start | bytes 196612
  3.2 13.3 %collective-permute-start = (f32[2064]{0:T(1024)S(1)}, f32[2064]{0:T(1024)S(1)}, u32[]{:S(2)}, u32[]{:S(2)}) collective-permute-start(f32[2064]{0:T(1024)S(1)} %pad_maximum_fusion.12), channel_id=1, source_target_pairs={{0,4},{4,8},{8,12},{12,16},{16,20},{20,24},{24,28},{1,5},{5,9},{9,... | collective-permute-start | bytes 24776 | tf_op jit(solution)/shard_map/ppermute | solution.py:13
  9.0 7.6 %copy-start.14 = (f32[16,1024]{1,0:T(8,128)}, f32[16,1024]{1,0:T(8,128)S(1)}, u32[]{:S(2)}) copy-start(f32[16,1024]{1,0:T(8,128)S(1)} %broadcast_select_fusion) | copy-start | bytes 196612
  9.0 7.6 %collective-permute-start.1 = (f32[1024]{0:T(1024)S(1)}, f32[1024]{0:T(1024)S(1)}, u32[]{:S(2)}, u32[]{:S(2)}) collective-permute-start(f32[1024]{0:T(1024)S(1)} %bitcast.405), channel_id=1, source_target_pairs={{0,1},{1,2},{2,3},{4,5},{5,6},{6,7},{8,9},{9,10},{10,11},{12,13},{... | collective-permute-start | bytes 12296 | tf_op jit(solution)/shard_map/ppermute | solution.py:13
  12.4 4.2 %copy-start.22 = (f32[16,1024]{1,0:T(8,128)S(1)}, f32[16,1024]{1,0:T(8,128)}, u32[]{:S(2)}) copy-start(f32[16,1024]{1,0:T(8,128)} %param.17) | copy-start | bytes 196612
  25.4 23.1 %collective-permute-start.6 = (f32[4,16]{1,0:T(4,128)}, f32[4,16]{1,0:T(4,128)}, u32[]{:S(2)}, u32[]{:S(2)}) collective-permute-start(f32[4,16]{1,0:T(4,128)} %pad_maximum_fusion.13), channel_id=1, source_target_pairs={{0,2},{1,3},{2,0},{3,1},{4,6},{5,7},{6,4},{7,5},{8,10},{9,11},{10,... | collective-permute-start | bytes 776 | tf_op jit(solution)/shard_map/ppermute | solution.py:165
  32.5 5.8 %copy-start.26 = (f32[6,1,1024]{2,1,0:T(1,128)S(1)}, f32[6,1,1024]{2,1,0:T(1,128)}, u32[]{:S(2)}) copy-start(f32[6,1,1024]{2,1,0:T(1,128)} %get-tuple-element.41) | copy-start | bytes 73732
  32.5 5.8 %copy-start.27 = (f32[6,1,1024]{2,1,0:T(1,128)S(1)}, f32[6,1,1024]{2,1,0:T(1,128)}, u32[]{:S(2)}) copy-start(f32[6,1,1024]{2,1,0:T(1,128)} %get-tuple-element.42) | copy-start | bytes 73732
  32.5 5.8 %copy-start.37 = (f32[64]{0:T(128)S(1)}, f32[64]{0:T(128)}, u32[]{:S(2)}) copy-start(f32[64]{0:T(128)} %reshape.486) | copy-start | bytes 772
  32.5 7.6 %copy-start.32 = (f32[6,16]{1,0:T(8,128)S(1)}, f32[6,16]{1,0:T(8,128)}, u32[]{:S(2)}) copy-start(f32[6,16]{1,0:T(8,128)} %get-tuple-element.4) | copy-start | bytes 1156
  32.5 9.6 %copy-start.36 = (f32[2064]{0:T(1024)S(1)}, f32[2064]{0:T(1024)}, u32[]{:S(2)}) copy-start(f32[2064]{0:T(1024)} %copy-done.35) | copy-start | bytes 24772
  34.2 19.6 %collective-permute-start.3 = (f32[6,2064]{1,0:T(8,128)}, f32[6,2064]{1,0:T(8,128)}, u32[]{:S(2)}, u32[]{:S(2)}) collective-permute-start(f32[6,2064]{1,0:T(8,128)} %pad_maximum_fusion.7), channel_id=1, source_target_pairs={{0,4},{4,8},{8,12},{12,16},{16,20},{20,24},{24,28},{1,5},{5,9},{9,... | collective-permute-start | bytes 148616 | tf_op jit(solution)/shard_map/ppermute | solution.py:13
  38.9 7.0 %collective-permute-start.4 = (f32[6208]{0:T(1024)}, f32[6208]{0:T(1024)}, u32[]{:S(2)}, u32[]{:S(2)}) collective-permute-start(f32[6208]{0:T(1024)} %get-tuple-element.71), channel_id=1, source_target_pairs={{0,3},{1,0},{2,1},{3,2},{4,7},{5,4},{6,5},{7,6},{8,11},{9,8},{10,9... | collective-permute-start | bytes 74504 | tf_op jit(solution)/shard_map/ppermute | solution.py:165
  40.1 3.3 %collective-permute-start.5 = (f32[6208]{0:T(1024)S(1)}, f32[6208]{0:T(1024)S(1)}, u32[]{:S(2)}, u32[]{:S(2)}) collective-permute-start(f32[6208]{0:T(1024)S(1)} %get-tuple-element.70), channel_id=1, source_target_pairs={{0,1},{1,2},{2,3},{3,0},{4,5},{5,6},{6,7},{7,4},{8,9},{9,10},{10,1... | collective-permute-start | bytes 74504 | tf_op jit(solution)/shard_map/ppermute | solution.py:165
  40.8 13.0 %collective-permute-start.2 = (f32[6,2064]{1,0:T(8,128)}, f32[6,2064]{1,0:T(8,128)}, u32[]{:S(2)}, u32[]{:S(2)}) collective-permute-start(f32[6,2064]{1,0:T(8,128)} %pad_maximum_fusion.6), channel_id=1, source_target_pairs={{4,0},{8,4},{12,8},{16,12},{20,16},{24,20},{28,24},{5,1},{9,5},{13... | collective-permute-start | bytes 148616 | tf_op jit(solution)/shard_map/ppermute | solution.py:13
  48.4 4.8 %copy-start.30 = (f32[6208]{0:T(1024)S(1)}, f32[6208]{0:T(1024)}, u32[]{:S(2)}) copy-start(f32[6208]{0:T(1024)} %copy-done.29) | copy-start | bytes 74500
  48.4 5.4 %copy-start.4 = (f32[6,4096]{1,0:T(8,128)S(1)}, f32[6,4096]{1,0:T(8,128)}, u32[]{:S(2)}) copy-start(f32[6,4096]{1,0:T(8,128)} %copy-done.3) | copy-start | bytes 294916
  48.4 5.4 %copy-start.28 = (f32[2048]{0:T(1024)S(1)}, f32[2048]{0:T(1024)}, u32[]{:S(2)}) copy-start(f32[2048]{0:T(1024)} %slice.445) | copy-start | bytes 24580
  55.7 7.0 %copy-start.13 = (f32[16,1024]{1,0:T(8,128)S(1)}, f32[16,1024]{1,0:T(8,128)}, u32[]{:S(2)}) copy-start(f32[16,1024]{1,0:T(8,128)} %copy-done.12) | copy-start | bytes 196612
  55.8 7.0 %copy-start.15 = (f32[16,1024]{1,0:T(8,128)S(1)}, f32[16,1024]{1,0:T(8,128)}, u32[]{:S(2)}) copy-start(f32[16,1024]{1,0:T(8,128)} %copy-done.14) | copy-start | bytes 196612
  55.8 7.0 %copy-start.20 = (f32[16,1024]{1,0:T(8,128)S(1)}, f32[16,1024]{1,0:T(8,128)}, u32[]{:S(2)}) copy-start(f32[16,1024]{1,0:T(8,128)} %get-tuple-element.28) | copy-start | bytes 196612
  55.8 7.0 %copy-start.21 = (f32[16,1024]{1,0:T(8,128)S(1)}, f32[16,1024]{1,0:T(8,128)}, u32[]{:S(2)}) copy-start(f32[16,1024]{1,0:T(8,128)} %get-tuple-element.29) | copy-start | bytes 196612
  64.4 13.8 %copy-start.8 = (f32[16,1024]{1,0:T(8,128)S(1)}, f32[16,1024]{1,0:T(8,128)}, u32[]{:S(2)}) copy-start(f32[16,1024]{1,0:T(8,128)} %copy-done.7) | copy-start | bytes 196612
  64.4 13.8 %copy-start.10 = (f32[16,1024]{1,0:T(8,128)S(1)}, f32[16,1024]{1,0:T(8,128)}, u32[]{:S(2)}) copy-start(f32[16,1024]{1,0:T(8,128)} %copy-done.9) | copy-start | bytes 196612
  64.4 13.8 %copy-start.25 = (f32[2,2,16,1024]{3,2,1,0:T(8,128)S(1)}, f32[2,2,16,1024]{3,2,1,0:T(8,128)}, u32[]{:S(2)}) copy-start(f32[2,2,16,1024]{3,2,1,0:T(8,128)} %param.16) | copy-start | bytes 786436
  64.6 17.1 %copy-start.6 = (f32[16,1024]{1,0:T(8,128)S(1)}, f32[16,1024]{1,0:T(8,128)}, u32[]{:S(2)}) copy-start(f32[16,1024]{1,0:T(8,128)} %copy-done.5) | copy-start | bytes 196612
  64.6 17.1 %copy-start.17 = (f32[16,1024]{1,0:T(8,128)S(1)}, f32[16,1024]{1,0:T(8,128)}, u32[]{:S(2)}) copy-start(f32[16,1024]{1,0:T(8,128)} %copy-done.16) | copy-start | bytes 196612
  64.6 17.1 %copy-start.19 = (f32[16,1024]{1,0:T(8,128)S(1)}, f32[16,1024]{1,0:T(8,128)}, u32[]{:S(2)}) copy-start(f32[16,1024]{1,0:T(8,128)} %copy-done.18) | copy-start | bytes 196612
  79.2 9.6 %all-to-all-start.1 = ((f32[32,1,3]{2,1,0:T(1,128)}), f32[32,1,3]{2,1,0:T(1,128)S(1)}, u32[]{:S(2)}, u32[]{:S(2)}) async-start(f32[32,1,3]{2,1,0:T(1,128)} %broadcast_in_dim.31), calls=%async_computation.1 | async-start | bytes 32768 | tf_op jit(solution)/shard_map/all_to_all | solution.py:36
  (21 other events, 33.2 us)

commit v8 on v7

--- a/solution.py
+++ b/solution.py
@@ -114,7 +114,7 @@
         cells = cells.reshape(-1)
         onehot = (cells % column_count)[:, None] == column_iota[None, :]
         rows = (layer_iota[:, None] == (cells // column_count)[None, :]).astype(jnp.float32)
-        return onehot.astype(jnp.bfloat16), rows
+        return onehot.astype(jnp.float8_e4m3fn), rows
 
     def gather(field, where, split=split3):
         onehot, rows = where

time: 92.4 us -> 92.4 us (level)
  no operation moved by 1% of the time
where the time goes in v8:
time: 92.4 us; the launch traced here: 91.5 us
  local copies, waits for them, and re-layouts  21.6 us (23%)
  other arithmetic  20 us (22%)
  starting transfers between devices  17.3 us (19%)
  blocking collectives  12.6 us (14%)
  matrix products  11.5 us (12%)
  waiting for transfers between devices  6.3 us (7%)
  between operations  2.19 us (2%)
    all_to_all x1, blocking collectives, global_sum(): gathered = lax.all_to_all(copies, axes, 0, 0, tiled=True)  12.6 us
    ppermute x4, starting transfers between devices, shifted(): return lax.ppermute(value, axis, pairs)  11.6 us
    dot_general x4, matrix products, onehot_dot(): lax.dot_general(pieces, onehot, (dims, ((), ())), preferred_element_type=...  9.7 us
    all_to_all x1, waiting for transfers between devices, global_sum(): gathered = lax.all_to_all(copies, axes, 0, 0, tiled=True)  5.68 us
    unnamed x103, local copies, waits for them, and re-layouts  3.8 us
    ppermute x3, starting transfers between devices, slab_shift(): lax.ppermute(value, 'slab', [(i, (i + by) % count) for i in range(count)])  3.14 us
    all_to_all x1, starting transfers between devices, global_sum(): gathered = lax.all_to_all(copies, axes, 0, 0, tiled=True)  2.49 us
    select_n x2, other arithmetic, locate(): cells // column_count  2 us
  transfers between devices with their start and end apart: 8, of which 2 were waited for; matrix products, arithmetic and copies ran while one was open for 29% of the time, Pallas kernels for 0%

profile of v8, /device:TPU:0, one launch (start us, length us, event | category | flops | bytes accessed | tf_op | source)
XLA Modules:
  0.0 91.5 jit_solution(7966570307976983944)
XLA Ops:
  0.7 0.9 broadcast_select_fusion.1
  3.2 4.9 %collective-permute-start = (f32[2064]{0:T(1024)S(1)}, f32[2064]{0:T(1024)S(1)}, u32[]{:S(2)}, u32[]{:S(2)}) collective-permute-start(f32[2064]{0:T(1024)S(1)} %pad_maximum_fusion.12), channel_id=1, source_target_pairs={{0,4},{4,8},{8,12},{12,16},{16,20},{20,24},{24,28},{1,5},{5,9},{9,... | collective-permute-start | bytes 24776 | tf_op jit(solution)/shard_map/ppermute | solution.py:13
  8.1 0.9 %broadcast_select_fusion = f32[16,1024]{1,0:T(8,128)S(1)} fusion(f32[16,1024]{1,0:T(8,128)} %param.18, pred[16]{0:T(512)(128)(4,1)S(1)} %compare_and_fusion), kind=kLoop, calls=%fused_computation.167 | loop fusion | flops 16384 | bytes 131088 | tf_op jit(solution)/shard_map/jit(_where)/select_n | solution.py:94
  9.0 1.5 %collective-permute-start.1 = (f32[1024]{0:T(1024)S(1)}, f32[1024]{0:T(1024)S(1)}, u32[]{:S(2)}, u32[]{:S(2)}) collective-permute-start(f32[1024]{0:T(1024)S(1)} %bitcast.405), channel_id=1, source_target_pairs={{0,1},{1,2},{2,3},{4,5},{5,6},{6,7},{8,9},{9,10},{10,11},{12,13},{... | collective-permute-start | bytes 12296 | tf_op jit(solution)/shard_map/ppermute | solution.py:13
  10.5 1.2 %and_select_fusion.2 = s32[128]{0:T(128)} fusion(s32[1,128]{1,0:T(1,128)} %param.23), kind=kLoop, calls=%fused_computation.206 | loop fusion | flops 1408 | bytes 1024 | tf_op jit(solution)/shard_map/jit(remainder)/select_n | solution.py:115
  12.4 1.0 %fusion.97 = (f32[1,2,16,1024]{3,2,1,0:T(8,128)S(1)}, f32[1,2,16,1024]{3,2,1,0:T(8,128)S(1)}) fusion(f32[2,2,16,1024]{3,2,1,0:T(8,128)} %param.15), kind=kLoop, calls=%fused_computation.229 | loop fusion | bytes 524288 | tf_op jit(solution)/shard_map/slice | solution.py:143
  13.5 1.3 %add_select_fusion = (s32[4096]{0:T(1024)S(1)}, s32[4096]{0:T(1024)}) fusion(s32[2048]{0:T(1024)} %bitcast.402, s32[2048]{0:T(1024)} %bitcast.403), kind=kLoop, calls=%fused_computation.176 | loop fusion | flops 81920 | bytes 49152 | tf_op jit(solution)/shard_map/jit(floor_divide)/jit(_where)/select_n | solution.py:116
  15.6 0.7 fusion.62
  18.2 0.8 fusion.22
  19.0 0.8 slice_reduce_fusion.1
  20.0 1.0 %fusion.95 = (f32[6,15,1024]{2,1,0:T(8,128)}, f32[6,15,1024]{2,1,0:T(8,128)}) fusion(f32[6,16,1024]{2,1,0:T(8,128)S(1)} %bitcast.343), kind=kLoop, calls=%fused_computation.227 | loop fusion | bytes 1474560 | tf_op jit(solution)/shard_map/slice | solution.py:201
  24.0 1.3 %reshape.486 = f32[64]{0:T(128)} reshape(f32[4,16]{1,0:T(4,128)} %pad_maximum_fusion.13) | data formatting | bytes 512 | tf_op jit(solution)/shard_map/reshape | solution.py:188
  25.4 2.0 %collective-permute-start.6 = (f32[4,16]{1,0:T(4,128)}, f32[4,16]{1,0:T(4,128)}, u32[]{:S(2)}, u32[]{:S(2)}) collective-permute-start(f32[4,16]{1,0:T(4,128)} %pad_maximum_fusion.13), channel_id=1, source_target_pairs={{0,2},{1,3},{2,0},{3,1},{4,6},{5,7},{6,4},{7,5},{8,10},{9,11},{10,... | collective-permute-start | bytes 776 | tf_op jit(solution)/shard_map/ppermute | solution.py:165
  27.3 4.9 %fusion.1 = f32[192,4096]{1,0:T(8,128)S(1)} fusion(s32[4096]{0:T(1024)} %get-tuple-element.69, bf16[96,1024]{1,0:T(8,128)(2,1)} %get-tuple-element.22, bf16[96,1024]{1,0:T(8,128)(2,1)} %get-tuple-element.23), kind=kOutput, calls=%fused_computation.2 | convolution fusion | flops 1615593472 | bytes 3555328 | tf_op jit(solution)/shard_map/dot_general | solution.py:58
  34.2 4.0 %collective-permute-start.3 = (f32[6,2064]{1,0:T(8,128)}, f32[6,2064]{1,0:T(8,128)}, u32[]{:S(2)}, u32[]{:S(2)}) collective-permute-start(f32[6,2064]{1,0:T(8,128)} %pad_maximum_fusion.7), channel_id=1, source_target_pairs={{0,4},{4,8},{8,12},{12,16},{16,20},{20,24},{24,28},{1,5},{5,9},{9,... | collective-permute-start | bytes 148616 | tf_op jit(solution)/shard_map/ppermute | solution.py:13
  38.9 1.2 %collective-permute-start.4 = (f32[6208]{0:T(1024)}, f32[6208]{0:T(1024)}, u32[]{:S(2)}, u32[]{:S(2)}) collective-permute-start(f32[6208]{0:T(1024)} %get-tuple-element.71), channel_id=1, source_target_pairs={{0,3},{1,0},{2,1},{3,2},{4,7},{5,4},{6,5},{7,6},{8,11},{9,8},{10,9... | collective-permute-start | bytes 74504 | tf_op jit(solution)/shard_map/ppermute | solution.py:165
  40.8 1.3 %collective-permute-start.2 = (f32[6,2064]{1,0:T(8,128)}, f32[6,2064]{1,0:T(8,128)}, u32[]{:S(2)}, u32[]{:S(2)}) collective-permute-start(f32[6,2064]{1,0:T(8,128)} %pad_maximum_fusion.6), channel_id=1, source_target_pairs={{4,0},{8,4},{12,8},{16,12},{20,16},{24,20},{28,24},{5,1},{9,5},{13... | collective-permute-start | bytes 148616 | tf_op jit(solution)/shard_map/ppermute | solution.py:13
  44.5 1.3 %reshape.488 = f32[4,16]{1,0:T(4,128)} reshape(f32[64]{0:T(128)} %slice.450) | data formatting | bytes 512 | tf_op jit(solution)/shard_map/reshape | solution.py:192
  45.9 1.2 %slice.451 = f32[64]{0:T(128)} slice(f32[6208]{0:T(1024)} %collective-permute-done.4), slice={[6144:6208]} | slice | bytes 512 | tf_op jit(solution)/shard_map/slice | solution.py:194
  47.1 1.3 %reshape.489 = f32[4,16]{1,0:T(4,128)} reshape(f32[64]{0:T(128)} %slice.451) | data formatting | bytes 512 | tf_op jit(solution)/shard_map/reshape | solution.py:194
  48.4 0.8 add_add_fusion.1
  49.2 0.9 fusion.8
  50.2 1.0 %fusion.9 = f32[144,1024]{1,0:T(8,128)S(1)} fusion(s32[128]{0:T(128)} %and_select_fusion.2, bf16[48,128]{1,0:T(8,128)(2,1)S(1)} %get-tuple-element.67, bf16[48,128]{1,0:T(8,128)(2,1)S(1)} %get-tuple-element.66, bf16[48,128]{1,0:T(8,128)(2,1)S(1)} %bitcast_convert_fusion.3), kind=kOutput, calls=%fused_computation.18 | convolution fusion | flops 37990400 | bytes 627200 | tf_op jit(solution)/shard_map/dot_general | solution.py:58
  51.9 1.3 %slice.440 = f32[6144]{0:T(1024)} slice(f32[6208]{0:T(1024)} %collective-permute-done.4), slice={[0:6144]} | slice | bytes 49152 | tf_op jit(solution)/shard_map/slice | solution.py:198
  53.8 1.0 %fusion.49 = (f32[6,2048]{1,0:T(8,128)S(1)}, f32[6,2048]{1,0:T(8,128)S(1)}) fusion(f32[6,2064]{1,0:T(8,128)} %collective-permute-done.2, f32[2048]{0:T(1024)S(1)} %bitcast.381, f32[6,4096]{1,0:T(8,128)S(1)} %copy-done.4, f32[6,2064]{1,0:T(8,128)} %collective-permute-done.3, f32[2048]{0:T(1024)S(1)} %copy-done.28), kind=kLoop, calls=%fused_computation.113 | loop fusion | flops 61440 | bytes 311296 | tf_op jit(solution)/shard_map/mul | solution.py:209
  55.8 3.4 %fusion = f32[192,1024]{1,0:T(8,128)S(1)} fusion(s32[4096]{0:T(1024)S(1)} %copy-done.31, bf16[96,4096]{1,0:T(8,128)(2,1)S(1)} %get-tuple-element.20, bf16[96,4096]{1,0:T(8,128)(2,1)S(1)} %get-tuple-element.21), kind=kOutput, calls=%fused_computation.1 | convolution fusion | flops 1617952768 | bytes 2375680 | tf_op jit(solution)/shard_map/dot_general | solution.py:58
  59.2 0.8 slice_add_fusion.1
  62.8 1.6 %fusion.18 = f32[3,2,16,1024]{3,2,1,0:T(8,128)S(1)} fusion(f32[3,2,16,1024]{3,2,1,0:T(8,128)} %bitcast.350, f32[3,2,16,1024]{3,2,1,0:T(8,128)S(1)} %get-tuple-element.46, f32[3,2,16,1]{3,2,1,0:T(8,128)} %concatenate.149, f32[3,2,16,1023]{3,2,1,0:T(8,128)S(1)} %bitcast.347, f32[3,2,16,1023]{3,2,1,0:T(8,128)S(1)} %bitcast.346, ...), kind=kLoop, calls=%fused_computation.35 | loop fusion | flops 1572864 | bytes 3014656 | tf_op jit(solution)/shard_map/add | solution.py:214
  65.4 12.6 %all_to_all.12 = f32[32,1,10]{2,1,0:T(1,128)S(1)} all-to-all(f32[32,1,10]{2,1,0:T(1,128)S(1)} %broadcast_in_dim.29), channel_id=1, replica_groups=mesh['cells'=8,'slab'=4] {'cells','slab'}, dimensions={0} | all-to-all | bytes 2560 | tf_op jit(solution)/shard_map/all_to_all | solution.py:36
  79.2 2.5 %all-to-all-start.1 = ((f32[32,1,3]{2,1,0:T(1,128)}), f32[32,1,3]{2,1,0:T(1,128)S(1)}, u32[]{:S(2)}, u32[]{:S(2)}) async-start(f32[32,1,3]{2,1,0:T(1,128)} %broadcast_in_dim.31), calls=%async_computation.1 | async-start | bytes 32768 | tf_op jit(solution)/shard_map/all_to_all | solution.py:36
  83.2 5.7 %all-to-all-done.1 = f32[32,1,3]{2,1,0:T(1,128)S(1)} async-done(((f32[32,1,3]{2,1,0:T(1,128)}), f32[32,1,3]{2,1,0:T(1,128)S(1)}, u32[]{:S(2)}, u32[]{:S(2)}) %all-to-all-start.1) | async-done | bytes 416 | tf_op jit(solution)/shard_map/all_to_all | solution.py:36
  89.5 1.4 %maximum_sqrt_fusion = f32[4]{0:T(128)S(1)} fusion(f32[1]{0:T(128)} %slice.413, f32[1]{0:T(128)} %slice.412, f32[2]{0:T(128)S(1)} %bitcast.406), kind=kLoop, calls=%fused_computation.215 | loop fusion | flops 8 | bytes 32 | tf_op jit(solution)/shard_map/sqrt | solution.py:293
  (183 shorter events, 22.7 us)
Async XLA Ops:
  0.6 14.9 %copy-start = (f32[2,4,16,1024]{3,2,1,0:T(8,128)S(1)}, f32[2,4,16,1024]{3,2,1,0:T(8,128)}, u32[]{:S(2)}) copy-start(f32[2,4,16,1024]{3,2,1,0:T(8,128)} %param.14) | copy-start | bytes 1572868
  0.6 15.0 %copy-start.41 = (s32[1,128]{1,0:T(1,128)S(1)}, s32[1,128]{1,0:T(1,128)}, u32[]{:S(2)}) copy-start(s32[1,128]{1,0:T(1,128)} %param.24) | copy-start | bytes 1540
  0.7 15.0 %copy-start.43 = (f32[1,128]{1,0:T(1,128)S(1)}, f32[1,128]{1,0:T(1,128)}, u32[]{:S(2)}) copy-start(f32[1,128]{1,0:T(1,128)} %param.25) | copy-start | bytes 1540
  1.6 15.0 %copy-start.12 = (f32[16,1024]{1,0:T(8,128)}, f32[16,1024]{1,0:T(8,128)S(1)}, u32[]{:S(2)}) copy-start(f32[16,1024]{1,0:T(8,128)S(1)} %broadcast_select_fusion.1) | copy-start | bytes 196612
  3.2 13.3 %collective-permute-start = (f32[2064]{0:T(1024)S(1)}, f32[2064]{0:T(1024)S(1)}, u32[]{:S(2)}, u32[]{:S(2)}) collective-permute-start(f32[2064]{0:T(1024)S(1)} %pad_maximum_fusion.12), channel_id=1, source_target_pairs={{0,4},{4,8},{8,12},{12,16},{16,20},{20,24},{24,28},{1,5},{5,9},{9,... | collective-permute-start | bytes 24776 | tf_op jit(solution)/shard_map/ppermute | solution.py:13
  9.0 7.6 %copy-start.14 = (f32[16,1024]{1,0:T(8,128)}, f32[16,1024]{1,0:T(8,128)S(1)}, u32[]{:S(2)}) copy-start(f32[16,1024]{1,0:T(8,128)S(1)} %broadcast_select_fusion) | copy-start | bytes 196612
  9.0 7.6 %collective-permute-start.1 = (f32[1024]{0:T(1024)S(1)}, f32[1024]{0:T(1024)S(1)}, u32[]{:S(2)}, u32[]{:S(2)}) collective-permute-start(f32[1024]{0:T(1024)S(1)} %bitcast.405), channel_id=1, source_target_pairs={{0,1},{1,2},{2,3},{4,5},{5,6},{6,7},{8,9},{9,10},{10,11},{12,13},{... | collective-permute-start | bytes 12296 | tf_op jit(solution)/shard_map/ppermute | solution.py:13
  12.4 4.2 %copy-start.22 = (f32[16,1024]{1,0:T(8,128)S(1)}, f32[16,1024]{1,0:T(8,128)}, u32[]{:S(2)}) copy-start(f32[16,1024]{1,0:T(8,128)} %param.17) | copy-start | bytes 196612
  25.4 23.1 %collective-permute-start.6 = (f32[4,16]{1,0:T(4,128)}, f32[4,16]{1,0:T(4,128)}, u32[]{:S(2)}, u32[]{:S(2)}) collective-permute-start(f32[4,16]{1,0:T(4,128)} %pad_maximum_fusion.13), channel_id=1, source_target_pairs={{0,2},{1,3},{2,0},{3,1},{4,6},{5,7},{6,4},{7,5},{8,10},{9,11},{10,... | collective-permute-start | bytes 776 | tf_op jit(solution)/shard_map/ppermute | solution.py:165
  32.5 5.8 %copy-start.26 = (f32[6,1,1024]{2,1,0:T(1,128)S(1)}, f32[6,1,1024]{2,1,0:T(1,128)}, u32[]{:S(2)}) copy-start(f32[6,1,1024]{2,1,0:T(1,128)} %get-tuple-element.41) | copy-start | bytes 73732
  32.5 5.8 %copy-start.27 = (f32[6,1,1024]{2,1,0:T(1,128)S(1)}, f32[6,1,1024]{2,1,0:T(1,128)}, u32[]{:S(2)}) copy-start(f32[6,1,1024]{2,1,0:T(1,128)} %get-tuple-element.42) | copy-start | bytes 73732
  32.5 5.8 %copy-start.37 = (f32[64]{0:T(128)S(1)}, f32[64]{0:T(128)}, u32[]{:S(2)}) copy-start(f32[64]{0:T(128)} %reshape.486) | copy-start | bytes 772
  32.5 7.6 %copy-start.32 = (f32[6,16]{1,0:T(8,128)S(1)}, f32[6,16]{1,0:T(8,128)}, u32[]{:S(2)}) copy-start(f32[6,16]{1,0:T(8,128)} %get-tuple-element.4) | copy-start | bytes 1156
  32.5 9.6 %copy-start.36 = (f32[2064]{0:T(1024)S(1)}, f32[2064]{0:T(1024)}, u32[]{:S(2)}) copy-start(f32[2064]{0:T(1024)} %copy-done.35) | copy-start | bytes 24772
  34.2 19.6 %collective-permute-start.3 = (f32[6,2064]{1,0:T(8,128)}, f32[6,2064]{1,0:T(8,128)}, u32[]{:S(2)}, u32[]{:S(2)}) collective-permute-start(f32[6,2064]{1,0:T(8,128)} %pad_maximum_fusion.7), channel_id=1, source_target_pairs={{0,4},{4,8},{8,12},{12,16},{16,20},{20,24},{24,28},{1,5},{5,9},{9,... | collective-permute-start | bytes 148616 | tf_op jit(solution)/shard_map/ppermute | solution.py:13
  38.9 7.0 %collective-permute-start.4 = (f32[6208]{0:T(1024)}, f32[6208]{0:T(1024)}, u32[]{:S(2)}, u32[]{:S(2)}) collective-permute-start(f32[6208]{0:T(1024)} %get-tuple-element.71), channel_id=1, source_target_pairs={{0,3},{1,0},{2,1},{3,2},{4,7},{5,4},{6,5},{7,6},{8,11},{9,8},{10,9... | collective-permute-start | bytes 74504 | tf_op jit(solution)/shard_map/ppermute | solution.py:165
  40.1 3.3 %collective-permute-start.5 = (f32[6208]{0:T(1024)S(1)}, f32[6208]{0:T(1024)S(1)}, u32[]{:S(2)}, u32[]{:S(2)}) collective-permute-start(f32[6208]{0:T(1024)S(1)} %get-tuple-element.70), channel_id=1, source_target_pairs={{0,1},{1,2},{2,3},{3,0},{4,5},{5,6},{6,7},{7,4},{8,9},{9,10},{10,1... | collective-permute-start | bytes 74504 | tf_op jit(solution)/shard_map/ppermute | solution.py:165
  40.8 13.0 %collective-permute-start.2 = (f32[6,2064]{1,0:T(8,128)}, f32[6,2064]{1,0:T(8,128)}, u32[]{:S(2)}, u32[]{:S(2)}) collective-permute-start(f32[6,2064]{1,0:T(8,128)} %pad_maximum_fusion.6), channel_id=1, source_target_pairs={{4,0},{8,4},{12,8},{16,12},{20,16},{24,20},{28,24},{5,1},{9,5},{13... | collective-permute-start | bytes 148616 | tf_op jit(solution)/shard_map/ppermute | solution.py:13
  48.4 4.8 %copy-start.30 = (f32[6208]{0:T(1024)S(1)}, f32[6208]{0:T(1024)}, u32[]{:S(2)}) copy-start(f32[6208]{0:T(1024)} %copy-done.29) | copy-start | bytes 74500
  48.4 5.4 %copy-start.4 = (f32[6,4096]{1,0:T(8,128)S(1)}, f32[6,4096]{1,0:T(8,128)}, u32[]{:S(2)}) copy-start(f32[6,4096]{1,0:T(8,128)} %copy-done.3) | copy-start | bytes 294916
  48.4 5.4 %copy-start.28 = (f32[2048]{0:T(1024)S(1)}, f32[2048]{0:T(1024)}, u32[]{:S(2)}) copy-start(f32[2048]{0:T(1024)} %slice.445) | copy-start | bytes 24580
  55.7 7.0 %copy-start.13 = (f32[16,1024]{1,0:T(8,128)S(1)}, f32[16,1024]{1,0:T(8,128)}, u32[]{:S(2)}) copy-start(f32[16,1024]{1,0:T(8,128)} %copy-done.12) | copy-start | bytes 196612
  55.8 7.0 %copy-start.15 = (f32[16,1024]{1,0:T(8,128)S(1)}, f32[16,1024]{1,0:T(8,128)}, u32[]{:S(2)}) copy-start(f32[16,1024]{1,0:T(8,128)} %copy-done.14) | copy-start | bytes 196612
  55.8 7.0 %copy-start.20 = (f32[16,1024]{1,0:T(8,128)S(1)}, f32[16,1024]{1,0:T(8,128)}, u32[]{:S(2)}) copy-start(f32[16,1024]{1,0:T(8,128)} %get-tuple-element.28) | copy-start | bytes 196612
  55.8 7.0 %copy-start.21 = (f32[16,1024]{1,0:T(8,128)S(1)}, f32[16,1024]{1,0:T(8,128)}, u32[]{:S(2)}) copy-start(f32[16,1024]{1,0:T(8,128)} %get-tuple-element.29) | copy-start | bytes 196612
  64.4 13.8 %copy-start.8 = (f32[16,1024]{1,0:T(8,128)S(1)}, f32[16,1024]{1,0:T(8,128)}, u32[]{:S(2)}) copy-start(f32[16,1024]{1,0:T(8,128)} %copy-done.7) | copy-start | bytes 196612
  64.4 13.8 %copy-start.10 = (f32[16,1024]{1,0:T(8,128)S(1)}, f32[16,1024]{1,0:T(8,128)}, u32[]{:S(2)}) copy-start(f32[16,1024]{1,0:T(8,128)} %copy-done.9) | copy-start | bytes 196612
  64.4 13.8 %copy-start.25 = (f32[2,2,16,1024]{3,2,1,0:T(8,128)S(1)}, f32[2,2,16,1024]{3,2,1,0:T(8,128)}, u32[]{:S(2)}) copy-start(f32[2,2,16,1024]{3,2,1,0:T(8,128)} %param.16) | copy-start | bytes 786436
  64.6 17.1 %copy-start.6 = (f32[16,1024]{1,0:T(8,128)S(1)}, f32[16,1024]{1,0:T(8,128)}, u32[]{:S(2)}) copy-start(f32[16,1024]{1,0:T(8,128)} %copy-done.5) | copy-start | bytes 196612
  64.6 17.1 %copy-start.17 = (f32[16,1024]{1,0:T(8,128)S(1)}, f32[16,1024]{1,0:T(8,128)}, u32[]{:S(2)}) copy-start(f32[16,1024]{1,0:T(8,128)} %copy-done.16) | copy-start | bytes 196612
  64.6 17.1 %copy-start.19 = (f32[16,1024]{1,0:T(8,128)S(1)}, f32[16,1024]{1,0:T(8,128)}, u32[]{:S(2)}) copy-start(f32[16,1024]{1,0:T(8,128)} %copy-done.18) | copy-start | bytes 196612
  79.2 9.6 %all-to-all-start.1 = ((f32[32,1,3]{2,1,0:T(1,128)}), f32[32,1,3]{2,1,0:T(1,128)S(1)}, u32[]{:S(2)}, u32[]{:S(2)}) async-start(f32[32,1,3]{2,1,0:T(1,128)} %broadcast_in_dim.31), calls=%async_computation.1 | async-start | bytes 32768 | tf_op jit(solution)/shard_map/all_to_all | solution.py:36
  (21 other events, 33.2 us)

commit v9 on v8

--- a/solution.py
+++ b/solution.py
@@ -286,13 +286,12 @@
             [
                 (residual_first, residual_first),
                 (closing_first, closing_first),
+                (grad_last, grad_last),
                 (residual_last, residual_last),
             ]
         )
     )
-    norms = jnp.sqrt(
-        jnp.concatenate([second_sums[0:2], first_sums[2:3], second_sums[2:3]])
-    ).reshape(2, 2)
+    norms = jnp.sqrt(second_sums).reshape(2, 2)
     return (jnp.stack([solution_first, solution_last]), norms)
 
 

time: 92.4 us -> 90.4 us (0.978)
  other arithmetic: 20 us -> 18.6 us
  local copies, waits for them, and re-layouts: 21.6 us -> 20.4 us
    sqrt x1 -> x0, other arithmetic: 1.35 us -> none  [per_device(): jnp.sqrt(jnp.concatenate([second_sums[0:2], first_sums[2:3], second_sums[...]
    slice x2 -> x0, local copies, waits for them, and re-layouts: 1.2 us -> none  [the longest x1 0.61 us: per_device(): first_sums[2:3]]
where the time goes in v9:
time: 90.4 us; the launch traced here: 89.6 us
  local copies, waits for them, and re-layouts  20.4 us (23%)
  other arithmetic  18.6 us (21%)
  starting transfers between devices  17.3 us (19%)
  blocking collectives  12.6 us (14%)
  matrix products  11.5 us (13%)
  waiting for transfers between devices  6.91 us (8%)
  between operations  2.19 us (2%)
    all_to_all x1, blocking collectives, global_sum(): gathered = lax.all_to_all(copies, axes, 0, 0, tiled=True)  12.6 us
    ppermute x4, starting transfers between devices, shifted(): return lax.ppermute(value, axis, pairs)  11.6 us
    dot_general x4, matrix products, onehot_dot(): lax.dot_general(pieces, onehot, (dims, ((), ())), preferred_element_type=...  9.7 us
    all_to_all x1, waiting for transfers between devices, global_sum(): gathered = lax.all_to_all(copies, axes, 0, 0, tiled=True)  6.3 us
    unnamed x103, local copies, waits for them, and re-layouts  3.8 us
    ppermute x3, starting transfers between devices, slab_shift(): lax.ppermute(value, 'slab', [(i, (i + by) % count) for i in range(count)])  3.14 us
    all_to_all x1, starting transfers between devices, global_sum(): gathered = lax.all_to_all(copies, axes, 0, 0, tiled=True)  2.49 us
    select_n x2, other arithmetic, locate(): cells // column_count  2 us
  transfers between devices with their start and end apart: 8, of which 2 were waited for; matrix products, arithmetic and copies ran while one was open for 29% of the time, Pallas kernels for 0%

profile of v9, /device:TPU:0, one launch (start us, length us, event | category | flops | bytes accessed | tf_op | source)
XLA Modules:
  0.0 89.6 jit_solution(6278938355179086523)
XLA Ops:
  0.7 0.9 %broadcast_select_fusion.1 = f32[16,1024]{1,0:T(8,128)S(1)} fusion(f32[16,1024]{1,0:T(8,128)} %param.17, pred[1024]{0:T(1024)(128)(4,1)S(1)} %fusion.76), kind=kLoop, calls=%fused_computation.168 | loop fusion | flops 16384 | bytes 132096 | tf_op jit(solution)/shard_map/jit(_where)/select_n | solution.py:91
  3.2 4.9 %collective-permute-start = (f32[2064]{0:T(1024)S(1)}, f32[2064]{0:T(1024)S(1)}, u32[]{:S(2)}, u32[]{:S(2)}) collective-permute-start(f32[2064]{0:T(1024)S(1)} %pad_maximum_fusion.12), channel_id=1, source_target_pairs={{0,4},{4,8},{8,12},{12,16},{16,20},{20,24},{24,28},{1,5},{5,9},{9,... | collective-permute-start | bytes 24776 | tf_op jit(solution)/shard_map/ppermute | solution.py:13
  8.1 0.9 %broadcast_select_fusion = f32[16,1024]{1,0:T(8,128)S(1)} fusion(f32[16,1024]{1,0:T(8,128)} %param.18, pred[16]{0:T(512)(128)(4,1)S(1)} %compare_and_fusion), kind=kLoop, calls=%fused_computation.167 | loop fusion | flops 16384 | bytes 131088 | tf_op jit(solution)/shard_map/jit(_where)/select_n | solution.py:94
  9.0 1.5 %collective-permute-start.1 = (f32[1024]{0:T(1024)S(1)}, f32[1024]{0:T(1024)S(1)}, u32[]{:S(2)}, u32[]{:S(2)}) collective-permute-start(f32[1024]{0:T(1024)S(1)} %bitcast.405), channel_id=1, source_target_pairs={{0,1},{1,2},{2,3},{4,5},{5,6},{6,7},{8,9},{9,10},{10,11},{12,13},{... | collective-permute-start | bytes 12296 | tf_op jit(solution)/shard_map/ppermute | solution.py:13
  10.5 1.2 %and_select_fusion.2 = s32[128]{0:T(128)} fusion(s32[1,128]{1,0:T(1,128)} %param.23), kind=kLoop, calls=%fused_computation.206 | loop fusion | flops 1408 | bytes 1024 | tf_op jit(solution)/shard_map/jit(remainder)/select_n | solution.py:115
  12.4 1.0 %fusion.97 = (f32[1,2,16,1024]{3,2,1,0:T(8,128)S(1)}, f32[1,2,16,1024]{3,2,1,0:T(8,128)S(1)}) fusion(f32[2,2,16,1024]{3,2,1,0:T(8,128)} %param.15), kind=kLoop, calls=%fused_computation.228 | loop fusion | bytes 524288 | tf_op jit(solution)/shard_map/slice | solution.py:143
  13.5 1.3 %add_select_fusion = (s32[4096]{0:T(1024)S(1)}, s32[4096]{0:T(1024)}) fusion(s32[2048]{0:T(1024)} %bitcast.402, s32[2048]{0:T(1024)} %bitcast.403), kind=kLoop, calls=%fused_computation.176 | loop fusion | flops 81920 | bytes 49152 | tf_op jit(solution)/shard_map/jit(floor_divide)/jit(_where)/select_n | solution.py:116
  15.6 0.7 fusion.62
  18.2 0.8 fusion.22
  19.0 0.8 slice_reduce_fusion.1
  20.0 1.0 %fusion.95 = (f32[6,15,1024]{2,1,0:T(8,128)}, f32[6,15,1024]{2,1,0:T(8,128)}) fusion(f32[6,16,1024]{2,1,0:T(8,128)S(1)} %bitcast.342), kind=kLoop, calls=%fused_computation.226 | loop fusion | bytes 1474560 | tf_op jit(solution)/shard_map/slice | solution.py:201
  24.0 1.3 %reshape.488 = f32[64]{0:T(128)} reshape(f32[4,16]{1,0:T(4,128)} %pad_maximum_fusion.13) | data formatting | bytes 512 | tf_op jit(solution)/shard_map/reshape | solution.py:188
  25.4 2.0 %collective-permute-start.6 = (f32[4,16]{1,0:T(4,128)}, f32[4,16]{1,0:T(4,128)}, u32[]{:S(2)}, u32[]{:S(2)}) collective-permute-start(f32[4,16]{1,0:T(4,128)} %pad_maximum_fusion.13), channel_id=1, source_target_pairs={{0,2},{1,3},{2,0},{3,1},{4,6},{5,7},{6,4},{7,5},{8,10},{9,11},{10,... | collective-permute-start | bytes 776 | tf_op jit(solution)/shard_map/ppermute | solution.py:165
  27.3 4.9 %fusion.1 = f32[192,4096]{1,0:T(8,128)S(1)} fusion(s32[4096]{0:T(1024)} %get-tuple-element.69, bf16[96,1024]{1,0:T(8,128)(2,1)} %get-tuple-element.22, bf16[96,1024]{1,0:T(8,128)(2,1)} %get-tuple-element.23), kind=kOutput, calls=%fused_computation.2 | convolution fusion | flops 1615593472 | bytes 3555328 | tf_op jit(solution)/shard_map/dot_general | solution.py:58
  34.2 4.0 %collective-permute-start.3 = (f32[6,2064]{1,0:T(8,128)}, f32[6,2064]{1,0:T(8,128)}, u32[]{:S(2)}, u32[]{:S(2)}) collective-permute-start(f32[6,2064]{1,0:T(8,128)} %pad_maximum_fusion.7), channel_id=1, source_target_pairs={{0,4},{4,8},{8,12},{12,16},{16,20},{20,24},{24,28},{1,5},{5,9},{9,... | collective-permute-start | bytes 148616 | tf_op jit(solution)/shard_map/ppermute | solution.py:13
  38.9 1.2 %collective-permute-start.4 = (f32[6208]{0:T(1024)}, f32[6208]{0:T(1024)}, u32[]{:S(2)}, u32[]{:S(2)}) collective-permute-start(f32[6208]{0:T(1024)} %get-tuple-element.71), channel_id=1, source_target_pairs={{0,3},{1,0},{2,1},{3,2},{4,7},{5,4},{6,5},{7,6},{8,11},{9,8},{10,9... | collective-permute-start | bytes 74504 | tf_op jit(solution)/shard_map/ppermute | solution.py:165
  40.1 0.7 pad_maximum_fusion.6
  40.8 1.3 %collective-permute-start.2 = (f32[6,2064]{1,0:T(8,128)}, f32[6,2064]{1,0:T(8,128)}, u32[]{:S(2)}, u32[]{:S(2)}) collective-permute-start(f32[6,2064]{1,0:T(8,128)} %pad_maximum_fusion.6), channel_id=1, source_target_pairs={{4,0},{8,4},{12,8},{16,12},{20,16},{24,20},{28,24},{5,1},{9,5},{13... | collective-permute-start | bytes 148616 | tf_op jit(solution)/shard_map/ppermute | solution.py:13
  44.5 1.3 %reshape.490 = f32[4,16]{1,0:T(4,128)} reshape(f32[64]{0:T(128)} %slice.438) | data formatting | bytes 512 | tf_op jit(solution)/shard_map/reshape | solution.py:192
  45.9 1.2 %slice.439 = f32[64]{0:T(128)} slice(f32[6208]{0:T(1024)} %collective-permute-done.4), slice={[6144:6208]} | slice | bytes 512 | tf_op jit(solution)/shard_map/slice | solution.py:194
  47.1 1.3 %reshape.491 = f32[4,16]{1,0:T(4,128)} reshape(f32[64]{0:T(128)} %slice.439) | data formatting | bytes 512 | tf_op jit(solution)/shard_map/reshape | solution.py:194
  48.4 0.8 add_add_fusion.1
  49.2 0.9 fusion.8
  50.2 1.0 %fusion.9 = f32[144,1024]{1,0:T(8,128)S(1)} fusion(s32[128]{0:T(128)} %and_select_fusion.2, bf16[48,128]{1,0:T(8,128)(2,1)S(1)} %get-tuple-element.67, bf16[48,128]{1,0:T(8,128)(2,1)S(1)} %get-tuple-element.66, bf16[48,128]{1,0:T(8,128)(2,1)S(1)} %bitcast_convert_fusion.3), kind=kOutput, calls=%fused_computation.18 | convolution fusion | flops 37990400 | bytes 627200 | tf_op jit(solution)/shard_map/dot_general | solution.py:58
  51.9 1.3 %slice.428 = f32[6144]{0:T(1024)} slice(f32[6208]{0:T(1024)} %collective-permute-done.4), slice={[0:6144]} | slice | bytes 49152 | tf_op jit(solution)/shard_map/slice | solution.py:198
  53.8 1.0 %fusion.49 = (f32[6,2048]{1,0:T(8,128)S(1)}, f32[6,2048]{1,0:T(8,128)S(1)}) fusion(f32[6,2064]{1,0:T(8,128)} %collective-permute-done.2, f32[2048]{0:T(1024)S(1)} %bitcast.382, f32[6,4096]{1,0:T(8,128)S(1)} %copy-done.4, f32[6,2064]{1,0:T(8,128)} %collective-permute-done.3, f32[2048]{0:T(1024)S(1)} %copy-done.28), kind=kLoop, calls=%fused_computation.113 | loop fusion | flops 61440 | bytes 311296 | tf_op jit(solution)/shard_map/mul | solution.py:209
  55.8 3.4 %fusion = f32[192,1024]{1,0:T(8,128)S(1)} fusion(s32[4096]{0:T(1024)S(1)} %copy-done.31, bf16[96,4096]{1,0:T(8,128)(2,1)S(1)} %get-tuple-element.20, bf16[96,4096]{1,0:T(8,128)(2,1)S(1)} %get-tuple-element.21), kind=kOutput, calls=%fused_computation.1 | convolution fusion | flops 1617952768 | bytes 2375680 | tf_op jit(solution)/shard_map/dot_general | solution.py:58
  59.2 0.8 slice_add_fusion.1
  62.8 1.6 %fusion.18 = f32[3,2,16,1024]{3,2,1,0:T(8,128)S(1)} fusion(f32[3,2,16,1024]{3,2,1,0:T(8,128)} %bitcast.349, f32[3,2,16,1024]{3,2,1,0:T(8,128)S(1)} %get-tuple-element.46, f32[3,2,16,1]{3,2,1,0:T(8,128)} %concatenate.145, f32[3,2,16,1023]{3,2,1,0:T(8,128)S(1)} %bitcast.346, f32[3,2,16,1023]{3,2,1,0:T(8,128)S(1)} %bitcast.345, ...), kind=kLoop, calls=%fused_computation.35 | loop fusion | flops 1572864 | bytes 3014656 | tf_op jit(solution)/shard_map/add | solution.py:214
  65.4 12.6 %all_to_all.12 = f32[32,1,10]{2,1,0:T(1,128)S(1)} all-to-all(f32[32,1,10]{2,1,0:T(1,128)S(1)} %broadcast_in_dim.29), channel_id=1, replica_groups=mesh['cells'=8,'slab'=4] {'cells','slab'}, dimensions={0} | all-to-all | bytes 2560 | tf_op jit(solution)/shard_map/all_to_all | solution.py:36
  79.2 2.5 %all-to-all-start.1 = ((f32[32,1,4]{2,1,0:T(1,128)}), f32[32,1,4]{2,1,0:T(1,128)S(1)}, u32[]{:S(2)}, u32[]{:S(2)}) async-start(f32[32,1,4]{2,1,0:T(1,128)} %broadcast_in_dim.31), calls=%async_computation.1 | async-start | bytes 32768 | tf_op jit(solution)/shard_map/all_to_all | solution.py:36
  82.5 6.3 %all-to-all-done.1 = f32[32,1,4]{2,1,0:T(1,128)S(1)} async-done(((f32[32,1,4]{2,1,0:T(1,128)}), f32[32,1,4]{2,1,0:T(1,128)S(1)}, u32[]{:S(2)}, u32[]{:S(2)}) %all-to-all-start.1) | async-done | bytes 544 | tf_op jit(solution)/shard_map/all_to_all | solution.py:36
  (181 shorter events, 20.8 us)
Async XLA Ops:
  0.6 14.9 %copy-start = (f32[2,4,16,1024]{3,2,1,0:T(8,128)S(1)}, f32[2,4,16,1024]{3,2,1,0:T(8,128)}, u32[]{:S(2)}) copy-start(f32[2,4,16,1024]{3,2,1,0:T(8,128)} %param.14) | copy-start | bytes 1572868
  0.6 15.0 %copy-start.41 = (s32[1,128]{1,0:T(1,128)S(1)}, s32[1,128]{1,0:T(1,128)}, u32[]{:S(2)}) copy-start(s32[1,128]{1,0:T(1,128)} %param.24) | copy-start | bytes 1540
  0.7 15.0 %copy-start.43 = (f32[1,128]{1,0:T(1,128)S(1)}, f32[1,128]{1,0:T(1,128)}, u32[]{:S(2)}) copy-start(f32[1,128]{1,0:T(1,128)} %param.25) | copy-start | bytes 1540
  1.6 15.0 %copy-start.12 = (f32[16,1024]{1,0:T(8,128)}, f32[16,1024]{1,0:T(8,128)S(1)}, u32[]{:S(2)}) copy-start(f32[16,1024]{1,0:T(8,128)S(1)} %broadcast_select_fusion.1) | copy-start | bytes 196612
  3.2 13.3 %collective-permute-start = (f32[2064]{0:T(1024)S(1)}, f32[2064]{0:T(1024)S(1)}, u32[]{:S(2)}, u32[]{:S(2)}) collective-permute-start(f32[2064]{0:T(1024)S(1)} %pad_maximum_fusion.12), channel_id=1, source_target_pairs={{0,4},{4,8},{8,12},{12,16},{16,20},{20,24},{24,28},{1,5},{5,9},{9,... | collective-permute-start | bytes 24776 | tf_op jit(solution)/shard_map/ppermute | solution.py:13
  9.0 7.6 %copy-start.14 = (f32[16,1024]{1,0:T(8,128)}, f32[16,1024]{1,0:T(8,128)S(1)}, u32[]{:S(2)}) copy-start(f32[16,1024]{1,0:T(8,128)S(1)} %broadcast_select_fusion) | copy-start | bytes 196612
  9.0 7.6 %collective-permute-start.1 = (f32[1024]{0:T(1024)S(1)}, f32[1024]{0:T(1024)S(1)}, u32[]{:S(2)}, u32[]{:S(2)}) collective-permute-start(f32[1024]{0:T(1024)S(1)} %bitcast.405), channel_id=1, source_target_pairs={{0,1},{1,2},{2,3},{4,5},{5,6},{6,7},{8,9},{9,10},{10,11},{12,13},{... | collective-permute-start | bytes 12296 | tf_op jit(solution)/shard_map/ppermute | solution.py:13
  12.4 4.2 %copy-start.22 = (f32[16,1024]{1,0:T(8,128)S(1)}, f32[16,1024]{1,0:T(8,128)}, u32[]{:S(2)}) copy-start(f32[16,1024]{1,0:T(8,128)} %param.17) | copy-start | bytes 196612
  25.4 23.1 %collective-permute-start.6 = (f32[4,16]{1,0:T(4,128)}, f32[4,16]{1,0:T(4,128)}, u32[]{:S(2)}, u32[]{:S(2)}) collective-permute-start(f32[4,16]{1,0:T(4,128)} %pad_maximum_fusion.13), channel_id=1, source_target_pairs={{0,2},{1,3},{2,0},{3,1},{4,6},{5,7},{6,4},{7,5},{8,10},{9,11},{10,... | collective-permute-start | bytes 776 | tf_op jit(solution)/shard_map/ppermute | solution.py:165
  32.5 5.8 %copy-start.26 = (f32[6,1,1024]{2,1,0:T(1,128)S(1)}, f32[6,1,1024]{2,1,0:T(1,128)}, u32[]{:S(2)}) copy-start(f32[6,1,1024]{2,1,0:T(1,128)} %get-tuple-element.41) | copy-start | bytes 73732
  32.5 5.8 %copy-start.27 = (f32[6,1,1024]{2,1,0:T(1,128)S(1)}, f32[6,1,1024]{2,1,0:T(1,128)}, u32[]{:S(2)}) copy-start(f32[6,1,1024]{2,1,0:T(1,128)} %get-tuple-element.42) | copy-start | bytes 73732
  32.5 5.8 %copy-start.37 = (f32[64]{0:T(128)S(1)}, f32[64]{0:T(128)}, u32[]{:S(2)}) copy-start(f32[64]{0:T(128)} %reshape.488) | copy-start | bytes 772
  32.5 7.6 %copy-start.32 = (f32[6,16]{1,0:T(8,128)S(1)}, f32[6,16]{1,0:T(8,128)}, u32[]{:S(2)}) copy-start(f32[6,16]{1,0:T(8,128)} %get-tuple-element.4) | copy-start | bytes 1156
  32.5 9.6 %copy-start.36 = (f32[2064]{0:T(1024)S(1)}, f32[2064]{0:T(1024)}, u32[]{:S(2)}) copy-start(f32[2064]{0:T(1024)} %copy-done.35) | copy-start | bytes 24772
  34.2 19.6 %collective-permute-start.3 = (f32[6,2064]{1,0:T(8,128)}, f32[6,2064]{1,0:T(8,128)}, u32[]{:S(2)}, u32[]{:S(2)}) collective-permute-start(f32[6,2064]{1,0:T(8,128)} %pad_maximum_fusion.7), channel_id=1, source_target_pairs={{0,4},{4,8},{8,12},{12,16},{16,20},{20,24},{24,28},{1,5},{5,9},{9,... | collective-permute-start | bytes 148616 | tf_op jit(solution)/shard_map/ppermute | solution.py:13
  38.9 7.0 %collective-permute-start.4 = (f32[6208]{0:T(1024)}, f32[6208]{0:T(1024)}, u32[]{:S(2)}, u32[]{:S(2)}) collective-permute-start(f32[6208]{0:T(1024)} %get-tuple-element.71), channel_id=1, source_target_pairs={{0,3},{1,0},{2,1},{3,2},{4,7},{5,4},{6,5},{7,6},{8,11},{9,8},{10,9... | collective-permute-start | bytes 74504 | tf_op jit(solution)/shard_map/ppermute | solution.py:165
  40.1 3.3 %collective-permute-start.5 = (f32[6208]{0:T(1024)S(1)}, f32[6208]{0:T(1024)S(1)}, u32[]{:S(2)}, u32[]{:S(2)}) collective-permute-start(f32[6208]{0:T(1024)S(1)} %get-tuple-element.70), channel_id=1, source_target_pairs={{0,1},{1,2},{2,3},{3,0},{4,5},{5,6},{6,7},{7,4},{8,9},{9,10},{10,1... | collective-permute-start | bytes 74504 | tf_op jit(solution)/shard_map/ppermute | solution.py:165
  40.8 13.0 %collective-permute-start.2 = (f32[6,2064]{1,0:T(8,128)}, f32[6,2064]{1,0:T(8,128)}, u32[]{:S(2)}, u32[]{:S(2)}) collective-permute-start(f32[6,2064]{1,0:T(8,128)} %pad_maximum_fusion.6), channel_id=1, source_target_pairs={{4,0},{8,4},{12,8},{16,12},{20,16},{24,20},{28,24},{5,1},{9,5},{13... | collective-permute-start | bytes 148616 | tf_op jit(solution)/shard_map/ppermute | solution.py:13
  48.4 4.8 %copy-start.30 = (f32[6208]{0:T(1024)S(1)}, f32[6208]{0:T(1024)}, u32[]{:S(2)}) copy-start(f32[6208]{0:T(1024)} %copy-done.29) | copy-start | bytes 74500
  48.4 5.4 %copy-start.4 = (f32[6,4096]{1,0:T(8,128)S(1)}, f32[6,4096]{1,0:T(8,128)}, u32[]{:S(2)}) copy-start(f32[6,4096]{1,0:T(8,128)} %copy-done.3) | copy-start | bytes 294916
  48.4 5.4 %copy-start.28 = (f32[2048]{0:T(1024)S(1)}, f32[2048]{0:T(1024)}, u32[]{:S(2)}) copy-start(f32[2048]{0:T(1024)} %slice.433) | copy-start | bytes 24580
  55.7 7.0 %copy-start.13 = (f32[16,1024]{1,0:T(8,128)S(1)}, f32[16,1024]{1,0:T(8,128)}, u32[]{:S(2)}) copy-start(f32[16,1024]{1,0:T(8,128)} %copy-done.12) | copy-start | bytes 196612
  55.8 7.0 %copy-start.15 = (f32[16,1024]{1,0:T(8,128)S(1)}, f32[16,1024]{1,0:T(8,128)}, u32[]{:S(2)}) copy-start(f32[16,1024]{1,0:T(8,128)} %copy-done.14) | copy-start | bytes 196612
  55.8 7.0 %copy-start.20 = (f32[16,1024]{1,0:T(8,128)S(1)}, f32[16,1024]{1,0:T(8,128)}, u32[]{:S(2)}) copy-start(f32[16,1024]{1,0:T(8,128)} %get-tuple-element.28) | copy-start | bytes 196612
  55.8 7.0 %copy-start.21 = (f32[16,1024]{1,0:T(8,128)S(1)}, f32[16,1024]{1,0:T(8,128)}, u32[]{:S(2)}) copy-start(f32[16,1024]{1,0:T(8,128)} %get-tuple-element.29) | copy-start | bytes 196612
  64.4 13.8 %copy-start.8 = (f32[16,1024]{1,0:T(8,128)S(1)}, f32[16,1024]{1,0:T(8,128)}, u32[]{:S(2)}) copy-start(f32[16,1024]{1,0:T(8,128)} %copy-done.7) | copy-start | bytes 196612
  64.4 13.8 %copy-start.10 = (f32[16,1024]{1,0:T(8,128)S(1)}, f32[16,1024]{1,0:T(8,128)}, u32[]{:S(2)}) copy-start(f32[16,1024]{1,0:T(8,128)} %copy-done.9) | copy-start | bytes 196612
  64.4 13.8 %copy-start.25 = (f32[2,2,16,1024]{3,2,1,0:T(8,128)S(1)}, f32[2,2,16,1024]{3,2,1,0:T(8,128)}, u32[]{:S(2)}) copy-start(f32[2,2,16,1024]{3,2,1,0:T(8,128)} %param.16) | copy-start | bytes 786436
  64.6 17.1 %copy-start.6 = (f32[16,1024]{1,0:T(8,128)S(1)}, f32[16,1024]{1,0:T(8,128)}, u32[]{:S(2)}) copy-start(f32[16,1024]{1,0:T(8,128)} %copy-done.5) | copy-start | bytes 196612
  64.6 17.1 %copy-start.17 = (f32[16,1024]{1,0:T(8,128)S(1)}, f32[16,1024]{1,0:T(8,128)}, u32[]{:S(2)}) copy-start(f32[16,1024]{1,0:T(8,128)} %copy-done.16) | copy-start | bytes 196612
  64.6 17.1 %copy-start.19 = (f32[16,1024]{1,0:T(8,128)S(1)}, f32[16,1024]{1,0:T(8,128)}, u32[]{:S(2)}) copy-start(f32[16,1024]{1,0:T(8,128)} %copy-done.18) | copy-start | bytes 196612
  79.2 9.6 %all-to-all-start.1 = ((f32[32,1,4]{2,1,0:T(1,128)}), f32[32,1,4]{2,1,0:T(1,128)S(1)}, u32[]{:S(2)}, u32[]{:S(2)}) async-start(f32[32,1,4]{2,1,0:T(1,128)} %broadcast_in_dim.31), calls=%async_computation.1 | async-start | bytes 32768 | tf_op jit(solution)/shard_map/all_to_all | solution.py:36
  (21 other events, 33.2 us)

commit v10 on v9

--- a/solution.py
+++ b/solution.py
@@ -180,22 +180,25 @@
                 jnp.dot(well_index * values, well_onehot, precision=highest),
             ]
         )
-        halo_size = count * 2 * column_count
-        from_above = slab_shift(
-            jnp.concatenate([scaled[:, -1, :].reshape(-1), local.reshape(-1)]), 1
-        )
-        from_below = slab_shift(
-            jnp.concatenate([scaled[:, 0, :].reshape(-1), local.reshape(-1)]), -1
-        )
+        halo_rows = count * 2
+        wells = local.shape[1]
+        lanes = -(-wells // column_count) * column_count
+        well_block = jnp.pad(local, ((0, 0), (0, lanes - wells))).reshape(-1, column_count)
+        from_above = slab_shift(jnp.concatenate([scaled[:, -1, :], well_block]), 1)
+        from_below = slab_shift(jnp.concatenate([scaled[:, 0, :], well_block]), -1)
+
+        def wells_of(message):
+            return message[halo_rows:].reshape(local.shape[0], lanes)[:, :wells]
+
         summed = local
         if slab_size > 1:
-            summed = summed + from_above[halo_size:].reshape(local.shape)
+            summed = summed + wells_of(from_above)
         if slab_size > 2:
-            summed = summed + from_below[halo_size:].reshape(local.shape)
+            summed = summed + wells_of(from_below)
         for by in range(2, slab_size - 1):
             summed = summed + slab_shift(local, by)
-        from_above = from_above[:halo_size].reshape(count * 2, column_count)
-        from_below = from_below[:halo_size].reshape(count * 2, column_count)
+        from_above = from_above[:halo_rows]
+        from_below = from_below[:halo_rows]
         west = jnp.concatenate([from_left[:, :layer_count, None], scaled[:, :, :-1]], axis=2)
         east = jnp.concatenate([scaled[:, :, 1:], from_right[:, :layer_count, None]], axis=2)
         above = jnp.concatenate([from_above[:, None, :], scaled[:, :-1, :]], axis=1)

time: 90.4 us -> 79.6 us (0.88)
  local copies, waits for them, and re-layouts: 20.4 us -> 14.5 us
  other arithmetic: 18.6 us -> 16 us
  matrix products: 11.5 us -> 9.12 us
    reshape x3 -> x0, local copies, waits for them, and re-layouts: 3.99 us -> none  [the longest x1 1.34 us: operator(): local.reshape(-1)]
    concatenate x0 -> x2, local copies, waits for them, and re-layouts: none -> 2.78 us  [the longest x1 1.39 us: operator(): above = jnp.concatenate([from_above[:, None, :], scaled[:, :-1, :]], axis=1)]
    slice x5 -> x3, local copies, waits for them, and re-layouts: 4.41 us -> 2 us  [the longest x1 1.36 us: operator(): from_above = from_above[:halo_rows]]
    unnamed x103 -> x89, local copies, waits for them, and re-layouts: 3.8 us -> 2.08 us
    dot_general x4, matrix products: 9.7 us -> 8 us  [onehot_dot(): lax.dot_general(pieces, onehot, (dims, ((), ())), preferred_element_type=...]
  transfers between devices with their start and end apart: 8 -> 8, of which waited for: 2 -> 2; matrix products, arithmetic and copies ran while one was open for 29% -> 20% of each run, Pallas kernels for 0% -> 0%
where the time goes in v10:
time: 79.6 us; the launch traced here: 78.7 us
  starting transfers between devices  17.4 us (22%)
  other arithmetic  16 us (20%)
  local copies, waits for them, and re-layouts  14.5 us (18%)
  blocking collectives  12.2 us (15%)
  matrix products  9.12 us (11%)
  waiting for transfers between devices  7.34 us (9%)
  between operations  2.19 us (3%)
    all_to_all x1, blocking collectives, global_sum(): gathered = lax.all_to_all(copies, axes, 0, 0, tiled=True)  12.2 us
    ppermute x4, starting transfers between devices, shifted(): return lax.ppermute(value, axis, pairs)  11.7 us
    dot_general x4, matrix products, onehot_dot(): lax.dot_general(pieces, onehot, (dims, ((), ())), preferred_element_type=...  8 us
    all_to_all x1, waiting for transfers between devices, global_sum(): gathered = lax.all_to_all(copies, axes, 0, 0, tiled=True)  6.31 us
    ppermute x3, starting transfers between devices, slab_shift(): lax.ppermute(value, 'slab', [(i, (i + by) % count) for i in range(count)])  3.25 us
    all_to_all x1, starting transfers between devices, global_sum(): gathered = lax.all_to_all(copies, axes, 0, 0, tiled=True)  2.48 us
    unnamed x89, local copies, waits for them, and re-layouts  2.08 us
    select_n x2, other arithmetic, locate(): cells // column_count  1.99 us
  transfers between devices with their start and end apart: 8, of which 2 were waited for; matrix products, arithmetic and copies ran while one was open for 20% of the time, Pallas kernels for 0%

profile of v10, /device:TPU:0, one launch (start us, length us, event | category | flops | bytes accessed | tf_op | source)
XLA Modules:
  0.0 78.7 jit_solution(6296059826272984369)
XLA Ops:
  0.7 0.9 %broadcast_select_fusion.1 = f32[16,1024]{1,0:T(8,128)S(1)} fusion(f32[16,1024]{1,0:T(8,128)} %param.17, pred[1024]{0:T(1024)(128)(4,1)S(1)} %fusion.78), kind=kLoop, calls=%fused_computation.172 | loop fusion | flops 16384 | bytes 132096 | tf_op jit(solution)/shard_map/jit(_where)/select_n | solution.py:91
  3.2 4.9 %collective-permute-start = (f32[2064]{0:T(1024)S(1)}, f32[2064]{0:T(1024)S(1)}, u32[]{:S(2)}, u32[]{:S(2)}) collective-permute-start(f32[2064]{0:T(1024)S(1)} %pad_maximum_fusion.10), channel_id=1, source_target_pairs={{0,4},{4,8},{8,12},{12,16},{16,20},{20,24},{24,28},{1,5},{5,9},{9,... | collective-permute-start | bytes 24776 | tf_op jit(solution)/shard_map/ppermute | solution.py:13
  8.1 0.9 %broadcast_select_fusion = f32[16,1024]{1,0:T(8,128)S(1)} fusion(f32[16,1024]{1,0:T(8,128)} %param.18, pred[16]{0:T(512)(128)(4,1)S(1)} %compare_and_fusion), kind=kLoop, calls=%fused_computation.171 | loop fusion | flops 16384 | bytes 131088 | tf_op jit(solution)/shard_map/jit(_where)/select_n | solution.py:94
  9.0 1.5 %collective-permute-start.1 = (f32[1024]{0:T(1024)S(1)}, f32[1024]{0:T(1024)S(1)}, u32[]{:S(2)}, u32[]{:S(2)}) collective-permute-start(f32[1024]{0:T(1024)S(1)} %bitcast.405), channel_id=1, source_target_pairs={{0,1},{1,2},{2,3},{4,5},{5,6},{6,7},{8,9},{9,10},{10,11},{12,13},{... | collective-permute-start | bytes 12296 | tf_op jit(solution)/shard_map/ppermute | solution.py:13
  10.5 1.2 %and_select_fusion.2 = s32[128]{0:T(128)} fusion(s32[1,128]{1,0:T(1,128)} %param.23), kind=kLoop, calls=%fused_computation.212 | loop fusion | flops 1408 | bytes 1024 | tf_op jit(solution)/shard_map/jit(remainder)/select_n | solution.py:115
  12.4 1.0 %fusion.100 = (f32[1,2,16,1024]{3,2,1,0:T(8,128)S(1)}, f32[1,2,16,1024]{3,2,1,0:T(8,128)S(1)}) fusion(f32[2,2,16,1024]{3,2,1,0:T(8,128)} %param.15), kind=kLoop, calls=%fused_computation.234 | loop fusion | bytes 524288 | tf_op jit(solution)/shard_map/slice | solution.py:143
  13.5 1.3 %add_select_fusion = (s32[4096]{0:T(1024)S(1)}, s32[4096]{0:T(1024)}) fusion(s32[2048]{0:T(1024)} %bitcast.402, s32[2048]{0:T(1024)} %bitcast.403), kind=kLoop, calls=%fused_computation.180 | loop fusion | flops 81920 | bytes 49152 | tf_op jit(solution)/shard_map/jit(floor_divide)/jit(_where)/select_n | solution.py:116
  14.8 0.7 and_select_fusion
  15.6 0.7 fusion.64
  17.1 0.7 fusion.53
  19.1 1.0 %fusion.98 = (f32[6,15,1024]{2,1,0:T(8,128)}, f32[6,15,1024]{2,1,0:T(8,128)}) fusion(f32[6,16,1024]{2,1,0:T(8,128)S(1)} %bitcast.345), kind=kLoop, calls=%fused_computation.232 | loop fusion | bytes 1474560 | tf_op jit(solution)/shard_map/slice | solution.py:204
  20.1 3.9 %fusion.1 = f32[192,4096]{1,0:T(8,128)S(1)} fusion(s32[4096]{0:T(1024)S(1)} %copy-done.27, bf16[96,1024]{1,0:T(8,128)(2,1)S(1)} %get-tuple-element.22, bf16[96,1024]{1,0:T(8,128)(2,1)S(1)} %get-tuple-element.23), kind=kOutput, calls=%fused_computation.2 | convolution fusion | flops 1615593472 | bytes 3555328 | tf_op jit(solution)/shard_map/dot_general | solution.py:58
  24.6 0.7 pad_maximum_fusion.7
  25.3 4.1 %collective-permute-start.3 = (f32[6,2064]{1,0:T(8,128)}, f32[6,2064]{1,0:T(8,128)}, u32[]{:S(2)}, u32[]{:S(2)}) collective-permute-start(f32[6,2064]{1,0:T(8,128)} %pad_maximum_fusion.7), channel_id=1, source_target_pairs={{0,4},{4,8},{8,12},{12,16},{16,20},{20,24},{24,28},{1,5},{5,9},{9,... | collective-permute-start | bytes 148616 | tf_op jit(solution)/shard_map/ppermute | solution.py:13
  30.0 2.0 %collective-permute-start.6 = (f32[4,16]{1,0:T(4,128)S(1)}, f32[4,16]{1,0:T(4,128)S(1)}, u32[]{:S(2)}, u32[]{:S(2)}) collective-permute-start(f32[4,16]{1,0:T(4,128)S(1)} %pad_maximum_fusion.11), channel_id=1, source_target_pairs={{0,2},{1,3},{2,0},{3,1},{4,6},{5,7},{6,4},{7,5},{8,10},{9,11},{10,... | collective-permute-start | bytes 776 | tf_op jit(solution)/shard_map/ppermute | solution.py:165
  32.0 1.2 %collective-permute-start.4 = (f32[10,1024]{1,0:T(8,128)S(1)}, f32[10,1024]{1,0:T(8,128)S(1)}, u32[]{:S(2)}, u32[]{:S(2)}) collective-permute-start(f32[10,1024]{1,0:T(8,128)S(1)} %get-tuple-element.71), channel_id=1, source_target_pairs={{0,3},{1,0},{2,1},{3,2},{4,7},{5,4},{6,5},{7,6},{8,11},{9,8},{10,9... | collective-permute-start | bytes 122888 | tf_op jit(solution)/shard_map/ppermute | solution.py:165
  33.2 0.7 pad_maximum_fusion.6
  34.0 1.3 %collective-permute-start.2 = (f32[6,2064]{1,0:T(8,128)}, f32[6,2064]{1,0:T(8,128)}, u32[]{:S(2)}, u32[]{:S(2)}) collective-permute-start(f32[6,2064]{1,0:T(8,128)} %pad_maximum_fusion.6), channel_id=1, source_target_pairs={{4,0},{8,4},{12,8},{16,12},{20,16},{24,20},{28,24},{5,1},{9,5},{13... | collective-permute-start | bytes 148616 | tf_op jit(solution)/shard_map/ppermute | solution.py:13
  35.9 1.0 %collective-permute-done.5 = f32[10,1024]{1,0:T(8,128)S(1)} collective-permute-done((f32[10,1024]{1,0:T(8,128)S(1)}, f32[10,1024]{1,0:T(8,128)S(1)}, u32[]{:S(2)}, u32[]{:S(2)}) %collective-permute-start.5) | collective-permute-done | bytes 40992 | tf_op jit(solution)/shard_map/ppermute | solution.py:165
  37.9 0.7 slice_add_fusion.3
  39.2 1.4 %concatenate.147 = f32[3,2,1,1024]{3,2,1,0:T(1,128)} reshape(f32[6,1024]{1,0:T(8,128)} %slice.416) | data formatting | bytes 49152 | tf_op jit(solution)/shard_map/concatenate | solution.py:205
  40.6 1.4 %slice.418 = f32[6,1024]{1,0:T(8,128)} slice(f32[10,1024]{1,0:T(8,128)} %copy-done.26), slice={[0:6], [0:1024]} | slice | bytes 49152 | tf_op jit(solution)/shard_map/slice | solution.py:200
  41.9 1.4 %concatenate.148 = f32[3,2,1,1024]{3,2,1,0:T(1,128)} reshape(f32[6,1024]{1,0:T(8,128)} %slice.418) | data formatting | bytes 49152 | tf_op jit(solution)/shard_map/concatenate | solution.py:204
  43.3 1.1 %fusion.49 = (f32[6,2048]{1,0:T(8,128)S(1)}, f32[6,2048]{1,0:T(8,128)S(1)}) fusion(f32[6,2064]{1,0:T(8,128)} %collective-permute-done.2, f32[2048]{0:T(1024)S(1)} %bitcast.382, f32[6,4096]{1,0:T(8,128)} %copy-done.3, f32[6,2064]{1,0:T(8,128)} %collective-permute-done.3, f32[2048]{0:T(1024)S(1)} %copy-done.25), kind=kLoop, calls=%fused_computation.113 | loop fusion | flops 61440 | bytes 311296 | tf_op jit(solution)/shard_map/mul | solution.py:212
  45.3 3.4 %fusion = f32[192,1024]{1,0:T(8,128)S(1)} fusion(s32[4096]{0:T(1024)S(1)} %copy-done.28, bf16[96,4096]{1,0:T(8,128)(2,1)S(1)} %get-tuple-element.20, bf16[96,4096]{1,0:T(8,128)(2,1)S(1)} %get-tuple-element.21), kind=kOutput, calls=%fused_computation.1 | convolution fusion | flops 1617952768 | bytes 2375680 | tf_op jit(solution)/shard_map/dot_general | solution.py:58
  48.8 0.8 %slice_add_fusion.1 = f32[96,1024]{1,0:T(8,128)} fusion(f32[192,1024]{1,0:T(8,128)S(1)} %fusion), kind=kLoop, calls=%fused_computation.24 | loop fusion | flops 98304 | bytes 1179648 | tf_op jit(solution)/shard_map/add | solution.py:63
  50.3 0.7 concatenate.146
  52.4 1.6 %fusion.18 = f32[3,2,16,1024]{3,2,1,0:T(8,128)S(1)} fusion(f32[3,2,16,1024]{3,2,1,0:T(8,128)} %bitcast.351, f32[3,2,16,1024]{3,2,1,0:T(8,128)S(1)} %get-tuple-element.46, f32[3,2,16,1]{3,2,1,0:T(8,128)} %concatenate.145, f32[3,2,16,1023]{3,2,1,0:T(8,128)S(1)} %bitcast.348, f32[3,2,16,1023]{3,2,1,0:T(8,128)S(1)} %bitcast.347, ...), kind=kLoop, calls=%fused_computation.35 | loop fusion | flops 1572864 | bytes 3014656 | tf_op jit(solution)/shard_map/add | solution.py:217
  55.0 12.2 %all_to_all.12 = f32[32,1,10]{2,1,0:T(1,128)S(1)} all-to-all(f32[32,1,10]{2,1,0:T(1,128)S(1)} %broadcast_in_dim.29), channel_id=1, replica_groups=mesh['cells'=8,'slab'=4] {'cells','slab'}, dimensions={0} | all-to-all | bytes 2560 | tf_op jit(solution)/shard_map/all_to_all | solution.py:36
  68.4 2.5 %all-to-all-start.1 = ((f32[32,1,4]{2,1,0:T(1,128)}), f32[32,1,4]{2,1,0:T(1,128)S(1)}, u32[]{:S(2)}, u32[]{:S(2)}) async-start(f32[32,1,4]{2,1,0:T(1,128)} %broadcast_in_dim.31), calls=%async_computation.1 | async-start | bytes 32768 | tf_op jit(solution)/shard_map/all_to_all | solution.py:36
  71.0 0.7 pad_maximum_fusion.2
  71.7 6.3 %all-to-all-done.1 = f32[32,1,4]{2,1,0:T(1,128)S(1)} async-done(((f32[32,1,4]{2,1,0:T(1,128)}), f32[32,1,4]{2,1,0:T(1,128)S(1)}, u32[]{:S(2)}, u32[]{:S(2)}) %all-to-all-start.1) | async-done | bytes 544 | tf_op jit(solution)/shard_map/all_to_all | solution.py:36
  (164 shorter events, 12.5 us)
Async XLA Ops:
  0.6 14.9 %copy-start = (f32[2,4,16,1024]{3,2,1,0:T(8,128)S(1)}, f32[2,4,16,1024]{3,2,1,0:T(8,128)}, u32[]{:S(2)}) copy-start(f32[2,4,16,1024]{3,2,1,0:T(8,128)} %param.14) | copy-start | bytes 1572868
  0.6 15.0 %copy-start.33 = (s32[1,128]{1,0:T(1,128)S(1)}, s32[1,128]{1,0:T(1,128)}, u32[]{:S(2)}) copy-start(s32[1,128]{1,0:T(1,128)} %param.24) | copy-start | bytes 1540
  0.7 15.0 %copy-start.35 = (f32[1,128]{1,0:T(1,128)S(1)}, f32[1,128]{1,0:T(1,128)}, u32[]{:S(2)}) copy-start(f32[1,128]{1,0:T(1,128)} %param.25) | copy-start | bytes 1540
  1.6 15.5 %copy-start.11 = (f32[16,1024]{1,0:T(8,128)}, f32[16,1024]{1,0:T(8,128)S(1)}, u32[]{:S(2)}) copy-start(f32[16,1024]{1,0:T(8,128)S(1)} %broadcast_select_fusion.1) | copy-start | bytes 196612
  3.2 13.3 %collective-permute-start = (f32[2064]{0:T(1024)S(1)}, f32[2064]{0:T(1024)S(1)}, u32[]{:S(2)}, u32[]{:S(2)}) collective-permute-start(f32[2064]{0:T(1024)S(1)} %pad_maximum_fusion.10), channel_id=1, source_target_pairs={{0,4},{4,8},{8,12},{12,16},{16,20},{20,24},{24,28},{1,5},{5,9},{9,... | collective-permute-start | bytes 24776 | tf_op jit(solution)/shard_map/ppermute | solution.py:13
  9.0 8.1 %copy-start.13 = (f32[16,1024]{1,0:T(8,128)}, f32[16,1024]{1,0:T(8,128)S(1)}, u32[]{:S(2)}) copy-start(f32[16,1024]{1,0:T(8,128)S(1)} %broadcast_select_fusion) | copy-start | bytes 196612
  9.0 7.6 %collective-permute-start.1 = (f32[1024]{0:T(1024)S(1)}, f32[1024]{0:T(1024)S(1)}, u32[]{:S(2)}, u32[]{:S(2)}) collective-permute-start(f32[1024]{0:T(1024)S(1)} %bitcast.405), channel_id=1, source_target_pairs={{0,1},{1,2},{2,3},{4,5},{5,6},{6,7},{8,9},{9,10},{10,11},{12,13},{... | collective-permute-start | bytes 12296 | tf_op jit(solution)/shard_map/ppermute | solution.py:13
  12.4 4.7 %copy-start.1 = (f32[2,2,16,1024]{3,2,1,0:T(8,128)S(1)}, f32[2,2,16,1024]{3,2,1,0:T(8,128)}, u32[]{:S(2)}) copy-start(f32[2,2,16,1024]{3,2,1,0:T(8,128)} %param.13) | copy-start | bytes 786436
  12.4 4.7 %copy-start.2 = (f32[2,2,16,1024]{3,2,1,0:T(8,128)S(1)}, f32[2,2,16,1024]{3,2,1,0:T(8,128)}, u32[]{:S(2)}) copy-start(f32[2,2,16,1024]{3,2,1,0:T(8,128)} %param.15) | copy-start | bytes 786436
  24.2 5.2 %copy-start.32 = (s32[128]{0:T(128)S(1)}, s32[128]{0:T(128)}, u32[]{:S(2)}) copy-start(s32[128]{0:T(128)} %and_select_fusion.2) | copy-start | bytes 1540
  24.2 5.6 %copy-start.34 = (s32[1,128]{1,0:T(1,128)S(1)}, s32[1,128]{1,0:T(1,128)}, u32[]{:S(2)}) copy-start(s32[1,128]{1,0:T(1,128)} %param.24) | copy-start | bytes 1540
  24.2 5.6 %copy-start.36 = (f32[1,128]{1,0:T(1,128)S(1)}, f32[1,128]{1,0:T(1,128)}, u32[]{:S(2)}) copy-start(f32[1,128]{1,0:T(1,128)} %param.25) | copy-start | bytes 1540
  24.2 5.8 %copy-start.31 = (f32[1,16]{1,0:T(1,128)S(1)}, f32[1,16]{1,0:T(1,128)}, u32[]{:S(2)}) copy-start(f32[1,16]{1,0:T(1,128)} %fusion.64) | copy-start | bytes 196
  24.2 11.0 %copy-start.30 = (f32[2064]{0:T(1024)S(1)}, f32[2064]{0:T(1024)}, u32[]{:S(2)}) copy-start(f32[2064]{0:T(1024)} %copy-done.29) | copy-start | bytes 24772
  24.5 14.1 %copy-start.3 = (f32[6,4096]{1,0:T(8,128)}, f32[6,4096]{1,0:T(8,128)S(1)}, u32[]{:S(2)}) copy-start(f32[6,4096]{1,0:T(8,128)S(1)} %multiply_reduce_fusion) | copy-start | bytes 294916
  25.3 18.1 %collective-permute-start.3 = (f32[6,2064]{1,0:T(8,128)}, f32[6,2064]{1,0:T(8,128)}, u32[]{:S(2)}, u32[]{:S(2)}) collective-permute-start(f32[6,2064]{1,0:T(8,128)} %pad_maximum_fusion.7), channel_id=1, source_target_pairs={{0,4},{4,8},{8,12},{12,16},{16,20},{20,24},{24,28},{1,5},{5,9},{9,... | collective-permute-start | bytes 148616 | tf_op jit(solution)/shard_map/ppermute | solution.py:13
  30.0 5.9 %collective-permute-start.6 = (f32[4,16]{1,0:T(4,128)S(1)}, f32[4,16]{1,0:T(4,128)S(1)}, u32[]{:S(2)}, u32[]{:S(2)}) collective-permute-start(f32[4,16]{1,0:T(4,128)S(1)} %pad_maximum_fusion.11), channel_id=1, source_target_pairs={{0,2},{1,3},{2,0},{3,1},{4,6},{5,7},{6,4},{7,5},{8,10},{9,11},{10,... | collective-permute-start | bytes 776 | tf_op jit(solution)/shard_map/ppermute | solution.py:165
  32.0 3.9 %collective-permute-start.4 = (f32[10,1024]{1,0:T(8,128)S(1)}, f32[10,1024]{1,0:T(8,128)S(1)}, u32[]{:S(2)}, u32[]{:S(2)}) collective-permute-start(f32[10,1024]{1,0:T(8,128)S(1)} %get-tuple-element.71), channel_id=1, source_target_pairs={{0,3},{1,0},{2,1},{3,2},{4,7},{5,4},{6,5},{7,6},{8,11},{9,8},{10,9... | collective-permute-start | bytes 122888 | tf_op jit(solution)/shard_map/ppermute | solution.py:165
  33.2 3.7 %collective-permute-start.5 = (f32[10,1024]{1,0:T(8,128)S(1)}, f32[10,1024]{1,0:T(8,128)S(1)}, u32[]{:S(2)}, u32[]{:S(2)}) collective-permute-start(f32[10,1024]{1,0:T(8,128)S(1)} %get-tuple-element.70), channel_id=1, source_target_pairs={{0,1},{1,2},{2,3},{3,0},{4,5},{5,6},{6,7},{7,4},{8,9},{9,10},{10,1... | collective-permute-start | bytes 122888 | tf_op jit(solution)/shard_map/ppermute | solution.py:165
  34.0 9.4 %collective-permute-start.2 = (f32[6,2064]{1,0:T(8,128)}, f32[6,2064]{1,0:T(8,128)}, u32[]{:S(2)}, u32[]{:S(2)}) collective-permute-start(f32[6,2064]{1,0:T(8,128)} %pad_maximum_fusion.6), channel_id=1, source_target_pairs={{4,0},{8,4},{12,8},{16,12},{20,16},{24,20},{28,24},{5,1},{9,5},{13... | collective-permute-start | bytes 148616 | tf_op jit(solution)/shard_map/ppermute | solution.py:13
  37.2 6.2 %copy-start.25 = (f32[2048]{0:T(1024)S(1)}, f32[2048]{0:T(1024)}, u32[]{:S(2)}) copy-start(f32[2048]{0:T(1024)} %slice.421) | copy-start | bytes 24580
  45.3 7.0 %copy-start.12 = (f32[16,1024]{1,0:T(8,128)S(1)}, f32[16,1024]{1,0:T(8,128)}, u32[]{:S(2)}) copy-start(f32[16,1024]{1,0:T(8,128)} %copy-done.11) | copy-start | bytes 196612
  45.3 7.0 %copy-start.14 = (f32[16,1024]{1,0:T(8,128)S(1)}, f32[16,1024]{1,0:T(8,128)}, u32[]{:S(2)}) copy-start(f32[16,1024]{1,0:T(8,128)} %copy-done.13) | copy-start | bytes 196612
  45.3 7.0 %copy-start.19 = (f32[16,1024]{1,0:T(8,128)S(1)}, f32[16,1024]{1,0:T(8,128)}, u32[]{:S(2)}) copy-start(f32[16,1024]{1,0:T(8,128)} %get-tuple-element.28) | copy-start | bytes 196612
  45.3 7.0 %copy-start.20 = (f32[16,1024]{1,0:T(8,128)S(1)}, f32[16,1024]{1,0:T(8,128)}, u32[]{:S(2)}) copy-start(f32[16,1024]{1,0:T(8,128)} %get-tuple-element.29) | copy-start | bytes 196612
  54.0 13.4 %copy-start.7 = (f32[16,1024]{1,0:T(8,128)S(1)}, f32[16,1024]{1,0:T(8,128)}, u32[]{:S(2)}) copy-start(f32[16,1024]{1,0:T(8,128)} %copy-done.6) | copy-start | bytes 196612
  54.0 13.4 %copy-start.9 = (f32[16,1024]{1,0:T(8,128)S(1)}, f32[16,1024]{1,0:T(8,128)}, u32[]{:S(2)}) copy-start(f32[16,1024]{1,0:T(8,128)} %copy-done.8) | copy-start | bytes 196612
  54.0 13.4 %copy-start.24 = (f32[2,2,16,1024]{3,2,1,0:T(8,128)S(1)}, f32[2,2,16,1024]{3,2,1,0:T(8,128)}, u32[]{:S(2)}) copy-start(f32[2,2,16,1024]{3,2,1,0:T(8,128)} %param.16) | copy-start | bytes 786436
  54.2 16.7 %copy-start.5 = (f32[16,1024]{1,0:T(8,128)S(1)}, f32[16,1024]{1,0:T(8,128)}, u32[]{:S(2)}) copy-start(f32[16,1024]{1,0:T(8,128)} %copy-done.4) | copy-start | bytes 196612
  54.2 16.7 %copy-start.16 = (f32[16,1024]{1,0:T(8,128)S(1)}, f32[16,1024]{1,0:T(8,128)}, u32[]{:S(2)}) copy-start(f32[16,1024]{1,0:T(8,128)} %copy-done.15) | copy-start | bytes 196612
  54.2 16.7 %copy-start.18 = (f32[16,1024]{1,0:T(8,128)S(1)}, f32[16,1024]{1,0:T(8,128)}, u32[]{:S(2)}) copy-start(f32[16,1024]{1,0:T(8,128)} %copy-done.17) | copy-start | bytes 196612
  68.4 9.6 %all-to-all-start.1 = ((f32[32,1,4]{2,1,0:T(1,128)}), f32[32,1,4]{2,1,0:T(1,128)S(1)}, u32[]{:S(2)}, u32[]{:S(2)}) async-start(f32[32,1,4]{2,1,0:T(1,128)} %broadcast_in_dim.31), calls=%async_computation.1 | async-start | bytes 32768 | tf_op jit(solution)/shard_map/all_to_all | solution.py:36
  (13 other events, 18.9 us)

commit v11 on v10

--- a/solution.py
+++ b/solution.py
@@ -131,7 +131,14 @@
         placed = onehot_dot(spread, onehot, ((1,), (0,)), split)
         return placed.reshape(parts, layer_count, column_count)
 
-    fault_at = locate(jnp.concatenate([fault_near.reshape(-1), fault_far.reshape(-1)]))
+    edge_cells = jnp.concatenate(
+        [layer_iota * column_count, layer_iota * column_count + (column_count - 1)]
+    )
+    fault_at = locate(
+        jnp.concatenate([fault_near.reshape(-1), fault_far.reshape(-1), edge_cells])
+    )
+    west_face = east_edge
+    east_face = trans_east[:, -1]
     well_at = locate(compl_cell)
     well_index = compl_wi.reshape(-1)
     well_onehot = (
@@ -169,7 +176,7 @@
         scaled = (mobile * fields).reshape(count * 2, layer_count, column_count)
         picks = gather(scaled, fault_at, split2)
         picks_near = picks[:, :slot_count]
-        picks_far = picks[:, slot_count:]
+        picks_far = picks[:, slot_count : 2 * slot_count]
         from_left = shifted(jnp.concatenate([scaled[:, :, -1], picks_near], axis=1), "cells", 1)
         from_right = shifted(jnp.concatenate([scaled[:, :, 0], picks_far], axis=1), "cells", -1)
         pressure = fields[:, 0]
@@ -199,10 +206,19 @@
             summed = summed + slab_shift(local, by)
         from_above = from_above[:halo_rows]
         from_below = from_below[:halo_rows]
-        west = jnp.concatenate([from_left[:, :layer_count, None], scaled[:, :, :-1]], axis=2)
-        east = jnp.concatenate([scaled[:, :, 1:], from_right[:, :layer_count, None]], axis=2)
-        above = jnp.concatenate([from_above[:, None, :], scaled[:, :-1, :]], axis=1)
-        below = jnp.concatenate([scaled[:, 1:, :], from_below[:, None, :]], axis=1)
+        zero_column = jnp.zeros_like(scaled[:, :, :1])
+        west = jnp.concatenate([zero_column, scaled[:, :, :-1]], axis=2)
+        east = jnp.concatenate([scaled[:, :, 1:], zero_column], axis=2)
+        above = jnp.where(
+            layer_ids == 0,
+            from_above[:, None, :],
+            jnp.pad(scaled[:, :-1, :], ((0, 0), (1, 0), (0, 0))),
+        )
+        below = jnp.where(
+            layer_ids == layer_count - 1,
+            from_below[:, None, :],
+            jnp.pad(scaled[:, 1:, :], ((0, 0), (0, 1), (0, 0))),
+        )
         laplace = (
             trans_east * (scaled - east)
             + trans_west * (scaled - west)
@@ -212,7 +228,17 @@
         flux_right = weight_here * (picks_near - from_right[:, layer_count:])
         flux_left = weight_left * (from_left[:, layer_count:] - picks_far)
         fault_term = scatter(
-            jnp.concatenate([flux_right, -flux_left], axis=1), fault_at, split2
+            jnp.concatenate(
+                [
+                    flux_right,
+                    -flux_left,
+                    -west_face * from_left[:, :layer_count],
+                    -east_face * from_right[:, :layer_count],
+                ],
+                axis=1,
+            ),
+            fault_at,
+            split2,
         )
         laplace = (laplace + fault_term).reshape(count, 2, layer_count, column_count)
         back = jnp.dot(summed[1:] / summed[0], well_onehot.T, precision=highest)

time: 79.6 us -> 74.7 us (0.938)
  local copies, waits for them, and re-layouts: 14.5 us -> 8.56 us
  blocking collectives: 12.2 us -> 13.7 us
  other arithmetic: 16 us -> 14.8 us
    neg x0 -> x3, other arithmetic: none -> 1.84 us  [the longest x1 0.75 us: operator(): -flux_left]
    concatenate x4 -> x2, local copies, waits for them, and re-layouts: 4.18 us -> 2.38 us  [the longest x1 1.59 us: operator(): jnp.concatenate([flux_right, -flux_left, -west_face * from_left[:, :layer...]
    all_to_all x1, blocking collectives: 12.2 us -> 13.7 us  [global_sum(): gathered = lax.all_to_all(copies, axes, 0, 0, tiled=True)]
    slice x1 -> x2, local copies, waits for them, and re-layouts: 1.36 us -> 0.01 us  [operator(): from_above = from_above[:halo_rows]]
    slice x7 -> x5, local copies, waits for them, and re-layouts: 2.69 us -> 1.34 us  [the longest x1 0.96 us: operator(): scaled[:, 1:, :]]
    add x1, other arithmetic: 1.63 us -> 0.37 us  [operator(): laplace + fault_term]
    mul x1 -> x3, other arithmetic: 1.09 us -> 0.01 us  [the longest x1 0.01 us: per_device(): layer_iota * column_count]
    ppermute x3, waiting for transfers between devices: 1.02 us -> 0.01 us  [slab_shift(): lax.ppermute(value, 'slab', [(i, (i + by) % count) for i in range(count)])]
  transfers between devices with their start and end apart: 8 -> 8, of which waited for: 2 -> 2; matrix products, arithmetic and copies ran while one was open for 20% -> 16% of each run, Pallas kernels for 0% -> 0%
where the time goes in v11:
time: 74.7 us; the launch traced here: 74.1 us
  starting transfers between devices  18 us (24%)
  other arithmetic  14.8 us (20%)
  blocking collectives  13.7 us (18%)
  matrix products  9.89 us (13%)
  local copies, waits for them, and re-layouts  8.56 us (11%)
  waiting for transfers between devices  6.85 us (9%)
  between operations  2.31 us (3%)
    all_to_all x1, blocking collectives, global_sum(): gathered = lax.all_to_all(copies, axes, 0, 0, tiled=True)  13.7 us
    ppermute x4, starting transfers between devices, shifted(): return lax.ppermute(value, axis, pairs)  11.9 us
    dot_general x4, matrix products, onehot_dot(): lax.dot_general(pieces, onehot, (dims, ((), ())), preferred_element_type=...  8.74 us
    all_to_all x1, waiting for transfers between devices, global_sum(): gathered = lax.all_to_all(copies, axes, 0, 0, tiled=True)  6.31 us
    ppermute x3, starting transfers between devices, slab_shift(): lax.ppermute(value, 'slab', [(i, (i + by) % count) for i in range(count)])  3.52 us
    all_to_all x1, starting transfers between devices, global_sum(): gathered = lax.all_to_all(copies, axes, 0, 0, tiled=True)  2.56 us
    select_n x2, other arithmetic, per_device(): weight_here = jnp.where(slot_live, fault_trans.reshape(-1), zero_value)  2.01 us
    unnamed x101, local copies, waits for them, and re-layouts  1.87 us
  transfers between devices with their start and end apart: 8, of which 2 were waited for; matrix products, arithmetic and copies ran while one was open for 16% of the time, Pallas kernels for 0%

profile of v11, /device:TPU:0, one launch (start us, length us, event | category | flops | bytes accessed | tf_op | source)
XLA Modules:
  0.0 74.1 jit_solution(6602518623416473526)
XLA Ops:
  0.7 0.9 %broadcast_select_fusion.1 = f32[16,1024]{1,0:T(8,128)S(1)} fusion(f32[16,1024]{1,0:T(8,128)} %param.17, pred[1024]{0:T(1024)(128)(4,1)S(1)} %fusion.71), kind=kLoop, calls=%fused_computation.160 | loop fusion | flops 16384 | bytes 132096 | tf_op jit(solution)/shard_map/jit(_where)/select_n | solution.py:91
  2.4 0.7 fusion.69
  3.2 4.9 %collective-permute-start = (f32[2064]{0:T(1024)S(1)}, f32[2064]{0:T(1024)S(1)}, u32[]{:S(2)}, u32[]{:S(2)}) collective-permute-start(f32[2064]{0:T(1024)S(1)} %pad_maximum_fusion.9), channel_id=1, source_target_pairs={{0,4},{4,8},{8,12},{12,16},{16,20},{20,24},{24,28},{1,5},{5,9},{9,... | collective-permute-start | bytes 24776 | tf_op jit(solution)/shard_map/ppermute | solution.py:13
  8.1 0.9 %broadcast_select_fusion = f32[16,1024]{1,0:T(8,128)S(1)} fusion(f32[16,1024]{1,0:T(8,128)} %param.18, pred[16]{0:T(512)(128)(4,1)S(1)} %broadcast_and_fusion), kind=kLoop, calls=%fused_computation.159 | loop fusion | flops 16384 | bytes 131088 | tf_op jit(solution)/shard_map/jit(_where)/select_n | solution.py:94
  9.0 1.5 %collective-permute-start.1 = (f32[1024]{0:T(1024)S(1)}, f32[1024]{0:T(1024)S(1)}, u32[]{:S(2)}, u32[]{:S(2)}) collective-permute-start(f32[1024]{0:T(1024)S(1)} %bitcast.400), channel_id=1, source_target_pairs={{0,1},{1,2},{2,3},{4,5},{5,6},{6,7},{8,9},{9,10},{10,11},{12,13},{... | collective-permute-start | bytes 12296 | tf_op jit(solution)/shard_map/ppermute | solution.py:13
  10.5 1.2 %and_select_fusion.2 = s32[128]{0:T(128)} fusion(s32[1,128]{1,0:T(1,128)} %param.23), kind=kLoop, calls=%fused_computation.201 | loop fusion | flops 1408 | bytes 1024 | tf_op jit(solution)/shard_map/jit(remainder)/select_n | solution.py:115
  11.7 0.7 fusion.78
  12.4 1.0 %fusion.93 = (f32[1,2,16,1024]{3,2,1,0:T(8,128)S(1)}, f32[1,2,16,1024]{3,2,1,0:T(8,128)S(1)}) fusion(f32[2,2,16,1024]{3,2,1,0:T(8,128)} %param.15), kind=kLoop, calls=%fused_computation.228 | loop fusion | bytes 524288 | tf_op jit(solution)/shard_map/slice | solution.py:150
  13.5 0.8 %concatenate.103 = s32[4128]{0:T(1024)S(1)} concatenate(s32[2048]{0:T(1024)} %bitcast.397, s32[2048]{0:T(1024)} %bitcast.398, s32[16]{0:T(128)S(1)} %get-tuple-element.76, s32[16]{0:T(128)S(1)} %get-tuple-element.77), dimensions={0} | concatenate | bytes 33024 | tf_op jit(solution)/shard_map/concatenate | solution.py:138
  14.3 0.6 add_select_fusion
  14.9 1.3 %and_select_fusion = f32[1,2048]{1,0:T(1,128)} fusion(f32[1,2048]{1,0:T(1,128)} %param.21, pred[]{:T(512)S(6)} %lt.34, s32[]{:T(128)} %bitcast.339), kind=kLoop, calls=%fused_computation.161 | loop fusion | flops 6144 | bytes 16389 | tf_op jit(solution)/shard_map/jit(_where)/select_n | solution.py:101
  16.3 0.8 %fusion.56 = f32[1,16]{1,0:T(1,128)} fusion(s32[128]{0:T(128)S(1)} %bitcast.401, f32[1,128]{1,0:T(1,128)S(1)} %copy-done.41), kind=kOutput, calls=%fused_computation.142 | convolution fusion | flops 26624 | bytes 1088 | tf_op jit(solution)/shard_map/dot_general | solution.py:186
  17.7 0.6 neg.47
  18.9 0.7 fusion.45
  21.1 1.0 %fusion.92 = (f32[6,15,1024]{2,1,0:T(8,128)}, f32[6,15,1024]{2,1,0:T(8,128)}) fusion(f32[6,16,1024]{2,1,0:T(8,128)S(1)} %bitcast.343), kind=kLoop, calls=%fused_computation.227 | loop fusion | bytes 1474560 | tf_op jit(solution)/shard_map/slice | solution.py:220
  22.0 4.3 %fusion.1 = f32[192,4128]{1,0:T(8,128)S(1)} fusion(s32[4128]{0:T(1024)S(1)} %copy-done.29, bf16[96,1024]{1,0:T(8,128)(2,1)S(1)} %get-tuple-element.22, bf16[96,1024]{1,0:T(8,128)(2,1)S(1)} %get-tuple-element.23), kind=kOutput, calls=%fused_computation.2 | convolution fusion | flops 1628209152 | bytes 3580032 | tf_op jit(solution)/shard_map/dot_general | solution.py:58
  27.0 1.3 %collective-permute-start.4 = (f32[6,2064]{1,0:T(8,128)S(1)}, f32[6,2064]{1,0:T(8,128)S(1)}, u32[]{:S(2)}, u32[]{:S(2)}) collective-permute-start(f32[6,2064]{1,0:T(8,128)S(1)} %pad_maximum_fusion.5), channel_id=1, source_target_pairs={{4,0},{8,4},{12,8},{16,12},{20,16},{24,20},{28,24},{5,1},{9,5},{13... | collective-permute-start | bytes 148616 | tf_op jit(solution)/shard_map/ppermute | solution.py:13
  29.0 2.0 %collective-permute-start.6 = (f32[4,16]{1,0:T(4,128)S(1)}, f32[4,16]{1,0:T(4,128)S(1)}, u32[]{:S(2)}, u32[]{:S(2)}) collective-permute-start(f32[4,16]{1,0:T(4,128)S(1)} %pad_maximum_fusion.10), channel_id=1, source_target_pairs={{0,2},{1,3},{2,0},{3,1},{4,6},{5,7},{6,4},{7,5},{8,10},{9,11},{10,... | collective-permute-start | bytes 776 | tf_op jit(solution)/shard_map/ppermute | solution.py:172
  31.0 1.5 %collective-permute-start.2 = (f32[10,1024]{1,0:T(8,128)S(1)}, f32[10,1024]{1,0:T(8,128)S(1)}, u32[]{:S(2)}, u32[]{:S(2)}) collective-permute-start(f32[10,1024]{1,0:T(8,128)S(1)} %get-tuple-element.72), channel_id=1, source_target_pairs={{0,3},{1,0},{2,1},{3,2},{4,7},{5,4},{6,5},{7,6},{8,11},{9,8},{10,9... | collective-permute-start | bytes 122888 | tf_op jit(solution)/shard_map/ppermute | solution.py:172
  32.6 4.3 %collective-permute-start.5 = (f32[6,2064]{1,0:T(8,128)S(1)}, f32[6,2064]{1,0:T(8,128)S(1)}, u32[]{:S(2)}, u32[]{:S(2)}) collective-permute-start(f32[6,2064]{1,0:T(8,128)S(1)} %pad_maximum_fusion.6), channel_id=1, source_target_pairs={{0,4},{4,8},{8,12},{12,16},{16,20},{20,24},{24,28},{1,5},{5,9},{9,... | collective-permute-start | bytes 148616 | tf_op jit(solution)/shard_map/ppermute | solution.py:13
  37.7 0.7 slice_add_fusion.3
  38.9 0.7 %fusion.40 = (f32[6,2048]{1,0:T(8,128)}, f32[6,2048]{1,0:T(8,128)}) fusion(f32[6,2064]{1,0:T(8,128)S(1)} %collective-permute-done.5, f32[2048]{0:T(1024)S(1)} %slice.419, f32[6,4128]{1,0:T(8,128)S(1)} %multiply_reduce_fusion, f32[6,2064]{1,0:T(8,128)S(1)} %collective-permute-done.4, f32[2048]{0:T(1024)S(1)} %bitcast.377), kind=kLoop, calls=%fused_computation.99 | loop fusion | flops 61440 | bytes 311296 | tf_op jit(solution)/shard_map/neg | solution.py:234
  39.7 1.6 %concatenate.106 = f32[6,4128]{1,0:T(8,128)} concatenate(f32[6,2048]{1,0:T(8,128)} %get-tuple-element.54, f32[6,2048]{1,0:T(8,128)} %get-tuple-element.53, f32[6,16]{1,0:T(8,128)S(1)} %slice_multiply_fusion.5, f32[6,16]{1,0:T(8,128)S(1)} %slice_multiply_fusion.4), dimensions={1} | concatenate | bytes 198144 | tf_op jit(solution)/shard_map/concatenate | solution.py:231
  41.3 1.0 %broadcast_multiply_fusion = f32[6,16,4128]{2,1,0:T(8,128)S(1)} fusion(f32[6,4128]{1,0:T(8,128)} %concatenate.106, f32[16,4128]{1,0:T(8,128)S(1)} %fusion.20), kind=kLoop, calls=%fused_computation.15 | loop fusion | flops 396288 | bytes 1948416 | tf_op jit(solution)/shard_map/mul | solution.py:130
  42.4 0.6 copy-done.30
  43.1 3.8 %fusion = f32[192,1024]{1,0:T(8,128)S(1)} fusion(s32[4128]{0:T(1024)S(1)} %copy-done.30, bf16[96,4128]{1,0:T(8,128)(2,1)S(1)} %get-tuple-element.20, bf16[96,4128]{1,0:T(8,128)(2,1)S(1)} %get-tuple-element.21), kind=kOutput, calls=%fused_computation.1 | convolution fusion | flops 1630593024 | bytes 2388096 | tf_op jit(solution)/shard_map/dot_general | solution.py:58
  48.8 13.7 %all_to_all.12 = f32[32,1,10]{2,1,0:T(1,128)S(1)} all-to-all(f32[32,1,10]{2,1,0:T(1,128)S(1)} %broadcast_in_dim.53), channel_id=1, replica_groups=mesh['cells'=8,'slab'=4] {'cells','slab'}, dimensions={0} | all-to-all | bytes 2560 | tf_op jit(solution)/shard_map/all_to_all | solution.py:36
  63.0 0.6 broadcast_in_dim.55
  63.7 2.6 %all-to-all-start.1 = ((f32[32,1,4]{2,1,0:T(1,128)}), f32[32,1,4]{2,1,0:T(1,128)S(1)}, u32[]{:S(2)}, u32[]{:S(2)}) async-start(f32[32,1,4]{2,1,0:T(1,128)} %broadcast_in_dim.55), calls=%async_computation.1 | async-start | bytes 32768 | tf_op jit(solution)/shard_map/all_to_all | solution.py:36
  66.3 0.7 pad_maximum_fusion.2
  67.1 6.3 %all-to-all-done.1 = f32[32,1,4]{2,1,0:T(1,128)S(1)} async-done(((f32[32,1,4]{2,1,0:T(1,128)}), f32[32,1,4]{2,1,0:T(1,128)S(1)}, u32[]{:S(2)}, u32[]{:S(2)}) %all-to-all-start.1) | async-done | bytes 544 | tf_op jit(solution)/shard_map/all_to_all | solution.py:36
  73.4 0.7 sqrt.8
  (178 shorter events, 7.9 us)
Async XLA Ops:
  0.6 15.6 %copy-start = (f32[2,4,16,1024]{3,2,1,0:T(8,128)S(1)}, f32[2,4,16,1024]{3,2,1,0:T(8,128)}, u32[]{:S(2)}) copy-start(f32[2,4,16,1024]{3,2,1,0:T(8,128)} %param.14) | copy-start | bytes 1572868
  0.6 15.6 %copy-start.39 = (s32[1,128]{1,0:T(1,128)S(1)}, s32[1,128]{1,0:T(1,128)}, u32[]{:S(2)}) copy-start(s32[1,128]{1,0:T(1,128)} %param.24) | copy-start | bytes 1540
  0.7 15.6 %copy-start.41 = (f32[1,128]{1,0:T(1,128)S(1)}, f32[1,128]{1,0:T(1,128)}, u32[]{:S(2)}) copy-start(f32[1,128]{1,0:T(1,128)} %param.25) | copy-start | bytes 1540
  1.6 17.3 %copy-start.12 = (f32[16,1024]{1,0:T(8,128)}, f32[16,1024]{1,0:T(8,128)S(1)}, u32[]{:S(2)}) copy-start(f32[16,1024]{1,0:T(8,128)S(1)} %broadcast_select_fusion.1) | copy-start | bytes 196612
  3.2 15.1 %collective-permute-start = (f32[2064]{0:T(1024)S(1)}, f32[2064]{0:T(1024)S(1)}, u32[]{:S(2)}, u32[]{:S(2)}) collective-permute-start(f32[2064]{0:T(1024)S(1)} %pad_maximum_fusion.9), channel_id=1, source_target_pairs={{0,4},{4,8},{8,12},{12,16},{16,20},{20,24},{24,28},{1,5},{5,9},{9,... | collective-permute-start | bytes 24776 | tf_op jit(solution)/shard_map/ppermute | solution.py:13
  9.0 9.9 %copy-start.14 = (f32[16,1024]{1,0:T(8,128)}, f32[16,1024]{1,0:T(8,128)S(1)}, u32[]{:S(2)}) copy-start(f32[16,1024]{1,0:T(8,128)S(1)} %broadcast_select_fusion) | copy-start | bytes 196612
  9.0 9.9 %collective-permute-start.1 = (f32[1024]{0:T(1024)S(1)}, f32[1024]{0:T(1024)S(1)}, u32[]{:S(2)}, u32[]{:S(2)}) collective-permute-start(f32[1024]{0:T(1024)S(1)} %bitcast.400), channel_id=1, source_target_pairs={{0,1},{1,2},{2,3},{4,5},{5,6},{6,7},{8,9},{9,10},{10,11},{12,13},{... | collective-permute-start | bytes 12296 | tf_op jit(solution)/shard_map/ppermute | solution.py:13
  12.4 6.5 %copy-start.1 = (f32[2,2,16,1024]{3,2,1,0:T(8,128)S(1)}, f32[2,2,16,1024]{3,2,1,0:T(8,128)}, u32[]{:S(2)}) copy-start(f32[2,2,16,1024]{3,2,1,0:T(8,128)} %param.13) | copy-start | bytes 786436
  12.4 6.5 %copy-start.2 = (f32[2,2,16,1024]{3,2,1,0:T(8,128)S(1)}, f32[2,2,16,1024]{3,2,1,0:T(8,128)}, u32[]{:S(2)}) copy-start(f32[2,2,16,1024]{3,2,1,0:T(8,128)} %param.15) | copy-start | bytes 786436
  12.4 6.5 %copy-start.22 = (f32[16,1024]{1,0:T(8,128)S(1)}, f32[16,1024]{1,0:T(8,128)}, u32[]{:S(2)}) copy-start(f32[16,1024]{1,0:T(8,128)} %param.17) | copy-start | bytes 196612
  12.4 6.5 %copy-start.23 = (f32[16,1024]{1,0:T(8,128)S(1)}, f32[16,1024]{1,0:T(8,128)}, u32[]{:S(2)}) copy-start(f32[16,1024]{1,0:T(8,128)} %param.18) | copy-start | bytes 196612
  26.6 10.3 %copy-start.32 = (f32[2064]{0:T(1024)S(1)}, f32[2064]{0:T(1024)}, u32[]{:S(2)}) copy-start(f32[2064]{0:T(1024)} %copy-done.31) | copy-start | bytes 24772
  27.0 11.4 %collective-permute-start.4 = (f32[6,2064]{1,0:T(8,128)S(1)}, f32[6,2064]{1,0:T(8,128)S(1)}, u32[]{:S(2)}, u32[]{:S(2)}) collective-permute-start(f32[6,2064]{1,0:T(8,128)S(1)} %pad_maximum_fusion.5), channel_id=1, source_target_pairs={{4,0},{8,4},{12,8},{16,12},{20,16},{24,20},{28,24},{5,1},{9,5},{13... | collective-permute-start | bytes 148616 | tf_op jit(solution)/shard_map/ppermute | solution.py:13
  28.3 10.1 %copy-start.34 = (f32[16]{0:T(128)S(1)}, f32[16]{0:T(128)}, u32[]{:S(2)}) copy-start(f32[16]{0:T(128)} %neg.47) | copy-start | bytes 196
  28.3 10.6 %copy-start.35 = (f32[16]{0:T(128)S(1)}, f32[16]{0:T(128)}, u32[]{:S(2)}) copy-start(f32[16]{0:T(128)} %get-tuple-element.70) | copy-start | bytes 196
  28.3 10.6 %copy-start.28 = (f32[1,2048]{1,0:T(1,128)S(1)}, f32[1,2048]{1,0:T(1,128)}, u32[]{:S(2)}) copy-start(f32[1,2048]{1,0:T(1,128)} %and_select_fusion) | copy-start | bytes 24580
  29.0 8.0 %collective-permute-start.6 = (f32[4,16]{1,0:T(4,128)S(1)}, f32[4,16]{1,0:T(4,128)S(1)}, u32[]{:S(2)}, u32[]{:S(2)}) collective-permute-start(f32[4,16]{1,0:T(4,128)S(1)} %pad_maximum_fusion.10), channel_id=1, source_target_pairs={{0,2},{1,3},{2,0},{3,1},{4,6},{5,7},{6,4},{7,5},{8,10},{9,11},{10,... | collective-permute-start | bytes 776 | tf_op jit(solution)/shard_map/ppermute | solution.py:172
  31.0 6.0 %collective-permute-start.2 = (f32[10,1024]{1,0:T(8,128)S(1)}, f32[10,1024]{1,0:T(8,128)S(1)}, u32[]{:S(2)}, u32[]{:S(2)}) collective-permute-start(f32[10,1024]{1,0:T(8,128)S(1)} %get-tuple-element.72), channel_id=1, source_target_pairs={{0,3},{1,0},{2,1},{3,2},{4,7},{5,4},{6,5},{7,6},{8,11},{9,8},{10,9... | collective-permute-start | bytes 122888 | tf_op jit(solution)/shard_map/ppermute | solution.py:172
  32.5 4.5 %collective-permute-start.3 = (f32[10,1024]{1,0:T(8,128)S(1)}, f32[10,1024]{1,0:T(8,128)S(1)}, u32[]{:S(2)}, u32[]{:S(2)}) collective-permute-start(f32[10,1024]{1,0:T(8,128)S(1)} %get-tuple-element.73), channel_id=1, source_target_pairs={{0,1},{1,2},{2,3},{3,0},{4,5},{5,6},{6,7},{7,4},{8,9},{9,10},{10,1... | collective-permute-start | bytes 122888 | tf_op jit(solution)/shard_map/ppermute | solution.py:172
  32.6 6.3 %collective-permute-start.5 = (f32[6,2064]{1,0:T(8,128)S(1)}, f32[6,2064]{1,0:T(8,128)S(1)}, u32[]{:S(2)}, u32[]{:S(2)}) collective-permute-start(f32[6,2064]{1,0:T(8,128)S(1)} %pad_maximum_fusion.6), channel_id=1, source_target_pairs={{0,4},{4,8},{8,12},{12,16},{16,20},{20,24},{24,28},{1,5},{5,9},{9,... | collective-permute-start | bytes 148616 | tf_op jit(solution)/shard_map/ppermute | solution.py:13
  43.0 3.9 %copy-start.20 = (f32[16,1024]{1,0:T(8,128)S(1)}, f32[16,1024]{1,0:T(8,128)}, u32[]{:S(2)}) copy-start(f32[16,1024]{1,0:T(8,128)} %get-tuple-element.28) | copy-start | bytes 196612
  43.0 3.9 %copy-start.21 = (f32[16,1024]{1,0:T(8,128)S(1)}, f32[16,1024]{1,0:T(8,128)}, u32[]{:S(2)}) copy-start(f32[16,1024]{1,0:T(8,128)} %get-tuple-element.29) | copy-start | bytes 196612
  43.0 3.9 %slice-start = ((f32[10,1024]{1,0:T(8,128)}), f32[6,1024]{1,0:T(8,128)S(1)}, s32[]{:S(2)}) async-start(f32[10,1024]{1,0:T(8,128)} %copy-done.26), calls=%async_computation.2 | async-start | bytes 65536 | tf_op jit(solution)/shard_map/slice | solution.py:208
  43.1 3.9 %slice-start.1 = ((f32[10,1024]{1,0:T(8,128)}), f32[6,1024]{1,0:T(8,128)S(1)}, s32[]{:S(2)}) async-start(f32[10,1024]{1,0:T(8,128)} %copy-done.27), calls=%async_computation.3 | async-start | bytes 65536 | tf_op jit(solution)/shard_map/slice | solution.py:207
  43.1 3.9 %copy-start.37 = (pred[16]{0:T(512)(128)(4,1)S(1)}, pred[16]{0:T(512)(128)(4,1)}, u32[]{:S(2)}) copy-start(pred[16]{0:T(512)(128)(4,1)} %get-tuple-element.78) | copy-start | bytes 52
  47.8 14.8 %copy-start.8 = (f32[16,1024]{1,0:T(8,128)S(1)}, f32[16,1024]{1,0:T(8,128)}, u32[]{:S(2)}) copy-start(f32[16,1024]{1,0:T(8,128)} %copy-done.7) | copy-start | bytes 196612
  47.8 14.8 %copy-start.10 = (f32[16,1024]{1,0:T(8,128)S(1)}, f32[16,1024]{1,0:T(8,128)}, u32[]{:S(2)}) copy-start(f32[16,1024]{1,0:T(8,128)} %copy-done.9) | copy-start | bytes 196612
  47.9 14.8 %copy-start.25 = (f32[2,2,16,1024]{3,2,1,0:T(8,128)S(1)}, f32[2,2,16,1024]{3,2,1,0:T(8,128)}, u32[]{:S(2)}) copy-start(f32[2,2,16,1024]{3,2,1,0:T(8,128)} %param.16) | copy-start | bytes 786436
  48.0 18.2 %copy-start.6 = (f32[16,1024]{1,0:T(8,128)S(1)}, f32[16,1024]{1,0:T(8,128)}, u32[]{:S(2)}) copy-start(f32[16,1024]{1,0:T(8,128)} %copy-done.5) | copy-start | bytes 196612
  48.0 18.2 %copy-start.17 = (f32[16,1024]{1,0:T(8,128)S(1)}, f32[16,1024]{1,0:T(8,128)}, u32[]{:S(2)}) copy-start(f32[16,1024]{1,0:T(8,128)} %copy-done.16) | copy-start | bytes 196612
  48.0 18.2 %copy-start.19 = (f32[16,1024]{1,0:T(8,128)S(1)}, f32[16,1024]{1,0:T(8,128)}, u32[]{:S(2)}) copy-start(f32[16,1024]{1,0:T(8,128)} %copy-done.18) | copy-start | bytes 196612
  63.7 9.7 %all-to-all-start.1 = ((f32[32,1,4]{2,1,0:T(1,128)}), f32[32,1,4]{2,1,0:T(1,128)S(1)}, u32[]{:S(2)}, u32[]{:S(2)}) async-start(f32[32,1,4]{2,1,0:T(1,128)} %broadcast_in_dim.55), calls=%async_computation.1 | async-start | bytes 32768 | tf_op jit(solution)/shard_map/all_to_all | solution.py:36
  (21 other events, 42.9 us)

commit v12 on v11

--- a/solution.py
+++ b/solution.py
@@ -131,8 +131,13 @@
         placed = onehot_dot(spread, onehot, ((1,), (0,)), split)
         return placed.reshape(parts, layer_count, column_count)
 
+    edge_pad = -(2 * layer_count) % 128
     edge_cells = jnp.concatenate(
-        [layer_iota * column_count, layer_iota * column_count + (column_count - 1)]
+        [
+            layer_iota * column_count,
+            layer_iota * column_count + (column_count - 1),
+            jnp.zeros((edge_pad,), jnp.int32),
+        ]
     )
     fault_at = locate(
         jnp.concatenate([fault_near.reshape(-1), fault_far.reshape(-1), edge_cells])
@@ -234,6 +239,7 @@
                     -flux_left,
                     -west_face * from_left[:, :layer_count],
                     -east_face * from_right[:, :layer_count],
+                    jnp.zeros((count * 2, edge_pad), scaled.dtype),
                 ],
                 axis=1,
             ),

time: 74.7 us -> 75.3 us (level)
  no operation moved by 1% of the time
where the time goes in v12:
time: 75.3 us; the launch traced here: 74.7 us
  starting transfers between devices  18 us (24%)
  other arithmetic  14.8 us (20%)
  blocking collectives  13.7 us (18%)
  matrix products  9.95 us (13%)
  local copies, waits for them, and re-layouts  9.15 us (12%)
  waiting for transfers between devices  6.84 us (9%)
  between operations  2.31 us (3%)
    all_to_all x1, blocking collectives, global_sum(): gathered = lax.all_to_all(copies, axes, 0, 0, tiled=True)  13.7 us
    ppermute x4, starting transfers between devices, shifted(): return lax.ppermute(value, axis, pairs)  11.9 us
    dot_general x4, matrix products, onehot_dot(): lax.dot_general(pieces, onehot, (dims, ((), ())), preferred_element_type=...  8.76 us
    all_to_all x1, waiting for transfers between devices, global_sum(): gathered = lax.all_to_all(copies, axes, 0, 0, tiled=True)  6.31 us
    ppermute x3, starting transfers between devices, slab_shift(): lax.ppermute(value, 'slab', [(i, (i + by) % count) for i in range(count)])  3.53 us
    all_to_all x1, starting transfers between devices, global_sum(): gathered = lax.all_to_all(copies, axes, 0, 0, tiled=True)  2.56 us
    select_n x2, other arithmetic, per_device(): weight_here = jnp.where(slot_live, fault_trans.reshape(-1), zero_value)  2.01 us
    unnamed x101, local copies, waits for them, and re-layouts  1.86 us
  transfers between devices with their start and end apart: 8, of which 2 were waited for; matrix products, arithmetic and copies ran while one was open for 16% of the time, Pallas kernels for 0%

profile of v12, /device:TPU:0, one launch (start us, length us, event | category | flops | bytes accessed | tf_op | source)
XLA Modules:
  0.0 74.7 jit_solution(5129306914504013306)
XLA Ops:
  0.7 0.9 %broadcast_select_fusion.1 = f32[16,1024]{1,0:T(8,128)S(1)} fusion(f32[16,1024]{1,0:T(8,128)} %param.17, pred[1024]{0:T(1024)(128)(4,1)S(1)} %fusion.71), kind=kLoop, calls=%fused_computation.160 | loop fusion | flops 16384 | bytes 132096 | tf_op jit(solution)/shard_map/jit(_where)/select_n | solution.py:91
  2.4 0.7 fusion.69
  3.2 4.9 %collective-permute-start = (f32[2064]{0:T(1024)S(1)}, f32[2064]{0:T(1024)S(1)}, u32[]{:S(2)}, u32[]{:S(2)}) collective-permute-start(f32[2064]{0:T(1024)S(1)} %pad_maximum_fusion.9), channel_id=1, source_target_pairs={{0,4},{4,8},{8,12},{12,16},{16,20},{20,24},{24,28},{1,5},{5,9},{9,... | collective-permute-start | bytes 24776 | tf_op jit(solution)/shard_map/ppermute | solution.py:13
  8.1 0.9 %broadcast_select_fusion = f32[16,1024]{1,0:T(8,128)S(1)} fusion(f32[16,1024]{1,0:T(8,128)} %param.18, pred[16]{0:T(512)(128)(4,1)S(1)} %broadcast_and_fusion), kind=kLoop, calls=%fused_computation.159 | loop fusion | flops 16384 | bytes 131088 | tf_op jit(solution)/shard_map/jit(_where)/select_n | solution.py:94
  9.0 1.5 %collective-permute-start.1 = (f32[1024]{0:T(1024)S(1)}, f32[1024]{0:T(1024)S(1)}, u32[]{:S(2)}, u32[]{:S(2)}) collective-permute-start(f32[1024]{0:T(1024)S(1)} %bitcast.400), channel_id=1, source_target_pairs={{0,1},{1,2},{2,3},{4,5},{5,6},{6,7},{8,9},{9,10},{10,11},{12,13},{... | collective-permute-start | bytes 12296 | tf_op jit(solution)/shard_map/ppermute | solution.py:13
  10.5 1.2 %and_select_fusion.2 = s32[128]{0:T(128)} fusion(s32[1,128]{1,0:T(1,128)} %param.23), kind=kLoop, calls=%fused_computation.201 | loop fusion | flops 1408 | bytes 1024 | tf_op jit(solution)/shard_map/jit(remainder)/select_n | solution.py:115
  11.7 0.7 fusion.78
  12.4 1.0 %fusion.93 = (f32[1,2,16,1024]{3,2,1,0:T(8,128)S(1)}, f32[1,2,16,1024]{3,2,1,0:T(8,128)S(1)}) fusion(f32[2,2,16,1024]{3,2,1,0:T(8,128)} %param.15), kind=kLoop, calls=%fused_computation.228 | loop fusion | bytes 524288 | tf_op jit(solution)/shard_map/slice | solution.py:155
  13.4 0.8 %concatenate.103 = s32[4224]{0:T(1024)S(1)} concatenate(s32[2048]{0:T(1024)} %bitcast.397, s32[2048]{0:T(1024)} %bitcast.398, s32[16]{0:T(128)S(1)} %get-tuple-element.76, s32[16]{0:T(128)S(1)} %get-tuple-element.77, s32[96]{0:T(128)S(1)} %broadcast_in_dim.57), dimensions={0} | concatenate | bytes 33792 | tf_op jit(solution)/shard_map/concatenate | solution.py:143
  14.2 0.6 add_select_fusion
  14.9 1.3 %and_select_fusion = f32[1,2048]{1,0:T(1,128)} fusion(f32[1,2048]{1,0:T(1,128)} %param.21, pred[]{:T(512)S(6)} %lt.34, s32[]{:T(128)} %bitcast.339), kind=kLoop, calls=%fused_computation.161 | loop fusion | flops 6144 | bytes 16389 | tf_op jit(solution)/shard_map/jit(_where)/select_n | solution.py:101
  16.3 0.8 %fusion.56 = f32[1,16]{1,0:T(1,128)} fusion(s32[128]{0:T(128)S(1)} %bitcast.401, f32[1,128]{1,0:T(1,128)S(1)} %copy-done.41), kind=kOutput, calls=%fused_computation.142 | convolution fusion | flops 26624 | bytes 1088 | tf_op jit(solution)/shard_map/dot_general | solution.py:191
  18.9 0.7 fusion.45
  21.0 1.0 %fusion.92 = (f32[6,15,1024]{2,1,0:T(8,128)}, f32[6,15,1024]{2,1,0:T(8,128)}) fusion(f32[6,16,1024]{2,1,0:T(8,128)S(1)} %bitcast.343), kind=kLoop, calls=%fused_computation.227 | loop fusion | bytes 1474560 | tf_op jit(solution)/shard_map/slice | solution.py:225
  22.0 4.3 %fusion.1 = f32[192,4224]{1,0:T(8,128)S(1)} fusion(s32[4224]{0:T(1024)S(1)} %copy-done.29, bf16[96,1024]{1,0:T(8,128)(2,1)S(1)} %get-tuple-element.22, bf16[96,1024]{1,0:T(8,128)(2,1)S(1)} %get-tuple-element.23), kind=kOutput, calls=%fused_computation.2 | convolution fusion | flops 1666056192 | bytes 3654144 | tf_op jit(solution)/shard_map/dot_general | solution.py:58
  27.0 1.3 %collective-permute-start.4 = (f32[6,2064]{1,0:T(8,128)S(1)}, f32[6,2064]{1,0:T(8,128)S(1)}, u32[]{:S(2)}, u32[]{:S(2)}) collective-permute-start(f32[6,2064]{1,0:T(8,128)S(1)} %pad_maximum_fusion.5), channel_id=1, source_target_pairs={{4,0},{8,4},{12,8},{16,12},{20,16},{24,20},{28,24},{5,1},{9,5},{13... | collective-permute-start | bytes 148616 | tf_op jit(solution)/shard_map/ppermute | solution.py:13
  29.0 2.0 %collective-permute-start.6 = (f32[4,16]{1,0:T(4,128)S(1)}, f32[4,16]{1,0:T(4,128)S(1)}, u32[]{:S(2)}, u32[]{:S(2)}) collective-permute-start(f32[4,16]{1,0:T(4,128)S(1)} %pad_maximum_fusion.10), channel_id=1, source_target_pairs={{0,2},{1,3},{2,0},{3,1},{4,6},{5,7},{6,4},{7,5},{8,10},{9,11},{10,... | collective-permute-start | bytes 776 | tf_op jit(solution)/shard_map/ppermute | solution.py:177
  31.0 1.5 %collective-permute-start.2 = (f32[10,1024]{1,0:T(8,128)S(1)}, f32[10,1024]{1,0:T(8,128)S(1)}, u32[]{:S(2)}, u32[]{:S(2)}) collective-permute-start(f32[10,1024]{1,0:T(8,128)S(1)} %get-tuple-element.72), channel_id=1, source_target_pairs={{0,3},{1,0},{2,1},{3,2},{4,7},{5,4},{6,5},{7,6},{8,11},{9,8},{10,9... | collective-permute-start | bytes 122888 | tf_op jit(solution)/shard_map/ppermute | solution.py:177
  32.6 4.3 %collective-permute-start.5 = (f32[6,2064]{1,0:T(8,128)S(1)}, f32[6,2064]{1,0:T(8,128)S(1)}, u32[]{:S(2)}, u32[]{:S(2)}) collective-permute-start(f32[6,2064]{1,0:T(8,128)S(1)} %pad_maximum_fusion.6), channel_id=1, source_target_pairs={{0,4},{4,8},{8,12},{12,16},{16,20},{20,24},{24,28},{1,5},{5,9},{9,... | collective-permute-start | bytes 148616 | tf_op jit(solution)/shard_map/ppermute | solution.py:13
  37.7 0.7 slice_add_fusion.3
  38.9 0.7 %fusion.40 = (f32[6,2048]{1,0:T(8,128)}, f32[6,2048]{1,0:T(8,128)}) fusion(f32[6,2064]{1,0:T(8,128)S(1)} %collective-permute-done.5, f32[2048]{0:T(1024)S(1)} %slice.419, f32[6,4224]{1,0:T(8,128)S(1)} %multiply_reduce_fusion, f32[6,2064]{1,0:T(8,128)S(1)} %collective-permute-done.4, f32[2048]{0:T(1024)S(1)} %bitcast.377), kind=kLoop, calls=%fused_computation.99 | loop fusion | flops 61440 | bytes 311296 | tf_op jit(solution)/shard_map/neg | solution.py:239
  39.7 0.6 broadcast_in_dim.58
  40.3 1.6 %concatenate.106 = f32[6,4224]{1,0:T(8,128)} concatenate(f32[6,2048]{1,0:T(8,128)} %get-tuple-element.54, f32[6,2048]{1,0:T(8,128)} %get-tuple-element.53, f32[6,16]{1,0:T(8,128)S(1)} %slice_multiply_fusion.5, f32[6,16]{1,0:T(8,128)S(1)} %slice_multiply_fusion.4, f32[6,96]{1,0:T(8,128)} %broadcast_in_dim.58), dimensions={1} | concatenate | bytes 202752 | tf_op jit(solution)/shard_map/concatenate | solution.py:236
  41.8 1.0 %broadcast_multiply_fusion = f32[6,16,4224]{2,1,0:T(8,128)S(1)} fusion(f32[6,4224]{1,0:T(8,128)} %concatenate.106, f32[16,4224]{1,0:T(8,128)S(1)} %fusion.20), kind=kLoop, calls=%fused_computation.15 | loop fusion | flops 405504 | bytes 1993728 | tf_op jit(solution)/shard_map/mul | solution.py:130
  43.0 0.6 copy-done.30
  43.7 3.8 %fusion = f32[192,1024]{1,0:T(8,128)S(1)} fusion(s32[4224]{0:T(1024)S(1)} %copy-done.30, bf16[96,4224]{1,0:T(8,128)(2,1)S(1)} %get-tuple-element.20, bf16[96,4224]{1,0:T(8,128)(2,1)S(1)} %get-tuple-element.21), kind=kOutput, calls=%fused_computation.1 | convolution fusion | flops 1668513792 | bytes 2425344 | tf_op jit(solution)/shard_map/dot_general | solution.py:58
  49.4 13.7 %all_to_all.12 = f32[32,1,10]{2,1,0:T(1,128)S(1)} all-to-all(f32[32,1,10]{2,1,0:T(1,128)S(1)} %broadcast_in_dim.59), channel_id=1, replica_groups=mesh['cells'=8,'slab'=4] {'cells','slab'}, dimensions={0} | all-to-all | bytes 2560 | tf_op jit(solution)/shard_map/all_to_all | solution.py:36
  63.7 0.6 broadcast_in_dim.109
  64.3 2.6 %all-to-all-start.1 = ((f32[32,1,4]{2,1,0:T(1,128)}), f32[32,1,4]{2,1,0:T(1,128)S(1)}, u32[]{:S(2)}, u32[]{:S(2)}) async-start(f32[32,1,4]{2,1,0:T(1,128)} %broadcast_in_dim.109), calls=%async_computation.1 | async-start | bytes 32768 | tf_op jit(solution)/shard_map/all_to_all | solution.py:36
  67.0 0.7 pad_maximum_fusion.2
  67.7 6.3 %all-to-all-done.1 = f32[32,1,4]{2,1,0:T(1,128)S(1)} async-done(((f32[32,1,4]{2,1,0:T(1,128)}), f32[32,1,4]{2,1,0:T(1,128)S(1)}, u32[]{:S(2)}, u32[]{:S(2)}) %all-to-all-start.1) | async-done | bytes 544 | tf_op jit(solution)/shard_map/all_to_all | solution.py:36
  74.0 0.7 sqrt.8
  (180 shorter events, 8.5 us)
Async XLA Ops:
  0.6 15.6 %copy-start = (f32[2,4,16,1024]{3,2,1,0:T(8,128)S(1)}, f32[2,4,16,1024]{3,2,1,0:T(8,128)}, u32[]{:S(2)}) copy-start(f32[2,4,16,1024]{3,2,1,0:T(8,128)} %param.14) | copy-start | bytes 1572868
  0.6 15.6 %copy-start.39 = (s32[1,128]{1,0:T(1,128)S(1)}, s32[1,128]{1,0:T(1,128)}, u32[]{:S(2)}) copy-start(s32[1,128]{1,0:T(1,128)} %param.24) | copy-start | bytes 1540
  0.7 15.6 %copy-start.41 = (f32[1,128]{1,0:T(1,128)S(1)}, f32[1,128]{1,0:T(1,128)}, u32[]{:S(2)}) copy-start(f32[1,128]{1,0:T(1,128)} %param.25) | copy-start | bytes 1540
  1.6 17.3 %copy-start.12 = (f32[16,1024]{1,0:T(8,128)}, f32[16,1024]{1,0:T(8,128)S(1)}, u32[]{:S(2)}) copy-start(f32[16,1024]{1,0:T(8,128)S(1)} %broadcast_select_fusion.1) | copy-start | bytes 196612
  3.2 15.1 %collective-permute-start = (f32[2064]{0:T(1024)S(1)}, f32[2064]{0:T(1024)S(1)}, u32[]{:S(2)}, u32[]{:S(2)}) collective-permute-start(f32[2064]{0:T(1024)S(1)} %pad_maximum_fusion.9), channel_id=1, source_target_pairs={{0,4},{4,8},{8,12},{12,16},{16,20},{20,24},{24,28},{1,5},{5,9},{9,... | collective-permute-start | bytes 24776 | tf_op jit(solution)/shard_map/ppermute | solution.py:13
  9.0 9.9 %copy-start.14 = (f32[16,1024]{1,0:T(8,128)}, f32[16,1024]{1,0:T(8,128)S(1)}, u32[]{:S(2)}) copy-start(f32[16,1024]{1,0:T(8,128)S(1)} %broadcast_select_fusion) | copy-start | bytes 196612
  9.0 9.9 %collective-permute-start.1 = (f32[1024]{0:T(1024)S(1)}, f32[1024]{0:T(1024)S(1)}, u32[]{:S(2)}, u32[]{:S(2)}) collective-permute-start(f32[1024]{0:T(1024)S(1)} %bitcast.400), channel_id=1, source_target_pairs={{0,1},{1,2},{2,3},{4,5},{5,6},{6,7},{8,9},{9,10},{10,11},{12,13},{... | collective-permute-start | bytes 12296 | tf_op jit(solution)/shard_map/ppermute | solution.py:13
  12.3 6.5 %copy-start.1 = (f32[2,2,16,1024]{3,2,1,0:T(8,128)S(1)}, f32[2,2,16,1024]{3,2,1,0:T(8,128)}, u32[]{:S(2)}) copy-start(f32[2,2,16,1024]{3,2,1,0:T(8,128)} %param.13) | copy-start | bytes 786436
  12.4 6.5 %copy-start.2 = (f32[2,2,16,1024]{3,2,1,0:T(8,128)S(1)}, f32[2,2,16,1024]{3,2,1,0:T(8,128)}, u32[]{:S(2)}) copy-start(f32[2,2,16,1024]{3,2,1,0:T(8,128)} %param.15) | copy-start | bytes 786436
  12.4 6.6 %copy-start.22 = (f32[16,1024]{1,0:T(8,128)S(1)}, f32[16,1024]{1,0:T(8,128)}, u32[]{:S(2)}) copy-start(f32[16,1024]{1,0:T(8,128)} %param.17) | copy-start | bytes 196612
  12.4 6.5 %copy-start.23 = (f32[16,1024]{1,0:T(8,128)S(1)}, f32[16,1024]{1,0:T(8,128)}, u32[]{:S(2)}) copy-start(f32[16,1024]{1,0:T(8,128)} %param.18) | copy-start | bytes 196612
  26.6 10.3 %copy-start.32 = (f32[2064]{0:T(1024)S(1)}, f32[2064]{0:T(1024)}, u32[]{:S(2)}) copy-start(f32[2064]{0:T(1024)} %copy-done.31) | copy-start | bytes 24772
  27.0 11.4 %collective-permute-start.4 = (f32[6,2064]{1,0:T(8,128)S(1)}, f32[6,2064]{1,0:T(8,128)S(1)}, u32[]{:S(2)}, u32[]{:S(2)}) collective-permute-start(f32[6,2064]{1,0:T(8,128)S(1)} %pad_maximum_fusion.5), channel_id=1, source_target_pairs={{4,0},{8,4},{12,8},{16,12},{20,16},{24,20},{28,24},{5,1},{9,5},{13... | collective-permute-start | bytes 148616 | tf_op jit(solution)/shard_map/ppermute | solution.py:13
  28.3 10.1 %copy-start.34 = (f32[16]{0:T(128)S(1)}, f32[16]{0:T(128)}, u32[]{:S(2)}) copy-start(f32[16]{0:T(128)} %neg.47) | copy-start | bytes 196
  28.3 10.6 %copy-start.35 = (f32[16]{0:T(128)S(1)}, f32[16]{0:T(128)}, u32[]{:S(2)}) copy-start(f32[16]{0:T(128)} %get-tuple-element.70) | copy-start | bytes 196
  28.3 10.6 %copy-start.28 = (f32[1,2048]{1,0:T(1,128)S(1)}, f32[1,2048]{1,0:T(1,128)}, u32[]{:S(2)}) copy-start(f32[1,2048]{1,0:T(1,128)} %and_select_fusion) | copy-start | bytes 24580
  29.0 8.0 %collective-permute-start.6 = (f32[4,16]{1,0:T(4,128)S(1)}, f32[4,16]{1,0:T(4,128)S(1)}, u32[]{:S(2)}, u32[]{:S(2)}) collective-permute-start(f32[4,16]{1,0:T(4,128)S(1)} %pad_maximum_fusion.10), channel_id=1, source_target_pairs={{0,2},{1,3},{2,0},{3,1},{4,6},{5,7},{6,4},{7,5},{8,10},{9,11},{10,... | collective-permute-start | bytes 776 | tf_op jit(solution)/shard_map/ppermute | solution.py:177
  31.0 6.0 %collective-permute-start.2 = (f32[10,1024]{1,0:T(8,128)S(1)}, f32[10,1024]{1,0:T(8,128)S(1)}, u32[]{:S(2)}, u32[]{:S(2)}) collective-permute-start(f32[10,1024]{1,0:T(8,128)S(1)} %get-tuple-element.72), channel_id=1, source_target_pairs={{0,3},{1,0},{2,1},{3,2},{4,7},{5,4},{6,5},{7,6},{8,11},{9,8},{10,9... | collective-permute-start | bytes 122888 | tf_op jit(solution)/shard_map/ppermute | solution.py:177
  32.5 4.5 %collective-permute-start.3 = (f32[10,1024]{1,0:T(8,128)S(1)}, f32[10,1024]{1,0:T(8,128)S(1)}, u32[]{:S(2)}, u32[]{:S(2)}) collective-permute-start(f32[10,1024]{1,0:T(8,128)S(1)} %get-tuple-element.73), channel_id=1, source_target_pairs={{0,1},{1,2},{2,3},{3,0},{4,5},{5,6},{6,7},{7,4},{8,9},{9,10},{10,1... | collective-permute-start | bytes 122888 | tf_op jit(solution)/shard_map/ppermute | solution.py:177
  32.6 6.3 %collective-permute-start.5 = (f32[6,2064]{1,0:T(8,128)S(1)}, f32[6,2064]{1,0:T(8,128)S(1)}, u32[]{:S(2)}, u32[]{:S(2)}) collective-permute-start(f32[6,2064]{1,0:T(8,128)S(1)} %pad_maximum_fusion.6), channel_id=1, source_target_pairs={{0,4},{4,8},{8,12},{12,16},{16,20},{20,24},{24,28},{1,5},{5,9},{9,... | collective-permute-start | bytes 148616 | tf_op jit(solution)/shard_map/ppermute | solution.py:13
  43.6 4.0 %copy-start.20 = (f32[16,1024]{1,0:T(8,128)S(1)}, f32[16,1024]{1,0:T(8,128)}, u32[]{:S(2)}) copy-start(f32[16,1024]{1,0:T(8,128)} %get-tuple-element.28) | copy-start | bytes 196612
  43.6 4.0 %copy-start.21 = (f32[16,1024]{1,0:T(8,128)S(1)}, f32[16,1024]{1,0:T(8,128)}, u32[]{:S(2)}) copy-start(f32[16,1024]{1,0:T(8,128)} %get-tuple-element.29) | copy-start | bytes 196612
  43.6 4.0 %slice-start = ((f32[10,1024]{1,0:T(8,128)}), f32[6,1024]{1,0:T(8,128)S(1)}, s32[]{:S(2)}) async-start(f32[10,1024]{1,0:T(8,128)} %copy-done.26), calls=%async_computation.2 | async-start | bytes 65536 | tf_op jit(solution)/shard_map/slice | solution.py:213
  43.6 4.0 %slice-start.1 = ((f32[10,1024]{1,0:T(8,128)}), f32[6,1024]{1,0:T(8,128)S(1)}, s32[]{:S(2)}) async-start(f32[10,1024]{1,0:T(8,128)} %copy-done.27), calls=%async_computation.3 | async-start | bytes 65536 | tf_op jit(solution)/shard_map/slice | solution.py:212
  43.6 4.0 %copy-start.37 = (pred[16]{0:T(512)(128)(4,1)S(1)}, pred[16]{0:T(512)(128)(4,1)}, u32[]{:S(2)}) copy-start(pred[16]{0:T(512)(128)(4,1)} %get-tuple-element.78) | copy-start | bytes 52
  48.5 14.8 %copy-start.8 = (f32[16,1024]{1,0:T(8,128)S(1)}, f32[16,1024]{1,0:T(8,128)}, u32[]{:S(2)}) copy-start(f32[16,1024]{1,0:T(8,128)} %copy-done.7) | copy-start | bytes 196612
  48.5 14.8 %copy-start.10 = (f32[16,1024]{1,0:T(8,128)S(1)}, f32[16,1024]{1,0:T(8,128)}, u32[]{:S(2)}) copy-start(f32[16,1024]{1,0:T(8,128)} %copy-done.9) | copy-start | bytes 196612
  48.5 14.8 %copy-start.25 = (f32[2,2,16,1024]{3,2,1,0:T(8,128)S(1)}, f32[2,2,16,1024]{3,2,1,0:T(8,128)}, u32[]{:S(2)}) copy-start(f32[2,2,16,1024]{3,2,1,0:T(8,128)} %param.16) | copy-start | bytes 786436
  48.6 18.2 %copy-start.6 = (f32[16,1024]{1,0:T(8,128)S(1)}, f32[16,1024]{1,0:T(8,128)}, u32[]{:S(2)}) copy-start(f32[16,1024]{1,0:T(8,128)} %copy-done.5) | copy-start | bytes 196612
  48.6 18.2 %copy-start.17 = (f32[16,1024]{1,0:T(8,128)S(1)}, f32[16,1024]{1,0:T(8,128)}, u32[]{:S(2)}) copy-start(f32[16,1024]{1,0:T(8,128)} %copy-done.16) | copy-start | bytes 196612
  48.6 18.2 %copy-start.19 = (f32[16,1024]{1,0:T(8,128)S(1)}, f32[16,1024]{1,0:T(8,128)}, u32[]{:S(2)}) copy-start(f32[16,1024]{1,0:T(8,128)} %copy-done.18) | copy-start | bytes 196612
  64.3 9.7 %all-to-all-start.1 = ((f32[32,1,4]{2,1,0:T(1,128)}), f32[32,1,4]{2,1,0:T(1,128)S(1)}, u32[]{:S(2)}, u32[]{:S(2)}) async-start(f32[32,1,4]{2,1,0:T(1,128)} %broadcast_in_dim.109), calls=%async_computation.1 | async-start | bytes 32768 | tf_op jit(solution)/shard_map/all_to_all | solution.py:36
  (21 other events, 44.0 us)

commit v13 on v11

--- a/solution.py
+++ b/solution.py
@@ -137,6 +137,8 @@
     fault_at = locate(
         jnp.concatenate([fault_near.reshape(-1), fault_far.reshape(-1), edge_cells])
     )
+    near_at = locate(fault_near)
+    far_at = locate(fault_far)
     west_face = east_edge
     east_face = trans_east[:, -1]
     well_at = locate(compl_cell)
@@ -174,9 +176,8 @@
     def operator(fields, mobile, block):
         count = fields.shape[0]
         scaled = (mobile * fields).reshape(count * 2, layer_count, column_count)
-        picks = gather(scaled, fault_at, split2)
-        picks_near = picks[:, :slot_count]
-        picks_far = picks[:, slot_count : 2 * slot_count]
+        picks_near = gather(scaled, near_at, split2)
+        picks_far = gather(scaled, far_at, split2)
         from_left = shifted(jnp.concatenate([scaled[:, :, -1], picks_near], axis=1), "cells", 1)
         from_right = shifted(jnp.concatenate([scaled[:, :, 0], picks_far], axis=1), "cells", -1)
         pressure = fields[:, 0]

time: 74.7 us -> 81.7 us (1.094)
  other arithmetic: 14.8 us -> 21.1 us
  waiting for transfers between devices: 6.85 us -> 9.27 us
  blocking collectives: 13.7 us -> 11.8 us
  local copies, waits for them, and re-layouts: 8.56 us -> 9.94 us
  starting transfers between devices: 18 us -> 16.8 us
    select_n x1 -> x3, other arithmetic: 1.24 us -> 3.79 us  [locate(): onehot = (cells % column_count)[:, None] == column_iota[None, :]]
    ppermute x3, waiting for transfers between devices: 0.01 us -> 2.06 us  [slab_shift(): lax.ppermute(value, 'slab', [(i, (i + by) % count) for i in range(count)])]
    convert_element_type x2 -> x4, other arithmetic: 0.03 us -> 2.06 us  [locate(): (layer_iota[:, None] == (cells // column_count)[None, :]).astype(jnp.floa...]
    all_to_all x1, blocking collectives: 13.7 us -> 11.8 us  [global_sum(): gathered = lax.all_to_all(copies, axes, 0, 0, tiled=True)]
    unnamed x101 -> x107, local copies, waits for them, and re-layouts: 1.87 us -> 3.48 us
    select_n x2 -> x4, other arithmetic: 1.28 us -> 2.82 us  [locate(): cells // column_count]
    ppermute x4, starting transfers between devices: 11.9 us -> 11 us  [shifted(): return lax.ppermute(value, axis, pairs)]
    dot_general x4 -> x5, matrix products: 8.74 us -> 8.55 us  [onehot_dot(): lax.dot_general(pieces, onehot, (dims, ((), ())), preferred_element_type=...]
  transfers between devices with their start and end apart: 8 -> 8, of which waited for: 2 -> 4; matrix products, arithmetic and copies ran while one was open for 16% -> 25% of each run, Pallas kernels for 0% -> 0%
where the time goes in v13:
time: 81.7 us; the launch traced here: 80.9 us
  other arithmetic  21.1 us (26%)
  starting transfers between devices  16.8 us (21%)
  blocking collectives  11.8 us (14%)
  local copies, waits for them, and re-layouts  9.94 us (12%)
  matrix products  9.74 us (12%)
  waiting for transfers between devices  9.27 us (11%)
  between operations  2.32 us (3%)
    all_to_all x1, blocking collectives, global_sum(): gathered = lax.all_to_all(copies, axes, 0, 0, tiled=True)  11.8 us
    ppermute x4, starting transfers between devices, shifted(): return lax.ppermute(value, axis, pairs)  11 us
    dot_general x5, matrix products, onehot_dot(): lax.dot_general(pieces, onehot, (dims, ((), ())), preferred_element_type=...  8.55 us
    all_to_all x1, waiting for transfers between devices, global_sum(): gathered = lax.all_to_all(copies, axes, 0, 0, tiled=True)  6.31 us
    select_n x3, other arithmetic, locate(): onehot = (cells % column_count)[:, None] == column_iota[None, :]  3.79 us
    unnamed x107, local copies, waits for them, and re-layouts  3.48 us
    ppermute x3, starting transfers between devices, slab_shift(): lax.ppermute(value, 'slab', [(i, (i + by) % count) for i in range(count)])  3.24 us
    select_n x4, other arithmetic, locate(): cells // column_count  2.82 us
  transfers between devices with their start and end apart: 8, of which 4 were waited for; matrix products, arithmetic and copies ran while one was open for 25% of the time, Pallas kernels for 0%

profile of v13, /device:TPU:0, one launch (start us, length us, event | category | flops | bytes accessed | tf_op | source)
XLA Modules:
  0.0 80.9 jit_solution(11822065534823629493)
XLA Ops:
  0.7 0.9 %broadcast_select_fusion.1 = f32[16,1024]{1,0:T(8,128)S(1)} fusion(f32[16,1024]{1,0:T(8,128)} %param.17, pred[1024]{0:T(1024)(128)(4,1)S(1)} %fusion.74), kind=kLoop, calls=%fused_computation.168 | loop fusion | flops 16384 | bytes 132096 | tf_op jit(solution)/shard_map/jit(_where)/select_n | solution.py:91
  3.2 4.9 %collective-permute-start = (f32[2064]{0:T(1024)S(1)}, f32[2064]{0:T(1024)S(1)}, u32[]{:S(2)}, u32[]{:S(2)}) collective-permute-start(f32[2064]{0:T(1024)S(1)} %pad_maximum_fusion.12), channel_id=1, source_target_pairs={{0,4},{4,8},{8,12},{12,16},{16,20},{20,24},{24,28},{1,5},{5,9},{9,... | collective-permute-start | bytes 24776 | tf_op jit(solution)/shard_map/ppermute | solution.py:13
  8.1 0.9 %broadcast_select_fusion = f32[16,1024]{1,0:T(8,128)S(1)} fusion(f32[16,1024]{1,0:T(8,128)} %param.18, pred[16]{0:T(512)(128)(4,1)S(1)} %broadcast_and_fusion), kind=kLoop, calls=%fused_computation.167 | loop fusion | flops 16384 | bytes 131088 | tf_op jit(solution)/shard_map/jit(_where)/select_n | solution.py:94
  9.0 1.5 %collective-permute-start.1 = (f32[1024]{0:T(1024)S(1)}, f32[1024]{0:T(1024)S(1)}, u32[]{:S(2)}, u32[]{:S(2)}) collective-permute-start(f32[1024]{0:T(1024)S(1)} %bitcast.409), channel_id=1, source_target_pairs={{0,1},{1,2},{2,3},{4,5},{5,6},{6,7},{8,9},{9,10},{10,11},{12,13},{... | collective-permute-start | bytes 12296 | tf_op jit(solution)/shard_map/ppermute | solution.py:13
  10.5 1.2 %and_select_fusion.4 = s32[128]{0:T(128)} fusion(s32[1,128]{1,0:T(1,128)} %param.23), kind=kLoop, calls=%fused_computation.225 | loop fusion | flops 1408 | bytes 1024 | tf_op jit(solution)/shard_map/jit(remainder)/select_n | solution.py:115
  12.3 1.0 %fusion.97 = (f32[1,2,16,1024]{3,2,1,0:T(8,128)S(1)}, f32[1,2,16,1024]{3,2,1,0:T(8,128)S(1)}) fusion(f32[2,2,16,1024]{3,2,1,0:T(8,128)} %param.15), kind=kLoop, calls=%fused_computation.253 | loop fusion | bytes 524288 | tf_op jit(solution)/shard_map/slice | solution.py:152
  13.4 0.8 and_select_fusion.1
  14.2 1.3 %add_select_fusion.3 = s32[2048]{0:T(1024)} fusion(s32[2048]{0:T(1024)} %bitcast.364), kind=kLoop, calls=%fused_computation.198 | loop fusion | flops 22528 | bytes 16384 | tf_op jit(solution)/shard_map/jit(remainder)/select_n | solution.py:115
  16.2 0.7 and_select_fusion
  16.9 1.3 %add_select_fusion.2 = s32[2048]{0:T(1024)} fusion(s32[2048]{0:T(1024)} %bitcast.366), kind=kLoop, calls=%fused_computation.195 | loop fusion | flops 22528 | bytes 16384 | tf_op jit(solution)/shard_map/jit(remainder)/select_n | solution.py:115
  18.9 0.7 and_select_fusion.2
  19.6 0.8 concatenate.101
  21.0 0.7 fusion.19
  21.8 0.8 fusion.57
  24.4 0.7 fusion.46
  26.6 0.8 fusion.96
  27.5 2.1 %fusion.2 = f32[192,2048]{1,0:T(8,128)S(1)} fusion(s32[2048]{0:T(1024)S(1)} %copy-done.33, bf16[96,1024]{1,0:T(8,128)(2,1)S(1)} %fusion.13, bf16[96,1024]{1,0:T(8,128)(2,1)S(1)} %bitcast_convert_fusion.1), kind=kOutput, calls=%fused_computation.5 | convolution fusion | flops 808189952 | bytes 1974272 | tf_op jit(solution)/shard_map/dot_general | solution.py:58
  29.6 0.8 copy-done.22
  30.7 3.4 %collective-permute-start.5 = (f32[6,2064]{1,0:T(8,128)S(1)}, f32[6,2064]{1,0:T(8,128)S(1)}, u32[]{:S(2)}, u32[]{:S(2)}) collective-permute-start(f32[6,2064]{1,0:T(8,128)S(1)} %pad_maximum_fusion.9), channel_id=1, source_target_pairs={{0,4},{4,8},{8,12},{12,16},{16,20},{20,24},{24,28},{1,5},{5,9},{9,... | collective-permute-start | bytes 148616 | tf_op jit(solution)/shard_map/ppermute | solution.py:13
  34.1 2.1 %fusion.3 = f32[192,2048]{1,0:T(8,128)S(1)} fusion(s32[2048]{0:T(1024)S(1)} %copy-done.32, bf16[96,1024]{1,0:T(8,128)(2,1)S(1)} %fusion.13, bf16[96,1024]{1,0:T(8,128)(2,1)S(1)} %bitcast_convert_fusion.1), kind=kOutput, calls=%fused_computation.6 | convolution fusion | flops 808189952 | bytes 1974272 | tf_op jit(solution)/shard_map/dot_general | solution.py:58
  37.5 2.0 %collective-permute-start.6 = (f32[4,16]{1,0:T(4,128)S(1)}, f32[4,16]{1,0:T(4,128)S(1)}, u32[]{:S(2)}, u32[]{:S(2)}) collective-permute-start(f32[4,16]{1,0:T(4,128)S(1)} %pad_maximum_fusion.13), channel_id=1, source_target_pairs={{0,2},{1,3},{2,0},{3,1},{4,6},{5,7},{6,4},{7,5},{8,10},{9,11},{10,... | collective-permute-start | bytes 776 | tf_op jit(solution)/shard_map/ppermute | solution.py:174
  39.5 1.2 %collective-permute-start.2 = (f32[10,1024]{1,0:T(8,128)S(1)}, f32[10,1024]{1,0:T(8,128)S(1)}, u32[]{:S(2)}, u32[]{:S(2)}) collective-permute-start(f32[10,1024]{1,0:T(8,128)S(1)} %get-tuple-element.66), channel_id=1, source_target_pairs={{0,3},{1,0},{2,1},{3,2},{4,7},{5,4},{6,5},{7,6},{8,11},{9,8},{10,9... | collective-permute-start | bytes 122888 | tf_op jit(solution)/shard_map/ppermute | solution.py:174
  41.0 1.3 %collective-permute-start.4 = (f32[6,2064]{1,0:T(8,128)S(1)}, f32[6,2064]{1,0:T(8,128)S(1)}, u32[]{:S(2)}, u32[]{:S(2)}) collective-permute-start(f32[6,2064]{1,0:T(8,128)S(1)} %pad_maximum_fusion.8), channel_id=1, source_target_pairs={{4,0},{8,4},{12,8},{16,12},{20,16},{24,20},{28,24},{5,1},{9,5},{13... | collective-permute-start | bytes 148616 | tf_op jit(solution)/shard_map/ppermute | solution.py:13
  43.0 1.5 %collective-permute-done.3 = f32[10,1024]{1,0:T(8,128)S(1)} collective-permute-done((f32[10,1024]{1,0:T(8,128)S(1)}, f32[10,1024]{1,0:T(8,128)S(1)}, u32[]{:S(2)}, u32[]{:S(2)}) %collective-permute-start.3) | collective-permute-done | bytes 40992 | tf_op jit(solution)/shard_map/ppermute | solution.py:174
  46.5 0.9 %collective-permute-done.4 = f32[6,2064]{1,0:T(8,128)S(1)} collective-permute-done((f32[6,2064]{1,0:T(8,128)S(1)}, f32[6,2064]{1,0:T(8,128)S(1)}, u32[]{:S(2)}, u32[]{:S(2)}) %collective-permute-start.4) | collective-permute-done | bytes 49568 | tf_op jit(solution)/shard_map/ppermute | solution.py:13
  48.1 1.6 %concatenate.100 = f32[6,4128]{1,0:T(8,128)} concatenate(f32[6,2048]{1,0:T(8,128)} %fusion.42, f32[6,2048]{1,0:T(8,128)} %fusion.41, f32[6,16]{1,0:T(8,128)S(1)} %slice_multiply_fusion.5, f32[6,16]{1,0:T(8,128)S(1)} %slice_multiply_fusion.4), dimensions={1} | concatenate | bytes 198144 | tf_op jit(solution)/shard_map/concatenate | solution.py:232
  49.7 1.1 %broadcast_multiply_fusion = f32[6,16,4128]{2,1,0:T(8,128)S(1)} fusion(f32[16,4128]{1,0:T(8,128)} %fusion.19, f32[6,4128]{1,0:T(8,128)} %concatenate.100), kind=kLoop, calls=%fused_computation.17 | loop fusion | flops 396288 | bytes 1948416 | tf_op jit(solution)/shard_map/mul | solution.py:130
  51.6 3.8 %fusion = f32[192,1024]{1,0:T(8,128)S(1)} fusion(s32[4128]{0:T(1024)S(1)} %copy-done.31, bf16[96,4128]{1,0:T(8,128)(2,1)S(1)} %get-tuple-element.20, bf16[96,4128]{1,0:T(8,128)(2,1)S(1)} %get-tuple-element.21), kind=kOutput, calls=%fused_computation.1 | convolution fusion | flops 1630593024 | bytes 2388096 | tf_op jit(solution)/shard_map/dot_general | solution.py:58
  57.6 11.8 %all_to_all.12 = f32[32,1,10]{2,1,0:T(1,128)S(1)} all-to-all(f32[32,1,10]{2,1,0:T(1,128)S(1)} %broadcast_in_dim.53), channel_id=1, replica_groups=mesh['cells'=8,'slab'=4] {'cells','slab'}, dimensions={0} | all-to-all | bytes 2560 | tf_op jit(solution)/shard_map/all_to_all | solution.py:36
  70.5 2.6 %all-to-all-start.1 = ((f32[32,1,4]{2,1,0:T(1,128)}), f32[32,1,4]{2,1,0:T(1,128)S(1)}, u32[]{:S(2)}, u32[]{:S(2)}) async-start(f32[32,1,4]{2,1,0:T(1,128)} %broadcast_in_dim.55), calls=%async_computation.1 | async-start | bytes 32768 | tf_op jit(solution)/shard_map/all_to_all | solution.py:36
  73.2 0.7 pad_maximum_fusion.3
  73.9 6.3 %all-to-all-done.1 = f32[32,1,4]{2,1,0:T(1,128)S(1)} async-done(((f32[32,1,4]{2,1,0:T(1,128)}), f32[32,1,4]{2,1,0:T(1,128)S(1)}, u32[]{:S(2)}, u32[]{:S(2)}) %all-to-all-start.1) | async-done | bytes 544 | tf_op jit(solution)/shard_map/all_to_all | solution.py:36
  (194 shorter events, 16.6 us)
Async XLA Ops:
  0.6 21.1 %copy-start = (f32[2,4,16,1024]{3,2,1,0:T(8,128)S(1)}, f32[2,4,16,1024]{3,2,1,0:T(8,128)}, u32[]{:S(2)}) copy-start(f32[2,4,16,1024]{3,2,1,0:T(8,128)} %param.14) | copy-start | bytes 1572868
  0.6 21.1 %copy-start.42 = (s32[1,128]{1,0:T(1,128)S(1)}, s32[1,128]{1,0:T(1,128)}, u32[]{:S(2)}) copy-start(s32[1,128]{1,0:T(1,128)} %param.24) | copy-start | bytes 1540
  0.7 21.1 %copy-start.44 = (f32[1,128]{1,0:T(1,128)S(1)}, f32[1,128]{1,0:T(1,128)}, u32[]{:S(2)}) copy-start(f32[1,128]{1,0:T(1,128)} %param.25) | copy-start | bytes 1540
  1.6 22.8 %copy-start.13 = (f32[16,1024]{1,0:T(8,128)}, f32[16,1024]{1,0:T(8,128)S(1)}, u32[]{:S(2)}) copy-start(f32[16,1024]{1,0:T(8,128)S(1)} %broadcast_select_fusion.1) | copy-start | bytes 196612
  3.2 20.6 %collective-permute-start = (f32[2064]{0:T(1024)S(1)}, f32[2064]{0:T(1024)S(1)}, u32[]{:S(2)}, u32[]{:S(2)}) collective-permute-start(f32[2064]{0:T(1024)S(1)} %pad_maximum_fusion.12), channel_id=1, source_target_pairs={{0,4},{4,8},{8,12},{12,16},{16,20},{20,24},{24,28},{1,5},{5,9},{9,... | collective-permute-start | bytes 24776 | tf_op jit(solution)/shard_map/ppermute | solution.py:13
  9.0 15.4 %copy-start.15 = (f32[16,1024]{1,0:T(8,128)}, f32[16,1024]{1,0:T(8,128)S(1)}, u32[]{:S(2)}) copy-start(f32[16,1024]{1,0:T(8,128)S(1)} %broadcast_select_fusion) | copy-start | bytes 196612
  9.0 15.4 %collective-permute-start.1 = (f32[1024]{0:T(1024)S(1)}, f32[1024]{0:T(1024)S(1)}, u32[]{:S(2)}, u32[]{:S(2)}) collective-permute-start(f32[1024]{0:T(1024)S(1)} %bitcast.409), channel_id=1, source_target_pairs={{0,1},{1,2},{2,3},{4,5},{5,6},{6,7},{8,9},{9,10},{10,11},{12,13},{... | collective-permute-start | bytes 12296 | tf_op jit(solution)/shard_map/ppermute | solution.py:13
  13.3 11.1 %copy-start.1 = (f32[2,2,16,1024]{3,2,1,0:T(8,128)S(1)}, f32[2,2,16,1024]{3,2,1,0:T(8,128)}, u32[]{:S(2)}) copy-start(f32[2,2,16,1024]{3,2,1,0:T(8,128)} %param.13) | copy-start | bytes 786436
  13.3 11.1 %copy-start.2 = (f32[2,2,16,1024]{3,2,1,0:T(8,128)S(1)}, f32[2,2,16,1024]{3,2,1,0:T(8,128)}, u32[]{:S(2)}) copy-start(f32[2,2,16,1024]{3,2,1,0:T(8,128)} %param.15) | copy-start | bytes 786436
  13.4 11.1 %copy-start.25 = (f32[16,1024]{1,0:T(8,128)S(1)}, f32[16,1024]{1,0:T(8,128)}, u32[]{:S(2)}) copy-start(f32[16,1024]{1,0:T(8,128)} %param.17) | copy-start | bytes 196612
  13.4 11.1 %copy-start.26 = (f32[16,1024]{1,0:T(8,128)S(1)}, f32[16,1024]{1,0:T(8,128)}, u32[]{:S(2)}) copy-start(f32[16,1024]{1,0:T(8,128)} %param.18) | copy-start | bytes 196612
  29.5 4.6 %copy-start.32 = (s32[2048]{0:T(1024)S(1)}, s32[2048]{0:T(1024)}, u32[]{:S(2)}) copy-start(s32[2048]{0:T(1024)} %add_select_fusion.2) | copy-start | bytes 24580
  30.7 15.1 %collective-permute-start.5 = (f32[6,2064]{1,0:T(8,128)S(1)}, f32[6,2064]{1,0:T(8,128)S(1)}, u32[]{:S(2)}, u32[]{:S(2)}) collective-permute-start(f32[6,2064]{1,0:T(8,128)S(1)} %pad_maximum_fusion.9), channel_id=1, source_target_pairs={{0,4},{4,8},{8,12},{12,16},{16,20},{20,24},{24,28},{1,5},{5,9},{9,... | collective-permute-start | bytes 148616 | tf_op jit(solution)/shard_map/ppermute | solution.py:13
  36.2 4.5 %copy-start.21 = (f32[16,2048]{1,0:T(8,128)S(1)}, f32[16,2048]{1,0:T(8,128)}, u32[]{:S(2)}) copy-start(f32[16,2048]{1,0:T(8,128)} %fusion.38) | copy-start | bytes 393220
  36.3 5.9 %copy-start.35 = (f32[2064]{0:T(1024)S(1)}, f32[2064]{0:T(1024)}, u32[]{:S(2)}) copy-start(f32[2064]{0:T(1024)} %copy-done.34) | copy-start | bytes 24772
  37.5 4.9 %collective-permute-start.6 = (f32[4,16]{1,0:T(4,128)S(1)}, f32[4,16]{1,0:T(4,128)S(1)}, u32[]{:S(2)}, u32[]{:S(2)}) collective-permute-start(f32[4,16]{1,0:T(4,128)S(1)} %pad_maximum_fusion.13), channel_id=1, source_target_pairs={{0,2},{1,3},{2,0},{3,1},{4,6},{5,7},{6,4},{7,5},{8,10},{9,11},{10,... | collective-permute-start | bytes 776 | tf_op jit(solution)/shard_map/ppermute | solution.py:174
  39.5 7.0 %copy-start.38 = (f32[16]{0:T(128)S(1)}, f32[16]{0:T(128)}, u32[]{:S(2)}) copy-start(f32[16]{0:T(128)} %get-tuple-element.64) | copy-start | bytes 196
  39.5 7.9 %copy-start.37 = (f32[16]{0:T(128)S(1)}, f32[16]{0:T(128)}, u32[]{:S(2)}) copy-start(f32[16]{0:T(128)} %neg.47) | copy-start | bytes 196
  39.5 3.5 %collective-permute-start.2 = (f32[10,1024]{1,0:T(8,128)S(1)}, f32[10,1024]{1,0:T(8,128)S(1)}, u32[]{:S(2)}, u32[]{:S(2)}) collective-permute-start(f32[10,1024]{1,0:T(8,128)S(1)} %get-tuple-element.66), channel_id=1, source_target_pairs={{0,3},{1,0},{2,1},{3,2},{4,7},{5,4},{6,5},{7,6},{8,11},{9,8},{10,9... | collective-permute-start | bytes 122888 | tf_op jit(solution)/shard_map/ppermute | solution.py:174
  40.7 3.7 %collective-permute-start.3 = (f32[10,1024]{1,0:T(8,128)S(1)}, f32[10,1024]{1,0:T(8,128)S(1)}, u32[]{:S(2)}, u32[]{:S(2)}) collective-permute-start(f32[10,1024]{1,0:T(8,128)S(1)} %get-tuple-element.67), channel_id=1, source_target_pairs={{0,1},{1,2},{2,3},{3,0},{4,5},{5,6},{6,7},{7,4},{8,9},{9,10},{10,1... | collective-permute-start | bytes 122888 | tf_op jit(solution)/shard_map/ppermute | solution.py:174
  41.0 6.4 %collective-permute-start.4 = (f32[6,2064]{1,0:T(8,128)S(1)}, f32[6,2064]{1,0:T(8,128)S(1)}, u32[]{:S(2)}, u32[]{:S(2)}) collective-permute-start(f32[6,2064]{1,0:T(8,128)S(1)} %pad_maximum_fusion.8), channel_id=1, source_target_pairs={{4,0},{8,4},{12,8},{16,12},{20,16},{24,20},{28,24},{5,1},{9,5},{13... | collective-permute-start | bytes 148616 | tf_op jit(solution)/shard_map/ppermute | solution.py:13
  51.5 3.9 %copy-start.24 = (f32[16,1024]{1,0:T(8,128)S(1)}, f32[16,1024]{1,0:T(8,128)}, u32[]{:S(2)}) copy-start(f32[16,1024]{1,0:T(8,128)} %get-tuple-element.27) | copy-start | bytes 196612
  51.5 3.9 %slice-start = ((f32[10,1024]{1,0:T(8,128)}), f32[6,1024]{1,0:T(8,128)S(1)}, s32[]{:S(2)}) async-start(f32[10,1024]{1,0:T(8,128)} %copy-done.29), calls=%async_computation.2 | async-start | bytes 65536 | tf_op jit(solution)/shard_map/slice | solution.py:209
  51.6 3.9 %slice-start.1 = ((f32[10,1024]{1,0:T(8,128)}), f32[6,1024]{1,0:T(8,128)S(1)}, s32[]{:S(2)}) async-start(f32[10,1024]{1,0:T(8,128)} %copy-done.30), calls=%async_computation.3 | async-start | bytes 65536 | tf_op jit(solution)/shard_map/slice | solution.py:208
  51.6 3.9 %copy-start.40 = (pred[16]{0:T(512)(128)(4,1)S(1)}, pred[16]{0:T(512)(128)(4,1)}, u32[]{:S(2)}) copy-start(pred[16]{0:T(512)(128)(4,1)} %get-tuple-element.72) | copy-start | bytes 52
  56.3 13.2 %copy-start.9 = (f32[16,1024]{1,0:T(8,128)S(1)}, f32[16,1024]{1,0:T(8,128)}, u32[]{:S(2)}) copy-start(f32[16,1024]{1,0:T(8,128)} %copy-done.8) | copy-start | bytes 196612
  56.3 13.2 %copy-start.11 = (f32[16,1024]{1,0:T(8,128)S(1)}, f32[16,1024]{1,0:T(8,128)}, u32[]{:S(2)}) copy-start(f32[16,1024]{1,0:T(8,128)} %copy-done.10) | copy-start | bytes 196612
  56.3 13.2 %copy-start.28 = (f32[2,2,16,1024]{3,2,1,0:T(8,128)S(1)}, f32[2,2,16,1024]{3,2,1,0:T(8,128)}, u32[]{:S(2)}) copy-start(f32[2,2,16,1024]{3,2,1,0:T(8,128)} %param.16) | copy-start | bytes 786436
  56.8 16.2 %copy-start.7 = (f32[16,1024]{1,0:T(8,128)S(1)}, f32[16,1024]{1,0:T(8,128)}, u32[]{:S(2)}) copy-start(f32[16,1024]{1,0:T(8,128)} %copy-done.6) | copy-start | bytes 196612
  56.8 16.3 %copy-start.18 = (f32[16,1024]{1,0:T(8,128)S(1)}, f32[16,1024]{1,0:T(8,128)}, u32[]{:S(2)}) copy-start(f32[16,1024]{1,0:T(8,128)} %copy-done.17) | copy-start | bytes 196612
  56.8 16.3 %copy-start.20 = (f32[16,1024]{1,0:T(8,128)S(1)}, f32[16,1024]{1,0:T(8,128)}, u32[]{:S(2)}) copy-start(f32[16,1024]{1,0:T(8,128)} %copy-done.19) | copy-start | bytes 196612
  70.5 9.7 %all-to-all-start.1 = ((f32[32,1,4]{2,1,0:T(1,128)}), f32[32,1,4]{2,1,0:T(1,128)S(1)}, u32[]{:S(2)}, u32[]{:S(2)}) async-start(f32[32,1,4]{2,1,0:T(1,128)} %broadcast_in_dim.55), calls=%async_computation.1 | async-start | bytes 32768 | tf_op jit(solution)/shard_map/all_to_all | solution.py:36
  (24 other events, 41.2 us)

commit v14 on v11

--- a/solution.py
+++ b/solution.py
@@ -151,11 +151,12 @@
         diag_first = block[0] + mobile[0] * face_total
         diag_second = block[3] + mobile[1] * face_total
         determinant = diag_first * diag_second - block[1] * block[2]
+        scale = 1.0 / determinant
         return (
-            diag_second / determinant,
-            -block[1] / determinant,
-            -block[2] / determinant,
-            diag_first / determinant,
+            diag_second * scale,
+            -block[1] * scale,
+            -block[2] * scale,
+            diag_first * scale,
         )
 
     def precondition(inverse, residual):

time: 74.7 us -> 74.7 us (level)
  no operation moved by 1% of the time
where the time goes in v14:
time: 74.7 us; the launch traced here: 74.1 us
  starting transfers between devices  18 us (24%)
  other arithmetic  14.8 us (20%)
  blocking collectives  13.7 us (18%)
  matrix products  9.88 us (13%)
  local copies, waits for them, and re-layouts  8.56 us (11%)
  waiting for transfers between devices  6.85 us (9%)
  between operations  2.3 us (3%)
    all_to_all x1, blocking collectives, global_sum(): gathered = lax.all_to_all(copies, axes, 0, 0, tiled=True)  13.7 us
    ppermute x4, starting transfers between devices, shifted(): return lax.ppermute(value, axis, pairs)  11.9 us
    dot_general x4, matrix products, onehot_dot(): lax.dot_general(pieces, onehot, (dims, ((), ())), preferred_element_type=...  8.73 us
    all_to_all x1, waiting for transfers between devices, global_sum(): gathered = lax.all_to_all(copies, axes, 0, 0, tiled=True)  6.31 us
    ppermute x3, starting transfers between devices, slab_shift(): lax.ppermute(value, 'slab', [(i, (i + by) % count) for i in range(count)])  3.53 us
    all_to_all x1, starting transfers between devices, global_sum(): gathered = lax.all_to_all(copies, axes, 0, 0, tiled=True)  2.56 us
    select_n x2, other arithmetic, per_device(): weight_here = jnp.where(slot_live, fault_trans.reshape(-1), zero_value)  2.01 us
    unnamed x101, local copies, waits for them, and re-layouts  1.88 us
  transfers between devices with their start and end apart: 8, of which 2 were waited for; matrix products, arithmetic and copies ran while one was open for 16% of the time, Pallas kernels for 0%

profile of v14, /device:TPU:0, one launch (start us, length us, event | category | flops | bytes accessed | tf_op | source)
XLA Modules:
  0.0 74.1 jit_solution(11422292390750141984)
XLA Ops:
  0.7 0.9 %broadcast_select_fusion.1 = f32[16,1024]{1,0:T(8,128)S(1)} fusion(f32[16,1024]{1,0:T(8,128)} %param.17, pred[1024]{0:T(1024)(128)(4,1)S(1)} %fusion.73), kind=kLoop, calls=%fused_computation.162 | loop fusion | flops 16384 | bytes 132096 | tf_op jit(solution)/shard_map/jit(_where)/select_n | solution.py:91
  2.4 0.7 fusion.71
  3.2 4.9 %collective-permute-start = (f32[2064]{0:T(1024)S(1)}, f32[2064]{0:T(1024)S(1)}, u32[]{:S(2)}, u32[]{:S(2)}) collective-permute-start(f32[2064]{0:T(1024)S(1)} %pad_maximum_fusion.9), channel_id=1, source_target_pairs={{0,4},{4,8},{8,12},{12,16},{16,20},{20,24},{24,28},{1,5},{5,9},{9,... | collective-permute-start | bytes 24776 | tf_op jit(solution)/shard_map/ppermute | solution.py:13
  8.1 0.9 %broadcast_select_fusion = f32[16,1024]{1,0:T(8,128)S(1)} fusion(f32[16,1024]{1,0:T(8,128)} %param.18, pred[16]{0:T(512)(128)(4,1)S(1)} %broadcast_and_fusion), kind=kLoop, calls=%fused_computation.161 | loop fusion | flops 16384 | bytes 131088 | tf_op jit(solution)/shard_map/jit(_where)/select_n | solution.py:94
  9.0 1.5 %collective-permute-start.1 = (f32[1024]{0:T(1024)S(1)}, f32[1024]{0:T(1024)S(1)}, u32[]{:S(2)}, u32[]{:S(2)}) collective-permute-start(f32[1024]{0:T(1024)S(1)} %bitcast.404), channel_id=1, source_target_pairs={{0,1},{1,2},{2,3},{4,5},{5,6},{6,7},{8,9},{9,10},{10,11},{12,13},{... | collective-permute-start | bytes 12296 | tf_op jit(solution)/shard_map/ppermute | solution.py:13
  10.5 1.2 %and_select_fusion.2 = s32[128]{0:T(128)} fusion(s32[1,128]{1,0:T(1,128)} %param.23), kind=kLoop, calls=%fused_computation.203 | loop fusion | flops 1408 | bytes 1024 | tf_op jit(solution)/shard_map/jit(remainder)/select_n | solution.py:115
  11.7 0.7 fusion.80
  12.4 1.0 %fusion.96 = (f32[1,2,16,1024]{3,2,1,0:T(8,128)S(1)}, f32[1,2,16,1024]{3,2,1,0:T(8,128)S(1)}) fusion(f32[2,2,16,1024]{3,2,1,0:T(8,128)} %param.15), kind=kLoop, calls=%fused_computation.230 | loop fusion | bytes 524288 | tf_op jit(solution)/shard_map/slice | solution.py:150
  13.5 0.8 %concatenate.103 = s32[4128]{0:T(1024)S(1)} concatenate(s32[2048]{0:T(1024)} %bitcast.401, s32[2048]{0:T(1024)} %bitcast.402, s32[16]{0:T(128)S(1)} %get-tuple-element.76, s32[16]{0:T(128)S(1)} %get-tuple-element.77), dimensions={0} | concatenate | bytes 33024 | tf_op jit(solution)/shard_map/concatenate | solution.py:138
  14.3 0.6 add_select_fusion
  14.9 1.3 %and_select_fusion = f32[1,2048]{1,0:T(1,128)} fusion(f32[1,2048]{1,0:T(1,128)} %param.21, pred[]{:T(512)S(6)} %lt.34, s32[]{:T(128)} %bitcast.343), kind=kLoop, calls=%fused_computation.163 | loop fusion | flops 6144 | bytes 16389 | tf_op jit(solution)/shard_map/jit(_where)/select_n | solution.py:101
  16.3 0.8 %fusion.58 = f32[1,16]{1,0:T(1,128)} fusion(s32[128]{0:T(128)S(1)} %bitcast.405, f32[1,128]{1,0:T(1,128)S(1)} %copy-done.41), kind=kOutput, calls=%fused_computation.144 | convolution fusion | flops 26624 | bytes 1088 | tf_op jit(solution)/shard_map/dot_general | solution.py:187
  17.7 0.6 neg.47
  18.9 0.7 fusion.45
  21.1 1.0 %fusion.95 = (f32[6,15,1024]{2,1,0:T(8,128)}, f32[6,15,1024]{2,1,0:T(8,128)}) fusion(f32[6,16,1024]{2,1,0:T(8,128)S(1)} %bitcast.347), kind=kLoop, calls=%fused_computation.229 | loop fusion | bytes 1474560 | tf_op jit(solution)/shard_map/slice | solution.py:221
  22.0 4.3 %fusion.1 = f32[192,4128]{1,0:T(8,128)S(1)} fusion(s32[4128]{0:T(1024)S(1)} %copy-done.29, bf16[96,1024]{1,0:T(8,128)(2,1)S(1)} %get-tuple-element.22, bf16[96,1024]{1,0:T(8,128)(2,1)S(1)} %get-tuple-element.23), kind=kOutput, calls=%fused_computation.2 | convolution fusion | flops 1628209152 | bytes 3580032 | tf_op jit(solution)/shard_map/dot_general | solution.py:58
  27.0 1.3 %collective-permute-start.4 = (f32[6,2064]{1,0:T(8,128)S(1)}, f32[6,2064]{1,0:T(8,128)S(1)}, u32[]{:S(2)}, u32[]{:S(2)}) collective-permute-start(f32[6,2064]{1,0:T(8,128)S(1)} %pad_maximum_fusion.5), channel_id=1, source_target_pairs={{4,0},{8,4},{12,8},{16,12},{20,16},{24,20},{28,24},{5,1},{9,5},{13... | collective-permute-start | bytes 148616 | tf_op jit(solution)/shard_map/ppermute | solution.py:13
  29.0 2.0 %collective-permute-start.6 = (f32[4,16]{1,0:T(4,128)S(1)}, f32[4,16]{1,0:T(4,128)S(1)}, u32[]{:S(2)}, u32[]{:S(2)}) collective-permute-start(f32[4,16]{1,0:T(4,128)S(1)} %pad_maximum_fusion.10), channel_id=1, source_target_pairs={{0,2},{1,3},{2,0},{3,1},{4,6},{5,7},{6,4},{7,5},{8,10},{9,11},{10,... | collective-permute-start | bytes 776 | tf_op jit(solution)/shard_map/ppermute | solution.py:173
  31.0 1.5 %collective-permute-start.2 = (f32[10,1024]{1,0:T(8,128)S(1)}, f32[10,1024]{1,0:T(8,128)S(1)}, u32[]{:S(2)}, u32[]{:S(2)}) collective-permute-start(f32[10,1024]{1,0:T(8,128)S(1)} %get-tuple-element.72), channel_id=1, source_target_pairs={{0,3},{1,0},{2,1},{3,2},{4,7},{5,4},{6,5},{7,6},{8,11},{9,8},{10,9... | collective-permute-start | bytes 122888 | tf_op jit(solution)/shard_map/ppermute | solution.py:173
  32.6 4.3 %collective-permute-start.5 = (f32[6,2064]{1,0:T(8,128)S(1)}, f32[6,2064]{1,0:T(8,128)S(1)}, u32[]{:S(2)}, u32[]{:S(2)}) collective-permute-start(f32[6,2064]{1,0:T(8,128)S(1)} %pad_maximum_fusion.6), channel_id=1, source_target_pairs={{0,4},{4,8},{8,12},{12,16},{16,20},{20,24},{24,28},{1,5},{5,9},{9,... | collective-permute-start | bytes 148616 | tf_op jit(solution)/shard_map/ppermute | solution.py:13
  37.7 0.7 slice_add_fusion.3
  38.9 0.7 %fusion.40 = (f32[6,2048]{1,0:T(8,128)}, f32[6,2048]{1,0:T(8,128)}) fusion(f32[6,2064]{1,0:T(8,128)S(1)} %collective-permute-done.5, f32[2048]{0:T(1024)S(1)} %slice.419, f32[6,4128]{1,0:T(8,128)S(1)} %multiply_reduce_fusion, f32[6,2064]{1,0:T(8,128)S(1)} %collective-permute-done.4, f32[2048]{0:T(1024)S(1)} %bitcast.381), kind=kLoop, calls=%fused_computation.99 | loop fusion | flops 61440 | bytes 311296 | tf_op jit(solution)/shard_map/neg | solution.py:235
  39.7 1.6 %concatenate.106 = f32[6,4128]{1,0:T(8,128)} concatenate(f32[6,2048]{1,0:T(8,128)} %get-tuple-element.54, f32[6,2048]{1,0:T(8,128)} %get-tuple-element.53, f32[6,16]{1,0:T(8,128)S(1)} %slice_multiply_fusion.5, f32[6,16]{1,0:T(8,128)S(1)} %slice_multiply_fusion.4), dimensions={1} | concatenate | bytes 198144 | tf_op jit(solution)/shard_map/concatenate | solution.py:232
  41.3 1.0 %broadcast_multiply_fusion = f32[6,16,4128]{2,1,0:T(8,128)S(1)} fusion(f32[6,4128]{1,0:T(8,128)} %concatenate.106, f32[16,4128]{1,0:T(8,128)S(1)} %fusion.20), kind=kLoop, calls=%fused_computation.15 | loop fusion | flops 396288 | bytes 1948416 | tf_op jit(solution)/shard_map/mul | solution.py:130
  42.4 0.6 copy-done.30
  43.1 3.8 %fusion = f32[192,1024]{1,0:T(8,128)S(1)} fusion(s32[4128]{0:T(1024)S(1)} %copy-done.30, bf16[96,4128]{1,0:T(8,128)(2,1)S(1)} %get-tuple-element.20, bf16[96,4128]{1,0:T(8,128)(2,1)S(1)} %get-tuple-element.21), kind=kOutput, calls=%fused_computation.1 | convolution fusion | flops 1630593024 | bytes 2388096 | tf_op jit(solution)/shard_map/dot_general | solution.py:58
  48.8 13.7 %all_to_all.12 = f32[32,1,10]{2,1,0:T(1,128)S(1)} all-to-all(f32[32,1,10]{2,1,0:T(1,128)S(1)} %broadcast_in_dim.53), channel_id=1, replica_groups=mesh['cells'=8,'slab'=4] {'cells','slab'}, dimensions={0} | all-to-all | bytes 2560 | tf_op jit(solution)/shard_map/all_to_all | solution.py:36
  63.0 0.6 broadcast_in_dim.55
  63.7 2.6 %all-to-all-start.1 = ((f32[32,1,4]{2,1,0:T(1,128)}), f32[32,1,4]{2,1,0:T(1,128)S(1)}, u32[]{:S(2)}, u32[]{:S(2)}) async-start(f32[32,1,4]{2,1,0:T(1,128)} %broadcast_in_dim.55), calls=%async_computation.1 | async-start | bytes 32768 | tf_op jit(solution)/shard_map/all_to_all | solution.py:36
  66.3 0.7 pad_maximum_fusion.2
  67.1 6.3 %all-to-all-done.1 = f32[32,1,4]{2,1,0:T(1,128)S(1)} async-done(((f32[32,1,4]{2,1,0:T(1,128)}), f32[32,1,4]{2,1,0:T(1,128)S(1)}, u32[]{:S(2)}, u32[]{:S(2)}) %all-to-all-start.1) | async-done | bytes 544 | tf_op jit(solution)/shard_map/all_to_all | solution.py:36
  73.4 0.7 sqrt.8
  (178 shorter events, 7.9 us)
Async XLA Ops:
  0.6 15.6 %copy-start = (f32[2,4,16,1024]{3,2,1,0:T(8,128)S(1)}, f32[2,4,16,1024]{3,2,1,0:T(8,128)}, u32[]{:S(2)}) copy-start(f32[2,4,16,1024]{3,2,1,0:T(8,128)} %param.14) | copy-start | bytes 1572868
  0.6 15.6 %copy-start.39 = (s32[1,128]{1,0:T(1,128)S(1)}, s32[1,128]{1,0:T(1,128)}, u32[]{:S(2)}) copy-start(s32[1,128]{1,0:T(1,128)} %param.24) | copy-start | bytes 1540
  0.7 15.6 %copy-start.41 = (f32[1,128]{1,0:T(1,128)S(1)}, f32[1,128]{1,0:T(1,128)}, u32[]{:S(2)}) copy-start(f32[1,128]{1,0:T(1,128)} %param.25) | copy-start | bytes 1540
  1.6 17.3 %copy-start.12 = (f32[16,1024]{1,0:T(8,128)}, f32[16,1024]{1,0:T(8,128)S(1)}, u32[]{:S(2)}) copy-start(f32[16,1024]{1,0:T(8,128)S(1)} %broadcast_select_fusion.1) | copy-start | bytes 196612
  3.2 15.1 %collective-permute-start = (f32[2064]{0:T(1024)S(1)}, f32[2064]{0:T(1024)S(1)}, u32[]{:S(2)}, u32[]{:S(2)}) collective-permute-start(f32[2064]{0:T(1024)S(1)} %pad_maximum_fusion.9), channel_id=1, source_target_pairs={{0,4},{4,8},{8,12},{12,16},{16,20},{20,24},{24,28},{1,5},{5,9},{9,... | collective-permute-start | bytes 24776 | tf_op jit(solution)/shard_map/ppermute | solution.py:13
  9.0 9.9 %copy-start.14 = (f32[16,1024]{1,0:T(8,128)}, f32[16,1024]{1,0:T(8,128)S(1)}, u32[]{:S(2)}) copy-start(f32[16,1024]{1,0:T(8,128)S(1)} %broadcast_select_fusion) | copy-start | bytes 196612
  9.0 9.9 %collective-permute-start.1 = (f32[1024]{0:T(1024)S(1)}, f32[1024]{0:T(1024)S(1)}, u32[]{:S(2)}, u32[]{:S(2)}) collective-permute-start(f32[1024]{0:T(1024)S(1)} %bitcast.404), channel_id=1, source_target_pairs={{0,1},{1,2},{2,3},{4,5},{5,6},{6,7},{8,9},{9,10},{10,11},{12,13},{... | collective-permute-start | bytes 12296 | tf_op jit(solution)/shard_map/ppermute | solution.py:13
  12.4 6.5 %copy-start.1 = (f32[2,2,16,1024]{3,2,1,0:T(8,128)S(1)}, f32[2,2,16,1024]{3,2,1,0:T(8,128)}, u32[]{:S(2)}) copy-start(f32[2,2,16,1024]{3,2,1,0:T(8,128)} %param.13) | copy-start | bytes 786436
  12.4 6.5 %copy-start.2 = (f32[2,2,16,1024]{3,2,1,0:T(8,128)S(1)}, f32[2,2,16,1024]{3,2,1,0:T(8,128)}, u32[]{:S(2)}) copy-start(f32[2,2,16,1024]{3,2,1,0:T(8,128)} %param.15) | copy-start | bytes 786436
  12.4 6.5 %copy-start.22 = (f32[16,1024]{1,0:T(8,128)S(1)}, f32[16,1024]{1,0:T(8,128)}, u32[]{:S(2)}) copy-start(f32[16,1024]{1,0:T(8,128)} %param.17) | copy-start | bytes 196612
  12.4 6.5 %copy-start.23 = (f32[16,1024]{1,0:T(8,128)S(1)}, f32[16,1024]{1,0:T(8,128)}, u32[]{:S(2)}) copy-start(f32[16,1024]{1,0:T(8,128)} %param.18) | copy-start | bytes 196612
  26.6 10.3 %copy-start.32 = (f32[2064]{0:T(1024)S(1)}, f32[2064]{0:T(1024)}, u32[]{:S(2)}) copy-start(f32[2064]{0:T(1024)} %copy-done.31) | copy-start | bytes 24772
  27.0 11.4 %collective-permute-start.4 = (f32[6,2064]{1,0:T(8,128)S(1)}, f32[6,2064]{1,0:T(8,128)S(1)}, u32[]{:S(2)}, u32[]{:S(2)}) collective-permute-start(f32[6,2064]{1,0:T(8,128)S(1)} %pad_maximum_fusion.5), channel_id=1, source_target_pairs={{4,0},{8,4},{12,8},{16,12},{20,16},{24,20},{28,24},{5,1},{9,5},{13... | collective-permute-start | bytes 148616 | tf_op jit(solution)/shard_map/ppermute | solution.py:13
  28.3 10.1 %copy-start.34 = (f32[16]{0:T(128)S(1)}, f32[16]{0:T(128)}, u32[]{:S(2)}) copy-start(f32[16]{0:T(128)} %neg.47) | copy-start | bytes 196
  28.3 10.6 %copy-start.35 = (f32[16]{0:T(128)S(1)}, f32[16]{0:T(128)}, u32[]{:S(2)}) copy-start(f32[16]{0:T(128)} %get-tuple-element.70) | copy-start | bytes 196
  28.3 10.6 %copy-start.28 = (f32[1,2048]{1,0:T(1,128)S(1)}, f32[1,2048]{1,0:T(1,128)}, u32[]{:S(2)}) copy-start(f32[1,2048]{1,0:T(1,128)} %and_select_fusion) | copy-start | bytes 24580
  29.0 8.0 %collective-permute-start.6 = (f32[4,16]{1,0:T(4,128)S(1)}, f32[4,16]{1,0:T(4,128)S(1)}, u32[]{:S(2)}, u32[]{:S(2)}) collective-permute-start(f32[4,16]{1,0:T(4,128)S(1)} %pad_maximum_fusion.10), channel_id=1, source_target_pairs={{0,2},{1,3},{2,0},{3,1},{4,6},{5,7},{6,4},{7,5},{8,10},{9,11},{10,... | collective-permute-start | bytes 776 | tf_op jit(solution)/shard_map/ppermute | solution.py:173
  31.0 6.0 %collective-permute-start.2 = (f32[10,1024]{1,0:T(8,128)S(1)}, f32[10,1024]{1,0:T(8,128)S(1)}, u32[]{:S(2)}, u32[]{:S(2)}) collective-permute-start(f32[10,1024]{1,0:T(8,128)S(1)} %get-tuple-element.72), channel_id=1, source_target_pairs={{0,3},{1,0},{2,1},{3,2},{4,7},{5,4},{6,5},{7,6},{8,11},{9,8},{10,9... | collective-permute-start | bytes 122888 | tf_op jit(solution)/shard_map/ppermute | solution.py:173
  32.5 4.5 %collective-permute-start.3 = (f32[10,1024]{1,0:T(8,128)S(1)}, f32[10,1024]{1,0:T(8,128)S(1)}, u32[]{:S(2)}, u32[]{:S(2)}) collective-permute-start(f32[10,1024]{1,0:T(8,128)S(1)} %get-tuple-element.73), channel_id=1, source_target_pairs={{0,1},{1,2},{2,3},{3,0},{4,5},{5,6},{6,7},{7,4},{8,9},{9,10},{10,1... | collective-permute-start | bytes 122888 | tf_op jit(solution)/shard_map/ppermute | solution.py:173
  32.6 6.3 %collective-permute-start.5 = (f32[6,2064]{1,0:T(8,128)S(1)}, f32[6,2064]{1,0:T(8,128)S(1)}, u32[]{:S(2)}, u32[]{:S(2)}) collective-permute-start(f32[6,2064]{1,0:T(8,128)S(1)} %pad_maximum_fusion.6), channel_id=1, source_target_pairs={{0,4},{4,8},{8,12},{12,16},{16,20},{20,24},{24,28},{1,5},{5,9},{9,... | collective-permute-start | bytes 148616 | tf_op jit(solution)/shard_map/ppermute | solution.py:13
  43.0 3.9 %copy-start.20 = (f32[16,1024]{1,0:T(8,128)S(1)}, f32[16,1024]{1,0:T(8,128)}, u32[]{:S(2)}) copy-start(f32[16,1024]{1,0:T(8,128)} %get-tuple-element.28) | copy-start | bytes 196612
  43.0 3.9 %copy-start.21 = (f32[16,1024]{1,0:T(8,128)S(1)}, f32[16,1024]{1,0:T(8,128)}, u32[]{:S(2)}) copy-start(f32[16,1024]{1,0:T(8,128)} %get-tuple-element.29) | copy-start | bytes 196612
  43.0 3.9 %slice-start = ((f32[10,1024]{1,0:T(8,128)}), f32[6,1024]{1,0:T(8,128)S(1)}, s32[]{:S(2)}) async-start(f32[10,1024]{1,0:T(8,128)} %copy-done.26), calls=%async_computation.2 | async-start | bytes 65536 | tf_op jit(solution)/shard_map/slice | solution.py:209
  43.1 3.9 %slice-start.1 = ((f32[10,1024]{1,0:T(8,128)}), f32[6,1024]{1,0:T(8,128)S(1)}, s32[]{:S(2)}) async-start(f32[10,1024]{1,0:T(8,128)} %copy-done.27), calls=%async_computation.3 | async-start | bytes 65536 | tf_op jit(solution)/shard_map/slice | solution.py:208
  43.1 3.9 %copy-start.37 = (pred[16]{0:T(512)(128)(4,1)S(1)}, pred[16]{0:T(512)(128)(4,1)}, u32[]{:S(2)}) copy-start(pred[16]{0:T(512)(128)(4,1)} %get-tuple-element.78) | copy-start | bytes 52
  47.8 14.8 %copy-start.8 = (f32[16,1024]{1,0:T(8,128)S(1)}, f32[16,1024]{1,0:T(8,128)}, u32[]{:S(2)}) copy-start(f32[16,1024]{1,0:T(8,128)} %copy-done.7) | copy-start | bytes 196612
  47.8 14.8 %copy-start.10 = (f32[16,1024]{1,0:T(8,128)S(1)}, f32[16,1024]{1,0:T(8,128)}, u32[]{:S(2)}) copy-start(f32[16,1024]{1,0:T(8,128)} %copy-done.9) | copy-start | bytes 196612
  47.9 14.8 %copy-start.25 = (f32[2,2,16,1024]{3,2,1,0:T(8,128)S(1)}, f32[2,2,16,1024]{3,2,1,0:T(8,128)}, u32[]{:S(2)}) copy-start(f32[2,2,16,1024]{3,2,1,0:T(8,128)} %param.16) | copy-start | bytes 786436
  48.0 18.2 %copy-start.6 = (f32[16,1024]{1,0:T(8,128)S(1)}, f32[16,1024]{1,0:T(8,128)}, u32[]{:S(2)}) copy-start(f32[16,1024]{1,0:T(8,128)} %copy-done.5) | copy-start | bytes 196612
  48.0 18.2 %copy-start.17 = (f32[16,1024]{1,0:T(8,128)S(1)}, f32[16,1024]{1,0:T(8,128)}, u32[]{:S(2)}) copy-start(f32[16,1024]{1,0:T(8,128)} %copy-done.16) | copy-start | bytes 196612
  48.0 18.2 %copy-start.19 = (f32[16,1024]{1,0:T(8,128)S(1)}, f32[16,1024]{1,0:T(8,128)}, u32[]{:S(2)}) copy-start(f32[16,1024]{1,0:T(8,128)} %copy-done.18) | copy-start | bytes 196612
  63.7 9.7 %all-to-all-start.1 = ((f32[32,1,4]{2,1,0:T(1,128)}), f32[32,1,4]{2,1,0:T(1,128)S(1)}, u32[]{:S(2)}, u32[]{:S(2)}) async-start(f32[32,1,4]{2,1,0:T(1,128)} %broadcast_in_dim.55), calls=%async_computation.1 | async-start | bytes 32768 | tf_op jit(solution)/shard_map/all_to_all | solution.py:36
  (21 other events, 42.9 us)

commit v15 on v14

--- a/solution.py
+++ b/solution.py
@@ -135,7 +135,9 @@
         [layer_iota * column_count, layer_iota * column_count + (column_count - 1)]
     )
     fault_at = locate(
-        jnp.concatenate([fault_near.reshape(-1), fault_far.reshape(-1), edge_cells])
+        jnp.concatenate(
+            [fault_near.reshape(-1), fault_far.reshape(-1), edge_cells, compl_cell.reshape(-1)]
+        )
     )
     west_face = east_edge
     east_face = trans_east[:, -1]
@@ -228,6 +230,9 @@
         )
         flux_right = weight_here * (picks_near - from_right[:, layer_count:])
         flux_left = weight_left * (from_left[:, layer_count:] - picks_far)
+        back = jnp.dot(summed[1:] / summed[0], well_onehot.T, precision=highest)
+        well_values = well_index * (values - back)
+        well_values = jnp.stack([well_values, jnp.zeros_like(well_values)], axis=1)
         fault_term = scatter(
             jnp.concatenate(
                 [
@@ -235,6 +240,7 @@
                     -flux_left,
                     -west_face * from_left[:, :layer_count],
                     -east_face * from_right[:, :layer_count],
+                    well_values.reshape(count * 2, -1),
                 ],
                 axis=1,
             ),
@@ -242,14 +248,7 @@
             split2,
         )
         laplace = (laplace + fault_term).reshape(count, 2, layer_count, column_count)
-        back = jnp.dot(summed[1:] / summed[0], well_onehot.T, precision=highest)
-        well_term = scatter(well_index * (values - back), well_at)
-        first = (
-            block[:, 0] * fields[:, 0]
-            + block[:, 1] * fields[:, 1]
-            + laplace[:, 0]
-            + well_term
-        )
+        first = block[:, 0] * fields[:, 0] + block[:, 1] * fields[:, 1] + laplace[:, 0]
         second = block[:, 2] * fields[:, 0] + block[:, 3] * fields[:, 1] + laplace[:, 1]
         return jnp.stack([first, second], axis=1)
 

time: 74.7 us -> 80.2 us (1.074)
  other arithmetic: 14.8 us -> 19.3 us
  local copies, waits for them, and re-layouts: 8.56 us -> 11.6 us
  blocking collectives: 13.7 us -> 12.2 us
    all_to_all x1, blocking collectives: 13.7 us -> 12.2 us  [global_sum(): gathered = lax.all_to_all(copies, axes, 0, 0, tiled=True)]
    mul x1, other arithmetic: 0.01 us -> 1.27 us  [operator(): -east_face * from_right[:, :layer_count]]
    mul x1, other arithmetic: 0.01 us -> 1.27 us  [operator(): -west_face * from_left[:, :layer_count]]
    reshape x0 -> x1, local copies, waits for them, and re-layouts: none -> 1.26 us  [operator(): well_values.reshape(count * 2, -1)]
    ppermute x3, waiting for transfers between devices: 0.01 us -> 1.02 us  [slab_shift(): lax.ppermute(value, 'slab', [(i, (i + by) % count) for i in range(count)])]
    neg x1, other arithmetic: 0.75 us -> 1.75 us  [operator(): -flux_left]
    slice x1, local copies, waits for them, and re-layouts: 0.96 us -> 0.06 us  [operator(): scaled[:, 1:, :]]
    slice x1, local copies, waits for them, and re-layouts: 0.17 us -> 1.01 us  [operator(): east = jnp.concatenate([scaled[:, :, 1:], zero_column], axis=2)]
  transfers between devices with their start and end apart: 8 -> 8, of which waited for: 2 -> 2; matrix products, arithmetic and copies ran while one was open for 16% -> 20% of each run, Pallas kernels for 0% -> 0%
where the time goes in v15:
time: 80.2 us; the launch traced here: 79.4 us
  other arithmetic  19.3 us (24%)
  starting transfers between devices  17.4 us (22%)
  blocking collectives  12.2 us (15%)
  local copies, waits for them, and re-layouts  11.6 us (14%)
  matrix products  9.09 us (11%)
  waiting for transfers between devices  7.41 us (9%)
  between operations  2.27 us (3%)
    all_to_all x1, blocking collectives, global_sum(): gathered = lax.all_to_all(copies, axes, 0, 0, tiled=True)  12.2 us
    ppermute x4, starting transfers between devices, shifted(): return lax.ppermute(value, axis, pairs)  11.6 us
    dot_general x3, matrix products, onehot_dot(): lax.dot_general(pieces, onehot, (dims, ((), ())), preferred_element_type=...  7.92 us
    all_to_all x1, waiting for transfers between devices, global_sum(): gathered = lax.all_to_all(copies, axes, 0, 0, tiled=True)  6.38 us
    ppermute x3, starting transfers between devices, slab_shift(): lax.ppermute(value, 'slab', [(i, (i + by) % count) for i in range(count)])  3.26 us
    unnamed x98, local copies, waits for them, and re-layouts  2.56 us
    all_to_all x1, starting transfers between devices, global_sum(): gathered = lax.all_to_all(copies, axes, 0, 0, tiled=True)  2.55 us
    select_n x2, other arithmetic, per_device(): weight_here = jnp.where(slot_live, fault_trans.reshape(-1), zero_value)  2.02 us
  transfers between devices with their start and end apart: 8, of which 2 were waited for; matrix products, arithmetic and copies ran while one was open for 20% of the time, Pallas kernels for 0%

profile of v15, /device:TPU:0, one launch (start us, length us, event | category | flops | bytes accessed | tf_op | source)
XLA Modules:
  0.0 79.4 jit_solution(14423883889286216258)
XLA Ops:
  1.4 0.9 %broadcast_select_fusion.1 = f32[16,1024]{1,0:T(8,128)S(1)} fusion(f32[16,1024]{1,0:T(8,128)} %param.17, pred[1024]{0:T(1024)(128)(4,1)S(1)} %fusion.65), kind=kLoop, calls=%fused_computation.153 | loop fusion | flops 16384 | bytes 132096 | tf_op jit(solution)/shard_map/jit(_where)/select_n | solution.py:91
  2.4 0.7 fusion.63
  3.2 4.9 %collective-permute-start = (f32[2064]{0:T(1024)S(1)}, f32[2064]{0:T(1024)S(1)}, u32[]{:S(2)}, u32[]{:S(2)}) collective-permute-start(f32[2064]{0:T(1024)S(1)} %pad_maximum_fusion.9), channel_id=1, source_target_pairs={{0,4},{4,8},{8,12},{12,16},{16,20},{20,24},{24,28},{1,5},{5,9},{9,... | collective-permute-start | bytes 24776 | tf_op jit(solution)/shard_map/ppermute | solution.py:13
  8.1 0.9 %broadcast_select_fusion = f32[16,1024]{1,0:T(8,128)S(1)} fusion(f32[16,1024]{1,0:T(8,128)} %param.18, pred[16]{0:T(512)(128)(4,1)S(1)} %broadcast_and_fusion), kind=kLoop, calls=%fused_computation.152 | loop fusion | flops 16384 | bytes 131088 | tf_op jit(solution)/shard_map/jit(_where)/select_n | solution.py:94
  9.0 1.5 %collective-permute-start.1 = (f32[1024]{0:T(1024)S(1)}, f32[1024]{0:T(1024)S(1)}, u32[]{:S(2)}, u32[]{:S(2)}) collective-permute-start(f32[1024]{0:T(1024)S(1)} %bitcast.389), channel_id=1, source_target_pairs={{0,1},{1,2},{2,3},{4,5},{5,6},{6,7},{8,9},{9,10},{10,11},{12,13},{... | collective-permute-start | bytes 12296 | tf_op jit(solution)/shard_map/ppermute | solution.py:13
  10.5 1.1 %and_select_fusion.2 = s32[128]{0:T(128)} fusion(s32[1,128]{1,0:T(1,128)} %param.23), kind=kLoop, calls=%fused_computation.189 | loop fusion | flops 1408 | bytes 1024 | tf_op jit(solution)/shard_map/jit(remainder)/select_n | solution.py:115
  12.3 0.8 concatenate.100
  13.7 1.0 %fusion.87 = (f32[1,2,16,1024]{3,2,1,0:T(8,128)S(1)}, f32[1,2,16,1024]{3,2,1,0:T(8,128)S(1)}) fusion(f32[2,2,16,1024]{3,2,1,0:T(8,128)} %param.15), kind=kLoop, calls=%fused_computation.215 | loop fusion | bytes 524288 | tf_op jit(solution)/shard_map/slice | solution.py:152
  14.7 1.3 %and_select_fusion = f32[1,2048]{1,0:T(1,128)} fusion(f32[1,2048]{1,0:T(1,128)} %param.21, pred[]{:T(512)S(6)} %lt.34, s32[]{:T(128)} %bitcast.329), kind=kLoop, calls=%fused_computation.154 | loop fusion | flops 6144 | bytes 16389 | tf_op jit(solution)/shard_map/jit(_where)/select_n | solution.py:101
  16.7 0.8 fusion.56
  19.4 0.7 fusion.43
  21.3 1.0 %fusion.84 = (f32[6,16,1023]{2,1,0:T(8,128)}, f32[6,16,1023]{2,1,0:T(8,128)}) fusion(f32[6,16,1024]{2,1,0:T(8,128)S(1)} %bitcast.333), kind=kLoop, calls=%fused_computation.212 | loop fusion | bytes 1571328 | tf_op jit(solution)/shard_map/slice | solution.py:214
  22.3 3.8 %fusion.1 = f32[192,4256]{1,0:T(8,128)S(1)} fusion(s32[4256]{0:T(1024)S(1)} %copy-done.29, bf16[96,1024]{1,0:T(8,128)(2,1)S(1)} %get-tuple-element.22, bf16[96,1024]{1,0:T(8,128)(2,1)S(1)} %get-tuple-element.23), kind=kOutput, calls=%fused_computation.2 | convolution fusion | flops 1678671872 | bytes 3678848 | tf_op jit(solution)/shard_map/dot_general | solution.py:58
  27.4 0.7 pad_maximum_fusion.6
  28.1 4.0 %collective-permute-start.5 = (f32[6,2064]{1,0:T(8,128)}, f32[6,2064]{1,0:T(8,128)}, u32[]{:S(2)}, u32[]{:S(2)}) collective-permute-start(f32[6,2064]{1,0:T(8,128)} %pad_maximum_fusion.6), channel_id=1, source_target_pairs={{0,4},{4,8},{8,12},{12,16},{16,20},{20,24},{24,28},{1,5},{5,9},{9,... | collective-permute-start | bytes 148616 | tf_op jit(solution)/shard_map/ppermute | solution.py:13
  32.8 2.0 %collective-permute-start.6 = (f32[4,16]{1,0:T(4,128)S(1)}, f32[4,16]{1,0:T(4,128)S(1)}, u32[]{:S(2)}, u32[]{:S(2)}) collective-permute-start(f32[4,16]{1,0:T(4,128)S(1)} %pad_maximum_fusion.10), channel_id=1, source_target_pairs={{0,2},{1,3},{2,0},{3,1},{4,6},{5,7},{6,4},{7,5},{8,10},{9,11},{10,... | collective-permute-start | bytes 776 | tf_op jit(solution)/shard_map/ppermute | solution.py:175
  34.8 1.2 %collective-permute-start.2 = (f32[10,1024]{1,0:T(8,128)S(1)}, f32[10,1024]{1,0:T(8,128)S(1)}, u32[]{:S(2)}, u32[]{:S(2)}) collective-permute-start(f32[10,1024]{1,0:T(8,128)S(1)} %get-tuple-element.71), channel_id=1, source_target_pairs={{0,3},{1,0},{2,1},{3,2},{4,7},{5,4},{6,5},{7,6},{8,11},{9,8},{10,9... | collective-permute-start | bytes 122888 | tf_op jit(solution)/shard_map/ppermute | solution.py:175
  36.1 0.7 pad_maximum_fusion.5
  36.8 1.3 %collective-permute-start.4 = (f32[6,2064]{1,0:T(8,128)}, f32[6,2064]{1,0:T(8,128)}, u32[]{:S(2)}, u32[]{:S(2)}) collective-permute-start(f32[6,2064]{1,0:T(8,128)} %pad_maximum_fusion.5), channel_id=1, source_target_pairs={{4,0},{8,4},{12,8},{16,12},{20,16},{24,20},{28,24},{5,1},{9,5},{13... | collective-permute-start | bytes 148616 | tf_op jit(solution)/shard_map/ppermute | solution.py:13
  38.1 0.7 slice.407
  38.7 1.0 %collective-permute-done.3 = f32[10,1024]{1,0:T(8,128)S(1)} collective-permute-done((f32[10,1024]{1,0:T(8,128)S(1)}, f32[10,1024]{1,0:T(8,128)S(1)}, u32[]{:S(2)}, u32[]{:S(2)}) %collective-permute-start.3) | collective-permute-done | bytes 40992 | tf_op jit(solution)/shard_map/ppermute | solution.py:175
  41.3 1.3 %reshape.560 = f32[6,128]{1,0:T(8,128)} reshape(f32[3,2,128]{2,1,0:T(2,128)} %stack.138.clone) | data formatting | bytes 6144 | tf_op jit(solution)/shard_map/reshape | solution.py:243
  42.5 1.3 %slice_multiply_fusion.5 = f32[6,16]{1,0:T(8,128)} fusion(f32[6,2064]{1,0:T(8,128)} %collective-permute-done.5, f32[16]{0:T(128)} %get-tuple-element.68), kind=kLoop, calls=%fused_computation.176 | loop fusion | flops 96 | bytes 832 | tf_op jit(solution)/shard_map/mul | solution.py:241
  43.8 1.3 %slice_multiply_fusion.4 = f32[6,16]{1,0:T(8,128)} fusion(f32[6,2064]{1,0:T(8,128)} %collective-permute-done.4, f32[16]{0:T(128)} %neg.47), kind=kLoop, calls=%fused_computation.175 | loop fusion | flops 96 | bytes 832 | tf_op jit(solution)/shard_map/mul | solution.py:242
  45.1 1.8 %fusion.38 = (f32[6,2048]{1,0:T(8,128)}, f32[6,2048]{1,0:T(8,128)}) fusion(f32[6,2064]{1,0:T(8,128)} %collective-permute-done.5, f32[2048]{0:T(1024)} %slice.407, f32[6,4256]{1,0:T(8,128)} %copy-done.5, f32[6,2064]{1,0:T(8,128)} %collective-permute-done.4, f32[2048]{0:T(1024)} %bitcast.366), kind=kLoop, calls=%fused_computation.95 | loop fusion | flops 61440 | bytes 311296 | tf_op jit(solution)/shard_map/neg | solution.py:240
  46.8 1.6 %concatenate.103 = f32[6,4256]{1,0:T(8,128)} concatenate(f32[6,2048]{1,0:T(8,128)} %get-tuple-element.54, f32[6,2048]{1,0:T(8,128)} %get-tuple-element.53, f32[6,16]{1,0:T(8,128)} %slice_multiply_fusion.5, f32[6,16]{1,0:T(8,128)} %slice_multiply_fusion.4, f32[6,128]{1,0:T(8,128)} %reshape.560), dimensions={1} | concatenate | bytes 204288 | tf_op jit(solution)/shard_map/concatenate | solution.py:237
  48.4 1.0 %broadcast_multiply_fusion = f32[6,16,4256]{2,1,0:T(8,128)S(1)} fusion(f32[6,4256]{1,0:T(8,128)} %concatenate.103, f32[16,4256]{1,0:T(8,128)S(1)} %fusion.20), kind=kLoop, calls=%fused_computation.16 | loop fusion | flops 408576 | bytes 2008832 | tf_op jit(solution)/shard_map/mul | solution.py:130
  50.2 3.8 %fusion = f32[192,1024]{1,0:T(8,128)S(1)} fusion(s32[4256]{0:T(1024)S(1)} %copy-done.30, bf16[96,4256]{1,0:T(8,128)(2,1)S(1)} %get-tuple-element.20, bf16[96,4256]{1,0:T(8,128)(2,1)S(1)} %get-tuple-element.21), kind=kOutput, calls=%fused_computation.1 | convolution fusion | flops 1681154048 | bytes 2437760 | tf_op jit(solution)/shard_map/dot_general | solution.py:58
  55.5 12.2 %all_to_all.12 = f32[32,1,10]{2,1,0:T(1,128)S(1)} all-to-all(f32[32,1,10]{2,1,0:T(1,128)S(1)} %broadcast_in_dim.53), channel_id=1, replica_groups=mesh['cells'=8,'slab'=4] {'cells','slab'}, dimensions={0} | all-to-all | bytes 2560 | tf_op jit(solution)/shard_map/all_to_all | solution.py:36
  69.0 2.6 %all-to-all-start.1 = ((f32[32,1,4]{2,1,0:T(1,128)}), f32[32,1,4]{2,1,0:T(1,128)S(1)}, u32[]{:S(2)}, u32[]{:S(2)}) async-start(f32[32,1,4]{2,1,0:T(1,128)} %broadcast_in_dim.55), calls=%async_computation.1 | async-start | bytes 32768 | tf_op jit(solution)/shard_map/all_to_all | solution.py:36
  71.6 0.7 pad_maximum_fusion.2
  72.3 6.4 %all-to-all-done.1 = f32[32,1,4]{2,1,0:T(1,128)S(1)} async-done(((f32[32,1,4]{2,1,0:T(1,128)}), f32[32,1,4]{2,1,0:T(1,128)S(1)}, u32[]{:S(2)}, u32[]{:S(2)}) %all-to-all-start.1) | async-done | bytes 544 | tf_op jit(solution)/shard_map/all_to_all | solution.py:36
  (172 shorter events, 12.3 us)
Async XLA Ops:
  0.6 16.0 %copy-start = (f32[2,4,16,1024]{3,2,1,0:T(8,128)S(1)}, f32[2,4,16,1024]{3,2,1,0:T(8,128)}, u32[]{:S(2)}) copy-start(f32[2,4,16,1024]{3,2,1,0:T(8,128)} %param.14) | copy-start | bytes 1572868
  0.6 16.1 %copy-start.36 = (s32[1,128]{1,0:T(1,128)S(1)}, s32[1,128]{1,0:T(1,128)}, u32[]{:S(2)}) copy-start(s32[1,128]{1,0:T(1,128)} %param.24) | copy-start | bytes 1540
  0.7 16.1 %copy-start.38 = (f32[1,128]{1,0:T(1,128)S(1)}, f32[1,128]{1,0:T(1,128)}, u32[]{:S(2)}) copy-start(f32[1,128]{1,0:T(1,128)} %param.25) | copy-start | bytes 1540
  2.2 17.1 %copy-start.12 = (f32[16,1024]{1,0:T(8,128)}, f32[16,1024]{1,0:T(8,128)S(1)}, u32[]{:S(2)}) copy-start(f32[16,1024]{1,0:T(8,128)S(1)} %broadcast_select_fusion.1) | copy-start | bytes 196612
  3.2 15.6 %collective-permute-start = (f32[2064]{0:T(1024)S(1)}, f32[2064]{0:T(1024)S(1)}, u32[]{:S(2)}, u32[]{:S(2)}) collective-permute-start(f32[2064]{0:T(1024)S(1)} %pad_maximum_fusion.9), channel_id=1, source_target_pairs={{0,4},{4,8},{8,12},{12,16},{16,20},{20,24},{24,28},{1,5},{5,9},{9,... | collective-permute-start | bytes 24776 | tf_op jit(solution)/shard_map/ppermute | solution.py:13
  9.0 10.4 %copy-start.14 = (f32[16,1024]{1,0:T(8,128)}, f32[16,1024]{1,0:T(8,128)S(1)}, u32[]{:S(2)}) copy-start(f32[16,1024]{1,0:T(8,128)S(1)} %broadcast_select_fusion) | copy-start | bytes 196612
  9.0 10.4 %collective-permute-start.1 = (f32[1024]{0:T(1024)S(1)}, f32[1024]{0:T(1024)S(1)}, u32[]{:S(2)}, u32[]{:S(2)}) collective-permute-start(f32[1024]{0:T(1024)S(1)} %bitcast.389), channel_id=1, source_target_pairs={{0,1},{1,2},{2,3},{4,5},{5,6},{6,7},{8,9},{9,10},{10,11},{12,13},{... | collective-permute-start | bytes 12296 | tf_op jit(solution)/shard_map/ppermute | solution.py:13
  13.1 6.3 %copy-start.1 = (f32[2,2,16,1024]{3,2,1,0:T(8,128)S(1)}, f32[2,2,16,1024]{3,2,1,0:T(8,128)}, u32[]{:S(2)}) copy-start(f32[2,2,16,1024]{3,2,1,0:T(8,128)} %param.13) | copy-start | bytes 786436
  13.1 6.3 %copy-start.2 = (f32[2,2,16,1024]{3,2,1,0:T(8,128)S(1)}, f32[2,2,16,1024]{3,2,1,0:T(8,128)}, u32[]{:S(2)}) copy-start(f32[2,2,16,1024]{3,2,1,0:T(8,128)} %param.15) | copy-start | bytes 786436
  13.1 6.3 %copy-start.22 = (f32[16,1024]{1,0:T(8,128)S(1)}, f32[16,1024]{1,0:T(8,128)}, u32[]{:S(2)}) copy-start(f32[16,1024]{1,0:T(8,128)} %param.17) | copy-start | bytes 196612
  13.1 6.3 %copy-start.23 = (f32[16,1024]{1,0:T(8,128)S(1)}, f32[16,1024]{1,0:T(8,128)}, u32[]{:S(2)}) copy-start(f32[16,1024]{1,0:T(8,128)} %param.18) | copy-start | bytes 196612
  26.3 5.8 %copy-start.40 = (s32[128]{0:T(128)S(1)}, s32[128]{0:T(128)}, u32[]{:S(2)}) copy-start(s32[128]{0:T(128)} %and_select_fusion.2) | copy-start | bytes 1540
  26.3 6.2 %copy-start.28 = (f32[16,128]{1,0:T(8,128)S(1)}, f32[16,128]{1,0:T(8,128)}, u32[]{:S(2)}) copy-start(f32[16,128]{1,0:T(8,128)} %fusion.64) | copy-start | bytes 24580
  26.3 6.2 %copy-start.37 = (s32[1,128]{1,0:T(1,128)S(1)}, s32[1,128]{1,0:T(1,128)}, u32[]{:S(2)}) copy-start(s32[1,128]{1,0:T(1,128)} %param.24) | copy-start | bytes 1540
  26.3 6.2 %copy-start.39 = (f32[1,128]{1,0:T(1,128)S(1)}, f32[1,128]{1,0:T(1,128)}, u32[]{:S(2)}) copy-start(f32[1,128]{1,0:T(1,128)} %param.25) | copy-start | bytes 1540
  26.3 6.4 %copy-start.33 = (f32[1,16]{1,0:T(1,128)S(1)}, f32[1,16]{1,0:T(1,128)}, u32[]{:S(2)}) copy-start(f32[1,16]{1,0:T(1,128)} %fusion.56) | copy-start | bytes 196
  26.4 11.7 %copy-start.32 = (f32[2064]{0:T(1024)S(1)}, f32[2064]{0:T(1024)}, u32[]{:S(2)}) copy-start(f32[2064]{0:T(1024)} %copy-done.31) | copy-start | bytes 24772
  28.1 14.4 %collective-permute-start.5 = (f32[6,2064]{1,0:T(8,128)}, f32[6,2064]{1,0:T(8,128)}, u32[]{:S(2)}, u32[]{:S(2)}) collective-permute-start(f32[6,2064]{1,0:T(8,128)} %pad_maximum_fusion.6), channel_id=1, source_target_pairs={{0,4},{4,8},{8,12},{12,16},{16,20},{20,24},{24,28},{1,5},{5,9},{9,... | collective-permute-start | bytes 148616 | tf_op jit(solution)/shard_map/ppermute | solution.py:13
  32.8 6.0 %collective-permute-start.6 = (f32[4,16]{1,0:T(4,128)S(1)}, f32[4,16]{1,0:T(4,128)S(1)}, u32[]{:S(2)}, u32[]{:S(2)}) collective-permute-start(f32[4,16]{1,0:T(4,128)S(1)} %pad_maximum_fusion.10), channel_id=1, source_target_pairs={{0,2},{1,3},{2,0},{3,1},{4,6},{5,7},{6,4},{7,5},{8,10},{9,11},{10,... | collective-permute-start | bytes 776 | tf_op jit(solution)/shard_map/ppermute | solution.py:175
  34.8 3.9 %collective-permute-start.2 = (f32[10,1024]{1,0:T(8,128)S(1)}, f32[10,1024]{1,0:T(8,128)S(1)}, u32[]{:S(2)}, u32[]{:S(2)}) collective-permute-start(f32[10,1024]{1,0:T(8,128)S(1)} %get-tuple-element.71), channel_id=1, source_target_pairs={{0,3},{1,0},{2,1},{3,2},{4,7},{5,4},{6,5},{7,6},{8,11},{9,8},{10,9... | collective-permute-start | bytes 122888 | tf_op jit(solution)/shard_map/ppermute | solution.py:175
  36.1 3.7 %collective-permute-start.3 = (f32[10,1024]{1,0:T(8,128)S(1)}, f32[10,1024]{1,0:T(8,128)S(1)}, u32[]{:S(2)}, u32[]{:S(2)}) collective-permute-start(f32[10,1024]{1,0:T(8,128)S(1)} %get-tuple-element.70), channel_id=1, source_target_pairs={{0,1},{1,2},{2,3},{3,0},{4,5},{5,6},{6,7},{7,4},{8,9},{9,10},{10,1... | collective-permute-start | bytes 122888 | tf_op jit(solution)/shard_map/ppermute | solution.py:175
  36.8 7.0 %collective-permute-start.4 = (f32[6,2064]{1,0:T(8,128)}, f32[6,2064]{1,0:T(8,128)}, u32[]{:S(2)}, u32[]{:S(2)}) collective-permute-start(f32[6,2064]{1,0:T(8,128)} %pad_maximum_fusion.5), channel_id=1, source_target_pairs={{4,0},{8,4},{12,8},{16,12},{20,16},{24,20},{28,24},{5,1},{9,5},{13... | collective-permute-start | bytes 148616 | tf_op jit(solution)/shard_map/ppermute | solution.py:13
  50.2 4.0 %copy-start.20 = (f32[16,1024]{1,0:T(8,128)S(1)}, f32[16,1024]{1,0:T(8,128)}, u32[]{:S(2)}) copy-start(f32[16,1024]{1,0:T(8,128)} %get-tuple-element.28) | copy-start | bytes 196612
  50.2 4.0 %copy-start.21 = (f32[16,1024]{1,0:T(8,128)S(1)}, f32[16,1024]{1,0:T(8,128)}, u32[]{:S(2)}) copy-start(f32[16,1024]{1,0:T(8,128)} %get-tuple-element.29) | copy-start | bytes 196612
  50.2 4.0 %slice-start = ((f32[10,1024]{1,0:T(8,128)}), f32[6,1024]{1,0:T(8,128)S(1)}, s32[]{:S(2)}) async-start(f32[10,1024]{1,0:T(8,128)} %copy-done.26), calls=%async_computation.2 | async-start | bytes 65536 | tf_op jit(solution)/shard_map/slice | solution.py:210
  54.6 13.4 %copy-start.9 = (f32[16,1024]{1,0:T(8,128)S(1)}, f32[16,1024]{1,0:T(8,128)}, u32[]{:S(2)}) copy-start(f32[16,1024]{1,0:T(8,128)} %copy-done.8) | copy-start | bytes 196612
  54.6 13.4 %copy-start.11 = (f32[16,1024]{1,0:T(8,128)S(1)}, f32[16,1024]{1,0:T(8,128)}, u32[]{:S(2)}) copy-start(f32[16,1024]{1,0:T(8,128)} %copy-done.10) | copy-start | bytes 196612
  54.6 13.4 %copy-start.25 = (f32[2,2,16,1024]{3,2,1,0:T(8,128)S(1)}, f32[2,2,16,1024]{3,2,1,0:T(8,128)}, u32[]{:S(2)}) copy-start(f32[2,2,16,1024]{3,2,1,0:T(8,128)} %param.16) | copy-start | bytes 786436
  54.7 13.4 %copy-start.7 = (f32[16,1024]{1,0:T(8,128)S(1)}, f32[16,1024]{1,0:T(8,128)}, u32[]{:S(2)}) copy-start(f32[16,1024]{1,0:T(8,128)} %copy-done.6) | copy-start | bytes 196612
  54.7 13.4 %copy-start.17 = (f32[16,1024]{1,0:T(8,128)S(1)}, f32[16,1024]{1,0:T(8,128)}, u32[]{:S(2)}) copy-start(f32[16,1024]{1,0:T(8,128)} %copy-done.16) | copy-start | bytes 196612
  54.7 13.4 %copy-start.19 = (f32[16,1024]{1,0:T(8,128)S(1)}, f32[16,1024]{1,0:T(8,128)}, u32[]{:S(2)}) copy-start(f32[16,1024]{1,0:T(8,128)} %copy-done.18) | copy-start | bytes 196612
  69.0 9.7 %all-to-all-start.1 = ((f32[32,1,4]{2,1,0:T(1,128)}), f32[32,1,4]{2,1,0:T(1,128)S(1)}, u32[]{:S(2)}, u32[]{:S(2)}) async-start(f32[32,1,4]{2,1,0:T(1,128)} %broadcast_in_dim.55), calls=%async_computation.1 | async-start | bytes 32768 | tf_op jit(solution)/shard_map/all_to_all | solution.py:36
  (19 other events, 40.1 us)

commit v16 on v14

--- a/solution.py
+++ b/solution.py
@@ -271,7 +271,6 @@
             [
                 (grad_last, image_last),
                 (image_last, image_last),
-                (grad_last, grad_last),
                 (grad_first, direct),
                 (grad_first, coupled),
                 (carried, direct),
@@ -288,7 +287,6 @@
     (
         along_last,
         energy_last,
-        norm_last,
         grad_direct,
         grad_coupled,
         carried_direct,

time: 74.7 us -> 75.3 us (level)
  blocking collectives: 13.7 us -> 0 us
  waiting for transfers between devices: 6.85 us -> 13.9 us
  starting transfers between devices: 18 us -> 24.6 us
    all_to_all x1 -> x0, blocking collectives: 13.7 us -> none  [global_sum(): gathered = lax.all_to_all(copies, axes, 0, 0, tiled=True)]
    all_to_all x1 -> x2, waiting for transfers between devices: 6.31 us -> 13.4 us  [global_sum(): gathered = lax.all_to_all(copies, axes, 0, 0, tiled=True)]
    all_to_all x1 -> x2, starting transfers between devices: 2.56 us -> 9.23 us  [global_sum(): gathered = lax.all_to_all(copies, axes, 0, 0, tiled=True)]
  transfers between devices with their start and end apart: 8 -> 9, of which waited for: 2 -> 3; matrix products, arithmetic and copies ran while one was open for 16% -> 16% of each run, Pallas kernels for 0% -> 0%
where the time goes in v16:
time: 75.3 us; the launch traced here: 74.7 us
  starting transfers between devices  24.6 us (33%)
  other arithmetic  14.8 us (20%)
  waiting for transfers between devices  13.9 us (18%)
  matrix products  9.9 us (13%)
  local copies, waits for them, and re-layouts  9.12 us (12%)
  between operations  2.31 us (3%)
    all_to_all x2, waiting for transfers between devices, global_sum(): gathered = lax.all_to_all(copies, axes, 0, 0, tiled=True)  13.4 us
    ppermute x4, starting transfers between devices, shifted(): return lax.ppermute(value, axis, pairs)  11.9 us
    all_to_all x2, starting transfers between devices, global_sum(): gathered = lax.all_to_all(copies, axes, 0, 0, tiled=True)  9.23 us
    dot_general x4, matrix products, onehot_dot(): lax.dot_general(pieces, onehot, (dims, ((), ())), preferred_element_type=...  8.72 us
    ppermute x3, starting transfers between devices, slab_shift(): lax.ppermute(value, 'slab', [(i, (i + by) % count) for i in range(count)])  3.53 us
    select_n x2, other arithmetic, per_device(): weight_here = jnp.where(slot_live, fault_trans.reshape(-1), zero_value)  2.02 us
    unnamed x101, local copies, waits for them, and re-layouts  1.86 us
    concatenate x1, local copies, waits for them, and re-layouts, operator(): jnp.concatenate([flux_right, -flux_left, -west_face * from_left[:, :layer...  1.59 us
  transfers between devices with their start and end apart: 9, of which 3 were waited for; matrix products, arithmetic and copies ran while one was open for 16% of the time, Pallas kernels for 0%

profile of v16, /device:TPU:0, one launch (start us, length us, event | category | flops | bytes accessed | tf_op | source)
XLA Modules:
  0.0 74.7 jit_solution(1190001011573831416)
XLA Ops:
  0.7 0.9 %broadcast_select_fusion.1 = f32[16,1024]{1,0:T(8,128)S(1)} fusion(f32[16,1024]{1,0:T(8,128)} %param.17, pred[1024]{0:T(1024)(128)(4,1)S(1)} %fusion.73), kind=kLoop, calls=%fused_computation.162 | loop fusion | flops 16384 | bytes 132096 | tf_op jit(solution)/shard_map/jit(_where)/select_n | solution.py:91
  2.4 0.7 fusion.71
  3.2 4.9 %collective-permute-start = (f32[2064]{0:T(1024)S(1)}, f32[2064]{0:T(1024)S(1)}, u32[]{:S(2)}, u32[]{:S(2)}) collective-permute-start(f32[2064]{0:T(1024)S(1)} %pad_maximum_fusion.9), channel_id=1, source_target_pairs={{0,4},{4,8},{8,12},{12,16},{16,20},{20,24},{24,28},{1,5},{5,9},{9,... | collective-permute-start | bytes 24776 | tf_op jit(solution)/shard_map/ppermute | solution.py:13
  8.1 0.9 %broadcast_select_fusion = f32[16,1024]{1,0:T(8,128)S(1)} fusion(f32[16,1024]{1,0:T(8,128)} %param.18, pred[16]{0:T(512)(128)(4,1)S(1)} %broadcast_and_fusion), kind=kLoop, calls=%fused_computation.161 | loop fusion | flops 16384 | bytes 131088 | tf_op jit(solution)/shard_map/jit(_where)/select_n | solution.py:94
  9.0 1.5 %collective-permute-start.1 = (f32[1024]{0:T(1024)S(1)}, f32[1024]{0:T(1024)S(1)}, u32[]{:S(2)}, u32[]{:S(2)}) collective-permute-start(f32[1024]{0:T(1024)S(1)} %bitcast.403), channel_id=1, source_target_pairs={{0,1},{1,2},{2,3},{4,5},{5,6},{6,7},{8,9},{9,10},{10,11},{12,13},{... | collective-permute-start | bytes 12296 | tf_op jit(solution)/shard_map/ppermute | solution.py:13
  10.5 1.2 %and_select_fusion.2 = s32[128]{0:T(128)} fusion(s32[1,128]{1,0:T(1,128)} %param.23), kind=kLoop, calls=%fused_computation.203 | loop fusion | flops 1408 | bytes 1024 | tf_op jit(solution)/shard_map/jit(remainder)/select_n | solution.py:115
  11.7 0.7 fusion.80
  12.4 1.0 %fusion.96 = (f32[1,2,16,1024]{3,2,1,0:T(8,128)S(1)}, f32[1,2,16,1024]{3,2,1,0:T(8,128)S(1)}) fusion(f32[2,2,16,1024]{3,2,1,0:T(8,128)} %param.15), kind=kLoop, calls=%fused_computation.230 | loop fusion | bytes 524288 | tf_op jit(solution)/shard_map/slice | solution.py:150
  13.5 0.8 %concatenate.103 = s32[4128]{0:T(1024)S(1)} concatenate(s32[2048]{0:T(1024)} %bitcast.400, s32[2048]{0:T(1024)} %bitcast.401, s32[16]{0:T(128)S(1)} %get-tuple-element.76, s32[16]{0:T(128)S(1)} %get-tuple-element.77), dimensions={0} | concatenate | bytes 33024 | tf_op jit(solution)/shard_map/concatenate | solution.py:138
  14.3 0.6 add_select_fusion
  14.9 1.3 %and_select_fusion = f32[1,2048]{1,0:T(1,128)} fusion(f32[1,2048]{1,0:T(1,128)} %param.21, pred[]{:T(512)S(6)} %lt.34, s32[]{:T(128)} %bitcast.343), kind=kLoop, calls=%fused_computation.163 | loop fusion | flops 6144 | bytes 16389 | tf_op jit(solution)/shard_map/jit(_where)/select_n | solution.py:101
  16.3 0.8 %fusion.58 = f32[1,16]{1,0:T(1,128)} fusion(s32[128]{0:T(128)S(1)} %bitcast.404, f32[1,128]{1,0:T(1,128)S(1)} %copy-done.41), kind=kOutput, calls=%fused_computation.144 | convolution fusion | flops 26624 | bytes 1088 | tf_op jit(solution)/shard_map/dot_general | solution.py:187
  18.9 0.7 fusion.45
  21.0 1.0 %fusion.95 = (f32[6,15,1024]{2,1,0:T(8,128)}, f32[6,15,1024]{2,1,0:T(8,128)}) fusion(f32[6,16,1024]{2,1,0:T(8,128)S(1)} %bitcast.347), kind=kLoop, calls=%fused_computation.229 | loop fusion | bytes 1474560 | tf_op jit(solution)/shard_map/slice | solution.py:221
  22.0 4.3 %fusion.1 = f32[192,4128]{1,0:T(8,128)S(1)} fusion(s32[4128]{0:T(1024)S(1)} %copy-done.29, bf16[96,1024]{1,0:T(8,128)(2,1)S(1)} %get-tuple-element.22, bf16[96,1024]{1,0:T(8,128)(2,1)S(1)} %get-tuple-element.23), kind=kOutput, calls=%fused_computation.2 | convolution fusion | flops 1628209152 | bytes 3580032 | tf_op jit(solution)/shard_map/dot_general | solution.py:58
  27.0 1.3 %collective-permute-start.4 = (f32[6,2064]{1,0:T(8,128)S(1)}, f32[6,2064]{1,0:T(8,128)S(1)}, u32[]{:S(2)}, u32[]{:S(2)}) collective-permute-start(f32[6,2064]{1,0:T(8,128)S(1)} %pad_maximum_fusion.5), channel_id=1, source_target_pairs={{4,0},{8,4},{12,8},{16,12},{20,16},{24,20},{28,24},{5,1},{9,5},{13... | collective-permute-start | bytes 148616 | tf_op jit(solution)/shard_map/ppermute | solution.py:13
  29.0 2.0 %collective-permute-start.6 = (f32[4,16]{1,0:T(4,128)S(1)}, f32[4,16]{1,0:T(4,128)S(1)}, u32[]{:S(2)}, u32[]{:S(2)}) collective-permute-start(f32[4,16]{1,0:T(4,128)S(1)} %pad_maximum_fusion.10), channel_id=1, source_target_pairs={{0,2},{1,3},{2,0},{3,1},{4,6},{5,7},{6,4},{7,5},{8,10},{9,11},{10,... | collective-permute-start | bytes 776 | tf_op jit(solution)/shard_map/ppermute | solution.py:173
  31.0 1.5 %collective-permute-start.2 = (f32[10,1024]{1,0:T(8,128)S(1)}, f32[10,1024]{1,0:T(8,128)S(1)}, u32[]{:S(2)}, u32[]{:S(2)}) collective-permute-start(f32[10,1024]{1,0:T(8,128)S(1)} %get-tuple-element.72), channel_id=1, source_target_pairs={{0,3},{1,0},{2,1},{3,2},{4,7},{5,4},{6,5},{7,6},{8,11},{9,8},{10,9... | collective-permute-start | bytes 122888 | tf_op jit(solution)/shard_map/ppermute | solution.py:173
  32.6 4.3 %collective-permute-start.5 = (f32[6,2064]{1,0:T(8,128)S(1)}, f32[6,2064]{1,0:T(8,128)S(1)}, u32[]{:S(2)}, u32[]{:S(2)}) collective-permute-start(f32[6,2064]{1,0:T(8,128)S(1)} %pad_maximum_fusion.6), channel_id=1, source_target_pairs={{0,4},{4,8},{8,12},{12,16},{16,20},{20,24},{24,28},{1,5},{5,9},{9,... | collective-permute-start | bytes 148616 | tf_op jit(solution)/shard_map/ppermute | solution.py:13
  37.6 0.7 slice_add_fusion.3
  38.9 0.7 fusion.40
  39.6 1.6 %concatenate.106 = f32[6,4128]{1,0:T(8,128)} concatenate(f32[6,2048]{1,0:T(8,128)} %get-tuple-element.54, f32[6,2048]{1,0:T(8,128)} %get-tuple-element.53, f32[6,16]{1,0:T(8,128)S(1)} %slice_multiply_fusion.5, f32[6,16]{1,0:T(8,128)S(1)} %slice_multiply_fusion.4), dimensions={1} | concatenate | bytes 198144 | tf_op jit(solution)/shard_map/concatenate | solution.py:232
  41.2 1.0 %broadcast_multiply_fusion = f32[6,16,4128]{2,1,0:T(8,128)S(1)} fusion(f32[6,4128]{1,0:T(8,128)} %concatenate.106, f32[16,4128]{1,0:T(8,128)S(1)} %fusion.20), kind=kLoop, calls=%fused_computation.15 | loop fusion | flops 396288 | bytes 1948416 | tf_op jit(solution)/shard_map/mul | solution.py:130
  43.0 3.8 %fusion = f32[192,1024]{1,0:T(8,128)S(1)} fusion(s32[4128]{0:T(1024)S(1)} %copy-done.30, bf16[96,4128]{1,0:T(8,128)(2,1)S(1)} %get-tuple-element.20, bf16[96,4128]{1,0:T(8,128)(2,1)S(1)} %get-tuple-element.21), kind=kOutput, calls=%fused_computation.1 | convolution fusion | flops 1630593024 | bytes 2388096 | tf_op jit(solution)/shard_map/dot_general | solution.py:58
  48.7 0.6 broadcast_in_dim.53
  49.3 6.7 %all-to-all-start = ((f32[32,1,9]{2,1,0:T(1,128)}), f32[32,1,9]{2,1,0:T(1,128)S(1)}, u32[]{:S(2)}, u32[]{:S(2)}) async-start(f32[32,1,9]{2,1,0:T(1,128)} %broadcast_in_dim.53), calls=%async_computation | async-start | bytes 32768 | tf_op jit(solution)/shard_map/all_to_all | solution.py:36
  56.1 7.1 %all-to-all-done = f32[32,1,9]{2,1,0:T(1,128)S(1)} async-done(((f32[32,1,9]{2,1,0:T(1,128)}), f32[32,1,9]{2,1,0:T(1,128)S(1)}, u32[]{:S(2)}, u32[]{:S(2)}) %all-to-all-start) | async-done | bytes 1184 | tf_op jit(solution)/shard_map/all_to_all | solution.py:36
  63.7 0.6 broadcast_in_dim.55
  64.3 2.5 %all-to-all-start.1 = ((f32[32,1,4]{2,1,0:T(1,128)}), f32[32,1,4]{2,1,0:T(1,128)S(1)}, u32[]{:S(2)}, u32[]{:S(2)}) async-start(f32[32,1,4]{2,1,0:T(1,128)} %broadcast_in_dim.55), calls=%async_computation.1 | async-start | bytes 32768 | tf_op jit(solution)/shard_map/all_to_all | solution.py:36
  66.9 0.7 pad_maximum_fusion.2
  67.6 6.3 %all-to-all-done.1 = f32[32,1,4]{2,1,0:T(1,128)S(1)} async-done(((f32[32,1,4]{2,1,0:T(1,128)}), f32[32,1,4]{2,1,0:T(1,128)S(1)}, u32[]{:S(2)}, u32[]{:S(2)}) %all-to-all-start.1) | async-done | bytes 544 | tf_op jit(solution)/shard_map/all_to_all | solution.py:36
  74.0 0.7 sqrt.8
  (179 shorter events, 8.9 us)
Async XLA Ops:
  0.6 15.6 %copy-start = (f32[2,4,16,1024]{3,2,1,0:T(8,128)S(1)}, f32[2,4,16,1024]{3,2,1,0:T(8,128)}, u32[]{:S(2)}) copy-start(f32[2,4,16,1024]{3,2,1,0:T(8,128)} %param.14) | copy-start | bytes 1572868
  0.6 15.7 %copy-start.39 = (s32[1,128]{1,0:T(1,128)S(1)}, s32[1,128]{1,0:T(1,128)}, u32[]{:S(2)}) copy-start(s32[1,128]{1,0:T(1,128)} %param.24) | copy-start | bytes 1540
  0.7 15.7 %copy-start.41 = (f32[1,128]{1,0:T(1,128)S(1)}, f32[1,128]{1,0:T(1,128)}, u32[]{:S(2)}) copy-start(f32[1,128]{1,0:T(1,128)} %param.25) | copy-start | bytes 1540
  1.6 17.3 %copy-start.12 = (f32[16,1024]{1,0:T(8,128)}, f32[16,1024]{1,0:T(8,128)S(1)}, u32[]{:S(2)}) copy-start(f32[16,1024]{1,0:T(8,128)S(1)} %broadcast_select_fusion.1) | copy-start | bytes 196612
  3.2 15.1 %collective-permute-start = (f32[2064]{0:T(1024)S(1)}, f32[2064]{0:T(1024)S(1)}, u32[]{:S(2)}, u32[]{:S(2)}) collective-permute-start(f32[2064]{0:T(1024)S(1)} %pad_maximum_fusion.9), channel_id=1, source_target_pairs={{0,4},{4,8},{8,12},{12,16},{16,20},{20,24},{24,28},{1,5},{5,9},{9,... | collective-permute-start | bytes 24776 | tf_op jit(solution)/shard_map/ppermute | solution.py:13
  9.0 9.9 %copy-start.14 = (f32[16,1024]{1,0:T(8,128)}, f32[16,1024]{1,0:T(8,128)S(1)}, u32[]{:S(2)}) copy-start(f32[16,1024]{1,0:T(8,128)S(1)} %broadcast_select_fusion) | copy-start | bytes 196612
  9.0 9.8 %collective-permute-start.1 = (f32[1024]{0:T(1024)S(1)}, f32[1024]{0:T(1024)S(1)}, u32[]{:S(2)}, u32[]{:S(2)}) collective-permute-start(f32[1024]{0:T(1024)S(1)} %bitcast.403), channel_id=1, source_target_pairs={{0,1},{1,2},{2,3},{4,5},{5,6},{6,7},{8,9},{9,10},{10,11},{12,13},{... | collective-permute-start | bytes 12296 | tf_op jit(solution)/shard_map/ppermute | solution.py:13
  12.4 6.5 %copy-start.1 = (f32[2,2,16,1024]{3,2,1,0:T(8,128)S(1)}, f32[2,2,16,1024]{3,2,1,0:T(8,128)}, u32[]{:S(2)}) copy-start(f32[2,2,16,1024]{3,2,1,0:T(8,128)} %param.13) | copy-start | bytes 786436
  12.4 6.5 %copy-start.2 = (f32[2,2,16,1024]{3,2,1,0:T(8,128)S(1)}, f32[2,2,16,1024]{3,2,1,0:T(8,128)}, u32[]{:S(2)}) copy-start(f32[2,2,16,1024]{3,2,1,0:T(8,128)} %param.15) | copy-start | bytes 786436
  12.4 6.5 %copy-start.22 = (f32[16,1024]{1,0:T(8,128)S(1)}, f32[16,1024]{1,0:T(8,128)}, u32[]{:S(2)}) copy-start(f32[16,1024]{1,0:T(8,128)} %param.17) | copy-start | bytes 196612
  12.4 6.5 %copy-start.23 = (f32[16,1024]{1,0:T(8,128)S(1)}, f32[16,1024]{1,0:T(8,128)}, u32[]{:S(2)}) copy-start(f32[16,1024]{1,0:T(8,128)} %param.18) | copy-start | bytes 196612
  26.5 10.3 %copy-start.32 = (f32[2064]{0:T(1024)S(1)}, f32[2064]{0:T(1024)}, u32[]{:S(2)}) copy-start(f32[2064]{0:T(1024)} %copy-done.31) | copy-start | bytes 24772
  27.0 11.4 %collective-permute-start.4 = (f32[6,2064]{1,0:T(8,128)S(1)}, f32[6,2064]{1,0:T(8,128)S(1)}, u32[]{:S(2)}, u32[]{:S(2)}) collective-permute-start(f32[6,2064]{1,0:T(8,128)S(1)} %pad_maximum_fusion.5), channel_id=1, source_target_pairs={{4,0},{8,4},{12,8},{16,12},{20,16},{24,20},{28,24},{5,1},{9,5},{13... | collective-permute-start | bytes 148616 | tf_op jit(solution)/shard_map/ppermute | solution.py:13
  28.3 10.1 %copy-start.34 = (f32[16]{0:T(128)S(1)}, f32[16]{0:T(128)}, u32[]{:S(2)}) copy-start(f32[16]{0:T(128)} %neg.47) | copy-start | bytes 196
  28.3 10.6 %copy-start.35 = (f32[16]{0:T(128)S(1)}, f32[16]{0:T(128)}, u32[]{:S(2)}) copy-start(f32[16]{0:T(128)} %get-tuple-element.70) | copy-start | bytes 196
  28.3 10.6 %copy-start.28 = (f32[1,2048]{1,0:T(1,128)S(1)}, f32[1,2048]{1,0:T(1,128)}, u32[]{:S(2)}) copy-start(f32[1,2048]{1,0:T(1,128)} %and_select_fusion) | copy-start | bytes 24580
  29.0 8.0 %collective-permute-start.6 = (f32[4,16]{1,0:T(4,128)S(1)}, f32[4,16]{1,0:T(4,128)S(1)}, u32[]{:S(2)}, u32[]{:S(2)}) collective-permute-start(f32[4,16]{1,0:T(4,128)S(1)} %pad_maximum_fusion.10), channel_id=1, source_target_pairs={{0,2},{1,3},{2,0},{3,1},{4,6},{5,7},{6,4},{7,5},{8,10},{9,11},{10,... | collective-permute-start | bytes 776 | tf_op jit(solution)/shard_map/ppermute | solution.py:173
  31.0 6.0 %collective-permute-start.2 = (f32[10,1024]{1,0:T(8,128)S(1)}, f32[10,1024]{1,0:T(8,128)S(1)}, u32[]{:S(2)}, u32[]{:S(2)}) collective-permute-start(f32[10,1024]{1,0:T(8,128)S(1)} %get-tuple-element.72), channel_id=1, source_target_pairs={{0,3},{1,0},{2,1},{3,2},{4,7},{5,4},{6,5},{7,6},{8,11},{9,8},{10,9... | collective-permute-start | bytes 122888 | tf_op jit(solution)/shard_map/ppermute | solution.py:173
  32.5 4.5 %collective-permute-start.3 = (f32[10,1024]{1,0:T(8,128)S(1)}, f32[10,1024]{1,0:T(8,128)S(1)}, u32[]{:S(2)}, u32[]{:S(2)}) collective-permute-start(f32[10,1024]{1,0:T(8,128)S(1)} %get-tuple-element.73), channel_id=1, source_target_pairs={{0,1},{1,2},{2,3},{3,0},{4,5},{5,6},{6,7},{7,4},{8,9},{9,10},{10,1... | collective-permute-start | bytes 122888 | tf_op jit(solution)/shard_map/ppermute | solution.py:173
  32.6 6.3 %collective-permute-start.5 = (f32[6,2064]{1,0:T(8,128)S(1)}, f32[6,2064]{1,0:T(8,128)S(1)}, u32[]{:S(2)}, u32[]{:S(2)}) collective-permute-start(f32[6,2064]{1,0:T(8,128)S(1)} %pad_maximum_fusion.6), channel_id=1, source_target_pairs={{0,4},{4,8},{8,12},{12,16},{16,20},{20,24},{24,28},{1,5},{5,9},{9,... | collective-permute-start | bytes 148616 | tf_op jit(solution)/shard_map/ppermute | solution.py:13
  43.0 3.9 %copy-start.20 = (f32[16,1024]{1,0:T(8,128)S(1)}, f32[16,1024]{1,0:T(8,128)}, u32[]{:S(2)}) copy-start(f32[16,1024]{1,0:T(8,128)} %get-tuple-element.28) | copy-start | bytes 196612
  43.0 3.9 %copy-start.21 = (f32[16,1024]{1,0:T(8,128)S(1)}, f32[16,1024]{1,0:T(8,128)}, u32[]{:S(2)}) copy-start(f32[16,1024]{1,0:T(8,128)} %get-tuple-element.29) | copy-start | bytes 196612
  43.0 3.9 %slice-start = ((f32[10,1024]{1,0:T(8,128)}), f32[6,1024]{1,0:T(8,128)S(1)}, s32[]{:S(2)}) async-start(f32[10,1024]{1,0:T(8,128)} %copy-done.26), calls=%async_computation.2 | async-start | bytes 65536 | tf_op jit(solution)/shard_map/slice | solution.py:209
  43.0 3.9 %slice-start.1 = ((f32[10,1024]{1,0:T(8,128)}), f32[6,1024]{1,0:T(8,128)S(1)}, s32[]{:S(2)}) async-start(f32[10,1024]{1,0:T(8,128)} %copy-done.27), calls=%async_computation.3 | async-start | bytes 65536 | tf_op jit(solution)/shard_map/slice | solution.py:208
  47.8 15.5 %copy-start.8 = (f32[16,1024]{1,0:T(8,128)S(1)}, f32[16,1024]{1,0:T(8,128)}, u32[]{:S(2)}) copy-start(f32[16,1024]{1,0:T(8,128)} %copy-done.7) | copy-start | bytes 196612
  47.8 15.5 %copy-start.10 = (f32[16,1024]{1,0:T(8,128)S(1)}, f32[16,1024]{1,0:T(8,128)}, u32[]{:S(2)}) copy-start(f32[16,1024]{1,0:T(8,128)} %copy-done.9) | copy-start | bytes 196612
  47.8 15.5 %copy-start.25 = (f32[2,2,16,1024]{3,2,1,0:T(8,128)S(1)}, f32[2,2,16,1024]{3,2,1,0:T(8,128)}, u32[]{:S(2)}) copy-start(f32[2,2,16,1024]{3,2,1,0:T(8,128)} %param.16) | copy-start | bytes 786436
  48.0 18.8 %copy-start.6 = (f32[16,1024]{1,0:T(8,128)S(1)}, f32[16,1024]{1,0:T(8,128)}, u32[]{:S(2)}) copy-start(f32[16,1024]{1,0:T(8,128)} %copy-done.5) | copy-start | bytes 196612
  48.0 18.8 %copy-start.17 = (f32[16,1024]{1,0:T(8,128)S(1)}, f32[16,1024]{1,0:T(8,128)}, u32[]{:S(2)}) copy-start(f32[16,1024]{1,0:T(8,128)} %copy-done.16) | copy-start | bytes 196612
  48.0 18.8 %copy-start.19 = (f32[16,1024]{1,0:T(8,128)S(1)}, f32[16,1024]{1,0:T(8,128)}, u32[]{:S(2)}) copy-start(f32[16,1024]{1,0:T(8,128)} %copy-done.18) | copy-start | bytes 196612
  49.3 13.8 %all-to-all-start = ((f32[32,1,9]{2,1,0:T(1,128)}), f32[32,1,9]{2,1,0:T(1,128)S(1)}, u32[]{:S(2)}, u32[]{:S(2)}) async-start(f32[32,1,9]{2,1,0:T(1,128)} %broadcast_in_dim.53), calls=%async_computation | async-start | bytes 32768 | tf_op jit(solution)/shard_map/all_to_all | solution.py:36
  64.3 9.6 %all-to-all-start.1 = ((f32[32,1,4]{2,1,0:T(1,128)}), f32[32,1,4]{2,1,0:T(1,128)S(1)}, u32[]{:S(2)}, u32[]{:S(2)}) async-start(f32[32,1,4]{2,1,0:T(1,128)} %broadcast_in_dim.55), calls=%async_computation.1 | async-start | bytes 32768 | tf_op jit(solution)/shard_map/all_to_all | solution.py:36
  (22 other events, 46.7 us)

commit v17 on v14

--- a/solution.py
+++ b/solution.py
@@ -181,7 +181,7 @@
         from_left = shifted(jnp.concatenate([scaled[:, :, -1], picks_near], axis=1), "cells", 1)
         from_right = shifted(jnp.concatenate([scaled[:, :, 0], picks_far], axis=1), "cells", -1)
         pressure = fields[:, 0]
-        values = gather(pressure, well_at)
+        values = gather(pressure, well_at, split2)
         local = jnp.concatenate(
             [
                 jnp.dot(well_index, well_onehot, precision=highest)[None],

time: 74.7 us -> 74.7 us (level)
  no operation moved by 1% of the time
where the time goes in v17:
time: 74.7 us; the launch traced here: 74 us
  starting transfers between devices  18 us (24%)
  other arithmetic  14.8 us (20%)
  blocking collectives  13.7 us (18%)
  matrix products  9.87 us (13%)
  local copies, waits for them, and re-layouts  8.56 us (11%)
  waiting for transfers between devices  6.85 us (9%)
  between operations  2.29 us (3%)
    all_to_all x1, blocking collectives, global_sum(): gathered = lax.all_to_all(copies, axes, 0, 0, tiled=True)  13.7 us
    ppermute x4, starting transfers between devices, shifted(): return lax.ppermute(value, axis, pairs)  11.9 us
    dot_general x4, matrix products, onehot_dot(): lax.dot_general(pieces, onehot, (dims, ((), ())), preferred_element_type=...  8.72 us
    all_to_all x1, waiting for transfers between devices, global_sum(): gathered = lax.all_to_all(copies, axes, 0, 0, tiled=True)  6.31 us
    ppermute x3, starting transfers between devices, slab_shift(): lax.ppermute(value, 'slab', [(i, (i + by) % count) for i in range(count)])  3.52 us
    all_to_all x1, starting transfers between devices, global_sum(): gathered = lax.all_to_all(copies, axes, 0, 0, tiled=True)  2.56 us
    select_n x2, other arithmetic, per_device(): weight_here = jnp.where(slot_live, fault_trans.reshape(-1), zero_value)  2.01 us
    unnamed x101, local copies, waits for them, and re-layouts  1.88 us
  transfers between devices with their start and end apart: 8, of which 2 were waited for; matrix products, arithmetic and copies ran while one was open for 16% of the time, Pallas kernels for 0%

profile of v17, /device:TPU:0, one launch (start us, length us, event | category | flops | bytes accessed | tf_op | source)
XLA Modules:
  0.0 74.0 jit_solution(4577007509587588353)
XLA Ops:
  0.7 0.9 %broadcast_select_fusion.1 = f32[16,1024]{1,0:T(8,128)S(1)} fusion(f32[16,1024]{1,0:T(8,128)} %param.17, pred[1024]{0:T(1024)(128)(4,1)S(1)} %fusion.71), kind=kLoop, calls=%fused_computation.159 | loop fusion | flops 16384 | bytes 132096 | tf_op jit(solution)/shard_map/jit(_where)/select_n | solution.py:91
  2.4 0.7 fusion.69
  3.2 4.9 %collective-permute-start = (f32[2064]{0:T(1024)S(1)}, f32[2064]{0:T(1024)S(1)}, u32[]{:S(2)}, u32[]{:S(2)}) collective-permute-start(f32[2064]{0:T(1024)S(1)} %pad_maximum_fusion.9), channel_id=1, source_target_pairs={{0,4},{4,8},{8,12},{12,16},{16,20},{20,24},{24,28},{1,5},{5,9},{9,... | collective-permute-start | bytes 24776 | tf_op jit(solution)/shard_map/ppermute | solution.py:13
  8.1 0.9 %broadcast_select_fusion = f32[16,1024]{1,0:T(8,128)S(1)} fusion(f32[16,1024]{1,0:T(8,128)} %param.18, pred[16]{0:T(512)(128)(4,1)S(1)} %broadcast_and_fusion), kind=kLoop, calls=%fused_computation.158 | loop fusion | flops 16384 | bytes 131088 | tf_op jit(solution)/shard_map/jit(_where)/select_n | solution.py:94
  9.0 1.5 %collective-permute-start.1 = (f32[1024]{0:T(1024)S(1)}, f32[1024]{0:T(1024)S(1)}, u32[]{:S(2)}, u32[]{:S(2)}) collective-permute-start(f32[1024]{0:T(1024)S(1)} %bitcast.397), channel_id=1, source_target_pairs={{0,1},{1,2},{2,3},{4,5},{5,6},{6,7},{8,9},{9,10},{10,11},{12,13},{... | collective-permute-start | bytes 12296 | tf_op jit(solution)/shard_map/ppermute | solution.py:13
  10.5 1.2 %and_select_fusion.2 = s32[128]{0:T(128)} fusion(s32[1,128]{1,0:T(1,128)} %param.23), kind=kLoop, calls=%fused_computation.199 | loop fusion | flops 1408 | bytes 1024 | tf_op jit(solution)/shard_map/jit(remainder)/select_n | solution.py:115
  11.7 0.7 fusion.78
  12.4 1.0 %fusion.94 = (f32[1,2,16,1024]{3,2,1,0:T(8,128)S(1)}, f32[1,2,16,1024]{3,2,1,0:T(8,128)S(1)}) fusion(f32[2,2,16,1024]{3,2,1,0:T(8,128)} %param.15), kind=kLoop, calls=%fused_computation.226 | loop fusion | bytes 524288 | tf_op jit(solution)/shard_map/slice | solution.py:150
  13.5 0.8 %concatenate.103 = s32[4128]{0:T(1024)S(1)} concatenate(s32[2048]{0:T(1024)} %bitcast.394, s32[2048]{0:T(1024)} %bitcast.395, s32[16]{0:T(128)S(1)} %get-tuple-element.76, s32[16]{0:T(128)S(1)} %get-tuple-element.77), dimensions={0} | concatenate | bytes 33024 | tf_op jit(solution)/shard_map/concatenate | solution.py:138
  14.3 0.6 add_select_fusion
  14.9 1.3 %and_select_fusion = f32[1,2048]{1,0:T(1,128)} fusion(f32[1,2048]{1,0:T(1,128)} %param.21, pred[]{:T(512)S(6)} %lt.34, s32[]{:T(128)} %bitcast.336), kind=kLoop, calls=%fused_computation.160 | loop fusion | flops 6144 | bytes 16389 | tf_op jit(solution)/shard_map/jit(_where)/select_n | solution.py:101
  16.3 0.8 %fusion.56 = f32[1,16]{1,0:T(1,128)} fusion(s32[128]{0:T(128)S(1)} %bitcast.398, f32[1,128]{1,0:T(1,128)S(1)} %copy-done.41), kind=kOutput, calls=%fused_computation.141 | convolution fusion | flops 26624 | bytes 1088 | tf_op jit(solution)/shard_map/dot_general | solution.py:187
  17.7 0.6 neg.47
  18.9 0.7 fusion.43
  21.0 1.0 %fusion.93 = (f32[6,15,1024]{2,1,0:T(8,128)}, f32[6,15,1024]{2,1,0:T(8,128)}) fusion(f32[6,16,1024]{2,1,0:T(8,128)S(1)} %bitcast.340), kind=kLoop, calls=%fused_computation.225 | loop fusion | bytes 1474560 | tf_op jit(solution)/shard_map/slice | solution.py:221
  21.9 4.3 %fusion.1 = f32[192,4128]{1,0:T(8,128)S(1)} fusion(s32[4128]{0:T(1024)S(1)} %copy-done.29, bf16[96,1024]{1,0:T(8,128)(2,1)S(1)} %get-tuple-element.24, bf16[96,1024]{1,0:T(8,128)(2,1)S(1)} %get-tuple-element.25), kind=kOutput, calls=%fused_computation.2 | convolution fusion | flops 1628209152 | bytes 3580032 | tf_op jit(solution)/shard_map/dot_general | solution.py:58
  26.9 1.3 %collective-permute-start.4 = (f32[6,2064]{1,0:T(8,128)S(1)}, f32[6,2064]{1,0:T(8,128)S(1)}, u32[]{:S(2)}, u32[]{:S(2)}) collective-permute-start(f32[6,2064]{1,0:T(8,128)S(1)} %pad_maximum_fusion.5), channel_id=1, source_target_pairs={{4,0},{8,4},{12,8},{16,12},{20,16},{24,20},{28,24},{5,1},{9,5},{13... | collective-permute-start | bytes 148616 | tf_op jit(solution)/shard_map/ppermute | solution.py:13
  29.0 2.0 %collective-permute-start.6 = (f32[4,16]{1,0:T(4,128)S(1)}, f32[4,16]{1,0:T(4,128)S(1)}, u32[]{:S(2)}, u32[]{:S(2)}) collective-permute-start(f32[4,16]{1,0:T(4,128)S(1)} %pad_maximum_fusion.10), channel_id=1, source_target_pairs={{0,2},{1,3},{2,0},{3,1},{4,6},{5,7},{6,4},{7,5},{8,10},{9,11},{10,... | collective-permute-start | bytes 776 | tf_op jit(solution)/shard_map/ppermute | solution.py:173
  31.0 1.5 %collective-permute-start.2 = (f32[10,1024]{1,0:T(8,128)S(1)}, f32[10,1024]{1,0:T(8,128)S(1)}, u32[]{:S(2)}, u32[]{:S(2)}) collective-permute-start(f32[10,1024]{1,0:T(8,128)S(1)} %get-tuple-element.72), channel_id=1, source_target_pairs={{0,3},{1,0},{2,1},{3,2},{4,7},{5,4},{6,5},{7,6},{8,11},{9,8},{10,9... | collective-permute-start | bytes 122888 | tf_op jit(solution)/shard_map/ppermute | solution.py:173
  32.6 4.3 %collective-permute-start.5 = (f32[6,2064]{1,0:T(8,128)S(1)}, f32[6,2064]{1,0:T(8,128)S(1)}, u32[]{:S(2)}, u32[]{:S(2)}) collective-permute-start(f32[6,2064]{1,0:T(8,128)S(1)} %pad_maximum_fusion.6), channel_id=1, source_target_pairs={{0,4},{4,8},{8,12},{12,16},{16,20},{20,24},{24,28},{1,5},{5,9},{9,... | collective-permute-start | bytes 148616 | tf_op jit(solution)/shard_map/ppermute | solution.py:13
  37.6 0.7 slice_add_fusion.3
  38.9 0.7 %fusion.38 = (f32[6,2048]{1,0:T(8,128)}, f32[6,2048]{1,0:T(8,128)}) fusion(f32[6,2064]{1,0:T(8,128)S(1)} %collective-permute-done.5, f32[2048]{0:T(1024)S(1)} %slice.414, f32[6,4128]{1,0:T(8,128)S(1)} %multiply_reduce_fusion, f32[6,2064]{1,0:T(8,128)S(1)} %collective-permute-done.4, f32[2048]{0:T(1024)S(1)} %bitcast.374), kind=kLoop, calls=%fused_computation.96 | loop fusion | flops 61440 | bytes 311296 | tf_op jit(solution)/shard_map/neg | solution.py:235
  39.6 1.6 %concatenate.106 = f32[6,4128]{1,0:T(8,128)} concatenate(f32[6,2048]{1,0:T(8,128)} %get-tuple-element.54, f32[6,2048]{1,0:T(8,128)} %get-tuple-element.53, f32[6,16]{1,0:T(8,128)S(1)} %slice_multiply_fusion.5, f32[6,16]{1,0:T(8,128)S(1)} %slice_multiply_fusion.4), dimensions={1} | concatenate | bytes 198144 | tf_op jit(solution)/shard_map/concatenate | solution.py:232
  41.2 1.0 %broadcast_multiply_fusion = f32[6,16,4128]{2,1,0:T(8,128)S(1)} fusion(f32[6,4128]{1,0:T(8,128)} %concatenate.106, f32[16,4128]{1,0:T(8,128)S(1)} %fusion.15), kind=kLoop, calls=%fused_computation.15 | loop fusion | flops 396288 | bytes 1948416 | tf_op jit(solution)/shard_map/mul | solution.py:130
  42.4 0.6 copy-done.30
  43.0 3.8 %fusion = f32[192,1024]{1,0:T(8,128)S(1)} fusion(s32[4128]{0:T(1024)S(1)} %copy-done.30, bf16[96,4128]{1,0:T(8,128)(2,1)S(1)} %get-tuple-element.22, bf16[96,4128]{1,0:T(8,128)(2,1)S(1)} %get-tuple-element.23), kind=kOutput, calls=%fused_computation.1 | convolution fusion | flops 1630593024 | bytes 2388096 | tf_op jit(solution)/shard_map/dot_general | solution.py:58
  48.7 13.7 %all_to_all.12 = f32[32,1,10]{2,1,0:T(1,128)S(1)} all-to-all(f32[32,1,10]{2,1,0:T(1,128)S(1)} %broadcast_in_dim.53), channel_id=1, replica_groups=mesh['cells'=8,'slab'=4] {'cells','slab'}, dimensions={0} | all-to-all | bytes 2560 | tf_op jit(solution)/shard_map/all_to_all | solution.py:36
  63.0 0.6 broadcast_in_dim.55
  63.6 2.6 %all-to-all-start.1 = ((f32[32,1,4]{2,1,0:T(1,128)}), f32[32,1,4]{2,1,0:T(1,128)S(1)}, u32[]{:S(2)}, u32[]{:S(2)}) async-start(f32[32,1,4]{2,1,0:T(1,128)} %broadcast_in_dim.55), calls=%async_computation.1 | async-start | bytes 32768 | tf_op jit(solution)/shard_map/all_to_all | solution.py:36
  66.3 0.7 pad_maximum_fusion.2
  67.0 6.3 %all-to-all-done.1 = f32[32,1,4]{2,1,0:T(1,128)S(1)} async-done(((f32[32,1,4]{2,1,0:T(1,128)}), f32[32,1,4]{2,1,0:T(1,128)S(1)}, u32[]{:S(2)}, u32[]{:S(2)}) %all-to-all-start.1) | async-done | bytes 544 | tf_op jit(solution)/shard_map/all_to_all | solution.py:36
  73.4 0.7 sqrt.8
  (177 shorter events, 7.9 us)
Async XLA Ops:
  0.6 15.6 %copy-start = (f32[2,4,16,1024]{3,2,1,0:T(8,128)S(1)}, f32[2,4,16,1024]{3,2,1,0:T(8,128)}, u32[]{:S(2)}) copy-start(f32[2,4,16,1024]{3,2,1,0:T(8,128)} %param.14) | copy-start | bytes 1572868
  0.6 15.6 %copy-start.39 = (s32[1,128]{1,0:T(1,128)S(1)}, s32[1,128]{1,0:T(1,128)}, u32[]{:S(2)}) copy-start(s32[1,128]{1,0:T(1,128)} %param.24) | copy-start | bytes 1540
  0.7 15.6 %copy-start.41 = (f32[1,128]{1,0:T(1,128)S(1)}, f32[1,128]{1,0:T(1,128)}, u32[]{:S(2)}) copy-start(f32[1,128]{1,0:T(1,128)} %param.25) | copy-start | bytes 1540
  1.6 17.3 %copy-start.12 = (f32[16,1024]{1,0:T(8,128)}, f32[16,1024]{1,0:T(8,128)S(1)}, u32[]{:S(2)}) copy-start(f32[16,1024]{1,0:T(8,128)S(1)} %broadcast_select_fusion.1) | copy-start | bytes 196612
  3.2 15.1 %collective-permute-start = (f32[2064]{0:T(1024)S(1)}, f32[2064]{0:T(1024)S(1)}, u32[]{:S(2)}, u32[]{:S(2)}) collective-permute-start(f32[2064]{0:T(1024)S(1)} %pad_maximum_fusion.9), channel_id=1, source_target_pairs={{0,4},{4,8},{8,12},{12,16},{16,20},{20,24},{24,28},{1,5},{5,9},{9,... | collective-permute-start | bytes 24776 | tf_op jit(solution)/shard_map/ppermute | solution.py:13
  9.0 9.9 %copy-start.14 = (f32[16,1024]{1,0:T(8,128)}, f32[16,1024]{1,0:T(8,128)S(1)}, u32[]{:S(2)}) copy-start(f32[16,1024]{1,0:T(8,128)S(1)} %broadcast_select_fusion) | copy-start | bytes 196612
  9.0 9.9 %collective-permute-start.1 = (f32[1024]{0:T(1024)S(1)}, f32[1024]{0:T(1024)S(1)}, u32[]{:S(2)}, u32[]{:S(2)}) collective-permute-start(f32[1024]{0:T(1024)S(1)} %bitcast.397), channel_id=1, source_target_pairs={{0,1},{1,2},{2,3},{4,5},{5,6},{6,7},{8,9},{9,10},{10,11},{12,13},{... | collective-permute-start | bytes 12296 | tf_op jit(solution)/shard_map/ppermute | solution.py:13
  12.4 6.5 %copy-start.1 = (f32[2,2,16,1024]{3,2,1,0:T(8,128)S(1)}, f32[2,2,16,1024]{3,2,1,0:T(8,128)}, u32[]{:S(2)}) copy-start(f32[2,2,16,1024]{3,2,1,0:T(8,128)} %param.13) | copy-start | bytes 786436
  12.4 6.5 %copy-start.2 = (f32[2,2,16,1024]{3,2,1,0:T(8,128)S(1)}, f32[2,2,16,1024]{3,2,1,0:T(8,128)}, u32[]{:S(2)}) copy-start(f32[2,2,16,1024]{3,2,1,0:T(8,128)} %param.15) | copy-start | bytes 786436
  12.4 6.5 %copy-start.22 = (f32[16,1024]{1,0:T(8,128)S(1)}, f32[16,1024]{1,0:T(8,128)}, u32[]{:S(2)}) copy-start(f32[16,1024]{1,0:T(8,128)} %param.17) | copy-start | bytes 196612
  12.4 6.5 %copy-start.23 = (f32[16,1024]{1,0:T(8,128)S(1)}, f32[16,1024]{1,0:T(8,128)}, u32[]{:S(2)}) copy-start(f32[16,1024]{1,0:T(8,128)} %param.18) | copy-start | bytes 196612
  26.8 10.0 %copy-start.32 = (f32[2064]{0:T(1024)S(1)}, f32[2064]{0:T(1024)}, u32[]{:S(2)}) copy-start(f32[2064]{0:T(1024)} %copy-done.31) | copy-start | bytes 24772
  26.9 11.4 %collective-permute-start.4 = (f32[6,2064]{1,0:T(8,128)S(1)}, f32[6,2064]{1,0:T(8,128)S(1)}, u32[]{:S(2)}, u32[]{:S(2)}) collective-permute-start(f32[6,2064]{1,0:T(8,128)S(1)} %pad_maximum_fusion.5), channel_id=1, source_target_pairs={{4,0},{8,4},{12,8},{16,12},{20,16},{24,20},{28,24},{5,1},{9,5},{13... | collective-permute-start | bytes 148616 | tf_op jit(solution)/shard_map/ppermute | solution.py:13
  28.2 10.1 %copy-start.34 = (f32[16]{0:T(128)S(1)}, f32[16]{0:T(128)}, u32[]{:S(2)}) copy-start(f32[16]{0:T(128)} %neg.47) | copy-start | bytes 196
  28.3 10.6 %copy-start.35 = (f32[16]{0:T(128)S(1)}, f32[16]{0:T(128)}, u32[]{:S(2)}) copy-start(f32[16]{0:T(128)} %get-tuple-element.70) | copy-start | bytes 196
  28.3 10.6 %copy-start.28 = (f32[1,2048]{1,0:T(1,128)S(1)}, f32[1,2048]{1,0:T(1,128)}, u32[]{:S(2)}) copy-start(f32[1,2048]{1,0:T(1,128)} %and_select_fusion) | copy-start | bytes 24580
  29.0 8.0 %collective-permute-start.6 = (f32[4,16]{1,0:T(4,128)S(1)}, f32[4,16]{1,0:T(4,128)S(1)}, u32[]{:S(2)}, u32[]{:S(2)}) collective-permute-start(f32[4,16]{1,0:T(4,128)S(1)} %pad_maximum_fusion.10), channel_id=1, source_target_pairs={{0,2},{1,3},{2,0},{3,1},{4,6},{5,7},{6,4},{7,5},{8,10},{9,11},{10,... | collective-permute-start | bytes 776 | tf_op jit(solution)/shard_map/ppermute | solution.py:173
  31.0 6.0 %collective-permute-start.2 = (f32[10,1024]{1,0:T(8,128)S(1)}, f32[10,1024]{1,0:T(8,128)S(1)}, u32[]{:S(2)}, u32[]{:S(2)}) collective-permute-start(f32[10,1024]{1,0:T(8,128)S(1)} %get-tuple-element.72), channel_id=1, source_target_pairs={{0,3},{1,0},{2,1},{3,2},{4,7},{5,4},{6,5},{7,6},{8,11},{9,8},{10,9... | collective-permute-start | bytes 122888 | tf_op jit(solution)/shard_map/ppermute | solution.py:173
  32.5 4.5 %collective-permute-start.3 = (f32[10,1024]{1,0:T(8,128)S(1)}, f32[10,1024]{1,0:T(8,128)S(1)}, u32[]{:S(2)}, u32[]{:S(2)}) collective-permute-start(f32[10,1024]{1,0:T(8,128)S(1)} %get-tuple-element.73), channel_id=1, source_target_pairs={{0,1},{1,2},{2,3},{3,0},{4,5},{5,6},{6,7},{7,4},{8,9},{9,10},{10,1... | collective-permute-start | bytes 122888 | tf_op jit(solution)/shard_map/ppermute | solution.py:173
  32.6 6.3 %collective-permute-start.5 = (f32[6,2064]{1,0:T(8,128)S(1)}, f32[6,2064]{1,0:T(8,128)S(1)}, u32[]{:S(2)}, u32[]{:S(2)}) collective-permute-start(f32[6,2064]{1,0:T(8,128)S(1)} %pad_maximum_fusion.6), channel_id=1, source_target_pairs={{0,4},{4,8},{8,12},{12,16},{16,20},{20,24},{24,28},{1,5},{5,9},{9,... | collective-permute-start | bytes 148616 | tf_op jit(solution)/shard_map/ppermute | solution.py:13
  43.0 3.9 %copy-start.20 = (f32[16,1024]{1,0:T(8,128)S(1)}, f32[16,1024]{1,0:T(8,128)}, u32[]{:S(2)}) copy-start(f32[16,1024]{1,0:T(8,128)} %get-tuple-element.30) | copy-start | bytes 196612
  43.0 3.9 %copy-start.21 = (f32[16,1024]{1,0:T(8,128)S(1)}, f32[16,1024]{1,0:T(8,128)}, u32[]{:S(2)}) copy-start(f32[16,1024]{1,0:T(8,128)} %get-tuple-element.31) | copy-start | bytes 196612
  43.0 3.9 %slice-start = ((f32[10,1024]{1,0:T(8,128)}), f32[6,1024]{1,0:T(8,128)S(1)}, s32[]{:S(2)}) async-start(f32[10,1024]{1,0:T(8,128)} %copy-done.26), calls=%async_computation.2 | async-start | bytes 65536 | tf_op jit(solution)/shard_map/slice | solution.py:209
  43.0 3.9 %slice-start.1 = ((f32[10,1024]{1,0:T(8,128)}), f32[6,1024]{1,0:T(8,128)S(1)}, s32[]{:S(2)}) async-start(f32[10,1024]{1,0:T(8,128)} %copy-done.27), calls=%async_computation.3 | async-start | bytes 65536 | tf_op jit(solution)/shard_map/slice | solution.py:208
  43.0 3.9 %copy-start.37 = (pred[16]{0:T(512)(128)(4,1)S(1)}, pred[16]{0:T(512)(128)(4,1)}, u32[]{:S(2)}) copy-start(pred[16]{0:T(512)(128)(4,1)} %get-tuple-element.78) | copy-start | bytes 52
  47.8 14.8 %copy-start.8 = (f32[16,1024]{1,0:T(8,128)S(1)}, f32[16,1024]{1,0:T(8,128)}, u32[]{:S(2)}) copy-start(f32[16,1024]{1,0:T(8,128)} %copy-done.7) | copy-start | bytes 196612
  47.8 14.8 %copy-start.10 = (f32[16,1024]{1,0:T(8,128)S(1)}, f32[16,1024]{1,0:T(8,128)}, u32[]{:S(2)}) copy-start(f32[16,1024]{1,0:T(8,128)} %copy-done.9) | copy-start | bytes 196612
  47.8 14.8 %copy-start.25 = (f32[2,2,16,1024]{3,2,1,0:T(8,128)S(1)}, f32[2,2,16,1024]{3,2,1,0:T(8,128)}, u32[]{:S(2)}) copy-start(f32[2,2,16,1024]{3,2,1,0:T(8,128)} %param.16) | copy-start | bytes 786436
  48.0 18.2 %copy-start.6 = (f32[16,1024]{1,0:T(8,128)S(1)}, f32[16,1024]{1,0:T(8,128)}, u32[]{:S(2)}) copy-start(f32[16,1024]{1,0:T(8,128)} %copy-done.5) | copy-start | bytes 196612
  48.0 18.2 %copy-start.17 = (f32[16,1024]{1,0:T(8,128)S(1)}, f32[16,1024]{1,0:T(8,128)}, u32[]{:S(2)}) copy-start(f32[16,1024]{1,0:T(8,128)} %copy-done.16) | copy-start | bytes 196612
  48.0 18.2 %copy-start.19 = (f32[16,1024]{1,0:T(8,128)S(1)}, f32[16,1024]{1,0:T(8,128)}, u32[]{:S(2)}) copy-start(f32[16,1024]{1,0:T(8,128)} %copy-done.18) | copy-start | bytes 196612
  63.6 9.7 %all-to-all-start.1 = ((f32[32,1,4]{2,1,0:T(1,128)}), f32[32,1,4]{2,1,0:T(1,128)S(1)}, u32[]{:S(2)}, u32[]{:S(2)}) async-start(f32[32,1,4]{2,1,0:T(1,128)} %broadcast_in_dim.55), calls=%async_computation.1 | async-start | bytes 32768 | tf_op jit(solution)/shard_map/all_to_all | solution.py:36
  (21 other events, 43.1 us)

commit v18 on v14

--- a/solution.py
+++ b/solution.py
@@ -99,9 +99,9 @@
         cells_place < cells_size - 1
     )
     weight_here = jnp.where(slot_live, fault_trans.reshape(-1), zero_value)
-    from_left_setup = shifted(jnp.concatenate([trans_east[:, -1], weight_here]), "cells", 1)
-    east_edge = from_left_setup[:layer_count]
-    weight_left = from_left_setup[layer_count:]
+    from_left_setup = shifted(jnp.concatenate([weight_here, trans_east[:, -1]]), "cells", 1)
+    weight_left = from_left_setup[:slot_count]
+    east_edge = from_left_setup[slot_count:]
     down_edge = shifted(trans_down[-1, :], "slab", 1)
     trans_west = jnp.concatenate([east_edge[:, None], trans_east[:, :-1]], axis=1)
     trans_up = jnp.concatenate([down_edge[None, :], trans_down[:-1, :]], axis=0)

time: 74.7 us -> 74.7 us (level)
    unnamed x101 -> x99, local copies, waits for them, and re-layouts: 1.88 us -> 1.88 us
where the time goes in v18:
time: 74.7 us; the launch traced here: 74.1 us
  starting transfers between devices  18 us (24%)
  other arithmetic  14.8 us (20%)
  blocking collectives  13.7 us (18%)
  matrix products  9.92 us (13%)
  local copies, waits for them, and re-layouts  8.49 us (11%)
  waiting for transfers between devices  6.91 us (9%)
  between operations  2.32 us (3%)
    all_to_all x1, blocking collectives, global_sum(): gathered = lax.all_to_all(copies, axes, 0, 0, tiled=True)  13.7 us
    ppermute x4, starting transfers between devices, shifted(): return lax.ppermute(value, axis, pairs)  11.9 us
    dot_general x4, matrix products, onehot_dot(): lax.dot_general(pieces, onehot, (dims, ((), ())), preferred_element_type=...  8.73 us
    all_to_all x1, waiting for transfers between devices, global_sum(): gathered = lax.all_to_all(copies, axes, 0, 0, tiled=True)  6.31 us
    ppermute x3, starting transfers between devices, slab_shift(): lax.ppermute(value, 'slab', [(i, (i + by) % count) for i in range(count)])  3.53 us
    all_to_all x1, starting transfers between devices, global_sum(): gathered = lax.all_to_all(copies, axes, 0, 0, tiled=True)  2.56 us
    select_n x2, other arithmetic, per_device(): weight_here = jnp.where(slot_live, fault_trans.reshape(-1), zero_value)  2.02 us
    unnamed x99, local copies, waits for them, and re-layouts  1.88 us
  transfers between devices with their start and end apart: 8, of which 2 were waited for; matrix products, arithmetic and copies ran while one was open for 16% of the time, Pallas kernels for 0%

profile of v18, /device:TPU:0, one launch (start us, length us, event | category | flops | bytes accessed | tf_op | source)
XLA Modules:
  0.0 74.1 jit_solution(16866514593930771886)
XLA Ops:
  0.7 0.9 %broadcast_select_fusion.1 = f32[16,1024]{1,0:T(8,128)S(1)} fusion(f32[16,1024]{1,0:T(8,128)} %param.17, pred[1024]{0:T(1024)(128)(4,1)S(1)} %fusion.73), kind=kLoop, calls=%fused_computation.162 | loop fusion | flops 16384 | bytes 132096 | tf_op jit(solution)/shard_map/jit(_where)/select_n | solution.py:91
  2.4 0.7 fusion.71
  3.1 4.9 %collective-permute-start = (f32[2064]{0:T(1024)S(1)}, f32[2064]{0:T(1024)S(1)}, u32[]{:S(2)}, u32[]{:S(2)}) collective-permute-start(f32[2064]{0:T(1024)S(1)} %pad_maximum_fusion.9), channel_id=1, source_target_pairs={{0,4},{4,8},{8,12},{12,16},{16,20},{20,24},{24,28},{1,5},{5,9},{9,... | collective-permute-start | bytes 24776 | tf_op jit(solution)/shard_map/ppermute | solution.py:13
  8.0 0.9 %broadcast_select_fusion = f32[16,1024]{1,0:T(8,128)S(1)} fusion(f32[16,1024]{1,0:T(8,128)} %param.18, pred[16]{0:T(512)(128)(4,1)S(1)} %broadcast_and_fusion), kind=kLoop, calls=%fused_computation.161 | loop fusion | flops 16384 | bytes 131088 | tf_op jit(solution)/shard_map/jit(_where)/select_n | solution.py:94
  9.0 1.5 %collective-permute-start.1 = (f32[1024]{0:T(1024)S(1)}, f32[1024]{0:T(1024)S(1)}, u32[]{:S(2)}, u32[]{:S(2)}) collective-permute-start(f32[1024]{0:T(1024)S(1)} %bitcast.404), channel_id=1, source_target_pairs={{0,1},{1,2},{2,3},{4,5},{5,6},{6,7},{8,9},{9,10},{10,11},{12,13},{... | collective-permute-start | bytes 12296 | tf_op jit(solution)/shard_map/ppermute | solution.py:13
  10.4 1.2 %and_select_fusion.2 = s32[128]{0:T(128)} fusion(s32[1,128]{1,0:T(1,128)} %param.23), kind=kLoop, calls=%fused_computation.203 | loop fusion | flops 1408 | bytes 1024 | tf_op jit(solution)/shard_map/jit(remainder)/select_n | solution.py:115
  11.6 0.7 fusion.80
  12.3 1.0 %fusion.96 = (f32[1,2,16,1024]{3,2,1,0:T(8,128)S(1)}, f32[1,2,16,1024]{3,2,1,0:T(8,128)S(1)}) fusion(f32[2,2,16,1024]{3,2,1,0:T(8,128)} %param.15), kind=kLoop, calls=%fused_computation.230 | loop fusion | bytes 524288 | tf_op jit(solution)/shard_map/slice | solution.py:150
  13.4 0.8 %concatenate.103 = s32[4128]{0:T(1024)S(1)} concatenate(s32[2048]{0:T(1024)} %bitcast.401, s32[2048]{0:T(1024)} %bitcast.402, s32[16]{0:T(128)S(1)} %get-tuple-element.76, s32[16]{0:T(128)S(1)} %get-tuple-element.77), dimensions={0} | concatenate | bytes 33024 | tf_op jit(solution)/shard_map/concatenate | solution.py:138
  14.2 0.6 add_select_fusion
  14.8 1.3 %and_select_fusion = f32[1,2048]{1,0:T(1,128)} fusion(f32[1,2048]{1,0:T(1,128)} %param.21, pred[]{:T(512)S(6)} %lt.34, s32[]{:T(128)} %bitcast.343), kind=kLoop, calls=%fused_computation.163 | loop fusion | flops 6144 | bytes 16389 | tf_op jit(solution)/shard_map/jit(_where)/select_n | solution.py:101
  16.2 0.8 %fusion.58 = f32[1,16]{1,0:T(1,128)} fusion(s32[128]{0:T(128)S(1)} %bitcast.405, f32[1,128]{1,0:T(1,128)S(1)} %copy-done.40), kind=kOutput, calls=%fused_computation.144 | convolution fusion | flops 26624 | bytes 1088 | tf_op jit(solution)/shard_map/dot_general | solution.py:187
  18.9 0.7 fusion.45
  21.1 1.0 %fusion.95 = (f32[6,15,1024]{2,1,0:T(8,128)}, f32[6,15,1024]{2,1,0:T(8,128)}) fusion(f32[6,16,1024]{2,1,0:T(8,128)S(1)} %bitcast.347), kind=kLoop, calls=%fused_computation.229 | loop fusion | bytes 1474560 | tf_op jit(solution)/shard_map/slice | solution.py:221
  22.0 4.3 %fusion.1 = f32[192,4128]{1,0:T(8,128)S(1)} fusion(s32[4128]{0:T(1024)S(1)} %copy-done.30, bf16[96,1024]{1,0:T(8,128)(2,1)S(1)} %get-tuple-element.22, bf16[96,1024]{1,0:T(8,128)(2,1)S(1)} %get-tuple-element.23), kind=kOutput, calls=%fused_computation.2 | convolution fusion | flops 1628209152 | bytes 3580032 | tf_op jit(solution)/shard_map/dot_general | solution.py:58
  27.0 1.3 %collective-permute-start.4 = (f32[6,2064]{1,0:T(8,128)S(1)}, f32[6,2064]{1,0:T(8,128)S(1)}, u32[]{:S(2)}, u32[]{:S(2)}) collective-permute-start(f32[6,2064]{1,0:T(8,128)S(1)} %pad_maximum_fusion.5), channel_id=1, source_target_pairs={{4,0},{8,4},{12,8},{16,12},{20,16},{24,20},{28,24},{5,1},{9,5},{13... | collective-permute-start | bytes 148616 | tf_op jit(solution)/shard_map/ppermute | solution.py:13
  29.0 2.0 %collective-permute-start.6 = (f32[4,16]{1,0:T(4,128)S(1)}, f32[4,16]{1,0:T(4,128)S(1)}, u32[]{:S(2)}, u32[]{:S(2)}) collective-permute-start(f32[4,16]{1,0:T(4,128)S(1)} %pad_maximum_fusion.10), channel_id=1, source_target_pairs={{0,2},{1,3},{2,0},{3,1},{4,6},{5,7},{6,4},{7,5},{8,10},{9,11},{10,... | collective-permute-start | bytes 776 | tf_op jit(solution)/shard_map/ppermute | solution.py:173
  31.0 1.5 %collective-permute-start.2 = (f32[10,1024]{1,0:T(8,128)S(1)}, f32[10,1024]{1,0:T(8,128)S(1)}, u32[]{:S(2)}, u32[]{:S(2)}) collective-permute-start(f32[10,1024]{1,0:T(8,128)S(1)} %get-tuple-element.72), channel_id=1, source_target_pairs={{0,3},{1,0},{2,1},{3,2},{4,7},{5,4},{6,5},{7,6},{8,11},{9,8},{10,9... | collective-permute-start | bytes 122888 | tf_op jit(solution)/shard_map/ppermute | solution.py:173
  32.6 4.3 %collective-permute-start.5 = (f32[6,2064]{1,0:T(8,128)S(1)}, f32[6,2064]{1,0:T(8,128)S(1)}, u32[]{:S(2)}, u32[]{:S(2)}) collective-permute-start(f32[6,2064]{1,0:T(8,128)S(1)} %pad_maximum_fusion.6), channel_id=1, source_target_pairs={{0,4},{4,8},{8,12},{12,16},{16,20},{20,24},{24,28},{1,5},{5,9},{9,... | collective-permute-start | bytes 148616 | tf_op jit(solution)/shard_map/ppermute | solution.py:13
  37.6 0.7 slice_add_fusion.3
  38.3 0.6 collective-permute-done.5
  38.9 0.7 %fusion.40 = (f32[6,2048]{1,0:T(8,128)}, f32[6,2048]{1,0:T(8,128)}) fusion(f32[6,2064]{1,0:T(8,128)S(1)} %collective-permute-done.5, f32[2048]{0:T(1024)S(1)} %slice-done.2, f32[6,4128]{1,0:T(8,128)S(1)} %multiply_reduce_fusion, f32[6,2064]{1,0:T(8,128)S(1)} %collective-permute-done.4, f32[2048]{0:T(1024)S(1)} %bitcast.381), kind=kLoop, calls=%fused_computation.99 | loop fusion | flops 61440 | bytes 311296 | tf_op jit(solution)/shard_map/neg | solution.py:235
  39.7 1.6 %concatenate.106 = f32[6,4128]{1,0:T(8,128)} concatenate(f32[6,2048]{1,0:T(8,128)} %get-tuple-element.54, f32[6,2048]{1,0:T(8,128)} %get-tuple-element.53, f32[6,16]{1,0:T(8,128)S(1)} %slice_multiply_fusion.5, f32[6,16]{1,0:T(8,128)S(1)} %slice_multiply_fusion.4), dimensions={1} | concatenate | bytes 198144 | tf_op jit(solution)/shard_map/concatenate | solution.py:232
  41.3 1.0 %broadcast_multiply_fusion = f32[6,16,4128]{2,1,0:T(8,128)S(1)} fusion(f32[6,4128]{1,0:T(8,128)} %concatenate.106, f32[16,4128]{1,0:T(8,128)S(1)} %fusion.20), kind=kLoop, calls=%fused_computation.15 | loop fusion | flops 396288 | bytes 1948416 | tf_op jit(solution)/shard_map/mul | solution.py:130
  42.4 0.6 copy-done.31
  43.1 3.8 %fusion = f32[192,1024]{1,0:T(8,128)S(1)} fusion(s32[4128]{0:T(1024)S(1)} %copy-done.31, bf16[96,4128]{1,0:T(8,128)(2,1)S(1)} %get-tuple-element.20, bf16[96,4128]{1,0:T(8,128)(2,1)S(1)} %get-tuple-element.21), kind=kOutput, calls=%fused_computation.1 | convolution fusion | flops 1630593024 | bytes 2388096 | tf_op jit(solution)/shard_map/dot_general | solution.py:58
  48.8 13.7 %all_to_all.12 = f32[32,1,10]{2,1,0:T(1,128)S(1)} all-to-all(f32[32,1,10]{2,1,0:T(1,128)S(1)} %broadcast_in_dim.53), channel_id=1, replica_groups=mesh['cells'=8,'slab'=4] {'cells','slab'}, dimensions={0} | all-to-all | bytes 2560 | tf_op jit(solution)/shard_map/all_to_all | solution.py:36
  63.0 0.6 broadcast_in_dim.55
  63.7 2.6 %all-to-all-start.1 = ((f32[32,1,4]{2,1,0:T(1,128)}), f32[32,1,4]{2,1,0:T(1,128)S(1)}, u32[]{:S(2)}, u32[]{:S(2)}) async-start(f32[32,1,4]{2,1,0:T(1,128)} %broadcast_in_dim.55), calls=%async_computation.1 | async-start | bytes 32768 | tf_op jit(solution)/shard_map/all_to_all | solution.py:36
  66.3 0.7 pad_maximum_fusion.2
  67.1 6.3 %all-to-all-done.1 = f32[32,1,4]{2,1,0:T(1,128)S(1)} async-done(((f32[32,1,4]{2,1,0:T(1,128)}), f32[32,1,4]{2,1,0:T(1,128)S(1)}, u32[]{:S(2)}, u32[]{:S(2)}) %all-to-all-start.1) | async-done | bytes 544 | tf_op jit(solution)/shard_map/all_to_all | solution.py:36
  73.4 0.7 sqrt.8
  (177 shorter events, 7.9 us)
Async XLA Ops:
  0.6 15.5 %copy-start = (f32[2,4,16,1024]{3,2,1,0:T(8,128)S(1)}, f32[2,4,16,1024]{3,2,1,0:T(8,128)}, u32[]{:S(2)}) copy-start(f32[2,4,16,1024]{3,2,1,0:T(8,128)} %param.14) | copy-start | bytes 1572868
  0.6 15.6 %copy-start.38 = (s32[1,128]{1,0:T(1,128)S(1)}, s32[1,128]{1,0:T(1,128)}, u32[]{:S(2)}) copy-start(s32[1,128]{1,0:T(1,128)} %param.24) | copy-start | bytes 1540
  0.7 15.5 %copy-start.40 = (f32[1,128]{1,0:T(1,128)S(1)}, f32[1,128]{1,0:T(1,128)}, u32[]{:S(2)}) copy-start(f32[1,128]{1,0:T(1,128)} %param.25) | copy-start | bytes 1540
  1.6 17.3 %copy-start.12 = (f32[16,1024]{1,0:T(8,128)}, f32[16,1024]{1,0:T(8,128)S(1)}, u32[]{:S(2)}) copy-start(f32[16,1024]{1,0:T(8,128)S(1)} %broadcast_select_fusion.1) | copy-start | bytes 196612
  3.1 15.1 %collective-permute-start = (f32[2064]{0:T(1024)S(1)}, f32[2064]{0:T(1024)S(1)}, u32[]{:S(2)}, u32[]{:S(2)}) collective-permute-start(f32[2064]{0:T(1024)S(1)} %pad_maximum_fusion.9), channel_id=1, source_target_pairs={{0,4},{4,8},{8,12},{12,16},{16,20},{20,24},{24,28},{1,5},{5,9},{9,... | collective-permute-start | bytes 24776 | tf_op jit(solution)/shard_map/ppermute | solution.py:13
  9.0 9.9 %copy-start.14 = (f32[16,1024]{1,0:T(8,128)}, f32[16,1024]{1,0:T(8,128)S(1)}, u32[]{:S(2)}) copy-start(f32[16,1024]{1,0:T(8,128)S(1)} %broadcast_select_fusion) | copy-start | bytes 196612
  9.0 9.9 %collective-permute-start.1 = (f32[1024]{0:T(1024)S(1)}, f32[1024]{0:T(1024)S(1)}, u32[]{:S(2)}, u32[]{:S(2)}) collective-permute-start(f32[1024]{0:T(1024)S(1)} %bitcast.404), channel_id=1, source_target_pairs={{0,1},{1,2},{2,3},{4,5},{5,6},{6,7},{8,9},{9,10},{10,11},{12,13},{... | collective-permute-start | bytes 12296 | tf_op jit(solution)/shard_map/ppermute | solution.py:13
  12.3 6.6 %copy-start.1 = (f32[2,2,16,1024]{3,2,1,0:T(8,128)S(1)}, f32[2,2,16,1024]{3,2,1,0:T(8,128)}, u32[]{:S(2)}) copy-start(f32[2,2,16,1024]{3,2,1,0:T(8,128)} %param.13) | copy-start | bytes 786436
  12.3 6.6 %copy-start.2 = (f32[2,2,16,1024]{3,2,1,0:T(8,128)S(1)}, f32[2,2,16,1024]{3,2,1,0:T(8,128)}, u32[]{:S(2)}) copy-start(f32[2,2,16,1024]{3,2,1,0:T(8,128)} %param.15) | copy-start | bytes 786436
  12.3 6.6 %copy-start.22 = (f32[16,1024]{1,0:T(8,128)S(1)}, f32[16,1024]{1,0:T(8,128)}, u32[]{:S(2)}) copy-start(f32[16,1024]{1,0:T(8,128)} %param.17) | copy-start | bytes 196612
  12.3 6.6 %copy-start.23 = (f32[16,1024]{1,0:T(8,128)S(1)}, f32[16,1024]{1,0:T(8,128)}, u32[]{:S(2)}) copy-start(f32[16,1024]{1,0:T(8,128)} %param.18) | copy-start | bytes 196612
  27.0 11.3 %collective-permute-start.4 = (f32[6,2064]{1,0:T(8,128)S(1)}, f32[6,2064]{1,0:T(8,128)S(1)}, u32[]{:S(2)}, u32[]{:S(2)}) collective-permute-start(f32[6,2064]{1,0:T(8,128)S(1)} %pad_maximum_fusion.5), channel_id=1, source_target_pairs={{4,0},{8,4},{12,8},{16,12},{20,16},{24,20},{28,24},{5,1},{9,5},{13... | collective-permute-start | bytes 148616 | tf_op jit(solution)/shard_map/ppermute | solution.py:13
  28.3 10.0 %copy-start.33 = (f32[16]{0:T(128)S(1)}, f32[16]{0:T(128)}, u32[]{:S(2)}) copy-start(f32[16]{0:T(128)} %neg.47) | copy-start | bytes 196
  28.3 10.6 %copy-start.34 = (f32[16]{0:T(128)S(1)}, f32[16]{0:T(128)}, u32[]{:S(2)}) copy-start(f32[16]{0:T(128)} %get-tuple-element.70) | copy-start | bytes 196
  28.3 10.6 %copy-start.28 = (f32[1,2048]{1,0:T(1,128)S(1)}, f32[1,2048]{1,0:T(1,128)}, u32[]{:S(2)}) copy-start(f32[1,2048]{1,0:T(1,128)} %and_select_fusion) | copy-start | bytes 24580
  28.3 10.6 %slice-start.2 = ((f32[2064]{0:T(1024)}), f32[2048]{0:T(1024)S(1)}, s32[]{:S(2)}) async-start(f32[2064]{0:T(1024)} %copy-done.29), calls=%async_computation.4 | async-start | bytes 16384 | tf_op jit(solution)/shard_map/slice | solution.py:103
  29.0 7.9 %collective-permute-start.6 = (f32[4,16]{1,0:T(4,128)S(1)}, f32[4,16]{1,0:T(4,128)S(1)}, u32[]{:S(2)}, u32[]{:S(2)}) collective-permute-start(f32[4,16]{1,0:T(4,128)S(1)} %pad_maximum_fusion.10), channel_id=1, source_target_pairs={{0,2},{1,3},{2,0},{3,1},{4,6},{5,7},{6,4},{7,5},{8,10},{9,11},{10,... | collective-permute-start | bytes 776 | tf_op jit(solution)/shard_map/ppermute | solution.py:173
  31.0 5.9 %collective-permute-start.2 = (f32[10,1024]{1,0:T(8,128)S(1)}, f32[10,1024]{1,0:T(8,128)S(1)}, u32[]{:S(2)}, u32[]{:S(2)}) collective-permute-start(f32[10,1024]{1,0:T(8,128)S(1)} %get-tuple-element.72), channel_id=1, source_target_pairs={{0,3},{1,0},{2,1},{3,2},{4,7},{5,4},{6,5},{7,6},{8,11},{9,8},{10,9... | collective-permute-start | bytes 122888 | tf_op jit(solution)/shard_map/ppermute | solution.py:173
  32.5 4.4 %collective-permute-start.3 = (f32[10,1024]{1,0:T(8,128)S(1)}, f32[10,1024]{1,0:T(8,128)S(1)}, u32[]{:S(2)}, u32[]{:S(2)}) collective-permute-start(f32[10,1024]{1,0:T(8,128)S(1)} %get-tuple-element.73), channel_id=1, source_target_pairs={{0,1},{1,2},{2,3},{3,0},{4,5},{5,6},{6,7},{7,4},{8,9},{9,10},{10,1... | collective-permute-start | bytes 122888 | tf_op jit(solution)/shard_map/ppermute | solution.py:173
  32.6 6.3 %collective-permute-start.5 = (f32[6,2064]{1,0:T(8,128)S(1)}, f32[6,2064]{1,0:T(8,128)S(1)}, u32[]{:S(2)}, u32[]{:S(2)}) collective-permute-start(f32[6,2064]{1,0:T(8,128)S(1)} %pad_maximum_fusion.6), channel_id=1, source_target_pairs={{0,4},{4,8},{8,12},{12,16},{16,20},{20,24},{24,28},{1,5},{5,9},{9,... | collective-permute-start | bytes 148616 | tf_op jit(solution)/shard_map/ppermute | solution.py:13
  43.0 3.9 %copy-start.20 = (f32[16,1024]{1,0:T(8,128)S(1)}, f32[16,1024]{1,0:T(8,128)}, u32[]{:S(2)}) copy-start(f32[16,1024]{1,0:T(8,128)} %get-tuple-element.28) | copy-start | bytes 196612
  43.0 3.9 %copy-start.21 = (f32[16,1024]{1,0:T(8,128)S(1)}, f32[16,1024]{1,0:T(8,128)}, u32[]{:S(2)}) copy-start(f32[16,1024]{1,0:T(8,128)} %get-tuple-element.29) | copy-start | bytes 196612
  43.0 3.9 %slice-start = ((f32[10,1024]{1,0:T(8,128)}), f32[6,1024]{1,0:T(8,128)S(1)}, s32[]{:S(2)}) async-start(f32[10,1024]{1,0:T(8,128)} %copy-done.26), calls=%async_computation.2 | async-start | bytes 65536 | tf_op jit(solution)/shard_map/slice | solution.py:209
  43.0 3.9 %slice-start.1 = ((f32[10,1024]{1,0:T(8,128)}), f32[6,1024]{1,0:T(8,128)S(1)}, s32[]{:S(2)}) async-start(f32[10,1024]{1,0:T(8,128)} %copy-done.27), calls=%async_computation.3 | async-start | bytes 65536 | tf_op jit(solution)/shard_map/slice | solution.py:208
  43.1 3.9 %copy-start.36 = (pred[16]{0:T(512)(128)(4,1)S(1)}, pred[16]{0:T(512)(128)(4,1)}, u32[]{:S(2)}) copy-start(pred[16]{0:T(512)(128)(4,1)} %get-tuple-element.78) | copy-start | bytes 52
  47.8 14.8 %copy-start.8 = (f32[16,1024]{1,0:T(8,128)S(1)}, f32[16,1024]{1,0:T(8,128)}, u32[]{:S(2)}) copy-start(f32[16,1024]{1,0:T(8,128)} %copy-done.7) | copy-start | bytes 196612
  47.8 14.8 %copy-start.10 = (f32[16,1024]{1,0:T(8,128)S(1)}, f32[16,1024]{1,0:T(8,128)}, u32[]{:S(2)}) copy-start(f32[16,1024]{1,0:T(8,128)} %copy-done.9) | copy-start | bytes 196612
  47.8 14.8 %copy-start.25 = (f32[2,2,16,1024]{3,2,1,0:T(8,128)S(1)}, f32[2,2,16,1024]{3,2,1,0:T(8,128)}, u32[]{:S(2)}) copy-start(f32[2,2,16,1024]{3,2,1,0:T(8,128)} %param.16) | copy-start | bytes 786436
  48.0 18.2 %copy-start.6 = (f32[16,1024]{1,0:T(8,128)S(1)}, f32[16,1024]{1,0:T(8,128)}, u32[]{:S(2)}) copy-start(f32[16,1024]{1,0:T(8,128)} %copy-done.5) | copy-start | bytes 196612
  48.0 18.2 %copy-start.17 = (f32[16,1024]{1,0:T(8,128)S(1)}, f32[16,1024]{1,0:T(8,128)}, u32[]{:S(2)}) copy-start(f32[16,1024]{1,0:T(8,128)} %copy-done.16) | copy-start | bytes 196612
  48.0 18.2 %copy-start.19 = (f32[16,1024]{1,0:T(8,128)S(1)}, f32[16,1024]{1,0:T(8,128)}, u32[]{:S(2)}) copy-start(f32[16,1024]{1,0:T(8,128)} %copy-done.18) | copy-start | bytes 196612
  63.7 9.7 %all-to-all-start.1 = ((f32[32,1,4]{2,1,0:T(1,128)}), f32[32,1,4]{2,1,0:T(1,128)S(1)}, u32[]{:S(2)}, u32[]{:S(2)}) async-start(f32[32,1,4]{2,1,0:T(1,128)} %broadcast_in_dim.55), calls=%async_computation.1 | async-start | bytes 32768 | tf_op jit(solution)/shard_map/all_to_all | solution.py:36
  (21 other events, 43.1 us)

commit v19 on v18

--- a/solution.py
+++ b/solution.py
@@ -178,8 +178,8 @@
         picks = gather(scaled, fault_at, split2)
         picks_near = picks[:, :slot_count]
         picks_far = picks[:, slot_count : 2 * slot_count]
-        from_left = shifted(jnp.concatenate([scaled[:, :, -1], picks_near], axis=1), "cells", 1)
-        from_right = shifted(jnp.concatenate([scaled[:, :, 0], picks_far], axis=1), "cells", -1)
+        from_left = shifted(jnp.concatenate([picks_near, scaled[:, :, -1]], axis=1), "cells", 1)
+        from_right = shifted(jnp.concatenate([picks_far, scaled[:, :, 0]], axis=1), "cells", -1)
         pressure = fields[:, 0]
         values = gather(pressure, well_at)
         local = jnp.concatenate(
@@ -226,15 +226,15 @@
             + trans_down * (scaled - below)
             + trans_up * (scaled - above)
         )
-        flux_right = weight_here * (picks_near - from_right[:, layer_count:])
-        flux_left = weight_left * (from_left[:, layer_count:] - picks_far)
+        flux_right = weight_here * (picks_near - from_right[:, :slot_count])
+        flux_left = weight_left * (from_left[:, :slot_count] - picks_far)
         fault_term = scatter(
             jnp.concatenate(
                 [
                     flux_right,
                     -flux_left,
-                    -west_face * from_left[:, :layer_count],
-                    -east_face * from_right[:, :layer_count],
+                    -west_face * from_left[:, slot_count:],
+                    -east_face * from_right[:, slot_count:],
                 ],
                 axis=1,
             ),

time: 74.7 us -> 74.5 us (level)
  no operation moved by 1% of the time
where the time goes in v19:
time: 74.5 us; the launch traced here: 73.9 us
  starting transfers between devices  18 us (24%)
  other arithmetic  14.6 us (20%)
  blocking collectives  13.7 us (18%)
  matrix products  9.91 us (13%)
  local copies, waits for them, and re-layouts  8.49 us (11%)
  waiting for transfers between devices  6.91 us (9%)
  between operations  2.32 us (3%)
    all_to_all x1, blocking collectives, global_sum(): gathered = lax.all_to_all(copies, axes, 0, 0, tiled=True)  13.7 us
    ppermute x4, starting transfers between devices, shifted(): return lax.ppermute(value, axis, pairs)  11.9 us
    dot_general x4, matrix products, onehot_dot(): lax.dot_general(pieces, onehot, (dims, ((), ())), preferred_element_type=...  8.72 us
    all_to_all x1, waiting for transfers between devices, global_sum(): gathered = lax.all_to_all(copies, axes, 0, 0, tiled=True)  6.31 us
    ppermute x3, starting transfers between devices, slab_shift(): lax.ppermute(value, 'slab', [(i, (i + by) % count) for i in range(count)])  3.53 us
    all_to_all x1, starting transfers between devices, global_sum(): gathered = lax.all_to_all(copies, axes, 0, 0, tiled=True)  2.56 us
    select_n x2, other arithmetic, per_device(): weight_here = jnp.where(slot_live, fault_trans.reshape(-1), zero_value)  2.02 us
    unnamed x99, local copies, waits for them, and re-layouts  1.88 us
  transfers between devices with their start and end apart: 8, of which 2 were waited for; matrix products, arithmetic and copies ran while one was open for 16% of the time, Pallas kernels for 0%

profile of v19, /device:TPU:0, one launch (start us, length us, event | category | flops | bytes accessed | tf_op | source)
XLA Modules:
  0.0 73.9 jit_solution(10149910647081059285)
XLA Ops:
  0.7 0.9 %broadcast_select_fusion.1 = f32[16,1024]{1,0:T(8,128)S(1)} fusion(f32[16,1024]{1,0:T(8,128)} %param.17, pred[1024]{0:T(1024)(128)(4,1)S(1)} %fusion.73), kind=kLoop, calls=%fused_computation.162 | loop fusion | flops 16384 | bytes 132096 | tf_op jit(solution)/shard_map/jit(_where)/select_n | solution.py:91
  2.4 0.7 fusion.71
  3.1 4.9 %collective-permute-start = (f32[2064]{0:T(1024)S(1)}, f32[2064]{0:T(1024)S(1)}, u32[]{:S(2)}, u32[]{:S(2)}) collective-permute-start(f32[2064]{0:T(1024)S(1)} %pad_maximum_fusion.9), channel_id=1, source_target_pairs={{0,4},{4,8},{8,12},{12,16},{16,20},{20,24},{24,28},{1,5},{5,9},{9,... | collective-permute-start | bytes 24776 | tf_op jit(solution)/shard_map/ppermute | solution.py:13
  8.0 0.9 %broadcast_select_fusion = f32[16,1024]{1,0:T(8,128)S(1)} fusion(f32[16,1024]{1,0:T(8,128)} %param.18, pred[16]{0:T(512)(128)(4,1)S(1)} %broadcast_and_fusion), kind=kLoop, calls=%fused_computation.161 | loop fusion | flops 16384 | bytes 131088 | tf_op jit(solution)/shard_map/jit(_where)/select_n | solution.py:94
  9.0 1.5 %collective-permute-start.1 = (f32[1024]{0:T(1024)S(1)}, f32[1024]{0:T(1024)S(1)}, u32[]{:S(2)}, u32[]{:S(2)}) collective-permute-start(f32[1024]{0:T(1024)S(1)} %bitcast.404), channel_id=1, source_target_pairs={{0,1},{1,2},{2,3},{4,5},{5,6},{6,7},{8,9},{9,10},{10,11},{12,13},{... | collective-permute-start | bytes 12296 | tf_op jit(solution)/shard_map/ppermute | solution.py:13
  10.4 1.2 %and_select_fusion.2 = s32[128]{0:T(128)} fusion(s32[1,128]{1,0:T(1,128)} %param.23), kind=kLoop, calls=%fused_computation.203 | loop fusion | flops 1408 | bytes 1024 | tf_op jit(solution)/shard_map/jit(remainder)/select_n | solution.py:115
  11.6 0.7 fusion.80
  12.3 1.0 %fusion.96 = (f32[1,2,16,1024]{3,2,1,0:T(8,128)S(1)}, f32[1,2,16,1024]{3,2,1,0:T(8,128)S(1)}) fusion(f32[2,2,16,1024]{3,2,1,0:T(8,128)} %param.15), kind=kLoop, calls=%fused_computation.230 | loop fusion | bytes 524288 | tf_op jit(solution)/shard_map/slice | solution.py:150
  13.4 0.8 %concatenate.103 = s32[4128]{0:T(1024)S(1)} concatenate(s32[2048]{0:T(1024)} %bitcast.401, s32[2048]{0:T(1024)} %bitcast.402, s32[16]{0:T(128)S(1)} %get-tuple-element.76, s32[16]{0:T(128)S(1)} %get-tuple-element.77), dimensions={0} | concatenate | bytes 33024 | tf_op jit(solution)/shard_map/concatenate | solution.py:138
  14.2 0.6 add_select_fusion
  14.8 1.3 %and_select_fusion = f32[1,2048]{1,0:T(1,128)} fusion(f32[1,2048]{1,0:T(1,128)} %param.21, pred[]{:T(512)S(6)} %lt.34, s32[]{:T(128)} %bitcast.343), kind=kLoop, calls=%fused_computation.163 | loop fusion | flops 6144 | bytes 16389 | tf_op jit(solution)/shard_map/jit(_where)/select_n | solution.py:101
  16.2 0.8 %fusion.58 = f32[1,16]{1,0:T(1,128)} fusion(s32[128]{0:T(128)S(1)} %bitcast.405, f32[1,128]{1,0:T(1,128)S(1)} %copy-done.40), kind=kOutput, calls=%fused_computation.144 | convolution fusion | flops 26624 | bytes 1088 | tf_op jit(solution)/shard_map/dot_general | solution.py:187
  18.9 0.7 fusion.45
  21.1 1.0 %fusion.95 = (f32[6,15,1024]{2,1,0:T(8,128)}, f32[6,15,1024]{2,1,0:T(8,128)}) fusion(f32[6,16,1024]{2,1,0:T(8,128)S(1)} %bitcast.347), kind=kLoop, calls=%fused_computation.229 | loop fusion | bytes 1474560 | tf_op jit(solution)/shard_map/slice | solution.py:221
  22.0 4.3 %fusion.1 = f32[192,4128]{1,0:T(8,128)S(1)} fusion(s32[4128]{0:T(1024)S(1)} %copy-done.30, bf16[96,1024]{1,0:T(8,128)(2,1)S(1)} %get-tuple-element.22, bf16[96,1024]{1,0:T(8,128)(2,1)S(1)} %get-tuple-element.23), kind=kOutput, calls=%fused_computation.2 | convolution fusion | flops 1628209152 | bytes 3580032 | tf_op jit(solution)/shard_map/dot_general | solution.py:58
  26.9 1.3 %collective-permute-start.4 = (f32[6,2064]{1,0:T(8,128)S(1)}, f32[6,2064]{1,0:T(8,128)S(1)}, u32[]{:S(2)}, u32[]{:S(2)}) collective-permute-start(f32[6,2064]{1,0:T(8,128)S(1)} %pad_maximum_fusion.5), channel_id=1, source_target_pairs={{4,0},{8,4},{12,8},{16,12},{20,16},{24,20},{28,24},{5,1},{9,5},{13... | collective-permute-start | bytes 148616 | tf_op jit(solution)/shard_map/ppermute | solution.py:13
  28.9 2.0 %collective-permute-start.6 = (f32[4,16]{1,0:T(4,128)S(1)}, f32[4,16]{1,0:T(4,128)S(1)}, u32[]{:S(2)}, u32[]{:S(2)}) collective-permute-start(f32[4,16]{1,0:T(4,128)S(1)} %pad_maximum_fusion.10), channel_id=1, source_target_pairs={{0,2},{1,3},{2,0},{3,1},{4,6},{5,7},{6,4},{7,5},{8,10},{9,11},{10,... | collective-permute-start | bytes 776 | tf_op jit(solution)/shard_map/ppermute | solution.py:173
  31.0 1.5 %collective-permute-start.2 = (f32[10,1024]{1,0:T(8,128)S(1)}, f32[10,1024]{1,0:T(8,128)S(1)}, u32[]{:S(2)}, u32[]{:S(2)}) collective-permute-start(f32[10,1024]{1,0:T(8,128)S(1)} %get-tuple-element.72), channel_id=1, source_target_pairs={{0,3},{1,0},{2,1},{3,2},{4,7},{5,4},{6,5},{7,6},{8,11},{9,8},{10,9... | collective-permute-start | bytes 122888 | tf_op jit(solution)/shard_map/ppermute | solution.py:173
  32.5 4.3 %collective-permute-start.5 = (f32[6,2064]{1,0:T(8,128)S(1)}, f32[6,2064]{1,0:T(8,128)S(1)}, u32[]{:S(2)}, u32[]{:S(2)}) collective-permute-start(f32[6,2064]{1,0:T(8,128)S(1)} %pad_maximum_fusion.6), channel_id=1, source_target_pairs={{0,4},{4,8},{8,12},{12,16},{16,20},{20,24},{24,28},{1,5},{5,9},{9,... | collective-permute-start | bytes 148616 | tf_op jit(solution)/shard_map/ppermute | solution.py:13
  37.5 0.7 slice_add_fusion.3
  38.2 0.6 collective-permute-done.5
  38.8 0.7 fusion.40
  39.5 1.6 %concatenate.106 = f32[6,4128]{1,0:T(8,128)} concatenate(f32[6,2048]{1,0:T(8,128)} %get-tuple-element.54, f32[6,2048]{1,0:T(8,128)} %get-tuple-element.53, f32[6,16]{1,0:T(8,128)S(1)} %slice_multiply_fusion.5, f32[6,16]{1,0:T(8,128)S(1)} %slice_multiply_fusion.4), dimensions={1} | concatenate | bytes 198144 | tf_op jit(solution)/shard_map/concatenate | solution.py:232
  41.1 1.0 %broadcast_multiply_fusion = f32[6,16,4128]{2,1,0:T(8,128)S(1)} fusion(f32[6,4128]{1,0:T(8,128)} %concatenate.106, f32[16,4128]{1,0:T(8,128)S(1)} %fusion.20), kind=kLoop, calls=%fused_computation.15 | loop fusion | flops 396288 | bytes 1948416 | tf_op jit(solution)/shard_map/mul | solution.py:130
  42.2 0.6 copy-done.31
  42.9 3.8 %fusion = f32[192,1024]{1,0:T(8,128)S(1)} fusion(s32[4128]{0:T(1024)S(1)} %copy-done.31, bf16[96,4128]{1,0:T(8,128)(2,1)S(1)} %get-tuple-element.20, bf16[96,4128]{1,0:T(8,128)(2,1)S(1)} %get-tuple-element.21), kind=kOutput, calls=%fused_computation.1 | convolution fusion | flops 1630593024 | bytes 2388096 | tf_op jit(solution)/shard_map/dot_general | solution.py:58
  48.6 13.7 %all_to_all.12 = f32[32,1,10]{2,1,0:T(1,128)S(1)} all-to-all(f32[32,1,10]{2,1,0:T(1,128)S(1)} %broadcast_in_dim.53), channel_id=1, replica_groups=mesh['cells'=8,'slab'=4] {'cells','slab'}, dimensions={0} | all-to-all | bytes 2560 | tf_op jit(solution)/shard_map/all_to_all | solution.py:36
  62.8 0.6 broadcast_in_dim.55
  63.4 2.6 %all-to-all-start.1 = ((f32[32,1,4]{2,1,0:T(1,128)}), f32[32,1,4]{2,1,0:T(1,128)S(1)}, u32[]{:S(2)}, u32[]{:S(2)}) async-start(f32[32,1,4]{2,1,0:T(1,128)} %broadcast_in_dim.55), calls=%async_computation.1 | async-start | bytes 32768 | tf_op jit(solution)/shard_map/all_to_all | solution.py:36
  66.1 0.7 pad_maximum_fusion.2
  66.9 6.3 %all-to-all-done.1 = f32[32,1,4]{2,1,0:T(1,128)S(1)} async-done(((f32[32,1,4]{2,1,0:T(1,128)}), f32[32,1,4]{2,1,0:T(1,128)S(1)}, u32[]{:S(2)}, u32[]{:S(2)}) %all-to-all-start.1) | async-done | bytes 544 | tf_op jit(solution)/shard_map/all_to_all | solution.py:36
  73.2 0.7 sqrt.8
  (177 shorter events, 7.7 us)
Async XLA Ops:
  0.6 15.5 %copy-start = (f32[2,4,16,1024]{3,2,1,0:T(8,128)S(1)}, f32[2,4,16,1024]{3,2,1,0:T(8,128)}, u32[]{:S(2)}) copy-start(f32[2,4,16,1024]{3,2,1,0:T(8,128)} %param.14) | copy-start | bytes 1572868
  0.6 15.6 %copy-start.38 = (s32[1,128]{1,0:T(1,128)S(1)}, s32[1,128]{1,0:T(1,128)}, u32[]{:S(2)}) copy-start(s32[1,128]{1,0:T(1,128)} %param.24) | copy-start | bytes 1540
  0.7 15.5 %copy-start.40 = (f32[1,128]{1,0:T(1,128)S(1)}, f32[1,128]{1,0:T(1,128)}, u32[]{:S(2)}) copy-start(f32[1,128]{1,0:T(1,128)} %param.25) | copy-start | bytes 1540
  1.6 17.3 %copy-start.12 = (f32[16,1024]{1,0:T(8,128)}, f32[16,1024]{1,0:T(8,128)S(1)}, u32[]{:S(2)}) copy-start(f32[16,1024]{1,0:T(8,128)S(1)} %broadcast_select_fusion.1) | copy-start | bytes 196612
  3.1 15.1 %collective-permute-start = (f32[2064]{0:T(1024)S(1)}, f32[2064]{0:T(1024)S(1)}, u32[]{:S(2)}, u32[]{:S(2)}) collective-permute-start(f32[2064]{0:T(1024)S(1)} %pad_maximum_fusion.9), channel_id=1, source_target_pairs={{0,4},{4,8},{8,12},{12,16},{16,20},{20,24},{24,28},{1,5},{5,9},{9,... | collective-permute-start | bytes 24776 | tf_op jit(solution)/shard_map/ppermute | solution.py:13
  9.0 9.9 %copy-start.14 = (f32[16,1024]{1,0:T(8,128)}, f32[16,1024]{1,0:T(8,128)S(1)}, u32[]{:S(2)}) copy-start(f32[16,1024]{1,0:T(8,128)S(1)} %broadcast_select_fusion) | copy-start | bytes 196612
  9.0 9.9 %collective-permute-start.1 = (f32[1024]{0:T(1024)S(1)}, f32[1024]{0:T(1024)S(1)}, u32[]{:S(2)}, u32[]{:S(2)}) collective-permute-start(f32[1024]{0:T(1024)S(1)} %bitcast.404), channel_id=1, source_target_pairs={{0,1},{1,2},{2,3},{4,5},{5,6},{6,7},{8,9},{9,10},{10,11},{12,13},{... | collective-permute-start | bytes 12296 | tf_op jit(solution)/shard_map/ppermute | solution.py:13
  12.3 6.6 %copy-start.1 = (f32[2,2,16,1024]{3,2,1,0:T(8,128)S(1)}, f32[2,2,16,1024]{3,2,1,0:T(8,128)}, u32[]{:S(2)}) copy-start(f32[2,2,16,1024]{3,2,1,0:T(8,128)} %param.13) | copy-start | bytes 786436
  12.3 6.6 %copy-start.2 = (f32[2,2,16,1024]{3,2,1,0:T(8,128)S(1)}, f32[2,2,16,1024]{3,2,1,0:T(8,128)}, u32[]{:S(2)}) copy-start(f32[2,2,16,1024]{3,2,1,0:T(8,128)} %param.15) | copy-start | bytes 786436
  12.3 6.6 %copy-start.22 = (f32[16,1024]{1,0:T(8,128)S(1)}, f32[16,1024]{1,0:T(8,128)}, u32[]{:S(2)}) copy-start(f32[16,1024]{1,0:T(8,128)} %param.17) | copy-start | bytes 196612
  12.3 6.6 %copy-start.23 = (f32[16,1024]{1,0:T(8,128)S(1)}, f32[16,1024]{1,0:T(8,128)}, u32[]{:S(2)}) copy-start(f32[16,1024]{1,0:T(8,128)} %param.18) | copy-start | bytes 196612
  26.9 11.3 %collective-permute-start.4 = (f32[6,2064]{1,0:T(8,128)S(1)}, f32[6,2064]{1,0:T(8,128)S(1)}, u32[]{:S(2)}, u32[]{:S(2)}) collective-permute-start(f32[6,2064]{1,0:T(8,128)S(1)} %pad_maximum_fusion.5), channel_id=1, source_target_pairs={{4,0},{8,4},{12,8},{16,12},{20,16},{24,20},{28,24},{5,1},{9,5},{13... | collective-permute-start | bytes 148616 | tf_op jit(solution)/shard_map/ppermute | solution.py:13
  28.2 10.0 %copy-start.33 = (f32[16]{0:T(128)S(1)}, f32[16]{0:T(128)}, u32[]{:S(2)}) copy-start(f32[16]{0:T(128)} %neg.47) | copy-start | bytes 196
  28.2 10.5 %copy-start.34 = (f32[16]{0:T(128)S(1)}, f32[16]{0:T(128)}, u32[]{:S(2)}) copy-start(f32[16]{0:T(128)} %get-tuple-element.70) | copy-start | bytes 196
  28.2 10.5 %copy-start.28 = (f32[1,2048]{1,0:T(1,128)S(1)}, f32[1,2048]{1,0:T(1,128)}, u32[]{:S(2)}) copy-start(f32[1,2048]{1,0:T(1,128)} %and_select_fusion) | copy-start | bytes 24580
  28.3 10.5 %slice-start.2 = ((f32[2064]{0:T(1024)}), f32[2048]{0:T(1024)S(1)}, s32[]{:S(2)}) async-start(f32[2064]{0:T(1024)} %copy-done.29), calls=%async_computation.4 | async-start | bytes 16384 | tf_op jit(solution)/shard_map/slice | solution.py:103
  28.9 7.8 %collective-permute-start.6 = (f32[4,16]{1,0:T(4,128)S(1)}, f32[4,16]{1,0:T(4,128)S(1)}, u32[]{:S(2)}, u32[]{:S(2)}) collective-permute-start(f32[4,16]{1,0:T(4,128)S(1)} %pad_maximum_fusion.10), channel_id=1, source_target_pairs={{0,2},{1,3},{2,0},{3,1},{4,6},{5,7},{6,4},{7,5},{8,10},{9,11},{10,... | collective-permute-start | bytes 776 | tf_op jit(solution)/shard_map/ppermute | solution.py:173
  31.0 5.8 %collective-permute-start.2 = (f32[10,1024]{1,0:T(8,128)S(1)}, f32[10,1024]{1,0:T(8,128)S(1)}, u32[]{:S(2)}, u32[]{:S(2)}) collective-permute-start(f32[10,1024]{1,0:T(8,128)S(1)} %get-tuple-element.72), channel_id=1, source_target_pairs={{0,3},{1,0},{2,1},{3,2},{4,7},{5,4},{6,5},{7,6},{8,11},{9,8},{10,9... | collective-permute-start | bytes 122888 | tf_op jit(solution)/shard_map/ppermute | solution.py:173
  32.5 4.3 %collective-permute-start.3 = (f32[10,1024]{1,0:T(8,128)S(1)}, f32[10,1024]{1,0:T(8,128)S(1)}, u32[]{:S(2)}, u32[]{:S(2)}) collective-permute-start(f32[10,1024]{1,0:T(8,128)S(1)} %get-tuple-element.73), channel_id=1, source_target_pairs={{0,1},{1,2},{2,3},{3,0},{4,5},{5,6},{6,7},{7,4},{8,9},{9,10},{10,1... | collective-permute-start | bytes 122888 | tf_op jit(solution)/shard_map/ppermute | solution.py:173
  32.5 6.3 %collective-permute-start.5 = (f32[6,2064]{1,0:T(8,128)S(1)}, f32[6,2064]{1,0:T(8,128)S(1)}, u32[]{:S(2)}, u32[]{:S(2)}) collective-permute-start(f32[6,2064]{1,0:T(8,128)S(1)} %pad_maximum_fusion.6), channel_id=1, source_target_pairs={{0,4},{4,8},{8,12},{12,16},{16,20},{20,24},{24,28},{1,5},{5,9},{9,... | collective-permute-start | bytes 148616 | tf_op jit(solution)/shard_map/ppermute | solution.py:13
  42.8 3.9 %copy-start.20 = (f32[16,1024]{1,0:T(8,128)S(1)}, f32[16,1024]{1,0:T(8,128)}, u32[]{:S(2)}) copy-start(f32[16,1024]{1,0:T(8,128)} %get-tuple-element.28) | copy-start | bytes 196612
  42.8 3.9 %copy-start.21 = (f32[16,1024]{1,0:T(8,128)S(1)}, f32[16,1024]{1,0:T(8,128)}, u32[]{:S(2)}) copy-start(f32[16,1024]{1,0:T(8,128)} %get-tuple-element.29) | copy-start | bytes 196612
  42.8 3.9 %slice-start = ((f32[10,1024]{1,0:T(8,128)}), f32[6,1024]{1,0:T(8,128)S(1)}, s32[]{:S(2)}) async-start(f32[10,1024]{1,0:T(8,128)} %copy-done.26), calls=%async_computation.2 | async-start | bytes 65536 | tf_op jit(solution)/shard_map/slice | solution.py:209
  42.8 3.9 %slice-start.1 = ((f32[10,1024]{1,0:T(8,128)}), f32[6,1024]{1,0:T(8,128)S(1)}, s32[]{:S(2)}) async-start(f32[10,1024]{1,0:T(8,128)} %copy-done.27), calls=%async_computation.3 | async-start | bytes 65536 | tf_op jit(solution)/shard_map/slice | solution.py:208
  42.9 3.9 %copy-start.36 = (pred[16]{0:T(512)(128)(4,1)S(1)}, pred[16]{0:T(512)(128)(4,1)}, u32[]{:S(2)}) copy-start(pred[16]{0:T(512)(128)(4,1)} %get-tuple-element.78) | copy-start | bytes 52
  47.6 14.8 %copy-start.8 = (f32[16,1024]{1,0:T(8,128)S(1)}, f32[16,1024]{1,0:T(8,128)}, u32[]{:S(2)}) copy-start(f32[16,1024]{1,0:T(8,128)} %copy-done.7) | copy-start | bytes 196612
  47.6 14.8 %copy-start.10 = (f32[16,1024]{1,0:T(8,128)S(1)}, f32[16,1024]{1,0:T(8,128)}, u32[]{:S(2)}) copy-start(f32[16,1024]{1,0:T(8,128)} %copy-done.9) | copy-start | bytes 196612
  47.6 14.8 %copy-start.25 = (f32[2,2,16,1024]{3,2,1,0:T(8,128)S(1)}, f32[2,2,16,1024]{3,2,1,0:T(8,128)}, u32[]{:S(2)}) copy-start(f32[2,2,16,1024]{3,2,1,0:T(8,128)} %param.16) | copy-start | bytes 786436
  47.8 18.2 %copy-start.6 = (f32[16,1024]{1,0:T(8,128)S(1)}, f32[16,1024]{1,0:T(8,128)}, u32[]{:S(2)}) copy-start(f32[16,1024]{1,0:T(8,128)} %copy-done.5) | copy-start | bytes 196612
  47.8 18.2 %copy-start.17 = (f32[16,1024]{1,0:T(8,128)S(1)}, f32[16,1024]{1,0:T(8,128)}, u32[]{:S(2)}) copy-start(f32[16,1024]{1,0:T(8,128)} %copy-done.16) | copy-start | bytes 196612
  47.8 18.2 %copy-start.19 = (f32[16,1024]{1,0:T(8,128)S(1)}, f32[16,1024]{1,0:T(8,128)}, u32[]{:S(2)}) copy-start(f32[16,1024]{1,0:T(8,128)} %copy-done.18) | copy-start | bytes 196612
  63.4 9.7 %all-to-all-start.1 = ((f32[32,1,4]{2,1,0:T(1,128)}), f32[32,1,4]{2,1,0:T(1,128)S(1)}, u32[]{:S(2)}, u32[]{:S(2)}) async-start(f32[32,1,4]{2,1,0:T(1,128)} %broadcast_in_dim.55), calls=%async_computation.1 | async-start | bytes 32768 | tf_op jit(solution)/shard_map/all_to_all | solution.py:36
  (21 other events, 42.7 us)
